TPU v7x, 32 devices: a whole 2x2x4 slice. The times are simulated.
32 devices in a mesh: band: 2 (over y), domain: 16 (over z, x, core).
Axes of the slice: x: 2, y: 2, z: 4, core: 2. Of those that a mesh axis runs over, the one named last changes fastest.
Arguments:
- orbitals: bfloat16 [128, 16, 32, 256], P('domain', None, None, 'band'), may hold values from -12 to 12
- potential: float32 [128, 16, 32], P('domain'), may hold values from -2 to 0
Outputs:
- filtered: bfloat16 [128, 16, 32, 256], P('domain', None, None, 'band')
- correlation: float32 [256, 256], P('band')
- projected: float32 [256, 256], P('band')
All inputs are finite; a program needn't handle non-finite values.
Results may differ from a plain program's by a relative error of at most 0.005.
Values may be sent and summed in bfloat16 or wider, within the bound.
No kernel may reach another device: no remote copies, remote signals or barrier semaphores. Data moves between devices by JAX's collectives and lax.ppermute only.
A program may use at most 64 MiB of HBM per device.

v0:
```python
import jax
import jax.numpy as jnp
from jax import lax
from jax.sharding import PartitionSpec as P

RADIUS = 4


stencil_weights = (-205.0 / 72.0, 8.0 / 5.0, -1.0 / 5.0, 8.0 / 315.0, -1.0 / 560.0)
spectrum_centre = 6.0
first_factor = -0.125
second_factor = -1.0 / 7.0
memory_factor = -1.0 / 7.0


def padded(block, sides, width):
    for axis, dim in sides:
        count = lax.axis_size(axis)
        forward = [(i, i + 1) for i in range(count - 1)]
        forward.append((count - 1, 0))
        backward = [(target, source) for source, target in forward]
        low = lax.ppermute(
            lax.slice_in_dim(block, block.shape[dim] - width, None, axis=dim), axis, forward
        )
        high = lax.ppermute(lax.slice_in_dim(block, 0, width, axis=dim), axis, backward)
        block = jnp.concatenate([low, block, high], axis=dim)
    return block


def planes_of(extended, first_plane, planes):
    return lax.slice_in_dim(extended, first_plane, first_plane + planes, axis=0)


def hamiltonian(extended, potential, planes):
    middle = planes_of(extended, RADIUS, planes)
    summed = 3.0 * stencil_weights[0] * middle
    for offset in range(1, RADIUS + 1):
        beside = planes_of(extended, RADIUS + offset, planes) + planes_of(
            extended, RADIUS - offset, planes
        )
        beside = beside + jnp.roll(middle, offset, axis=1) + jnp.roll(middle, -offset, axis=1)
        beside = beside + jnp.roll(middle, offset, axis=2) + jnp.roll(middle, -offset, axis=2)
        summed = summed + stencil_weights[offset] * beside
    return -0.5 * summed + potential[:, :, :, None] * middle


def widened(values):
    return padded(values, (("domain", 0),), RADIUS)


def energy_block(filtered, potential, cell_count):
    extended = padded(filtered, (("domain", 0),), RADIUS).astype(jnp.float32)
    applied = hamiltonian(extended, potential, filtered.shape[0]).astype(jnp.bfloat16)
    return applied.reshape(cell_count, filtered.shape[3])


def shards(orbitals, potential):
    planes = orbitals.shape[0]
    initial = orbitals.astype(jnp.float32)
    extended = widened(orbitals).astype(jnp.float32)
    first = (
        (hamiltonian(extended, potential, planes) - spectrum_centre * initial) * first_factor
    ).astype(jnp.bfloat16)
    first_wide = widened(first).astype(jnp.float32)
    first_own = planes_of(first_wide, RADIUS, planes)
    filtered = (
        (hamiltonian(first_wide, potential, planes) - spectrum_centre * first_own) * second_factor
        + memory_factor * initial
    ).astype(jnp.bfloat16)
    cell_count = planes * filtered.shape[1] * filtered.shape[2]
    cell_weight = 1.0 / (cell_count * lax.axis_size("domain"))
    own_block = filtered.reshape(cell_count, filtered.shape[3])
    applied = energy_block(filtered, potential, cell_count)
    piece = lax.all_gather(own_block, "band", axis=1, tiled=True)
    correlation_piece = jnp.einsum(
        "cb,ck->bk", own_block, piece, preferred_element_type=jnp.float32
    )
    energy_piece = jnp.einsum("cb,ck->bk", applied, piece, preferred_element_type=jnp.float32)
    partial_terms = jnp.stack((correlation_piece, energy_piece))
    summed = lax.psum(partial_terms, "domain") * cell_weight
    correlation = summed[0]
    projected = summed[1]
    return (filtered, correlation, projected)


def solution(mesh):
    placed = (P("domain", None, None, "band"), P("domain", None, None))
    return jax.shard_map(
        shards,
        mesh=mesh,
        in_specs=placed,
        out_specs=(P("domain", None, None, "band"), P("band", None), P("band", None)),
        check_vma=False,
    )
```

profile of v0, /device:TPU:0, one launch (start us, length us, event | category | flops | bytes accessed | tf_op | source)
XLA Modules:
  0.0 240.0 jit_solution(3765272262205652214)
XLA Ops:
  7.2 1.3 fusion.132
  8.6 5.5 %collective-permute-start.1 = (bf16[4,16,32,128]{3,2,1,0:T(8,128)(2,1)S(1)}, bf16[4,16,32,128]{3,2,1,0:T(8,128)(2,1)S(1)}, u32[]{:S(2)}, u32[]{:S(2)}) collective-permute-start(bf16[4,16,32,128]{3,2,1,0:T(8,128)(2,1)S(1)} %get-tuple-element.104), channel_id=1, source_target_pairs={{1,0},{2,1},{3,2},{4,3},{5,4},{6,5},{7,6},{8,7},{9,8},{10,9},{11,1... | collective-permute-start | bytes 1572872 | tf_op jit(solution)/shard_map/ppermute | solution.py:25
  14.0 6.7 %collective-permute-done.1 = bf16[4,16,32,128]{3,2,1,0:T(8,128)(2,1)S(1)} collective-permute-done((bf16[4,16,32,128]{3,2,1,0:T(8,128)(2,1)S(1)}, bf16[4,16,32,128]{3,2,1,0:T(8,128)(2,1)S(1)}, u32[]{:S(2)}, u32[]{:S(2)}) %collective-permute-start.1) | collective-permute-done | bytes 524320 | tf_op jit(solution)/shard_map/ppermute | solution.py:25
  20.7 4.6 %collective-permute-done = bf16[4,16,32,128]{3,2,1,0:T(8,128)(2,1)S(1)} collective-permute-done((bf16[4,16,32,128]{3,2,1,0:T(8,128)(2,1)S(1)}, bf16[4,16,32,128]{3,2,1,0:T(8,128)(2,1)S(1)}, u32[]{:S(2)}, u32[]{:S(2)}) %collective-permute-start) | collective-permute-done | bytes 524320 | tf_op jit(solution)/shard_map/ppermute | solution.py:22
  25.7 2.5 %fusion.128 = (f32[8,15,32,128]{3,2,1,0:T(8,128)}, f32[8,15,32,128]{3,2,1,0:T(8,128)}) fusion(f32[16,16,32,128]{3,2,1,0:T(8,128)S(1)} %maximum_convert_fusion), kind=kLoop, calls=%fused_computation.157 | loop fusion | bytes 7864320 | tf_op jit(solution)/shard_map/jit(_roll_static)/slice | solution.py:41
  29.5 2.4 fusion.125
  34.2 2.2 fusion.121
  37.8 0.9 fusion.120
  38.8 2.1 fusion.117
  43.9 10.1 %fusion.2 = bf16[8,16,32,128]{3,2,1,0:T(8,128)(2,1)S(1)} fusion(bf16[8,16,32,128]{3,2,1,0:T(8,128)(2,1)S(1)} %copy-done.2, f32[16,16,32,128]{3,2,1,0:T(8,128)S(1)} %maximum_convert_fusion, f32[8,15,32,128]{3,2,1,0:T(8,128)} %get-tuple-element.90, f32[8,1,32,128]{3,2,1,0:T(8,128)} %get-tuple-element.92, f32[8,1,32,128]{3,2,1,0:T(8,128)} %get-tuple-element.91, ...), kind=kLoop, calls=%fused_computation.4 | loop fusion | flops 27787264 | bytes 54542336 | tf_op jit(solution)/shard_map/convert_element_type | solution.py:63
  54.6 6.3 %collective-permute-done.3 = bf16[4,16,32,128]{3,2,1,0:T(8,128)(2,1)S(1)} collective-permute-done((bf16[4,16,32,128]{3,2,1,0:T(8,128)(2,1)S(1)}, bf16[4,16,32,128]{3,2,1,0:T(8,128)(2,1)S(1)}, u32[]{:S(2)}, u32[]{:S(2)}) %collective-permute-start.3) | collective-permute-done | bytes 524320 | tf_op jit(solution)/shard_map/ppermute | solution.py:25
  60.9 4.8 %collective-permute-done.2 = bf16[4,16,32,128]{3,2,1,0:T(8,128)(2,1)S(1)} collective-permute-done((bf16[4,16,32,128]{3,2,1,0:T(8,128)(2,1)S(1)}, bf16[4,16,32,128]{3,2,1,0:T(8,128)(2,1)S(1)}, u32[]{:S(2)}, u32[]{:S(2)}) %collective-permute-start.2) | collective-permute-done | bytes 524320 | tf_op jit(solution)/shard_map/ppermute | solution.py:22
  66.1 2.5 %fusion.113 = (f32[8,15,32,128]{3,2,1,0:T(8,128)}, f32[8,15,32,128]{3,2,1,0:T(8,128)}) fusion(f32[16,16,32,128]{3,2,1,0:T(8,128)S(1)} %maximum_convert_fusion.1), kind=kLoop, calls=%fused_computation.142 | loop fusion | bytes 7864320 | tf_op jit(solution)/shard_map/jit(_roll_static)/slice | solution.py:41
  69.8 2.4 fusion.110
  74.5 2.3 fusion.106
  78.4 2.1 fusion.102
  80.5 1.8 fusion.100
  82.3 0.9 fusion.101
  84.0 10.1 %fusion.4 = bf16[8,16,32,128]{3,2,1,0:T(8,128)(2,1)S(1)} fusion(bf16[8,16,32,128]{3,2,1,0:T(8,128)(2,1)S(1)} %copy-done.2, f32[16,16,32,128]{3,2,1,0:T(8,128)S(1)} %maximum_convert_fusion.1, f32[8,15,32,128]{3,2,1,0:T(8,128)} %get-tuple-element.60, f32[8,1,32,128]{3,2,1,0:T(8,128)} %get-tuple-element.62, f32[8,1,32,128]{3,2,1,0:T(8,128)S(1)} %get-tuple-element.61, ...), kind=kLoop, calls=%fused_computation.6 | loop fusion | flops 28311552 | bytes 54542336 | tf_op jit(solution)/shard_map/convert_element_type | solution.py:69
  94.3 1.5 collective-permute-start.4
  96.1 4.9 %collective-permute-done.5 = bf16[4,16,32,128]{3,2,1,0:T(8,128)(2,1)S(1)} collective-permute-done((bf16[4,16,32,128]{3,2,1,0:T(8,128)(2,1)S(1)}, bf16[4,16,32,128]{3,2,1,0:T(8,128)(2,1)S(1)}, u32[]{:S(2)}, u32[]{:S(2)}) %collective-permute-start.5) | collective-permute-done | bytes 524320 | tf_op jit(solution)/shard_map/ppermute | solution.py:25
  101.0 6.3 %collective-permute-done.4 = bf16[4,16,32,128]{3,2,1,0:T(8,128)(2,1)S(1)} collective-permute-done((bf16[4,16,32,128]{3,2,1,0:T(8,128)(2,1)S(1)}, bf16[4,16,32,128]{3,2,1,0:T(8,128)(2,1)S(1)}, u32[]{:S(2)}, u32[]{:S(2)}) %collective-permute-start.4) | collective-permute-done | bytes 524320 | tf_op jit(solution)/shard_map/ppermute | solution.py:22
  107.3 1.6 maximum_convert_fusion.2
  108.9 2.5 %fusion.98 = (f32[8,15,32,128]{3,2,1,0:T(8,128)}, f32[8,15,32,128]{3,2,1,0:T(8,128)}) fusion(f32[16,16,32,128]{3,2,1,0:T(8,128)S(1)} %maximum_convert_fusion.2), kind=kLoop, calls=%fused_computation.127 | loop fusion | bytes 7864320 | tf_op jit(solution)/shard_map/jit(_roll_static)/slice | solution.py:41
  112.7 2.4 fusion.95
  117.4 1.5 fusion.91
  120.7 2.1 fusion.87
  122.8 1.1 fusion.88
  126.7 10.8 %fusion.13 = bf16[8,16,32,128]{3,2,1,0:T(8,128)(2,1)} fusion(f32[16,16,32,128]{3,2,1,0:T(8,128)S(1)} %maximum_convert_fusion.2, f32[8,15,32,128]{3,2,1,0:T(8,128)} %get-tuple-element.30, f32[8,1,32,128]{3,2,1,0:T(8,128)} %get-tuple-element.32, f32[8,1,32,128]{3,2,1,0:T(8,128)} %get-tuple-element.31, f32[8,15,32,128]{3,2,1,0:T(8,128)} %get-tuple-element.29, ...), kind=kLoop, calls=%fused_computation.16 | loop fusion | flops 25690112 | bytes 53493760 | tf_op jit(solution)/shard_map/convert_element_type | solution.py:53
  137.5 2.2 convolution_bitcast_fusion.1
  141.3 90.1 %all-reduce.2.cloned.1.call-done = f32[2,128,256]{2,1,0:T(8,128)} async-done(((f32[2,128,256]{2,1,0:T(8,128)}), f32[2,128,256]{2,1,0:T(8,128)}) %all-reduce.2.cloned.1.call-update) | async-done | bytes 262160 | tf_op jit(solution)/shard_map/psum | solution.py:80
  231.5 1.0 broadcast_multiply_fusion
  (60 shorter events, 26.2 us)
Async XLA Ops:
  7.2 18.2 %copy-start.2 = (bf16[8,16,32,128]{3,2,1,0:T(8,128)(2,1)S(1)}, bf16[8,16,32,128]{3,2,1,0:T(8,128)(2,1)}, u32[]{:S(2)}) copy-start(bf16[8,16,32,128]{3,2,1,0:T(8,128)(2,1)} %param.2) | copy-start | bytes 3145732
  7.2 130.3 %all-gather.2.cloned.1.call-start = ((), (), s32[]{:S(2)}) async-start(), calls=%async_computation | async-start | bytes 3145728 | tf_op jit(solution)/shard_map/all_gather | solution.py:74
  8.6 12.2 %collective-permute-start.1 = (bf16[4,16,32,128]{3,2,1,0:T(8,128)(2,1)S(1)}, bf16[4,16,32,128]{3,2,1,0:T(8,128)(2,1)S(1)}, u32[]{:S(2)}, u32[]{:S(2)}) collective-permute-start(bf16[4,16,32,128]{3,2,1,0:T(8,128)(2,1)S(1)} %get-tuple-element.104), channel_id=1, source_target_pairs={{1,0},{2,1},{3,2},{4,3},{5,4},{6,5},{7,6},{8,7},{9,8},{10,9},{11,1... | collective-permute-start | bytes 1572872 | tf_op jit(solution)/shard_map/ppermute | solution.py:25
  14.0 11.3 %collective-permute-start = (bf16[4,16,32,128]{3,2,1,0:T(8,128)(2,1)S(1)}, bf16[4,16,32,128]{3,2,1,0:T(8,128)(2,1)S(1)}, u32[]{:S(2)}, u32[]{:S(2)}) collective-permute-start(bf16[4,16,32,128]{3,2,1,0:T(8,128)(2,1)S(1)} %get-tuple-element.103), channel_id=1, source_target_pairs={{0,1},{1,2},{2,3},{3,4},{4,5},{5,6},{6,7},{7,8},{8,9},{9,10},{10,1... | collective-permute-start | bytes 1572872 | tf_op jit(solution)/shard_map/ppermute | solution.py:22
  42.3 1.6 copy-start.5
  54.0 6.9 %collective-permute-start.3 = (bf16[4,16,32,128]{3,2,1,0:T(8,128)(2,1)S(1)}, bf16[4,16,32,128]{3,2,1,0:T(8,128)(2,1)S(1)}, u32[]{:S(2)}, u32[]{:S(2)}) collective-permute-start(bf16[4,16,32,128]{3,2,1,0:T(8,128)(2,1)S(1)} %get-tuple-element.102), channel_id=1, source_target_pairs={{1,0},{2,1},{3,2},{4,3},{5,4},{6,5},{7,6},{8,7},{9,8},{10,9},{11,1... | collective-permute-start | bytes 1572872 | tf_op jit(solution)/shard_map/ppermute | solution.py:25
  54.2 11.5 %collective-permute-start.2 = (bf16[4,16,32,128]{3,2,1,0:T(8,128)(2,1)S(1)}, bf16[4,16,32,128]{3,2,1,0:T(8,128)(2,1)S(1)}, u32[]{:S(2)}, u32[]{:S(2)}) collective-permute-start(bf16[4,16,32,128]{3,2,1,0:T(8,128)(2,1)S(1)} %get-tuple-element.101), channel_id=1, source_target_pairs={{0,1},{1,2},{2,3},{3,4},{4,5},{5,6},{6,7},{7,8},{8,9},{9,10},{10,1... | collective-permute-start | bytes 1572872 | tf_op jit(solution)/shard_map/ppermute | solution.py:22
  94.1 1.7 copy-start
  94.2 6.8 %collective-permute-start.5 = (bf16[4,16,32,128]{3,2,1,0:T(8,128)(2,1)S(1)}, bf16[4,16,32,128]{3,2,1,0:T(8,128)(2,1)S(1)}, u32[]{:S(2)}, u32[]{:S(2)}) collective-permute-start(bf16[4,16,32,128]{3,2,1,0:T(8,128)(2,1)S(1)} %get-tuple-element.100), channel_id=1, source_target_pairs={{1,0},{2,1},{3,2},{4,3},{5,4},{6,5},{7,6},{8,7},{9,8},{10,9},{11,1... | collective-permute-start | bytes 1572872 | tf_op jit(solution)/shard_map/ppermute | solution.py:25
  94.3 13.0 %collective-permute-start.4 = (bf16[4,16,32,128]{3,2,1,0:T(8,128)(2,1)S(1)}, bf16[4,16,32,128]{3,2,1,0:T(8,128)(2,1)S(1)}, u32[]{:S(2)}, u32[]{:S(2)}) collective-permute-start(bf16[4,16,32,128]{3,2,1,0:T(8,128)(2,1)S(1)} %get-tuple-element.99), channel_id=1, source_target_pairs={{0,1},{1,2},{2,3},{3,4},{4,5},{5,6},{6,7},{7,8},{8,9},{9,10},{10,1... | collective-permute-start | bytes 1572872 | tf_op jit(solution)/shard_map/ppermute | solution.py:22
  95.8 135.7 %all-reduce.2.cloned.1.call-start = ((), (), s32[]{:S(2)}) async-start(), calls=%async_computation.1 | async-start | bytes 524288 | tf_op jit(solution)/shard_map/psum | solution.py:80
  122.8 2.0 copy-start.1
  137.5 2.3 copy-start.4
  137.5 2.5 %copy-start.3 = (bf16[4096,256]{1,0:T(8,128)(2,1)S(1)}, bf16[4096,256]{1,0:T(8,128)(2,1)}, u32[]{:S(2)}) copy-start(bf16[4096,256]{1,0:T(8,128)(2,1)} %all-gather.2.cloned.1.call-done) | copy-start | bytes 6291460
Sparse Core Ops, SparseCore 0:
  95.9 35.0 all-gather.1
  141.5 89.9 all-reduce.1
where the time goes:
time: 240 us
  waiting for transfers between devices  124 us (52%)
  local copies, waits for them, and re-layouts  54.2 us (23%)
  other arithmetic  37 us (15%)
  between operations  14.3 us (6%)
  starting transfers between devices  7.9 us (3%)
  matrix products  2.76 us (1%)
    psum x1, waiting for transfers between devices, shards(): summed = lax.psum(partial_terms, 'domain') * cell_weight  90.1 us
    slice x24, local copies, waits for them, and re-layouts, hamiltonian(): jnp.roll(middle, -offset, axis=1)  35.2 us
    ppermute x3, waiting for transfers between devices, padded(): lax.ppermute(lax.slice_in_dim(block, 0, width, axis=dim), axis, backward)  17.9 us
    slice x21, local copies, waits for them, and re-layouts, hamiltonian(): jnp.roll(middle, -offset, axis=2)  16.5 us
    ppermute x3, waiting for transfers between devices, padded(): lax.ppermute(lax.slice_in_dim(block, block.shape[dim] - width, None, axis...  15.8 us
    convert_element_type x1, other arithmetic, energy_block(): hamiltonian(extended, potential, filtered.shape[0]).astype(jnp.bfloat16)  10.8 us
    convert_element_type x1, other arithmetic, shards(): filtered = ((hamiltonian(first_wide, potential, planes) - spectrum_centre...  10.1 us
    convert_element_type x1, other arithmetic, shards(): first = ((hamiltonian(extended, potential, planes) - spectrum_centre * in...  10.1 us
  transfers between devices with their start and end apart: 8, of which 7 were waited for; matrix products, arithmetic and copies ran while one was open for 13% of the time, Pallas kernels for 0%

commit v1 on v0

--- a/solution.py
+++ b/solution.py
@@ -77,10 +77,20 @@
     )
     energy_piece = jnp.einsum("cb,ck->bk", applied, piece, preferred_element_type=jnp.float32)
     partial_terms = jnp.stack((correlation_piece, energy_piece))
-    summed = lax.psum(partial_terms, "domain") * cell_weight
+    summed = butterfly_sum(partial_terms, "domain") * cell_weight
     correlation = summed[0]
     projected = summed[1]
     return (filtered, correlation, projected)
+
+
+def butterfly_sum(values, axis):
+    count = lax.axis_size(axis)
+    bit = 1
+    while bit < count:
+        pairs = [(i, i ^ bit) for i in range(count)]
+        values = values + lax.ppermute(values, axis, pairs)
+        bit *= 2
+    return values
 
 
 def solution(mesh):

time: 240 us -> 183 us (0.76)
  waiting for transfers between devices: 124 us -> 64.6 us
  starting transfers between devices: 7.9 us -> 11.2 us
    psum x1 -> x0, waiting for transfers between devices: 90.1 us -> none  [shards(): summed = lax.psum(partial_terms, 'domain') * cell_weight]
    ppermute x0 -> x4, waiting for transfers between devices: none -> 30.8 us  [butterfly_sum(): values = values + lax.ppermute(values, axis, pairs)]
    ppermute x0 -> x4, starting transfers between devices: none -> 3.31 us  [butterfly_sum(): values = values + lax.ppermute(values, axis, pairs)]
  transfers between devices with their start and end apart: 8 -> 11, of which waited for: 7 -> 10; matrix products, arithmetic and copies ran while one was open for 13% -> 16% of each run, Pallas kernels for 0% -> 0%
where the time goes in v1:
time: 183 us
  waiting for transfers between devices  64.6 us (35%)
  local copies, waits for them, and re-layouts  54.2 us (30%)
  other arithmetic  35.5 us (19%)
  between operations  14.3 us (8%)
  starting transfers between devices  11.2 us (6%)
  matrix products  2.76 us (2%)
    slice x24, local copies, waits for them, and re-layouts, hamiltonian(): jnp.roll(middle, -offset, axis=1)  35.2 us
    ppermute x4, waiting for transfers between devices, butterfly_sum(): values = values + lax.ppermute(values, axis, pairs)  30.8 us
    ppermute x3, waiting for transfers between devices, padded(): lax.ppermute(lax.slice_in_dim(block, 0, width, axis=dim), axis, backward)  17.9 us
    slice x21, local copies, waits for them, and re-layouts, hamiltonian(): jnp.roll(middle, -offset, axis=2)  16.5 us
    ppermute x3, waiting for transfers between devices, padded(): lax.ppermute(lax.slice_in_dim(block, block.shape[dim] - width, None, axis...  15.8 us
    convert_element_type x1, other arithmetic, energy_block(): hamiltonian(extended, potential, filtered.shape[0]).astype(jnp.bfloat16)  10.8 us
    convert_element_type x1, other arithmetic, shards(): filtered = ((hamiltonian(first_wide, potential, planes) - spectrum_centre...  10.1 us
    convert_element_type x1, other arithmetic, shards(): first = ((hamiltonian(extended, potential, planes) - spectrum_centre * in...  10.1 us
  transfers between devices with their start and end apart: 11, of which 10 were waited for; matrix products, arithmetic and copies ran while one was open for 16% of the time, Pallas kernels for 0%

profile of v1, /device:TPU:0, one launch (start us, length us, event | category | flops | bytes accessed | tf_op | source)
XLA Modules:
  0.0 182.6 jit_solution(15299667440635415303)
XLA Ops:
  7.2 1.3 fusion.133
  8.6 5.5 %collective-permute-start.1 = (bf16[4,16,32,128]{3,2,1,0:T(8,128)(2,1)S(1)}, bf16[4,16,32,128]{3,2,1,0:T(8,128)(2,1)S(1)}, u32[]{:S(2)}, u32[]{:S(2)}) collective-permute-start(bf16[4,16,32,128]{3,2,1,0:T(8,128)(2,1)S(1)} %get-tuple-element.104), channel_id=1, source_target_pairs={{1,0},{2,1},{3,2},{4,3},{5,4},{6,5},{7,6},{8,7},{9,8},{10,9},{11,1... | collective-permute-start | bytes 1572872 | tf_op jit(solution)/shard_map/ppermute | solution.py:25
  14.0 6.7 %collective-permute-done.1 = bf16[4,16,32,128]{3,2,1,0:T(8,128)(2,1)S(1)} collective-permute-done((bf16[4,16,32,128]{3,2,1,0:T(8,128)(2,1)S(1)}, bf16[4,16,32,128]{3,2,1,0:T(8,128)(2,1)S(1)}, u32[]{:S(2)}, u32[]{:S(2)}) %collective-permute-start.1) | collective-permute-done | bytes 524320 | tf_op jit(solution)/shard_map/ppermute | solution.py:25
  20.7 4.6 %collective-permute-done = bf16[4,16,32,128]{3,2,1,0:T(8,128)(2,1)S(1)} collective-permute-done((bf16[4,16,32,128]{3,2,1,0:T(8,128)(2,1)S(1)}, bf16[4,16,32,128]{3,2,1,0:T(8,128)(2,1)S(1)}, u32[]{:S(2)}, u32[]{:S(2)}) %collective-permute-start) | collective-permute-done | bytes 524320 | tf_op jit(solution)/shard_map/ppermute | solution.py:22
  25.7 2.5 %fusion.129 = (f32[8,15,32,128]{3,2,1,0:T(8,128)}, f32[8,15,32,128]{3,2,1,0:T(8,128)}) fusion(f32[16,16,32,128]{3,2,1,0:T(8,128)S(1)} %maximum_convert_fusion), kind=kLoop, calls=%fused_computation.158 | loop fusion | bytes 7864320 | tf_op jit(solution)/shard_map/jit(_roll_static)/slice | solution.py:41
  29.5 2.4 %fusion.126 = (f32[8,14,32,128]{3,2,1,0:T(8,128)}, f32[8,14,32,128]{3,2,1,0:T(8,128)}) fusion(f32[16,16,32,128]{3,2,1,0:T(8,128)S(1)} %maximum_convert_fusion), kind=kLoop, calls=%fused_computation.155 | loop fusion | bytes 7340032 | tf_op jit(solution)/shard_map/jit(_roll_static)/slice | solution.py:41
  34.2 2.2 %fusion.122 = (f32[8,13,32,128]{3,2,1,0:T(8,128)}, f32[8,13,32,128]{3,2,1,0:T(8,128)}) fusion(f32[16,16,32,128]{3,2,1,0:T(8,128)S(1)} %maximum_convert_fusion), kind=kLoop, calls=%fused_computation.151 | loop fusion | bytes 6815744 | tf_op jit(solution)/shard_map/jit(_roll_static)/slice | solution.py:41
  38.9 2.1 %fusion.118 = (f32[8,12,32,128]{3,2,1,0:T(8,128)}, f32[8,12,32,128]{3,2,1,0:T(8,128)}) fusion(f32[16,16,32,128]{3,2,1,0:T(8,128)S(1)} %maximum_convert_fusion), kind=kLoop, calls=%fused_computation.147 | loop fusion | bytes 6291456 | tf_op jit(solution)/shard_map/jit(_roll_static)/slice | solution.py:41
  44.0 10.1 %fusion.2 = bf16[8,16,32,128]{3,2,1,0:T(8,128)(2,1)S(1)} fusion(bf16[8,16,32,128]{3,2,1,0:T(8,128)(2,1)S(1)} %copy-done.2, f32[16,16,32,128]{3,2,1,0:T(8,128)S(1)} %maximum_convert_fusion, f32[8,15,32,128]{3,2,1,0:T(8,128)} %get-tuple-element.90, f32[8,1,32,128]{3,2,1,0:T(8,128)} %get-tuple-element.92, f32[8,1,32,128]{3,2,1,0:T(8,128)} %get-tuple-element.91, ...), kind=kLoop, calls=%fused_computation.4 | loop fusion | flops 27787264 | bytes 54542336 | tf_op jit(solution)/shard_map/convert_element_type | solution.py:63
  54.7 6.3 %collective-permute-done.3 = bf16[4,16,32,128]{3,2,1,0:T(8,128)(2,1)S(1)} collective-permute-done((bf16[4,16,32,128]{3,2,1,0:T(8,128)(2,1)S(1)}, bf16[4,16,32,128]{3,2,1,0:T(8,128)(2,1)S(1)}, u32[]{:S(2)}, u32[]{:S(2)}) %collective-permute-start.3) | collective-permute-done | bytes 524320 | tf_op jit(solution)/shard_map/ppermute | solution.py:25
  61.0 4.8 %collective-permute-done.2 = bf16[4,16,32,128]{3,2,1,0:T(8,128)(2,1)S(1)} collective-permute-done((bf16[4,16,32,128]{3,2,1,0:T(8,128)(2,1)S(1)}, bf16[4,16,32,128]{3,2,1,0:T(8,128)(2,1)S(1)}, u32[]{:S(2)}, u32[]{:S(2)}) %collective-permute-start.2) | collective-permute-done | bytes 524320 | tf_op jit(solution)/shard_map/ppermute | solution.py:22
  66.2 2.5 %fusion.114 = (f32[8,15,32,128]{3,2,1,0:T(8,128)}, f32[8,15,32,128]{3,2,1,0:T(8,128)}) fusion(f32[16,16,32,128]{3,2,1,0:T(8,128)S(1)} %maximum_convert_fusion.1), kind=kLoop, calls=%fused_computation.143 | loop fusion | bytes 7864320 | tf_op jit(solution)/shard_map/jit(_roll_static)/slice | solution.py:41
  70.0 2.4 %fusion.111 = (f32[8,14,32,128]{3,2,1,0:T(8,128)}, f32[8,14,32,128]{3,2,1,0:T(8,128)}) fusion(f32[16,16,32,128]{3,2,1,0:T(8,128)S(1)} %maximum_convert_fusion.1), kind=kLoop, calls=%fused_computation.140 | loop fusion | bytes 7340032 | tf_op jit(solution)/shard_map/jit(_roll_static)/slice | solution.py:41
  74.6 2.3 %fusion.107 = (f32[8,13,32,128]{3,2,1,0:T(8,128)}, f32[8,13,32,128]{3,2,1,0:T(8,128)}) fusion(f32[16,16,32,128]{3,2,1,0:T(8,128)S(1)} %maximum_convert_fusion.1), kind=kLoop, calls=%fused_computation.136 | loop fusion | bytes 6815744 | tf_op jit(solution)/shard_map/jit(_roll_static)/slice | solution.py:41
  78.5 2.0 %fusion.103 = (f32[8,12,32,128]{3,2,1,0:T(8,128)}, f32[8,12,32,128]{3,2,1,0:T(8,128)}) fusion(f32[16,16,32,128]{3,2,1,0:T(8,128)S(1)} %maximum_convert_fusion.1), kind=kLoop, calls=%fused_computation.132 | loop fusion | bytes 6291456 | tf_op jit(solution)/shard_map/jit(_roll_static)/slice | solution.py:41
  80.6 1.8 fusion.101
  84.1 10.1 %fusion.4 = bf16[8,16,32,128]{3,2,1,0:T(8,128)(2,1)S(1)} fusion(bf16[8,16,32,128]{3,2,1,0:T(8,128)(2,1)S(1)} %copy-done.2, f32[16,16,32,128]{3,2,1,0:T(8,128)S(1)} %maximum_convert_fusion.1, f32[8,15,32,128]{3,2,1,0:T(8,128)} %get-tuple-element.60, f32[8,1,32,128]{3,2,1,0:T(8,128)} %get-tuple-element.62, f32[8,1,32,128]{3,2,1,0:T(8,128)S(1)} %get-tuple-element.61, ...), kind=kLoop, calls=%fused_computation.6 | loop fusion | flops 28311552 | bytes 54542336 | tf_op jit(solution)/shard_map/convert_element_type | solution.py:69
  94.4 1.7 collective-permute-start.4
  96.1 4.9 %collective-permute-done.5 = bf16[4,16,32,128]{3,2,1,0:T(8,128)(2,1)S(1)} collective-permute-done((bf16[4,16,32,128]{3,2,1,0:T(8,128)(2,1)S(1)}, bf16[4,16,32,128]{3,2,1,0:T(8,128)(2,1)S(1)}, u32[]{:S(2)}, u32[]{:S(2)}) %collective-permute-start.5) | collective-permute-done | bytes 524320 | tf_op jit(solution)/shard_map/ppermute | solution.py:25
  101.1 6.3 %collective-permute-done.4 = bf16[4,16,32,128]{3,2,1,0:T(8,128)(2,1)S(1)} collective-permute-done((bf16[4,16,32,128]{3,2,1,0:T(8,128)(2,1)S(1)}, bf16[4,16,32,128]{3,2,1,0:T(8,128)(2,1)S(1)}, u32[]{:S(2)}, u32[]{:S(2)}) %collective-permute-start.4) | collective-permute-done | bytes 524320 | tf_op jit(solution)/shard_map/ppermute | solution.py:22
  107.4 1.6 maximum_convert_fusion.2
  109.0 2.5 %fusion.99 = (f32[8,15,32,128]{3,2,1,0:T(8,128)}, f32[8,15,32,128]{3,2,1,0:T(8,128)}) fusion(f32[16,16,32,128]{3,2,1,0:T(8,128)S(1)} %maximum_convert_fusion.2), kind=kLoop, calls=%fused_computation.128 | loop fusion | bytes 7864320 | tf_op jit(solution)/shard_map/jit(_roll_static)/slice | solution.py:41
  112.8 2.4 %fusion.96 = (f32[8,14,32,128]{3,2,1,0:T(8,128)}, f32[8,14,32,128]{3,2,1,0:T(8,128)}) fusion(f32[16,16,32,128]{3,2,1,0:T(8,128)S(1)} %maximum_convert_fusion.2), kind=kLoop, calls=%fused_computation.125 | loop fusion | bytes 7340032 | tf_op jit(solution)/shard_map/jit(_roll_static)/slice | solution.py:41
  117.5 1.5 fusion.92
  120.7 2.1 %fusion.88 = (f32[8,12,32,128]{3,2,1,0:T(8,128)}, f32[8,12,32,128]{3,2,1,0:T(8,128)}) fusion(f32[16,16,32,128]{3,2,1,0:T(8,128)S(1)} %maximum_convert_fusion.2), kind=kLoop, calls=%fused_computation.117 | loop fusion | bytes 6291456 | tf_op jit(solution)/shard_map/jit(_roll_static)/slice | solution.py:41
  126.7 10.8 %fusion.13 = bf16[8,16,32,128]{3,2,1,0:T(8,128)(2,1)} fusion(f32[16,16,32,128]{3,2,1,0:T(8,128)S(1)} %maximum_convert_fusion.2, f32[8,15,32,128]{3,2,1,0:T(8,128)} %get-tuple-element.30, f32[8,1,32,128]{3,2,1,0:T(8,128)} %get-tuple-element.32, f32[8,1,32,128]{3,2,1,0:T(8,128)} %get-tuple-element.31, f32[8,15,32,128]{3,2,1,0:T(8,128)} %get-tuple-element.29, ...), kind=kLoop, calls=%fused_computation.16 | loop fusion | flops 25690112 | bytes 53493760 | tf_op jit(solution)/shard_map/convert_element_type | solution.py:53
  137.6 2.2 %convolution_bitcast_fusion.1 = f32[1,128,256]{2,1,0:T(8,128)S(1)} fusion(bf16[4096,128]{1,0:T(8,128)(2,1)S(1)} %bitcast.15, bf16[4096,256]{1,0:T(8,128)(2,1)} %all-gather.2.cloned.1.call-done), kind=kOutput, calls=%fused_computation.103 | convolution fusion | flops 268435456 | bytes 3276800 | tf_op jit(solution)/shard_map/cb,ck->bk/dot_general | solution.py:75
  140.7 3.1 %collective-permute-start.6 = (f32[2,128,256]{2,1,0:T(8,128)S(1)}, f32[2,128,256]{2,1,0:T(8,128)S(1)}, u32[]{:S(2)}, u32[]{:S(2)}) collective-permute-start(f32[2,128,256]{2,1,0:T(8,128)S(1)} %pad_maximum_fusion), channel_id=1, source_target_pairs={{0,1},{1,0},{2,3},{3,2},{4,5},{5,4},{6,7},{7,6},{8,9},{9,8},{10,11... | collective-permute-start | bytes 786440 | tf_op jit(solution)/shard_map/ppermute | solution.py:91
  143.8 1.2 collective-permute-done.6
  145.0 8.6 %collective-permute-done.7 = f32[2,128,256]{2,1,0:T(8,128)S(1)} collective-permute-done((f32[2,128,256]{2,1,0:T(8,128)S(1)}, f32[2,128,256]{2,1,0:T(8,128)S(1)}, u32[]{:S(2)}, u32[]{:S(2)}) %collective-permute-start.7) | collective-permute-done | bytes 262176 | tf_op jit(solution)/shard_map/ppermute | solution.py:91
  153.7 7.8 %collective-permute-done.8 = f32[2,128,256]{2,1,0:T(8,128)S(1)} collective-permute-done((f32[2,128,256]{2,1,0:T(8,128)S(1)}, f32[2,128,256]{2,1,0:T(8,128)S(1)}, u32[]{:S(2)}, u32[]{:S(2)}) %collective-permute-start.8) | collective-permute-done | bytes 262176 | tf_op jit(solution)/shard_map/ppermute | solution.py:91
  161.6 13.4 %collective-permute-done.9 = f32[2,128,256]{2,1,0:T(8,128)S(1)} collective-permute-done((f32[2,128,256]{2,1,0:T(8,128)S(1)}, f32[2,128,256]{2,1,0:T(8,128)S(1)}, u32[]{:S(2)}, u32[]{:S(2)}) %collective-permute-start.9) | collective-permute-done | bytes 262176 | tf_op jit(solution)/shard_map/ppermute | solution.py:91
  (68 shorter events, 28.5 us)
Async XLA Ops:
  7.2 18.2 %copy-start.2 = (bf16[8,16,32,128]{3,2,1,0:T(8,128)(2,1)S(1)}, bf16[8,16,32,128]{3,2,1,0:T(8,128)(2,1)}, u32[]{:S(2)}) copy-start(bf16[8,16,32,128]{3,2,1,0:T(8,128)(2,1)} %param.2) | copy-start | bytes 3145732
  7.2 130.4 %all-gather.2.cloned.1.call-start = ((), (), s32[]{:S(2)}) async-start(), calls=%async_computation | async-start | bytes 3145728 | tf_op jit(solution)/shard_map/all_gather | solution.py:74
  8.6 12.2 %collective-permute-start.1 = (bf16[4,16,32,128]{3,2,1,0:T(8,128)(2,1)S(1)}, bf16[4,16,32,128]{3,2,1,0:T(8,128)(2,1)S(1)}, u32[]{:S(2)}, u32[]{:S(2)}) collective-permute-start(bf16[4,16,32,128]{3,2,1,0:T(8,128)(2,1)S(1)} %get-tuple-element.104), channel_id=1, source_target_pairs={{1,0},{2,1},{3,2},{4,3},{5,4},{6,5},{7,6},{8,7},{9,8},{10,9},{11,1... | collective-permute-start | bytes 1572872 | tf_op jit(solution)/shard_map/ppermute | solution.py:25
  14.0 11.3 %collective-permute-start = (bf16[4,16,32,128]{3,2,1,0:T(8,128)(2,1)S(1)}, bf16[4,16,32,128]{3,2,1,0:T(8,128)(2,1)S(1)}, u32[]{:S(2)}, u32[]{:S(2)}) collective-permute-start(bf16[4,16,32,128]{3,2,1,0:T(8,128)(2,1)S(1)} %get-tuple-element.103), channel_id=1, source_target_pairs={{0,1},{1,2},{2,3},{3,4},{4,5},{5,6},{6,7},{7,8},{8,9},{9,10},{10,1... | collective-permute-start | bytes 1572872 | tf_op jit(solution)/shard_map/ppermute | solution.py:22
  42.3 1.6 copy-start.5
  54.1 6.9 %collective-permute-start.3 = (bf16[4,16,32,128]{3,2,1,0:T(8,128)(2,1)S(1)}, bf16[4,16,32,128]{3,2,1,0:T(8,128)(2,1)S(1)}, u32[]{:S(2)}, u32[]{:S(2)}) collective-permute-start(bf16[4,16,32,128]{3,2,1,0:T(8,128)(2,1)S(1)} %get-tuple-element.102), channel_id=1, source_target_pairs={{1,0},{2,1},{3,2},{4,3},{5,4},{6,5},{7,6},{8,7},{9,8},{10,9},{11,1... | collective-permute-start | bytes 1572872 | tf_op jit(solution)/shard_map/ppermute | solution.py:25
  54.3 11.5 %collective-permute-start.2 = (bf16[4,16,32,128]{3,2,1,0:T(8,128)(2,1)S(1)}, bf16[4,16,32,128]{3,2,1,0:T(8,128)(2,1)S(1)}, u32[]{:S(2)}, u32[]{:S(2)}) collective-permute-start(bf16[4,16,32,128]{3,2,1,0:T(8,128)(2,1)S(1)} %get-tuple-element.101), channel_id=1, source_target_pairs={{0,1},{1,2},{2,3},{3,4},{4,5},{5,6},{6,7},{7,8},{8,9},{9,10},{10,1... | collective-permute-start | bytes 1572872 | tf_op jit(solution)/shard_map/ppermute | solution.py:22
  94.2 1.9 %copy-start = (bf16[8,16,32,128]{3,2,1,0:T(8,128)(2,1)}, bf16[8,16,32,128]{3,2,1,0:T(8,128)(2,1)S(1)}, u32[]{:S(2)}) copy-start(bf16[8,16,32,128]{3,2,1,0:T(8,128)(2,1)S(1)} %fusion.4) | copy-start | bytes 3145732
  94.3 6.8 %collective-permute-start.5 = (bf16[4,16,32,128]{3,2,1,0:T(8,128)(2,1)S(1)}, bf16[4,16,32,128]{3,2,1,0:T(8,128)(2,1)S(1)}, u32[]{:S(2)}, u32[]{:S(2)}) collective-permute-start(bf16[4,16,32,128]{3,2,1,0:T(8,128)(2,1)S(1)} %get-tuple-element.100), channel_id=1, source_target_pairs={{1,0},{2,1},{3,2},{4,3},{5,4},{6,5},{7,6},{8,7},{9,8},{10,9},{11,1... | collective-permute-start | bytes 1572872 | tf_op jit(solution)/shard_map/ppermute | solution.py:25
  94.4 13.0 %collective-permute-start.4 = (bf16[4,16,32,128]{3,2,1,0:T(8,128)(2,1)S(1)}, bf16[4,16,32,128]{3,2,1,0:T(8,128)(2,1)S(1)}, u32[]{:S(2)}, u32[]{:S(2)}) collective-permute-start(bf16[4,16,32,128]{3,2,1,0:T(8,128)(2,1)S(1)} %get-tuple-element.99), channel_id=1, source_target_pairs={{0,1},{1,2},{2,3},{3,4},{4,5},{5,6},{6,7},{7,8},{8,9},{9,10},{10,1... | collective-permute-start | bytes 1572872 | tf_op jit(solution)/shard_map/ppermute | solution.py:22
  122.9 2.0 %copy-start.1 = (bf16[8,16,32,128]{3,2,1,0:T(8,128)(2,1)S(1)}, bf16[8,16,32,128]{3,2,1,0:T(8,128)(2,1)}, u32[]{:S(2)}) copy-start(bf16[8,16,32,128]{3,2,1,0:T(8,128)(2,1)} %copy-done) | copy-start | bytes 3145732
  137.6 2.3 %copy-start.4 = (bf16[8,16,32,128]{3,2,1,0:T(8,128)(2,1)S(1)}, bf16[8,16,32,128]{3,2,1,0:T(8,128)(2,1)}, u32[]{:S(2)}) copy-start(bf16[8,16,32,128]{3,2,1,0:T(8,128)(2,1)} %fusion.13) | copy-start | bytes 3145732
  137.6 2.5 %copy-start.3 = (bf16[4096,256]{1,0:T(8,128)(2,1)S(1)}, bf16[4096,256]{1,0:T(8,128)(2,1)}, u32[]{:S(2)}) copy-start(bf16[4096,256]{1,0:T(8,128)(2,1)} %all-gather.2.cloned.1.call-done) | copy-start | bytes 6291460
  140.7 4.3 %collective-permute-start.6 = (f32[2,128,256]{2,1,0:T(8,128)S(1)}, f32[2,128,256]{2,1,0:T(8,128)S(1)}, u32[]{:S(2)}, u32[]{:S(2)}) collective-permute-start(f32[2,128,256]{2,1,0:T(8,128)S(1)} %pad_maximum_fusion), channel_id=1, source_target_pairs={{0,1},{1,0},{2,3},{3,2},{4,5},{5,4},{6,7},{7,6},{8,9},{9,8},{10,11... | collective-permute-start | bytes 786440 | tf_op jit(solution)/shard_map/ppermute | solution.py:91
  145.0 8.7 %collective-permute-start.7 = (f32[2,128,256]{2,1,0:T(8,128)S(1)}, f32[2,128,256]{2,1,0:T(8,128)S(1)}, u32[]{:S(2)}, u32[]{:S(2)}) collective-permute-start(f32[2,128,256]{2,1,0:T(8,128)S(1)} %fusion.85), channel_id=1, source_target_pairs={{0,2},{1,3},{2,0},{3,1},{4,6},{5,7},{6,4},{7,5},{8,10},{9,11},{10,... | collective-permute-start | bytes 786440 | tf_op jit(solution)/shard_map/ppermute | solution.py:91
  153.7 7.8 %collective-permute-start.8 = (f32[2,128,256]{2,1,0:T(8,128)S(1)}, f32[2,128,256]{2,1,0:T(8,128)S(1)}, u32[]{:S(2)}, u32[]{:S(2)}) collective-permute-start(f32[2,128,256]{2,1,0:T(8,128)S(1)} %fusion.138), channel_id=1, source_target_pairs={{0,4},{1,5},{2,6},{3,7},{4,0},{5,1},{6,2},{7,3},{8,12},{9,13},{10,... | collective-permute-start | bytes 786440 | tf_op jit(solution)/shard_map/ppermute | solution.py:91
  161.5 13.4 %collective-permute-start.9 = (f32[2,128,256]{2,1,0:T(8,128)S(1)}, f32[2,128,256]{2,1,0:T(8,128)S(1)}, u32[]{:S(2)}, u32[]{:S(2)}) collective-permute-start(f32[2,128,256]{2,1,0:T(8,128)S(1)} %add.318), channel_id=1, source_target_pairs={{0,8},{1,9},{2,10},{3,11},{4,12},{5,13},{6,14},{7,15},{8,0},{9,1},... | collective-permute-start | bytes 786440 | tf_op jit(solution)/shard_map/ppermute | solution.py:91
Sparse Core Ops, SparseCore 0:
  96.3 34.8 all-gather.1

commit v2 on v0

v2 whole, which is shorter than its diff:
```python
import jax
import jax.numpy as jnp
from jax import lax
from jax.experimental import pallas as pl
from jax.experimental.pallas import tpu as pltpu
from jax.sharding import PartitionSpec as P

RADIUS = 4


stencil_weights = (-205.0 / 72.0, 8.0 / 5.0, -1.0 / 5.0, 8.0 / 315.0, -1.0 / 560.0)
spectrum_centre = 6.0
first_factor = -0.125
second_factor = -1.0 / 7.0
memory_factor = -1.0 / 7.0


def halos(block, axis, width):
    count = lax.axis_size(axis)
    forward = [(i, (i + 1) % count) for i in range(count)]
    backward = [(target, source) for source, target in forward]
    low = lax.ppermute(lax.slice_in_dim(block, block.shape[0] - width, None, axis=0), axis, forward)
    high = lax.ppermute(lax.slice_in_dim(block, 0, width, axis=0), axis, backward)
    return low, high


def stencil_kernel(stage, planes, ny, nz):
    def kernel(*refs):
        if stage == "filtered":
            low, own, high, pot, initial, out = refs
        else:
            low, own, high, pot, out = refs

        def plane_ref(p):
            if p < 0:
                return low, p + RADIUS
            if p >= planes:
                return high, p - planes
            return own, p

        for x in range(planes):
            def row(y, carry, x=x):
                centre = own[x, y].astype(jnp.float32)
                summed = (3.0 * stencil_weights[0]) * centre
                for k in range(1, RADIUS + 1):
                    above, ia = plane_ref(x + k)
                    below, ib = plane_ref(x - k)
                    beside = above[ia, y].astype(jnp.float32) + below[ib, y].astype(jnp.float32)
                    beside = beside + own[x, (y + k) % ny].astype(jnp.float32)
                    beside = beside + own[x, (y + ny - k) % ny].astype(jnp.float32)
                    beside = beside + (
                        pltpu.roll(centre, k, 0) + pltpu.roll(centre, nz - k, 0)
                    )
                    summed = summed + stencil_weights[k] * beside
                applied = -0.5 * summed + pot[x, y] * centre
                if stage == "first":
                    result = (applied - spectrum_centre * centre) * first_factor
                elif stage == "filtered":
                    result = (applied - spectrum_centre * centre) * second_factor + (
                        memory_factor * initial[x, y].astype(jnp.float32)
                    )
                else:
                    result = applied
                out[x, y] = result.astype(out.dtype)
                return carry

            lax.fori_loop(0, ny, row, 0)

    return kernel


def stencil_stage(stage, block, potential_wide, initial=None):
    planes, ny, nz, nb = block.shape
    low, high = halos(block, "domain", RADIUS)
    operands = [low, block, high, potential_wide]
    if initial is not None:
        operands.append(initial)
    return pl.pallas_call(
        stencil_kernel(stage, planes, ny, nz),
        out_shape=jax.ShapeDtypeStruct(block.shape, jnp.bfloat16),
        name=f"stencil_{stage}",
    )(*operands)


def butterfly_sum(values, axis):
    count = lax.axis_size(axis)
    bit = 1
    while bit < count:
        pairs = [(i, i ^ bit) for i in range(count)]
        values = values + lax.ppermute(values, axis, pairs)
        bit *= 2
    return values


def shards(orbitals, potential):
    planes, ny, nz, nb = orbitals.shape
    potential_wide = jnp.broadcast_to(potential[:, :, :, None], (planes, ny, nz, nb))
    first = stencil_stage("first", orbitals, potential_wide)
    filtered = stencil_stage("filtered", first, potential_wide, orbitals)
    applied_grid = stencil_stage("applied", filtered, potential_wide)
    cell_count = planes * ny * nz
    cell_weight = 1.0 / (cell_count * lax.axis_size("domain"))
    own_block = filtered.reshape(cell_count, nb)
    applied = applied_grid.reshape(cell_count, nb)
    piece = lax.all_gather(own_block, "band", axis=1, tiled=True)
    correlation_piece = jnp.einsum(
        "cb,ck->bk", own_block, piece, preferred_element_type=jnp.float32
    )
    energy_piece = jnp.einsum("cb,ck->bk", applied, piece, preferred_element_type=jnp.float32)
    partial_terms = jnp.stack((correlation_piece, energy_piece))
    summed = butterfly_sum(partial_terms, "domain") * cell_weight
    correlation = summed[0]
    projected = summed[1]
    return (filtered, correlation, projected)


def solution(mesh):
    placed = (P("domain", None, None, "band"), P("domain", None, None))
    return jax.shard_map(
        shards,
        mesh=mesh,
        in_specs=placed,
        out_specs=(P("domain", None, None, "band"), P("band", None), P("band", None)),
        check_vma=False,
    )
```

time: 240 us -> 137 us (0.57)
  waiting for transfers between devices: 124 us -> 63 us
  local copies, waits for them, and re-layouts: 54.2 us -> 9.13 us
  other arithmetic: 37 us -> 0.18 us
  Pallas kernels: 0 us -> 26.4 us
  starting transfers between devices: 7.9 us -> 21.4 us
    psum x1 -> x0, waiting for transfers between devices: 90.1 us -> none  [shards(): summed = lax.psum(partial_terms, 'domain') * cell_weight]
    slice x48 -> x3, local copies, waits for them, and re-layouts: 53.2 us -> 3.91 us  [halos(): lax.slice_in_dim(block, 0, width, axis=0)]
    convert_element_type x6 -> x0, other arithmetic: 33.2 us -> none  [the longest x1 10.8 us: energy_block(): hamiltonian(extended, potential, filtered.shape[0]).astype(jnp.bfloat16)]
    pallas_call x0 -> x3, Pallas kernels: none -> 26.4 us  [stencil_stage(): pl.pallas_call(stencil_kernel(stage, planes, ny, nz), out_shape=jax.Shape...]
    all_gather x1, waiting for transfers between devices: 0.02 us -> 17.6 us  [shards(): piece = lax.all_gather(own_block, 'band', axis=1, tiled=True)]
    ppermute x6 -> x10, starting transfers between devices: 7.6 us -> 21.3 us  [the longest x3 10.7 us: halos(): lax.ppermute(lax.slice_in_dim(block, block.shape[0] - width, None, axis=0...]
    ppermute x6 -> x10, waiting for transfers between devices: 33.7 us -> 45.4 us  [the longest x4 25.1 us: butterfly_sum(): values = values + lax.ppermute(values, axis, pairs)]
  transfers between devices with their start and end apart: 8 -> 11, of which waited for: 7 -> 10; matrix products, arithmetic and copies ran while one was open for 13% -> 1% of each run, Pallas kernels for 0% -> 6%
where the time goes in v2:
time: 137 us
  waiting for transfers between devices  63 us (46%)
  Pallas kernels  26.4 us (19%)
  starting transfers between devices  21.4 us (16%)
  between operations  14.1 us (10%)
  local copies, waits for them, and re-layouts  9.13 us (7%)
  matrix products  2.76 us (2%)
    pallas_call x3, Pallas kernels, stencil_stage(): pl.pallas_call(stencil_kernel(stage, planes, ny, nz), out_shape=jax.Shape...  26.4 us
    ppermute x4, waiting for transfers between devices, butterfly_sum(): values = values + lax.ppermute(values, axis, pairs)  25.1 us
    ppermute x3, waiting for transfers between devices, halos(): lax.ppermute(lax.slice_in_dim(block, block.shape[0] - width, None, axis=0...  19.7 us
    all_gather x1, waiting for transfers between devices, shards(): piece = lax.all_gather(own_block, 'band', axis=1, tiled=True)  17.6 us
    ppermute x3, starting transfers between devices, halos(): lax.ppermute(lax.slice_in_dim(block, block.shape[0] - width, None, axis=0...  10.7 us
    ppermute x4, starting transfers between devices, butterfly_sum(): values = values + lax.ppermute(values, axis, pairs)  5.63 us
    ppermute x3, starting transfers between devices, halos(): lax.ppermute(lax.slice_in_dim(block, 0, width, axis=0), axis, backward)  5.03 us
    slice x3, local copies, waits for them, and re-layouts, halos(): lax.slice_in_dim(block, 0, width, axis=0)  3.91 us
  transfers between devices with their start and end apart: 11, of which 10 were waited for; matrix products, arithmetic and copies ran while one was open for 1% of the time, Pallas kernels for 6%

profile of v2, /device:TPU:0, one launch (start us, length us, event | category | flops | bytes accessed | tf_op | source)
XLA Modules:
  0.0 137.0 jit_solution(6097763687559911681)
XLA Ops:
  7.2 1.3 fusion.3
  8.5 0.5 collective-permute-start
  9.0 5.0 %collective-permute-start.1 = (bf16[4,16,32,128]{3,2,1,0:T(8,128)(2,1)S(1)}, bf16[4,16,32,128]{3,2,1,0:T(8,128)(2,1)S(1)}, u32[]{:S(2)}, u32[]{:S(2)}) collective-permute-start(bf16[4,16,32,128]{3,2,1,0:T(8,128)(2,1)S(1)} %get-tuple-element.7), channel_id=1, source_target_pairs={{1,0},{2,1},{3,2},{4,3},{5,4},{6,5},{7,6},{8,7},{9,8},{10,9},{11,1... | collective-permute-start | bytes 1572872 | tf_op jit(solution)/shard_map/ppermute | solution.py:23
  14.1 6.9 %collective-permute-done.refs_0_ = bf16[4,16,32,128]{3,2,1,0:T(8,128)(2,1)S(1)} collective-permute-done((bf16[4,16,32,128]{3,2,1,0:T(8,128)(2,1)S(1)}, bf16[4,16,32,128]{3,2,1,0:T(8,128)(2,1)S(1)}, u32[]{:S(2)}, u32[]{:S(2)}) %collective-permute-start) | collective-permute-done | bytes 524320 | tf_op jit(solution)/shard_map/ppermute | solution.py:22
  21.0 1.9 %broadcast_in_dim.2.refs_3_ = f32[8,16,32,128]{3,2,1,0:T(8,128)} broadcast(f32[8,16,32]{2,1,0:T(8,128)S(1)} %copy-done.9), dimensions={0,1,2} | broadcast | bytes 2113536 | tf_op jit(solution)/shard_map/broadcast_in_dim | solution.py:97
  22.9 8.7 %stencil_first.1.refs_1_ = bf16[8,16,32,128]{3,2,1,0:T(8,128)(2,1)} custom-call(bf16[4,16,32,128]{3,2,1,0:T(8,128)(2,1)} %copy-done.3, bf16[8,16,32,128]{3,2,1,0:T(8,128)(2,1)} %refs_4_.1, bf16[4,16,32,128]{3,2,1,0:T(8,128)(2,1)} %copy-done.6, f32[8,16,32,128]{3,2,1,0:T(8,128)} %broadcast_in_dim.2.refs_3_), custom_call_target="tpu_custom_call" | custom-call | tf_op jit(solution)/shard_map/stencil_first/pallas_call | solution.py:78
  31.6 1.3 fusion.2
  32.9 4.9 %collective-permute-start.2 = (bf16[4,16,32,128]{3,2,1,0:T(8,128)(2,1)S(1)}, bf16[4,16,32,128]{3,2,1,0:T(8,128)(2,1)S(1)}, u32[]{:S(2)}, u32[]{:S(2)}) collective-permute-start(bf16[4,16,32,128]{3,2,1,0:T(8,128)(2,1)S(1)} %get-tuple-element.6), channel_id=1, source_target_pairs={{0,1},{1,2},{2,3},{3,4},{4,5},{5,6},{6,7},{7,8},{8,9},{9,10},{10,1... | collective-permute-start | bytes 1572872 | tf_op jit(solution)/shard_map/ppermute | solution.py:22
  37.9 6.6 %collective-permute-done.2.refs_0_ = bf16[4,16,32,128]{3,2,1,0:T(8,128)(2,1)S(1)} collective-permute-done((bf16[4,16,32,128]{3,2,1,0:T(8,128)(2,1)S(1)}, bf16[4,16,32,128]{3,2,1,0:T(8,128)(2,1)S(1)}, u32[]{:S(2)}, u32[]{:S(2)}) %collective-permute-start.2) | collective-permute-done | bytes 524320 | tf_op jit(solution)/shard_map/ppermute | solution.py:22
  44.4 0.1 collective-permute-done.3.refs_2_
  44.6 0.7 copy-done.4
  45.2 0.8 copy-done.7
  46.0 9.1 %stencil_filtered.1.refs_1_ = bf16[8,16,32,128]{3,2,1,0:T(8,128)(2,1)} custom-call(bf16[4,16,32,128]{3,2,1,0:T(8,128)(2,1)} %copy-done.4, bf16[8,16,32,128]{3,2,1,0:T(8,128)(2,1)} %stencil_first.1.refs_1_, bf16[4,16,32,128]{3,2,1,0:T(8,128)(2,1)} %copy-done.7, f32[8,16,32,128]{3,2,1,0:T(8,128)} %broadcast_in_dim.2.refs_3_, bf16[8,16,32,128]{3,2,1,0:T(8,128)(2,1)} %refs_4_.1), custom_call_target="tpu_custom_call" | custom-call | tf_op jit(solution)/shard_map/stencil_filtered/pallas_call | solution.py:78
  55.1 1.3 fusion.1
  56.5 5.2 %collective-permute-start.4 = (bf16[4,16,32,128]{3,2,1,0:T(8,128)(2,1)S(1)}, bf16[4,16,32,128]{3,2,1,0:T(8,128)(2,1)S(1)}, u32[]{:S(2)}, u32[]{:S(2)}) collective-permute-start(bf16[4,16,32,128]{3,2,1,0:T(8,128)(2,1)S(1)} %get-tuple-element.4), channel_id=1, source_target_pairs={{0,1},{1,2},{2,3},{3,4},{4,5},{5,6},{6,7},{7,8},{8,9},{9,10},{10,1... | collective-permute-start | bytes 1572872 | tf_op jit(solution)/shard_map/ppermute | solution.py:22
  61.7 6.2 %collective-permute-done.4.refs_0_ = bf16[4,16,32,128]{3,2,1,0:T(8,128)(2,1)S(1)} collective-permute-done((bf16[4,16,32,128]{3,2,1,0:T(8,128)(2,1)S(1)}, bf16[4,16,32,128]{3,2,1,0:T(8,128)(2,1)S(1)}, u32[]{:S(2)}, u32[]{:S(2)}) %collective-permute-start.4) | collective-permute-done | bytes 524320 | tf_op jit(solution)/shard_map/ppermute | solution.py:22
  67.9 0.5 collective-permute-done.5.refs_2_
  68.4 0.3 copy-done.5
  68.7 0.8 copy-done.8
  69.5 8.6 %stencil_applied.1 = bf16[8,16,32,128]{3,2,1,0:T(8,128)(2,1)} custom-call(bf16[4,16,32,128]{3,2,1,0:T(8,128)(2,1)} %copy-done.5, bf16[8,16,32,128]{3,2,1,0:T(8,128)(2,1)} %stencil_filtered.1.refs_1_, bf16[4,16,32,128]{3,2,1,0:T(8,128)(2,1)} %copy-done.8, f32[8,16,32,128]{3,2,1,0:T(8,128)} %broadcast_in_dim.2.refs_3_), custom_call_target="tpu_custom_call" | custom-call | tf_op jit(solution)/shard_map/stencil_applied/pallas_call | solution.py:78
  78.1 17.6 %all-gather.2.cloned.1.call-done = bf16[4096,256]{1,0:T(8,128)(2,1)} async-done(((bf16[4096,128]{1,0:T(8,128)(2,1)}), bf16[4096,256]{1,0:T(8,128)(2,1)}) %all-gather.2.cloned.1.call-update) | async-done | bytes 2097168 | tf_op jit(solution)/shard_map/all_gather | solution.py:105
  95.7 2.2 %convolution_bitcast_fusion.1 = f32[1,128,256]{2,1,0:T(8,128)S(1)} fusion(bf16[4096,128]{1,0:T(8,128)(2,1)S(1)} %bitcast.15, bf16[4096,256]{1,0:T(8,128)(2,1)} %all-gather.2.cloned.1.call-done), kind=kOutput, calls=%fused_computation.1 | convolution fusion | flops 268435456 | bytes 3276800 | tf_op jit(solution)/shard_map/cb,ck->bk/dot_general | solution.py:106
  98.0 0.5 convolution_bitcast_fusion
  98.5 0.1 collective-permute-start.6
  98.6 1.5 %collective-permute-done.6 = f32[2,128,256]{2,1,0:T(8,128)S(1)} collective-permute-done((f32[2,128,256]{2,1,0:T(8,128)S(1)}, f32[2,128,256]{2,1,0:T(8,128)S(1)}, u32[]{:S(2)}, u32[]{:S(2)}) %collective-permute-start.6) | collective-permute-done | bytes 262176 | tf_op jit(solution)/shard_map/ppermute | solution.py:90
  100.2 1.5 %collective-permute-start.7 = (f32[2,128,256]{2,1,0:T(8,128)S(1)}, f32[2,128,256]{2,1,0:T(8,128)S(1)}, u32[]{:S(2)}, u32[]{:S(2)}) collective-permute-start(f32[2,128,256]{2,1,0:T(8,128)S(1)} %fusion), channel_id=1, source_target_pairs={{0,2},{1,3},{2,0},{3,1},{4,6},{5,7},{6,4},{7,5},{8,10},{9,11},{10,... | collective-permute-start | bytes 786440 | tf_op jit(solution)/shard_map/ppermute | solution.py:90
  101.7 6.9 %collective-permute-done.7 = f32[2,128,256]{2,1,0:T(8,128)S(1)} collective-permute-done((f32[2,128,256]{2,1,0:T(8,128)S(1)}, f32[2,128,256]{2,1,0:T(8,128)S(1)}, u32[]{:S(2)}, u32[]{:S(2)}) %collective-permute-start.7) | collective-permute-done | bytes 262176 | tf_op jit(solution)/shard_map/ppermute | solution.py:90
  108.6 1.6 %collective-permute-start.8 = (f32[2,128,256]{2,1,0:T(8,128)S(1)}, f32[2,128,256]{2,1,0:T(8,128)S(1)}, u32[]{:S(2)}, u32[]{:S(2)}) collective-permute-start(f32[2,128,256]{2,1,0:T(8,128)S(1)} %fusion.8), channel_id=1, source_target_pairs={{0,4},{1,5},{2,6},{3,7},{4,0},{5,1},{6,2},{7,3},{8,12},{9,13},{10,... | collective-permute-start | bytes 786440 | tf_op jit(solution)/shard_map/ppermute | solution.py:90
  110.2 6.0 %collective-permute-done.8 = f32[2,128,256]{2,1,0:T(8,128)S(1)} collective-permute-done((f32[2,128,256]{2,1,0:T(8,128)S(1)}, f32[2,128,256]{2,1,0:T(8,128)S(1)}, u32[]{:S(2)}, u32[]{:S(2)}) %collective-permute-start.8) | collective-permute-done | bytes 262176 | tf_op jit(solution)/shard_map/ppermute | solution.py:90
  116.2 2.5 %collective-permute-start.9 = (f32[2,128,256]{2,1,0:T(8,128)S(1)}, f32[2,128,256]{2,1,0:T(8,128)S(1)}, u32[]{:S(2)}, u32[]{:S(2)}) collective-permute-start(f32[2,128,256]{2,1,0:T(8,128)S(1)} %add.14), channel_id=1, source_target_pairs={{0,8},{1,9},{2,10},{3,11},{4,12},{5,13},{6,14},{7,15},{8,0},{9,1},... | collective-permute-start | bytes 786440 | tf_op jit(solution)/shard_map/ppermute | solution.py:90
  118.7 10.7 %collective-permute-done.9 = f32[2,128,256]{2,1,0:T(8,128)S(1)} collective-permute-done((f32[2,128,256]{2,1,0:T(8,128)S(1)}, f32[2,128,256]{2,1,0:T(8,128)S(1)}, u32[]{:S(2)}, u32[]{:S(2)}) %collective-permute-start.9) | collective-permute-done | bytes 262176 | tf_op jit(solution)/shard_map/ppermute | solution.py:90
  129.5 0.7 slice_bitcast_fusion
  (26 shorter events, 0.3 us)
Async XLA Ops:
  7.2 13.8 %copy-start.9 = (f32[8,16,32]{2,1,0:T(8,128)S(1)}, f32[8,16,32]{2,1,0:T(8,128)}, u32[]{:S(2)}) copy-start(f32[8,16,32]{2,1,0:T(8,128)} %param.3) | copy-start | bytes 49156
  7.2 88.5 %all-gather.2.cloned.1.call-start = ((), (), s32[]{:S(2)}) async-start(), calls=%async_computation | async-start | bytes 3145728 | tf_op jit(solution)/shard_map/all_gather | solution.py:105
  8.5 12.4 %collective-permute-start = (bf16[4,16,32,128]{3,2,1,0:T(8,128)(2,1)S(1)}, bf16[4,16,32,128]{3,2,1,0:T(8,128)(2,1)S(1)}, u32[]{:S(2)}, u32[]{:S(2)}) collective-permute-start(bf16[4,16,32,128]{3,2,1,0:T(8,128)(2,1)S(1)} %get-tuple-element.8), channel_id=1, source_target_pairs={{0,1},{1,2},{2,3},{3,4},{4,5},{5,6},{6,7},{7,8},{8,9},{9,10},{10,1... | collective-permute-start | bytes 1572872 | tf_op jit(solution)/shard_map/ppermute | solution.py:22
  9.0 11.9 %collective-permute-start.1 = (bf16[4,16,32,128]{3,2,1,0:T(8,128)(2,1)S(1)}, bf16[4,16,32,128]{3,2,1,0:T(8,128)(2,1)S(1)}, u32[]{:S(2)}, u32[]{:S(2)}) collective-permute-start(bf16[4,16,32,128]{3,2,1,0:T(8,128)(2,1)S(1)} %get-tuple-element.7), channel_id=1, source_target_pairs={{1,0},{2,1},{3,2},{4,3},{5,4},{6,5},{7,6},{8,7},{9,8},{10,9},{11,1... | collective-permute-start | bytes 1572872 | tf_op jit(solution)/shard_map/ppermute | solution.py:23
  21.0 2.0 %copy-start.3 = (bf16[4,16,32,128]{3,2,1,0:T(8,128)(2,1)}, bf16[4,16,32,128]{3,2,1,0:T(8,128)(2,1)S(1)}, u32[]{:S(2)}) copy-start(bf16[4,16,32,128]{3,2,1,0:T(8,128)(2,1)S(1)} %collective-permute-done.refs_0_) | copy-start | bytes 1572868
  21.0 2.0 %copy-start.6 = (bf16[4,16,32,128]{3,2,1,0:T(8,128)(2,1)}, bf16[4,16,32,128]{3,2,1,0:T(8,128)(2,1)S(1)}, u32[]{:S(2)}) copy-start(bf16[4,16,32,128]{3,2,1,0:T(8,128)(2,1)S(1)} %collective-permute-done.1.refs_2_) | copy-start | bytes 1572868
  32.9 11.5 %collective-permute-start.2 = (bf16[4,16,32,128]{3,2,1,0:T(8,128)(2,1)S(1)}, bf16[4,16,32,128]{3,2,1,0:T(8,128)(2,1)S(1)}, u32[]{:S(2)}, u32[]{:S(2)}) collective-permute-start(bf16[4,16,32,128]{3,2,1,0:T(8,128)(2,1)S(1)} %get-tuple-element.6), channel_id=1, source_target_pairs={{0,1},{1,2},{2,3},{3,4},{4,5},{5,6},{6,7},{7,8},{8,9},{9,10},{10,1... | collective-permute-start | bytes 1572872 | tf_op jit(solution)/shard_map/ppermute | solution.py:22
  37.9 6.7 %collective-permute-start.3 = (bf16[4,16,32,128]{3,2,1,0:T(8,128)(2,1)S(1)}, bf16[4,16,32,128]{3,2,1,0:T(8,128)(2,1)S(1)}, u32[]{:S(2)}, u32[]{:S(2)}) collective-permute-start(bf16[4,16,32,128]{3,2,1,0:T(8,128)(2,1)S(1)} %get-tuple-element.5), channel_id=1, source_target_pairs={{1,0},{2,1},{3,2},{4,3},{5,4},{6,5},{7,6},{8,7},{9,8},{10,9},{11,1... | collective-permute-start | bytes 1572872 | tf_op jit(solution)/shard_map/ppermute | solution.py:23
  44.4 0.8 copy-start.4
  45.2 0.8 copy-start.7
  56.5 11.4 %collective-permute-start.4 = (bf16[4,16,32,128]{3,2,1,0:T(8,128)(2,1)S(1)}, bf16[4,16,32,128]{3,2,1,0:T(8,128)(2,1)S(1)}, u32[]{:S(2)}, u32[]{:S(2)}) collective-permute-start(bf16[4,16,32,128]{3,2,1,0:T(8,128)(2,1)S(1)} %get-tuple-element.4), channel_id=1, source_target_pairs={{0,1},{1,2},{2,3},{3,4},{4,5},{5,6},{6,7},{7,8},{8,9},{9,10},{10,1... | collective-permute-start | bytes 1572872 | tf_op jit(solution)/shard_map/ppermute | solution.py:22
  61.7 34.0 %copy-start = (bf16[8,16,32,128]{3,2,1,0:T(8,128)(2,1)S(1)}, bf16[8,16,32,128]{3,2,1,0:T(8,128)(2,1)}, u32[]{:S(2)}) copy-start(bf16[8,16,32,128]{3,2,1,0:T(8,128)(2,1)} %stencil_filtered.1.refs_1_) | copy-start | bytes 3145732
  61.7 6.7 %collective-permute-start.5 = (bf16[4,16,32,128]{3,2,1,0:T(8,128)(2,1)S(1)}, bf16[4,16,32,128]{3,2,1,0:T(8,128)(2,1)S(1)}, u32[]{:S(2)}, u32[]{:S(2)}) collective-permute-start(bf16[4,16,32,128]{3,2,1,0:T(8,128)(2,1)S(1)} %get-tuple-element.3), channel_id=1, source_target_pairs={{1,0},{2,1},{3,2},{4,3},{5,4},{6,5},{7,6},{8,7},{9,8},{10,9},{11,1... | collective-permute-start | bytes 1572872 | tf_op jit(solution)/shard_map/ppermute | solution.py:23
  67.9 0.8 copy-start.5
  68.7 0.8 copy-start.8
  78.1 19.9 %copy-start.2 = (bf16[8,16,32,128]{3,2,1,0:T(8,128)(2,1)S(1)}, bf16[8,16,32,128]{3,2,1,0:T(8,128)(2,1)}, u32[]{:S(2)}) copy-start(bf16[8,16,32,128]{3,2,1,0:T(8,128)(2,1)} %stencil_applied.1) | copy-start | bytes 3145732
  95.7 2.3 %copy-start.1 = (bf16[4096,256]{1,0:T(8,128)(2,1)S(1)}, bf16[4096,256]{1,0:T(8,128)(2,1)}, u32[]{:S(2)}) copy-start(bf16[4096,256]{1,0:T(8,128)(2,1)} %all-gather.2.cloned.1.call-done) | copy-start | bytes 6291460
  98.5 1.6 %collective-permute-start.6 = (f32[2,128,256]{2,1,0:T(8,128)S(1)}, f32[2,128,256]{2,1,0:T(8,128)S(1)}, u32[]{:S(2)}, u32[]{:S(2)}) collective-permute-start(f32[2,128,256]{2,1,0:T(8,128)S(1)} %pad_maximum_fusion), channel_id=1, source_target_pairs={{0,1},{1,0},{2,3},{3,2},{4,5},{5,4},{6,7},{7,6},{8,9},{9,8},{10,11... | collective-permute-start | bytes 786440 | tf_op jit(solution)/shard_map/ppermute | solution.py:90
  100.2 8.4 %collective-permute-start.7 = (f32[2,128,256]{2,1,0:T(8,128)S(1)}, f32[2,128,256]{2,1,0:T(8,128)S(1)}, u32[]{:S(2)}, u32[]{:S(2)}) collective-permute-start(f32[2,128,256]{2,1,0:T(8,128)S(1)} %fusion), channel_id=1, source_target_pairs={{0,2},{1,3},{2,0},{3,1},{4,6},{5,7},{6,4},{7,5},{8,10},{9,11},{10,... | collective-permute-start | bytes 786440 | tf_op jit(solution)/shard_map/ppermute | solution.py:90
  108.6 7.6 %collective-permute-start.8 = (f32[2,128,256]{2,1,0:T(8,128)S(1)}, f32[2,128,256]{2,1,0:T(8,128)S(1)}, u32[]{:S(2)}, u32[]{:S(2)}) collective-permute-start(f32[2,128,256]{2,1,0:T(8,128)S(1)} %fusion.8), channel_id=1, source_target_pairs={{0,4},{1,5},{2,6},{3,7},{4,0},{5,1},{6,2},{7,3},{8,12},{9,13},{10,... | collective-permute-start | bytes 786440 | tf_op jit(solution)/shard_map/ppermute | solution.py:90
  116.2 13.2 %collective-permute-start.9 = (f32[2,128,256]{2,1,0:T(8,128)S(1)}, f32[2,128,256]{2,1,0:T(8,128)S(1)}, u32[]{:S(2)}, u32[]{:S(2)}) collective-permute-start(f32[2,128,256]{2,1,0:T(8,128)S(1)} %add.14), channel_id=1, source_target_pairs={{0,8},{1,9},{2,10},{3,11},{4,12},{5,13},{6,14},{7,15},{8,0},{9,1},... | collective-permute-start | bytes 786440 | tf_op jit(solution)/shard_map/ppermute | solution.py:90
Sparse Core Ops, SparseCore 0:
  55.3 40.3 all-gather.1

commit v3 on v2

--- a/solution.py
+++ b/solution.py
@@ -82,13 +82,30 @@
     )(*operands)
 
 
-def butterfly_sum(values, axis):
+def halving_sum(values, axis):
     count = lax.axis_size(axis)
+    index = lax.axis_index(axis)
+    bits = []
     bit = 1
     while bit < count:
+        bits.append(bit)
+        bit *= 2
+    for bit in bits:
         pairs = [(i, i ^ bit) for i in range(count)]
-        values = values + lax.ppermute(values, axis, pairs)
-        bit *= 2
+        half = values.shape[1] // 2
+        upper = (index // bit) % 2
+        keep = lax.dynamic_slice_in_dim(values, upper * half, half, axis=1)
+        send = lax.dynamic_slice_in_dim(values, (1 - upper) * half, half, axis=1)
+        values = keep + lax.ppermute(send, axis, pairs)
+    for bit in reversed(bits):
+        pairs = [(i, i ^ bit) for i in range(count)]
+        upper = (index // bit) % 2
+        other = lax.ppermute(values, axis, pairs)
+        values = jnp.where(
+            upper == 0,
+            jnp.concatenate([values, other], axis=1),
+            jnp.concatenate([other, values], axis=1),
+        )
     return values
 
 
@@ -102,13 +119,20 @@
     cell_weight = 1.0 / (cell_count * lax.axis_size("domain"))
     own_block = filtered.reshape(cell_count, nb)
     applied = applied_grid.reshape(cell_count, nb)
-    piece = lax.all_gather(own_block, "band", axis=1, tiled=True)
-    correlation_piece = jnp.einsum(
-        "cb,ck->bk", own_block, piece, preferred_element_type=jnp.float32
+    band = lax.axis_index("band")
+    partner = lax.ppermute(own_block, "band", [(0, 1), (1, 0)])
+    gram = lambda rows, cols: jnp.einsum(
+        "cb,ck->bk", rows, cols, preferred_element_type=jnp.float32
     )
-    energy_piece = jnp.einsum("cb,ck->bk", applied, piece, preferred_element_type=jnp.float32)
+    placed = lambda mine, theirs: jnp.where(
+        band == 0,
+        jnp.concatenate([mine, theirs], axis=1),
+        jnp.concatenate([theirs, mine], axis=1),
+    )
+    correlation_piece = placed(gram(own_block, own_block), gram(own_block, partner))
+    energy_piece = placed(gram(applied, own_block), gram(applied, partner))
     partial_terms = jnp.stack((correlation_piece, energy_piece))
-    summed = butterfly_sum(partial_terms, "domain") * cell_weight
+    summed = halving_sum(partial_terms, "domain") * cell_weight
     correlation = summed[0]
     projected = summed[1]
     return (filtered, correlation, projected)

time: 137 us -> 141 us (1.029)
  between operations: 14.1 us -> 0.85 us
  starting transfers between devices: 21.4 us -> 31.9 us
  waiting for transfers between devices: 63 us -> 66.7 us
  local copies, waits for them, and re-layouts: 9.13 us -> 11.2 us
    ppermute x4 -> x9, waiting for transfers between devices: 25.1 us -> 46.5 us  [the longest x4 24.9 us: halving_sum(): values = keep + lax.ppermute(send, axis, pairs)]
    all_gather x1 -> x0, waiting for transfers between devices: 17.6 us -> none  [shards(): piece = lax.all_gather(own_block, 'band', axis=1, tiled=True)]
    ppermute x4 -> x9, starting transfers between devices: 5.63 us -> 17 us  [the longest x4 13.7 us: halving_sum(): values = keep + lax.ppermute(send, axis, pairs)]
    dot_general x2 -> x4, matrix products: 2.76 us -> 3.22 us  [shards(): jnp.einsum('cb,ck->bk', rows, cols, preferred_element_type=jnp.float32)]
  transfers between devices with their start and end apart: 11 -> 15, of which waited for: 10 -> 12; matrix products, arithmetic and copies ran while one was open for 1% -> 3% of each run, Pallas kernels for 6% -> 6%
where the time goes in v3:
time: 141 us
  waiting for transfers between devices  66.7 us (47%)
  starting transfers between devices  31.9 us (23%)
  Pallas kernels  26.2 us (19%)
  local copies, waits for them, and re-layouts  11.2 us (8%)
  matrix products  3.22 us (2%)
    pallas_call x3, Pallas kernels, stencil_stage(): pl.pallas_call(stencil_kernel(stage, planes, ny, nz), out_shape=jax.Shape...  26.2 us
    ppermute x4, waiting for transfers between devices, halving_sum(): values = keep + lax.ppermute(send, axis, pairs)  24.9 us
    ppermute x4, waiting for transfers between devices, halving_sum(): other = lax.ppermute(values, axis, pairs)  21.6 us
    ppermute x3, waiting for transfers between devices, halos(): lax.ppermute(lax.slice_in_dim(block, block.shape[0] - width, None, axis=0...  20.1 us
    ppermute x4, starting transfers between devices, halving_sum(): values = keep + lax.ppermute(send, axis, pairs)  13.7 us
    ppermute x3, starting transfers between devices, halos(): lax.ppermute(lax.slice_in_dim(block, block.shape[0] - width, None, axis=0...  9.91 us
    ppermute x3, starting transfers between devices, halos(): lax.ppermute(lax.slice_in_dim(block, 0, width, axis=0), axis, backward)  5.03 us
    slice x3, local copies, waits for them, and re-layouts, halos(): lax.slice_in_dim(block, 0, width, axis=0)  4.9 us
  transfers between devices with their start and end apart: 15, of which 12 were waited for; matrix products, arithmetic and copies ran while one was open for 3% of the time, Pallas kernels for 6%

profile of v3, /device:TPU:0, one launch (start us, length us, event | category | flops | bytes accessed | tf_op | source)
XLA Modules:
  0.0 140.9 jit_solution(3218765126053818861)
XLA Ops:
  0.6 1.3 fusion.6
  2.5 5.0 %collective-permute-start.1 = (bf16[4,16,32,128]{3,2,1,0:T(8,128)(2,1)S(1)}, bf16[4,16,32,128]{3,2,1,0:T(8,128)(2,1)S(1)}, u32[]{:S(2)}, u32[]{:S(2)}) collective-permute-start(bf16[4,16,32,128]{3,2,1,0:T(8,128)(2,1)S(1)} %get-tuple-element.10), channel_id=1, source_target_pairs={{1,0},{2,1},{3,2},{4,3},{5,4},{6,5},{7,6},{8,7},{9,8},{10,9},{11,1... | collective-permute-start | bytes 1572872 | tf_op jit(solution)/shard_map/ppermute | solution.py:23
  7.5 6.9 %collective-permute-done.refs_0_ = bf16[4,16,32,128]{3,2,1,0:T(8,128)(2,1)S(1)} collective-permute-done((bf16[4,16,32,128]{3,2,1,0:T(8,128)(2,1)S(1)}, bf16[4,16,32,128]{3,2,1,0:T(8,128)(2,1)S(1)}, u32[]{:S(2)}, u32[]{:S(2)}) %collective-permute-start) | collective-permute-done | bytes 524320 | tf_op jit(solution)/shard_map/ppermute | solution.py:22
  14.4 2.0 %broadcast_in_dim.2.refs_3_ = f32[8,16,32,128]{3,2,1,0:T(8,128)} broadcast(f32[8,16,32]{2,1,0:T(8,128)S(1)} %copy-done.9), dimensions={0,1,2} | broadcast | bytes 2113536 | tf_op jit(solution)/shard_map/broadcast_in_dim | solution.py:114
  16.4 8.7 %stencil_first.1.refs_1_ = bf16[8,16,32,128]{3,2,1,0:T(8,128)(2,1)} custom-call(bf16[4,16,32,128]{3,2,1,0:T(8,128)(2,1)} %copy-done.5, bf16[8,16,32,128]{3,2,1,0:T(8,128)(2,1)} %refs_4_.1, bf16[4,16,32,128]{3,2,1,0:T(8,128)(2,1)} %copy-done.7, f32[8,16,32,128]{3,2,1,0:T(8,128)} %broadcast_in_dim.2.refs_3_), custom_call_target="tpu_custom_call" | custom-call | tf_op jit(solution)/shard_map/stencil_first/pallas_call | solution.py:78
  25.1 1.3 fusion.5
  26.4 4.9 %collective-permute-start.2 = (bf16[4,16,32,128]{3,2,1,0:T(8,128)(2,1)S(1)}, bf16[4,16,32,128]{3,2,1,0:T(8,128)(2,1)S(1)}, u32[]{:S(2)}, u32[]{:S(2)}) collective-permute-start(bf16[4,16,32,128]{3,2,1,0:T(8,128)(2,1)S(1)} %get-tuple-element.9), channel_id=1, source_target_pairs={{0,1},{1,2},{2,3},{3,4},{4,5},{5,6},{6,7},{7,8},{8,9},{9,10},{10,1... | collective-permute-start | bytes 1572872 | tf_op jit(solution)/shard_map/ppermute | solution.py:22
  31.3 6.6 %collective-permute-done.2.refs_0_ = bf16[4,16,32,128]{3,2,1,0:T(8,128)(2,1)S(1)} collective-permute-done((bf16[4,16,32,128]{3,2,1,0:T(8,128)(2,1)S(1)}, bf16[4,16,32,128]{3,2,1,0:T(8,128)(2,1)S(1)}, u32[]{:S(2)}, u32[]{:S(2)}) %collective-permute-start.2) | collective-permute-done | bytes 524320 | tf_op jit(solution)/shard_map/ppermute | solution.py:22
  38.7 0.8 copy-done.8
  39.5 9.1 %stencil_filtered.1.refs_1_ = bf16[8,16,32,128]{3,2,1,0:T(8,128)(2,1)} custom-call(bf16[4,16,32,128]{3,2,1,0:T(8,128)(2,1)} %copy-done.6, bf16[8,16,32,128]{3,2,1,0:T(8,128)(2,1)} %stencil_first.1.refs_1_, bf16[4,16,32,128]{3,2,1,0:T(8,128)(2,1)} %copy-done.8, f32[8,16,32,128]{3,2,1,0:T(8,128)} %broadcast_in_dim.2.refs_3_, bf16[8,16,32,128]{3,2,1,0:T(8,128)(2,1)} %refs_4_.1), custom_call_target="tpu_custom_call" | custom-call | tf_op jit(solution)/shard_map/stencil_filtered/pallas_call | solution.py:78
  48.6 1.9 %collective-permute-start.4 = (bf16[4096,128]{1,0:T(8,128)(2,1)}, bf16[4096,128]{1,0:T(8,128)(2,1)S(1)}, u32[]{:S(2)}, u32[]{:S(2)}) collective-permute-start(bf16[4096,128]{1,0:T(8,128)(2,1)} %bitcast.30), channel_id=1, source_target_pairs={{0,16},{16,0},{1,17},{17,1},{2,18},{18,2},{3,19},{19,3},{4,20},{20... | collective-permute-start | bytes 3145736 | tf_op jit(solution)/shard_map/ppermute | solution.py:123
  50.5 2.3 %fusion.4 = (bf16[4,16,32,128]{3,2,1,0:T(8,128)(2,1)}, bf16[4,16,32,128]{3,2,1,0:T(8,128)(2,1)}) fusion(bf16[8,16,32,128]{3,2,1,0:T(8,128)(2,1)} %stencil_filtered.1.refs_1_), kind=kLoop, calls=%fused_computation.26 | loop fusion | bytes 2097152 | tf_op jit(solution)/shard_map/slice | solution.py:23
  52.8 4.5 %collective-permute-start.5 = (bf16[4,16,32,128]{3,2,1,0:T(8,128)(2,1)}, bf16[4,16,32,128]{3,2,1,0:T(8,128)(2,1)S(1)}, u32[]{:S(2)}, u32[]{:S(2)}) collective-permute-start(bf16[4,16,32,128]{3,2,1,0:T(8,128)(2,1)} %get-tuple-element.7), channel_id=1, source_target_pairs={{0,1},{1,2},{2,3},{3,4},{4,5},{5,6},{6,7},{7,8},{8,9},{9,10},{10,1... | collective-permute-start | bytes 1572872 | tf_op jit(solution)/shard_map/ppermute | solution.py:22
  57.8 6.6 %collective-permute-done.5.refs_0_ = bf16[4,16,32,128]{3,2,1,0:T(8,128)(2,1)S(1)} collective-permute-done((bf16[4,16,32,128]{3,2,1,0:T(8,128)(2,1)}, bf16[4,16,32,128]{3,2,1,0:T(8,128)(2,1)S(1)}, u32[]{:S(2)}, u32[]{:S(2)}) %collective-permute-start.5) | collective-permute-done | bytes 524320 | tf_op jit(solution)/shard_map/ppermute | solution.py:22
  64.4 0.8 copy-done.3
  65.2 0.8 copy-done.4
  66.0 8.4 %stencil_applied.1 = bf16[8,16,32,128]{3,2,1,0:T(8,128)(2,1)} custom-call(bf16[4,16,32,128]{3,2,1,0:T(8,128)(2,1)} %copy-done.3, bf16[8,16,32,128]{3,2,1,0:T(8,128)(2,1)} %stencil_filtered.1.refs_1_, bf16[4,16,32,128]{3,2,1,0:T(8,128)(2,1)} %copy-done.4, f32[8,16,32,128]{3,2,1,0:T(8,128)} %broadcast_in_dim.2.refs_3_), custom_call_target="tpu_custom_call" | custom-call | tf_op jit(solution)/shard_map/stencil_applied/pallas_call | solution.py:78
  74.4 1.8 %convolution_bitcast_fusion.1 = f32[1,128,128]{1,2,0:T(8,128)S(1)} fusion(bf16[8,16,32,128]{3,2,1,0:T(8,128)(2,1)} %stencil_applied.1, bf16[8,16,32,128]{3,2,1,0:T(8,128)(2,1)S(1)} %copy-done.1), kind=kOutput, calls=%fused_computation.1 | convolution fusion | flops 134217728 | bytes 2162688 | tf_op jit(solution)/shard_map/cb,ck->bk/dot_general | solution.py:124
  77.3 6.7 %collective-permute-start.7 = (f32[2,64,256]{1,2,0:T(8,128)S(1)}, f32[2,64,256]{1,2,0:T(8,128)S(1)}, u32[]{:S(2)}, u32[]{:S(2)}) collective-permute-start(f32[2,64,256]{1,2,0:T(8,128)S(1)} %fusion), channel_id=1, source_target_pairs={{0,1},{1,0},{2,3},{3,2},{4,5},{5,4},{6,7},{7,6},{8,9},{9,8},{10,11... | collective-permute-start | bytes 393224 | tf_op jit(solution)/shard_map/ppermute | solution.py:99
  84.1 1.2 collective-permute-done.7
  85.5 2.7 %collective-permute-start.8 = (f32[2,32,256]{1,2,0:T(8,128)S(1)}, f32[2,32,256]{1,2,0:T(8,128)S(1)}, u32[]{:S(2)}, u32[]{:S(2)}) collective-permute-start(f32[2,32,256]{1,2,0:T(8,128)S(1)} %constant_dynamic-slice_fusion.2), channel_id=1, source_target_pairs={{0,2},{1,3},{2,0},{3,1},{4,6},{5,7},{6,4},{7,5},{8,10},{9,11},{10,... | collective-permute-start | bytes 196616 | tf_op jit(solution)/shard_map/ppermute | solution.py:99
  88.2 6.6 %collective-permute-done.8 = f32[2,32,256]{1,2,0:T(8,128)S(1)} collective-permute-done((f32[2,32,256]{1,2,0:T(8,128)S(1)}, f32[2,32,256]{1,2,0:T(8,128)S(1)}, u32[]{:S(2)}, u32[]{:S(2)}) %collective-permute-start.8) | collective-permute-done | bytes 65568 | tf_op jit(solution)/shard_map/ppermute | solution.py:99
  95.1 1.6 %collective-permute-start.9 = (f32[2,16,256]{1,2,0:T(8,128)S(1)}, f32[2,16,256]{1,2,0:T(8,128)S(1)}, u32[]{:S(2)}, u32[]{:S(2)}) collective-permute-start(f32[2,16,256]{1,2,0:T(8,128)S(1)} %constant_dynamic-slice_fusion.1), channel_id=1, source_target_pairs={{0,4},{1,5},{2,6},{3,7},{4,0},{5,1},{6,2},{7,3},{8,12},{9,13},{10,... | collective-permute-start | bytes 98312 | tf_op jit(solution)/shard_map/ppermute | solution.py:99
  96.7 6.3 %collective-permute-done.9 = f32[2,16,256]{1,2,0:T(8,128)S(1)} collective-permute-done((f32[2,16,256]{1,2,0:T(8,128)S(1)}, f32[2,16,256]{1,2,0:T(8,128)S(1)}, u32[]{:S(2)}, u32[]{:S(2)}) %collective-permute-start.9) | collective-permute-done | bytes 32800 | tf_op jit(solution)/shard_map/ppermute | solution.py:99
  103.3 2.7 %collective-permute-start.10 = (f32[2,8,256]{1,2,0:T(8,128)S(1)}, f32[2,8,256]{1,2,0:T(8,128)S(1)}, u32[]{:S(2)}, u32[]{:S(2)}) collective-permute-start(f32[2,8,256]{1,2,0:T(8,128)S(1)} %constant_dynamic-slice_fusion), channel_id=1, source_target_pairs={{0,8},{1,9},{2,10},{3,11},{4,12},{5,13},{6,14},{7,15},{8,0},{9,1},... | collective-permute-start | bytes 49160 | tf_op jit(solution)/shard_map/ppermute | solution.py:99
  105.9 10.9 %collective-permute-done.10 = f32[2,8,256]{1,2,0:T(8,128)S(1)} collective-permute-done((f32[2,8,256]{1,2,0:T(8,128)S(1)}, f32[2,8,256]{1,2,0:T(8,128)S(1)}, u32[]{:S(2)}, u32[]{:S(2)}) %collective-permute-start.10) | collective-permute-done | bytes 16416 | tf_op jit(solution)/shard_map/ppermute | solution.py:99
  117.1 13.2 %collective-permute-done.11 = f32[2,8,256]{1,2,0:T(8,128)S(1)} collective-permute-done((f32[2,8,256]{1,2,0:T(8,128)S(1)}, f32[2,8,256]{1,2,0:T(8,128)S(1)}, u32[]{:S(2)}, u32[]{:S(2)}) %collective-permute-start.11) | collective-permute-done | bytes 16416 | tf_op jit(solution)/shard_map/ppermute | solution.py:103
  130.4 3.9 %collective-permute-done.12 = f32[2,16,256]{2,1,0:T(8,128)S(1)} collective-permute-done((f32[2,16,256]{2,1,0:T(8,128)S(1)}, f32[2,16,256]{2,1,0:T(8,128)S(1)}, u32[]{:S(2)}, u32[]{:S(2)}) %collective-permute-start.12) | collective-permute-done | bytes 32800 | tf_op jit(solution)/shard_map/ppermute | solution.py:103
  134.4 1.1 collective-permute-start.13
  135.5 3.2 %collective-permute-done.13 = f32[2,32,256]{2,1,0:T(8,128)S(1)} collective-permute-done((f32[2,32,256]{2,1,0:T(8,128)S(1)}, f32[2,32,256]{2,1,0:T(8,128)S(1)}, u32[]{:S(2)}, u32[]{:S(2)}) %collective-permute-start.13) | collective-permute-done | bytes 65568 | tf_op jit(solution)/shard_map/ppermute | solution.py:103
  138.8 1.3 collective-permute-done.14
  140.1 0.7 slice_bitcast_fusion
  (46 shorter events, 4.3 us)
Async XLA Ops:
  0.6 13.8 %copy-start.9 = (f32[8,16,32]{2,1,0:T(8,128)S(1)}, f32[8,16,32]{2,1,0:T(8,128)}, u32[]{:S(2)}) copy-start(f32[8,16,32]{2,1,0:T(8,128)} %param.3) | copy-start | bytes 49156
  2.0 12.4 %collective-permute-start = (bf16[4,16,32,128]{3,2,1,0:T(8,128)(2,1)S(1)}, bf16[4,16,32,128]{3,2,1,0:T(8,128)(2,1)S(1)}, u32[]{:S(2)}, u32[]{:S(2)}) collective-permute-start(bf16[4,16,32,128]{3,2,1,0:T(8,128)(2,1)S(1)} %get-tuple-element.11), channel_id=1, source_target_pairs={{0,1},{1,2},{2,3},{3,4},{4,5},{5,6},{6,7},{7,8},{8,9},{9,10},{10,1... | collective-permute-start | bytes 1572872 | tf_op jit(solution)/shard_map/ppermute | solution.py:22
  2.5 11.9 %collective-permute-start.1 = (bf16[4,16,32,128]{3,2,1,0:T(8,128)(2,1)S(1)}, bf16[4,16,32,128]{3,2,1,0:T(8,128)(2,1)S(1)}, u32[]{:S(2)}, u32[]{:S(2)}) collective-permute-start(bf16[4,16,32,128]{3,2,1,0:T(8,128)(2,1)S(1)} %get-tuple-element.10), channel_id=1, source_target_pairs={{1,0},{2,1},{3,2},{4,3},{5,4},{6,5},{7,6},{8,7},{9,8},{10,9},{11,1... | collective-permute-start | bytes 1572872 | tf_op jit(solution)/shard_map/ppermute | solution.py:23
  14.4 2.0 %copy-start.5 = (bf16[4,16,32,128]{3,2,1,0:T(8,128)(2,1)}, bf16[4,16,32,128]{3,2,1,0:T(8,128)(2,1)S(1)}, u32[]{:S(2)}) copy-start(bf16[4,16,32,128]{3,2,1,0:T(8,128)(2,1)S(1)} %collective-permute-done.refs_0_) | copy-start | bytes 1572868
  14.4 2.0 %copy-start.7 = (bf16[4,16,32,128]{3,2,1,0:T(8,128)(2,1)}, bf16[4,16,32,128]{3,2,1,0:T(8,128)(2,1)S(1)}, u32[]{:S(2)}) copy-start(bf16[4,16,32,128]{3,2,1,0:T(8,128)(2,1)S(1)} %collective-permute-done.1.refs_2_) | copy-start | bytes 1572868
  26.4 11.5 %collective-permute-start.2 = (bf16[4,16,32,128]{3,2,1,0:T(8,128)(2,1)S(1)}, bf16[4,16,32,128]{3,2,1,0:T(8,128)(2,1)S(1)}, u32[]{:S(2)}, u32[]{:S(2)}) collective-permute-start(bf16[4,16,32,128]{3,2,1,0:T(8,128)(2,1)S(1)} %get-tuple-element.9), channel_id=1, source_target_pairs={{0,1},{1,2},{2,3},{3,4},{4,5},{5,6},{6,7},{7,8},{8,9},{9,10},{10,1... | collective-permute-start | bytes 1572872 | tf_op jit(solution)/shard_map/ppermute | solution.py:22
  31.3 6.7 %collective-permute-start.3 = (bf16[4,16,32,128]{3,2,1,0:T(8,128)(2,1)S(1)}, bf16[4,16,32,128]{3,2,1,0:T(8,128)(2,1)S(1)}, u32[]{:S(2)}, u32[]{:S(2)}) collective-permute-start(bf16[4,16,32,128]{3,2,1,0:T(8,128)(2,1)S(1)} %get-tuple-element.8), channel_id=1, source_target_pairs={{1,0},{2,1},{3,2},{4,3},{5,4},{6,5},{7,6},{8,7},{9,8},{10,9},{11,1... | collective-permute-start | bytes 1572872 | tf_op jit(solution)/shard_map/ppermute | solution.py:23
  37.9 0.8 copy-start.6
  38.7 0.8 copy-start.8
  48.6 8.7 %copy-start = (bf16[8,16,32,128]{3,2,1,0:T(8,128)(2,1)S(1)}, bf16[8,16,32,128]{3,2,1,0:T(8,128)(2,1)}, u32[]{:S(2)}) copy-start(bf16[8,16,32,128]{3,2,1,0:T(8,128)(2,1)} %stencil_filtered.1.refs_1_) | copy-start | bytes 3145732
  48.6 27.6 %collective-permute-start.4 = (bf16[4096,128]{1,0:T(8,128)(2,1)}, bf16[4096,128]{1,0:T(8,128)(2,1)S(1)}, u32[]{:S(2)}, u32[]{:S(2)}) collective-permute-start(bf16[4096,128]{1,0:T(8,128)(2,1)} %bitcast.30), channel_id=1, source_target_pairs={{0,16},{16,0},{1,17},{17,1},{2,18},{18,2},{3,19},{19,3},{4,20},{20... | collective-permute-start | bytes 3145736 | tf_op jit(solution)/shard_map/ppermute | solution.py:123
  52.8 11.6 %collective-permute-start.5 = (bf16[4,16,32,128]{3,2,1,0:T(8,128)(2,1)}, bf16[4,16,32,128]{3,2,1,0:T(8,128)(2,1)S(1)}, u32[]{:S(2)}, u32[]{:S(2)}) collective-permute-start(bf16[4,16,32,128]{3,2,1,0:T(8,128)(2,1)} %get-tuple-element.7), channel_id=1, source_target_pairs={{0,1},{1,2},{2,3},{3,4},{4,5},{5,6},{6,7},{7,8},{8,9},{9,10},{10,1... | collective-permute-start | bytes 1572872 | tf_op jit(solution)/shard_map/ppermute | solution.py:22
  57.3 7.1 %collective-permute-start.6 = (bf16[4,16,32,128]{3,2,1,0:T(8,128)(2,1)}, bf16[4,16,32,128]{3,2,1,0:T(8,128)(2,1)S(1)}, u32[]{:S(2)}, u32[]{:S(2)}) collective-permute-start(bf16[4,16,32,128]{3,2,1,0:T(8,128)(2,1)} %get-tuple-element.6), channel_id=1, source_target_pairs={{1,0},{2,1},{3,2},{4,3},{5,4},{6,5},{7,6},{8,7},{9,8},{10,9},{11,1... | collective-permute-start | bytes 1572872 | tf_op jit(solution)/shard_map/ppermute | solution.py:23
  57.8 16.6 %copy-start.1 = (bf16[8,16,32,128]{3,2,1,0:T(8,128)(2,1)S(1)}, bf16[8,16,32,128]{3,2,1,0:T(8,128)(2,1)}, u32[]{:S(2)}) copy-start(bf16[8,16,32,128]{3,2,1,0:T(8,128)(2,1)} %stencil_filtered.1.refs_1_) | copy-start | bytes 3145732
  64.4 0.8 copy-start.3
  65.2 0.8 copy-start.4
  74.4 1.8 %copy-start.2 = (bf16[8,16,32,128]{3,2,1,0:T(8,128)(2,1)S(1)}, bf16[8,16,32,128]{3,2,1,0:T(8,128)(2,1)}, u32[]{:S(2)}) copy-start(bf16[8,16,32,128]{3,2,1,0:T(8,128)(2,1)} %stencil_applied.1) | copy-start | bytes 3145732
  77.3 7.9 %collective-permute-start.7 = (f32[2,64,256]{1,2,0:T(8,128)S(1)}, f32[2,64,256]{1,2,0:T(8,128)S(1)}, u32[]{:S(2)}, u32[]{:S(2)}) collective-permute-start(f32[2,64,256]{1,2,0:T(8,128)S(1)} %fusion), channel_id=1, source_target_pairs={{0,1},{1,0},{2,3},{3,2},{4,5},{5,4},{6,7},{7,6},{8,9},{9,8},{10,11... | collective-permute-start | bytes 393224 | tf_op jit(solution)/shard_map/ppermute | solution.py:99
  85.5 9.3 %collective-permute-start.8 = (f32[2,32,256]{1,2,0:T(8,128)S(1)}, f32[2,32,256]{1,2,0:T(8,128)S(1)}, u32[]{:S(2)}, u32[]{:S(2)}) collective-permute-start(f32[2,32,256]{1,2,0:T(8,128)S(1)} %constant_dynamic-slice_fusion.2), channel_id=1, source_target_pairs={{0,2},{1,3},{2,0},{3,1},{4,6},{5,7},{6,4},{7,5},{8,10},{9,11},{10,... | collective-permute-start | bytes 196616 | tf_op jit(solution)/shard_map/ppermute | solution.py:99
  95.1 7.9 %collective-permute-start.9 = (f32[2,16,256]{1,2,0:T(8,128)S(1)}, f32[2,16,256]{1,2,0:T(8,128)S(1)}, u32[]{:S(2)}, u32[]{:S(2)}) collective-permute-start(f32[2,16,256]{1,2,0:T(8,128)S(1)} %constant_dynamic-slice_fusion.1), channel_id=1, source_target_pairs={{0,4},{1,5},{2,6},{3,7},{4,0},{5,1},{6,2},{7,3},{8,12},{9,13},{10,... | collective-permute-start | bytes 98312 | tf_op jit(solution)/shard_map/ppermute | solution.py:99
  103.3 13.5 %collective-permute-start.10 = (f32[2,8,256]{1,2,0:T(8,128)S(1)}, f32[2,8,256]{1,2,0:T(8,128)S(1)}, u32[]{:S(2)}, u32[]{:S(2)}) collective-permute-start(f32[2,8,256]{1,2,0:T(8,128)S(1)} %constant_dynamic-slice_fusion), channel_id=1, source_target_pairs={{0,8},{1,9},{2,10},{3,11},{4,12},{5,13},{6,14},{7,15},{8,0},{9,1},... | collective-permute-start | bytes 49160 | tf_op jit(solution)/shard_map/ppermute | solution.py:99
  116.9 13.4 %collective-permute-start.11 = (f32[2,8,256]{1,2,0:T(8,128)S(1)}, f32[2,8,256]{1,2,0:T(8,128)S(1)}, u32[]{:S(2)}, u32[]{:S(2)}) collective-permute-start(f32[2,8,256]{1,2,0:T(8,128)S(1)} %dynamic-slice_add_fusion), channel_id=1, source_target_pairs={{0,8},{1,9},{2,10},{3,11},{4,12},{5,13},{6,14},{7,15},{8,0},{9,1},... | collective-permute-start | bytes 49160 | tf_op jit(solution)/shard_map/ppermute | solution.py:103
  130.4 4.0 %collective-permute-start.12 = (f32[2,16,256]{2,1,0:T(8,128)S(1)}, f32[2,16,256]{2,1,0:T(8,128)S(1)}, u32[]{:S(2)}, u32[]{:S(2)}) collective-permute-start(f32[2,16,256]{2,1,0:T(8,128)S(1)} %maximum_select_fusion.5), channel_id=1, source_target_pairs={{0,4},{1,5},{2,6},{3,7},{4,0},{5,1},{6,2},{7,3},{8,12},{9,13},{10,... | collective-permute-start | bytes 98312 | tf_op jit(solution)/shard_map/ppermute | solution.py:103
  134.4 4.3 %collective-permute-start.13 = (f32[2,32,256]{2,1,0:T(8,128)S(1)}, f32[2,32,256]{2,1,0:T(8,128)S(1)}, u32[]{:S(2)}, u32[]{:S(2)}) collective-permute-start(f32[2,32,256]{2,1,0:T(8,128)S(1)} %maximum_select_fusion.4), channel_id=1, source_target_pairs={{0,2},{1,3},{2,0},{3,1},{4,6},{5,7},{6,4},{7,5},{8,10},{9,11},{10,... | collective-permute-start | bytes 196616 | tf_op jit(solution)/shard_map/ppermute | solution.py:103
  138.7 1.4 %collective-permute-start.14 = (f32[2,64,256]{2,1,0:T(8,128)S(1)}, f32[2,64,256]{2,1,0:T(8,128)S(1)}, u32[]{:S(2)}, u32[]{:S(2)}) collective-permute-start(f32[2,64,256]{2,1,0:T(8,128)S(1)} %maximum_select_fusion.3), channel_id=1, source_target_pairs={{0,1},{1,0},{2,3},{3,2},{4,5},{5,4},{6,7},{7,6},{8,9},{9,8},{10,11... | collective-permute-start | bytes 393224 | tf_op jit(solution)/shard_map/ppermute | solution.py:103

commit v4 on v2

--- a/solution.py
+++ b/solution.py
@@ -95,22 +95,26 @@
 def shards(orbitals, potential):
     planes, ny, nz, nb = orbitals.shape
     potential_wide = jnp.broadcast_to(potential[:, :, :, None], (planes, ny, nz, nb))
+    cell_count = planes * ny * nz
+    cell_weight = 1.0 / (cell_count * lax.axis_size("domain"))
+    band = lax.axis_index("band")
+    gram = lambda rows, cols: jnp.einsum(
+        "cb,ck->bk", rows, cols, preferred_element_type=jnp.float32
+    )
+    placed = lambda mine, theirs: jnp.where(
+        band == 0,
+        jnp.concatenate([mine, theirs], axis=1),
+        jnp.concatenate([theirs, mine], axis=1),
+    )
     first = stencil_stage("first", orbitals, potential_wide)
     filtered = stencil_stage("filtered", first, potential_wide, orbitals)
-    applied_grid = stencil_stage("applied", filtered, potential_wide)
-    cell_count = planes * ny * nz
-    cell_weight = 1.0 / (cell_count * lax.axis_size("domain"))
     own_block = filtered.reshape(cell_count, nb)
-    applied = applied_grid.reshape(cell_count, nb)
-    piece = lax.all_gather(own_block, "band", axis=1, tiled=True)
-    correlation_piece = jnp.einsum(
-        "cb,ck->bk", own_block, piece, preferred_element_type=jnp.float32
-    )
-    energy_piece = jnp.einsum("cb,ck->bk", applied, piece, preferred_element_type=jnp.float32)
-    partial_terms = jnp.stack((correlation_piece, energy_piece))
-    summed = butterfly_sum(partial_terms, "domain") * cell_weight
-    correlation = summed[0]
-    projected = summed[1]
+    partner = lax.ppermute(own_block, "band", [(0, 1), (1, 0)])
+    correlation_piece = placed(gram(own_block, own_block), gram(own_block, partner))
+    correlation = butterfly_sum(correlation_piece, "domain") * cell_weight
+    applied = stencil_stage("applied", filtered, potential_wide).reshape(cell_count, nb)
+    energy_piece = placed(gram(applied, own_block), gram(applied, partner))
+    projected = butterfly_sum(energy_piece, "domain") * cell_weight
     return (filtered, correlation, projected)
 
 

time: 137 us -> 113 us (0.82)
  waiting for transfers between devices: 63 us -> 42.9 us
  between operations: 14.1 us -> 0.77 us
  starting transfers between devices: 21.4 us -> 28.7 us
  local copies, waits for them, and re-layouts: 9.13 us -> 10.6 us
    all_gather x1 -> x0, waiting for transfers between devices: 17.6 us -> none  [shards(): piece = lax.all_gather(own_block, 'band', axis=1, tiled=True)]
    ppermute x4 -> x8, waiting for transfers between devices: 25.1 us -> 16.8 us  [butterfly_sum(): values = values + lax.ppermute(values, axis, pairs)]
    ppermute x4 -> x8, starting transfers between devices: 5.63 us -> 11.8 us  [butterfly_sum(): values = values + lax.ppermute(values, axis, pairs)]
    ppermute x3, waiting for transfers between devices: 0.64 us -> 5.58 us  [halos(): lax.ppermute(lax.slice_in_dim(block, 0, width, axis=0), axis, backward)]
    ppermute x3, starting transfers between devices: 10.7 us -> 6.49 us  [halos(): lax.ppermute(lax.slice_in_dim(block, block.shape[0] - width, None, axis=0...]
    ppermute x3, starting transfers between devices: 5.03 us -> 8.46 us  [halos(): lax.ppermute(lax.slice_in_dim(block, 0, width, axis=0), axis, backward)]
    ppermute x0 -> x1, starting transfers between devices: none -> 1.93 us  [shards(): partner = lax.ppermute(own_block, 'band', [(0, 1), (1, 0)])]
    unnamed x20 -> x22, local copies, waits for them, and re-layouts: 2.57 us -> 3.8 us
  transfers between devices with their start and end apart: 11 -> 15, of which waited for: 10 -> 13; matrix products, arithmetic and copies ran while one was open for 1% -> 5% of each run, Pallas kernels for 6% -> 7%
where the time goes in v4:
time: 113 us
  waiting for transfers between devices  42.9 us (38%)
  starting transfers between devices  28.7 us (25%)
  Pallas kernels  26.2 us (23%)
  local copies, waits for them, and re-layouts  10.6 us (9%)
  matrix products  3.22 us (3%)
    pallas_call x3, Pallas kernels, stencil_stage(): pl.pallas_call(stencil_kernel(stage, planes, ny, nz), out_shape=jax.Shape...  26.2 us
    ppermute x3, waiting for transfers between devices, halos(): lax.ppermute(lax.slice_in_dim(block, block.shape[0] - width, None, axis=0...  20.5 us
    ppermute x8, waiting for transfers between devices, butterfly_sum(): values = values + lax.ppermute(values, axis, pairs)  16.8 us
    ppermute x8, starting transfers between devices, butterfly_sum(): values = values + lax.ppermute(values, axis, pairs)  11.8 us
    ppermute x3, starting transfers between devices, halos(): lax.ppermute(lax.slice_in_dim(block, 0, width, axis=0), axis, backward)  8.46 us
    ppermute x3, starting transfers between devices, halos(): lax.ppermute(lax.slice_in_dim(block, block.shape[0] - width, None, axis=0...  6.49 us
    ppermute x3, waiting for transfers between devices, halos(): lax.ppermute(lax.slice_in_dim(block, 0, width, axis=0), axis, backward)  5.58 us
    slice x3, local copies, waits for them, and re-layouts, halos(): lax.slice_in_dim(block, 0, width, axis=0)  4.88 us
  transfers between devices with their start and end apart: 15, of which 13 were waited for; matrix products, arithmetic and copies ran while one was open for 5% of the time, Pallas kernels for 7%

profile of v4, /device:TPU:0, one launch (start us, length us, event | category | flops | bytes accessed | tf_op | source)
XLA Modules:
  0.0 112.5 jit_solution(15612453509458014896)
XLA Ops:
  0.6 1.3 %fusion.2 = (bf16[4,16,32,128]{3,2,1,0:T(8,128)(2,1)S(1)}, bf16[4,16,32,128]{3,2,1,0:T(8,128)(2,1)S(1)}) fusion(bf16[8,16,32,128]{3,2,1,0:T(8,128)(2,1)} %refs_4_.1), kind=kLoop, calls=%fused_computation.8 | loop fusion | bytes 2097152 | tf_op jit(solution)/shard_map/slice | solution.py:23
  2.5 5.0 %collective-permute-start.1 = (bf16[4,16,32,128]{3,2,1,0:T(8,128)(2,1)S(1)}, bf16[4,16,32,128]{3,2,1,0:T(8,128)(2,1)S(1)}, u32[]{:S(2)}, u32[]{:S(2)}) collective-permute-start(bf16[4,16,32,128]{3,2,1,0:T(8,128)(2,1)S(1)} %get-tuple-element.10), channel_id=1, source_target_pairs={{1,0},{2,1},{3,2},{4,3},{5,4},{6,5},{7,6},{8,7},{9,8},{10,9},{11,1... | collective-permute-start | bytes 1572872 | tf_op jit(solution)/shard_map/ppermute | solution.py:23
  7.5 6.9 %collective-permute-done.refs_0_ = bf16[4,16,32,128]{3,2,1,0:T(8,128)(2,1)S(1)} collective-permute-done((bf16[4,16,32,128]{3,2,1,0:T(8,128)(2,1)S(1)}, bf16[4,16,32,128]{3,2,1,0:T(8,128)(2,1)S(1)}, u32[]{:S(2)}, u32[]{:S(2)}) %collective-permute-start) | collective-permute-done | bytes 524320 | tf_op jit(solution)/shard_map/ppermute | solution.py:22
  14.4 1.9 %broadcast_in_dim.2.refs_3_ = f32[8,16,32,128]{3,2,1,0:T(8,128)} broadcast(f32[8,16,32]{2,1,0:T(8,128)S(1)} %copy-done.9), dimensions={0,1,2} | broadcast | bytes 2113536 | tf_op jit(solution)/shard_map/broadcast_in_dim | solution.py:97
  16.4 8.7 %stencil_first.1.refs_1_ = bf16[8,16,32,128]{3,2,1,0:T(8,128)(2,1)} custom-call(bf16[4,16,32,128]{3,2,1,0:T(8,128)(2,1)} %copy-done.5, bf16[8,16,32,128]{3,2,1,0:T(8,128)(2,1)} %refs_4_.1, bf16[4,16,32,128]{3,2,1,0:T(8,128)(2,1)} %copy-done.7, f32[8,16,32,128]{3,2,1,0:T(8,128)} %broadcast_in_dim.2.refs_3_), custom_call_target="tpu_custom_call" | custom-call | tf_op jit(solution)/shard_map/stencil_first/pallas_call | solution.py:78
  25.1 1.3 %fusion.1 = (bf16[4,16,32,128]{3,2,1,0:T(8,128)(2,1)S(1)}, bf16[4,16,32,128]{3,2,1,0:T(8,128)(2,1)S(1)}) fusion(bf16[8,16,32,128]{3,2,1,0:T(8,128)(2,1)} %stencil_first.1.refs_1_), kind=kLoop, calls=%fused_computation.7 | loop fusion | bytes 2097152 | tf_op jit(solution)/shard_map/slice | solution.py:23
  26.4 4.9 %collective-permute-start.2 = (bf16[4,16,32,128]{3,2,1,0:T(8,128)(2,1)S(1)}, bf16[4,16,32,128]{3,2,1,0:T(8,128)(2,1)S(1)}, u32[]{:S(2)}, u32[]{:S(2)}) collective-permute-start(bf16[4,16,32,128]{3,2,1,0:T(8,128)(2,1)S(1)} %get-tuple-element.9), channel_id=1, source_target_pairs={{0,1},{1,2},{2,3},{3,4},{4,5},{5,6},{6,7},{7,8},{8,9},{9,10},{10,1... | collective-permute-start | bytes 1572872 | tf_op jit(solution)/shard_map/ppermute | solution.py:22
  31.3 6.6 %collective-permute-done.2.refs_0_ = bf16[4,16,32,128]{3,2,1,0:T(8,128)(2,1)S(1)} collective-permute-done((bf16[4,16,32,128]{3,2,1,0:T(8,128)(2,1)S(1)}, bf16[4,16,32,128]{3,2,1,0:T(8,128)(2,1)S(1)}, u32[]{:S(2)}, u32[]{:S(2)}) %collective-permute-start.2) | collective-permute-done | bytes 524320 | tf_op jit(solution)/shard_map/ppermute | solution.py:22
  38.7 0.8 copy-done.8
  39.5 9.1 %stencil_filtered.1.refs_1_ = bf16[8,16,32,128]{3,2,1,0:T(8,128)(2,1)} custom-call(bf16[4,16,32,128]{3,2,1,0:T(8,128)(2,1)} %copy-done.6, bf16[8,16,32,128]{3,2,1,0:T(8,128)(2,1)} %stencil_first.1.refs_1_, bf16[4,16,32,128]{3,2,1,0:T(8,128)(2,1)} %copy-done.8, f32[8,16,32,128]{3,2,1,0:T(8,128)} %broadcast_in_dim.2.refs_3_, bf16[8,16,32,128]{3,2,1,0:T(8,128)(2,1)} %refs_4_.1), custom_call_target="tpu_custom_call" | custom-call | tf_op jit(solution)/shard_map/stencil_filtered/pallas_call | solution.py:78
  48.6 1.9 %collective-permute-start.4 = (bf16[4096,128]{1,0:T(8,128)(2,1)}, bf16[4096,128]{1,0:T(8,128)(2,1)S(1)}, u32[]{:S(2)}, u32[]{:S(2)}) collective-permute-start(bf16[4096,128]{1,0:T(8,128)(2,1)} %bitcast.18), channel_id=1, source_target_pairs={{0,16},{16,0},{1,17},{17,1},{2,18},{18,2},{3,19},{19,3},{4,20},{20... | collective-permute-start | bytes 3145736 | tf_op jit(solution)/shard_map/ppermute | solution.py:112
  50.5 2.2 %fusion = (bf16[4,16,32,128]{3,2,1,0:T(8,128)(2,1)}, bf16[4,16,32,128]{3,2,1,0:T(8,128)(2,1)}) fusion(bf16[8,16,32,128]{3,2,1,0:T(8,128)(2,1)} %stencil_filtered.1.refs_1_), kind=kLoop, calls=%fused_computation.6 | loop fusion | bytes 2097152 | tf_op jit(solution)/shard_map/slice | solution.py:23
  52.8 3.4 %collective-permute-start.10 = (bf16[4,16,32,128]{3,2,1,0:T(8,128)(2,1)}, bf16[4,16,32,128]{3,2,1,0:T(8,128)(2,1)S(1)}, u32[]{:S(2)}, u32[]{:S(2)}) collective-permute-start(bf16[4,16,32,128]{3,2,1,0:T(8,128)(2,1)} %get-tuple-element.6), channel_id=1, source_target_pairs={{1,0},{2,1},{3,2},{4,3},{5,4},{6,5},{7,6},{8,7},{9,8},{10,9},{11,1... | collective-permute-start | bytes 1572872 | tf_op jit(solution)/shard_map/ppermute | solution.py:23
  56.2 1.1 collective-permute-start.9
  57.7 5.5 %collective-permute-done.10.refs_2_ = bf16[4,16,32,128]{3,2,1,0:T(8,128)(2,1)S(1)} collective-permute-done((bf16[4,16,32,128]{3,2,1,0:T(8,128)(2,1)}, bf16[4,16,32,128]{3,2,1,0:T(8,128)(2,1)S(1)}, u32[]{:S(2)}, u32[]{:S(2)}) %collective-permute-start.10) | collective-permute-done | bytes 524320 | tf_op jit(solution)/shard_map/ppermute | solution.py:23
  63.2 7.0 %collective-permute-done.9.refs_0_ = bf16[4,16,32,128]{3,2,1,0:T(8,128)(2,1)S(1)} collective-permute-done((bf16[4,16,32,128]{3,2,1,0:T(8,128)(2,1)}, bf16[4,16,32,128]{3,2,1,0:T(8,128)(2,1)S(1)}, u32[]{:S(2)}, u32[]{:S(2)}) %collective-permute-start.9) | collective-permute-done | bytes 524320 | tf_op jit(solution)/shard_map/ppermute | solution.py:22
  70.2 0.8 copy-done.4
  71.0 8.4 %stencil_applied.1 = bf16[8,16,32,128]{3,2,1,0:T(8,128)(2,1)} custom-call(bf16[4,16,32,128]{3,2,1,0:T(8,128)(2,1)} %copy-done.4, bf16[8,16,32,128]{3,2,1,0:T(8,128)(2,1)} %stencil_filtered.1.refs_1_, bf16[4,16,32,128]{3,2,1,0:T(8,128)(2,1)} %copy-done.3, f32[8,16,32,128]{3,2,1,0:T(8,128)} %broadcast_in_dim.2.refs_3_), custom_call_target="tpu_custom_call" | custom-call | tf_op jit(solution)/shard_map/stencil_applied/pallas_call | solution.py:78
  79.4 1.8 %convolution_bitcast_fusion = f32[128,128]{0,1:T(8,128)S(1)} fusion(bf16[8,16,32,128]{3,2,1,0:T(8,128)(2,1)} %stencil_applied.1, bf16[8,16,32,128]{3,2,1,0:T(8,128)(2,1)S(1)} %copy-done.1), kind=kOutput, calls=%fused_computation | convolution fusion | flops 134217728 | bytes 2162688 | tf_op jit(solution)/shard_map/cb,ck->bk/dot_general | solution.py:101
  81.7 3.3 %collective-permute-start.11 = (f32[128,256]{0,1:T(8,128)S(1)}, f32[128,256]{0,1:T(8,128)S(1)}, u32[]{:S(2)}, u32[]{:S(2)}) collective-permute-start(f32[128,256]{0,1:T(8,128)S(1)} %maximum_select_fusion.1), channel_id=1, source_target_pairs={{0,1},{1,0},{2,3},{3,2},{4,5},{5,4},{6,7},{7,6},{8,9},{9,8},{10,11... | collective-permute-start | bytes 393224 | tf_op jit(solution)/shard_map/ppermute | solution.py:90
  87.0 1.3 %collective-permute-start.6 = (f32[128,256]{0,1:T(8,128)S(1)}, f32[128,256]{0,1:T(8,128)S(1)}, u32[]{:S(2)}, u32[]{:S(2)}) collective-permute-start(f32[128,256]{0,1:T(8,128)S(1)} %add.24), channel_id=1, source_target_pairs={{0,2},{1,3},{2,0},{3,1},{4,6},{5,7},{6,4},{7,5},{8,10},{9,11},{10,... | collective-permute-start | bytes 393224 | tf_op jit(solution)/shard_map/ppermute | solution.py:90
  88.3 4.2 %collective-permute-done.12 = f32[128,256]{0,1:T(8,128)S(1)} collective-permute-done((f32[128,256]{0,1:T(8,128)S(1)}, f32[128,256]{0,1:T(8,128)S(1)}, u32[]{:S(2)}, u32[]{:S(2)}) %collective-permute-start.12) | collective-permute-done | bytes 131104 | tf_op jit(solution)/shard_map/ppermute | solution.py:90
  92.5 1.4 %collective-permute-start.13 = (f32[128,256]{0,1:T(8,128)S(1)}, f32[128,256]{0,1:T(8,128)S(1)}, u32[]{:S(2)}, u32[]{:S(2)}) collective-permute-start(f32[128,256]{0,1:T(8,128)S(1)} %add.29), channel_id=1, source_target_pairs={{0,4},{1,5},{2,6},{3,7},{4,0},{5,1},{6,2},{7,3},{8,12},{9,13},{10,... | collective-permute-start | bytes 393224 | tf_op jit(solution)/shard_map/ppermute | solution.py:90
  93.8 0.9 collective-permute-done.6
  94.7 1.4 %collective-permute-start.7 = (f32[128,256]{0,1:T(8,128)S(1)}, f32[128,256]{0,1:T(8,128)S(1)}, u32[]{:S(2)}, u32[]{:S(2)}) collective-permute-start(f32[128,256]{0,1:T(8,128)S(1)} %add.25), channel_id=1, source_target_pairs={{0,4},{1,5},{2,6},{3,7},{4,0},{5,1},{6,2},{7,3},{8,12},{9,13},{10,... | collective-permute-start | bytes 393224 | tf_op jit(solution)/shard_map/ppermute | solution.py:90
  96.1 2.0 %collective-permute-done.13 = f32[128,256]{0,1:T(8,128)S(1)} collective-permute-done((f32[128,256]{0,1:T(8,128)S(1)}, f32[128,256]{0,1:T(8,128)S(1)}, u32[]{:S(2)}, u32[]{:S(2)}) %collective-permute-start.13) | collective-permute-done | bytes 131104 | tf_op jit(solution)/shard_map/ppermute | solution.py:90
  98.1 2.4 %collective-permute-start.14 = (f32[128,256]{0,1:T(8,128)S(1)}, f32[128,256]{0,1:T(8,128)S(1)}, u32[]{:S(2)}, u32[]{:S(2)}) collective-permute-start(f32[128,256]{0,1:T(8,128)S(1)} %add.30), channel_id=1, source_target_pairs={{0,8},{1,9},{2,10},{3,11},{4,12},{5,13},{6,14},{7,15},{8,0},{9,1},... | collective-permute-start | bytes 393224 | tf_op jit(solution)/shard_map/ppermute | solution.py:90
  100.5 1.2 %collective-permute-done.7 = f32[128,256]{0,1:T(8,128)S(1)} collective-permute-done((f32[128,256]{0,1:T(8,128)S(1)}, f32[128,256]{0,1:T(8,128)S(1)}, u32[]{:S(2)}, u32[]{:S(2)}) %collective-permute-start.7) | collective-permute-done | bytes 131104 | tf_op jit(solution)/shard_map/ppermute | solution.py:90
  101.7 1.8 %collective-permute-start.8 = (f32[128,256]{0,1:T(8,128)S(1)}, f32[128,256]{0,1:T(8,128)S(1)}, u32[]{:S(2)}, u32[]{:S(2)}) collective-permute-start(f32[128,256]{0,1:T(8,128)S(1)} %add.26), channel_id=1, source_target_pairs={{0,8},{1,9},{2,10},{3,11},{4,12},{5,13},{6,14},{7,15},{8,0},{9,1},... | collective-permute-start | bytes 393224 | tf_op jit(solution)/shard_map/ppermute | solution.py:90
  103.6 6.5 %collective-permute-done.14 = f32[128,256]{0,1:T(8,128)S(1)} collective-permute-done((f32[128,256]{0,1:T(8,128)S(1)}, f32[128,256]{0,1:T(8,128)S(1)}, u32[]{:S(2)}, u32[]{:S(2)}) %collective-permute-start.14) | collective-permute-done | bytes 131104 | tf_op jit(solution)/shard_map/ppermute | solution.py:90
  110.1 0.8 copy.6
  110.9 0.9 collective-permute-done.8
  (41 shorter events, 5.1 us)
Async XLA Ops:
  0.6 13.8 %copy-start.9 = (f32[8,16,32]{2,1,0:T(8,128)S(1)}, f32[8,16,32]{2,1,0:T(8,128)}, u32[]{:S(2)}) copy-start(f32[8,16,32]{2,1,0:T(8,128)} %param.3) | copy-start | bytes 49156
  2.0 12.4 %collective-permute-start = (bf16[4,16,32,128]{3,2,1,0:T(8,128)(2,1)S(1)}, bf16[4,16,32,128]{3,2,1,0:T(8,128)(2,1)S(1)}, u32[]{:S(2)}, u32[]{:S(2)}) collective-permute-start(bf16[4,16,32,128]{3,2,1,0:T(8,128)(2,1)S(1)} %get-tuple-element.11), channel_id=1, source_target_pairs={{0,1},{1,2},{2,3},{3,4},{4,5},{5,6},{6,7},{7,8},{8,9},{9,10},{10,1... | collective-permute-start | bytes 1572872 | tf_op jit(solution)/shard_map/ppermute | solution.py:22
  2.5 11.9 %collective-permute-start.1 = (bf16[4,16,32,128]{3,2,1,0:T(8,128)(2,1)S(1)}, bf16[4,16,32,128]{3,2,1,0:T(8,128)(2,1)S(1)}, u32[]{:S(2)}, u32[]{:S(2)}) collective-permute-start(bf16[4,16,32,128]{3,2,1,0:T(8,128)(2,1)S(1)} %get-tuple-element.10), channel_id=1, source_target_pairs={{1,0},{2,1},{3,2},{4,3},{5,4},{6,5},{7,6},{8,7},{9,8},{10,9},{11,1... | collective-permute-start | bytes 1572872 | tf_op jit(solution)/shard_map/ppermute | solution.py:23
  14.4 2.0 %copy-start.5 = (bf16[4,16,32,128]{3,2,1,0:T(8,128)(2,1)}, bf16[4,16,32,128]{3,2,1,0:T(8,128)(2,1)S(1)}, u32[]{:S(2)}) copy-start(bf16[4,16,32,128]{3,2,1,0:T(8,128)(2,1)S(1)} %collective-permute-done.refs_0_) | copy-start | bytes 1572868
  14.4 2.0 %copy-start.7 = (bf16[4,16,32,128]{3,2,1,0:T(8,128)(2,1)}, bf16[4,16,32,128]{3,2,1,0:T(8,128)(2,1)S(1)}, u32[]{:S(2)}) copy-start(bf16[4,16,32,128]{3,2,1,0:T(8,128)(2,1)S(1)} %collective-permute-done.1.refs_2_) | copy-start | bytes 1572868
  26.4 11.5 %collective-permute-start.2 = (bf16[4,16,32,128]{3,2,1,0:T(8,128)(2,1)S(1)}, bf16[4,16,32,128]{3,2,1,0:T(8,128)(2,1)S(1)}, u32[]{:S(2)}, u32[]{:S(2)}) collective-permute-start(bf16[4,16,32,128]{3,2,1,0:T(8,128)(2,1)S(1)} %get-tuple-element.9), channel_id=1, source_target_pairs={{0,1},{1,2},{2,3},{3,4},{4,5},{5,6},{6,7},{7,8},{8,9},{9,10},{10,1... | collective-permute-start | bytes 1572872 | tf_op jit(solution)/shard_map/ppermute | solution.py:22
  31.3 6.7 %collective-permute-start.3 = (bf16[4,16,32,128]{3,2,1,0:T(8,128)(2,1)S(1)}, bf16[4,16,32,128]{3,2,1,0:T(8,128)(2,1)S(1)}, u32[]{:S(2)}, u32[]{:S(2)}) collective-permute-start(bf16[4,16,32,128]{3,2,1,0:T(8,128)(2,1)S(1)} %get-tuple-element.8), channel_id=1, source_target_pairs={{1,0},{2,1},{3,2},{4,3},{5,4},{6,5},{7,6},{8,7},{9,8},{10,9},{11,1... | collective-permute-start | bytes 1572872 | tf_op jit(solution)/shard_map/ppermute | solution.py:23
  37.9 0.8 copy-start.6
  38.7 0.8 copy-start.8
  48.6 8.7 %copy-start = (bf16[8,16,32,128]{3,2,1,0:T(8,128)(2,1)S(1)}, bf16[8,16,32,128]{3,2,1,0:T(8,128)(2,1)}, u32[]{:S(2)}) copy-start(bf16[8,16,32,128]{3,2,1,0:T(8,128)(2,1)} %stencil_filtered.1.refs_1_) | copy-start | bytes 3145732
  48.6 32.6 %collective-permute-start.4 = (bf16[4096,128]{1,0:T(8,128)(2,1)}, bf16[4096,128]{1,0:T(8,128)(2,1)S(1)}, u32[]{:S(2)}, u32[]{:S(2)}) collective-permute-start(bf16[4096,128]{1,0:T(8,128)(2,1)} %bitcast.18), channel_id=1, source_target_pairs={{0,16},{16,0},{1,17},{17,1},{2,18},{18,2},{3,19},{19,3},{4,20},{20... | collective-permute-start | bytes 3145736 | tf_op jit(solution)/shard_map/ppermute | solution.py:112
  52.8 10.4 %collective-permute-start.10 = (bf16[4,16,32,128]{3,2,1,0:T(8,128)(2,1)}, bf16[4,16,32,128]{3,2,1,0:T(8,128)(2,1)S(1)}, u32[]{:S(2)}, u32[]{:S(2)}) collective-permute-start(bf16[4,16,32,128]{3,2,1,0:T(8,128)(2,1)} %get-tuple-element.6), channel_id=1, source_target_pairs={{1,0},{2,1},{3,2},{4,3},{5,4},{6,5},{7,6},{8,7},{9,8},{10,9},{11,1... | collective-permute-start | bytes 1572872 | tf_op jit(solution)/shard_map/ppermute | solution.py:23
  56.2 14.0 %collective-permute-start.9 = (bf16[4,16,32,128]{3,2,1,0:T(8,128)(2,1)}, bf16[4,16,32,128]{3,2,1,0:T(8,128)(2,1)S(1)}, u32[]{:S(2)}, u32[]{:S(2)}) collective-permute-start(bf16[4,16,32,128]{3,2,1,0:T(8,128)(2,1)} %get-tuple-element.7), channel_id=1, source_target_pairs={{0,1},{1,2},{2,3},{3,4},{4,5},{5,6},{6,7},{7,8},{8,9},{9,10},{10,1... | collective-permute-start | bytes 1572872 | tf_op jit(solution)/shard_map/ppermute | solution.py:22
  57.7 21.7 %copy-start.1 = (bf16[8,16,32,128]{3,2,1,0:T(8,128)(2,1)S(1)}, bf16[8,16,32,128]{3,2,1,0:T(8,128)(2,1)}, u32[]{:S(2)}) copy-start(bf16[8,16,32,128]{3,2,1,0:T(8,128)(2,1)} %stencil_filtered.1.refs_1_) | copy-start | bytes 3145732
  63.2 7.0 %copy-start.3 = (bf16[4,16,32,128]{3,2,1,0:T(8,128)(2,1)}, bf16[4,16,32,128]{3,2,1,0:T(8,128)(2,1)S(1)}, u32[]{:S(2)}) copy-start(bf16[4,16,32,128]{3,2,1,0:T(8,128)(2,1)S(1)} %collective-permute-done.10.refs_2_) | copy-start | bytes 1572868
  70.2 0.8 copy-start.4
  79.4 1.8 %copy-start.2 = (bf16[8,16,32,128]{3,2,1,0:T(8,128)(2,1)S(1)}, bf16[8,16,32,128]{3,2,1,0:T(8,128)(2,1)}, u32[]{:S(2)}) copy-start(bf16[8,16,32,128]{3,2,1,0:T(8,128)(2,1)} %stencil_applied.1) | copy-start | bytes 3145732
  81.7 4.3 %collective-permute-start.11 = (f32[128,256]{0,1:T(8,128)S(1)}, f32[128,256]{0,1:T(8,128)S(1)}, u32[]{:S(2)}, u32[]{:S(2)}) collective-permute-start(f32[128,256]{0,1:T(8,128)S(1)} %maximum_select_fusion.1), channel_id=1, source_target_pairs={{0,1},{1,0},{2,3},{3,2},{4,5},{5,4},{6,7},{7,6},{8,9},{9,8},{10,11... | collective-permute-start | bytes 393224 | tf_op jit(solution)/shard_map/ppermute | solution.py:90
  85.6 1.4 %collective-permute-start.5 = (f32[128,256]{0,1:T(8,128)S(1)}, f32[128,256]{0,1:T(8,128)S(1)}, u32[]{:S(2)}, u32[]{:S(2)}) collective-permute-start(f32[128,256]{0,1:T(8,128)S(1)} %maximum_select_fusion), channel_id=1, source_target_pairs={{0,1},{1,0},{2,3},{3,2},{4,5},{5,4},{6,7},{7,6},{8,9},{9,8},{10,11... | collective-permute-start | bytes 393224 | tf_op jit(solution)/shard_map/ppermute | solution.py:90
  86.1 6.4 %collective-permute-start.12 = (f32[128,256]{0,1:T(8,128)S(1)}, f32[128,256]{0,1:T(8,128)S(1)}, u32[]{:S(2)}, u32[]{:S(2)}) collective-permute-start(f32[128,256]{0,1:T(8,128)S(1)} %add.28), channel_id=1, source_target_pairs={{0,2},{1,3},{2,0},{3,1},{4,6},{5,7},{6,4},{7,5},{8,10},{9,11},{10,... | collective-permute-start | bytes 393224 | tf_op jit(solution)/shard_map/ppermute | solution.py:90
  87.0 7.7 %collective-permute-start.6 = (f32[128,256]{0,1:T(8,128)S(1)}, f32[128,256]{0,1:T(8,128)S(1)}, u32[]{:S(2)}, u32[]{:S(2)}) collective-permute-start(f32[128,256]{0,1:T(8,128)S(1)} %add.24), channel_id=1, source_target_pairs={{0,2},{1,3},{2,0},{3,1},{4,6},{5,7},{6,4},{7,5},{8,10},{9,11},{10,... | collective-permute-start | bytes 393224 | tf_op jit(solution)/shard_map/ppermute | solution.py:90
  92.5 5.6 %collective-permute-start.13 = (f32[128,256]{0,1:T(8,128)S(1)}, f32[128,256]{0,1:T(8,128)S(1)}, u32[]{:S(2)}, u32[]{:S(2)}) collective-permute-start(f32[128,256]{0,1:T(8,128)S(1)} %add.29), channel_id=1, source_target_pairs={{0,4},{1,5},{2,6},{3,7},{4,0},{5,1},{6,2},{7,3},{8,12},{9,13},{10,... | collective-permute-start | bytes 393224 | tf_op jit(solution)/shard_map/ppermute | solution.py:90
  94.7 7.0 %collective-permute-start.7 = (f32[128,256]{0,1:T(8,128)S(1)}, f32[128,256]{0,1:T(8,128)S(1)}, u32[]{:S(2)}, u32[]{:S(2)}) collective-permute-start(f32[128,256]{0,1:T(8,128)S(1)} %add.25), channel_id=1, source_target_pairs={{0,4},{1,5},{2,6},{3,7},{4,0},{5,1},{6,2},{7,3},{8,12},{9,13},{10,... | collective-permute-start | bytes 393224 | tf_op jit(solution)/shard_map/ppermute | solution.py:90
  98.1 12.0 %collective-permute-start.14 = (f32[128,256]{0,1:T(8,128)S(1)}, f32[128,256]{0,1:T(8,128)S(1)}, u32[]{:S(2)}, u32[]{:S(2)}) collective-permute-start(f32[128,256]{0,1:T(8,128)S(1)} %add.30), channel_id=1, source_target_pairs={{0,8},{1,9},{2,10},{3,11},{4,12},{5,13},{6,14},{7,15},{8,0},{9,1},... | collective-permute-start | bytes 393224 | tf_op jit(solution)/shard_map/ppermute | solution.py:90
  101.7 10.0 %collective-permute-start.8 = (f32[128,256]{0,1:T(8,128)S(1)}, f32[128,256]{0,1:T(8,128)S(1)}, u32[]{:S(2)}, u32[]{:S(2)}) collective-permute-start(f32[128,256]{0,1:T(8,128)S(1)} %add.26), channel_id=1, source_target_pairs={{0,8},{1,9},{2,10},{3,11},{4,12},{5,13},{6,14},{7,15},{8,0},{9,1},... | collective-permute-start | bytes 393224 | tf_op jit(solution)/shard_map/ppermute | solution.py:90

commit v5 on v4

--- a/solution.py
+++ b/solution.py
@@ -24,34 +24,50 @@
     return low, high
 
 
-def stencil_kernel(stage, planes, ny, nz):
-    def kernel(*refs):
-        if stage == "filtered":
-            low, own, high, pot, initial, out = refs
-        else:
-            low, own, high, pot, out = refs
-
-        def plane_ref(p):
-            if p < 0:
-                return low, p + RADIUS
-            if p >= planes:
-                return high, p - planes
-            return own, p
-
+def interior_kernel(planes, ny, nz):
+    def kernel(own, out):
         for x in range(planes):
             def row(y, carry, x=x):
                 centre = own[x, y].astype(jnp.float32)
                 summed = (3.0 * stencil_weights[0]) * centre
                 for k in range(1, RADIUS + 1):
-                    above, ia = plane_ref(x + k)
-                    below, ib = plane_ref(x - k)
-                    beside = above[ia, y].astype(jnp.float32) + below[ib, y].astype(jnp.float32)
-                    beside = beside + own[x, (y + k) % ny].astype(jnp.float32)
+                    beside = own[x, (y + k) % ny].astype(jnp.float32)
                     beside = beside + own[x, (y + ny - k) % ny].astype(jnp.float32)
                     beside = beside + (
                         pltpu.roll(centre, k, 0) + pltpu.roll(centre, nz - k, 0)
                     )
+                    if x + k < planes:
+                        beside = beside + own[x + k, y].astype(jnp.float32)
+                    if x - k >= 0:
+                        beside = beside + own[x - k, y].astype(jnp.float32)
                     summed = summed + stencil_weights[k] * beside
+                out[x, y] = summed
+                return carry
+
+            lax.fori_loop(0, ny, row, 0)
+
+    return kernel
+
+
+def finish_kernel(stage, planes, ny):
+    def kernel(*refs):
+        if stage == "filtered":
+            low, high, own, partial, pot, initial, out = refs
+        else:
+            low, high, own, partial, pot, out = refs
+        for x in range(planes):
+            def row(y, carry, x=x):
+                summed = partial[x, y]
+                for k in range(1, RADIUS + 1):
+                    outside = []
+                    if x + k >= planes:
+                        outside.append(high[x + k - planes, y].astype(jnp.float32))
+                    if x - k < 0:
+                        outside.append(low[x - k + RADIUS, y].astype(jnp.float32))
+                    if outside:
+                        term = outside[0] if len(outside) == 1 else outside[0] + outside[1]
+                        summed = summed + stencil_weights[k] * term
+                centre = own[x, y].astype(jnp.float32)
                 applied = -0.5 * summed + pot[x, y] * centre
                 if stage == "first":
                     result = (applied - spectrum_centre * centre) * first_factor
@@ -72,13 +88,18 @@
 def stencil_stage(stage, block, potential_wide, initial=None):
     planes, ny, nz, nb = block.shape
     low, high = halos(block, "domain", RADIUS)
-    operands = [low, block, high, potential_wide]
+    partial = pl.pallas_call(
+        interior_kernel(planes, ny, nz),
+        out_shape=jax.ShapeDtypeStruct(block.shape, jnp.float32),
+        name=f"interior_{stage}",
+    )(block)
+    operands = [low, high, block, partial, potential_wide]
     if initial is not None:
         operands.append(initial)
     return pl.pallas_call(
-        stencil_kernel(stage, planes, ny, nz),
+        finish_kernel(stage, planes, ny),
         out_shape=jax.ShapeDtypeStruct(block.shape, jnp.bfloat16),
-        name=f"stencil_{stage}",
+        name=f"finish_{stage}",
     )(*operands)
 
 

time: 113 us -> 104 us (0.920)
  waiting for transfers between devices: 42.9 us -> 22 us
  Pallas kernels: 26.2 us -> 39 us
    ppermute x3, waiting for transfers between devices: 20.5 us -> 5.19 us  [halos(): lax.ppermute(lax.slice_in_dim(block, block.shape[0] - width, None, axis=0...]
    pallas_call x3 -> x6, Pallas kernels: 26.2 us -> 39 us  [the longest x3 21.7 us: stencil_stage(): pl.pallas_call(interior_kernel(planes, ny, nz), out_shape=jax.ShapeDtypeS...]
    ppermute x3, waiting for transfers between devices: 5.58 us -> 0.01 us  [halos(): lax.ppermute(lax.slice_in_dim(block, 0, width, axis=0), axis, backward)]
  transfers between devices with their start and end apart: 15 -> 15, of which waited for: 13 -> 9; matrix products, arithmetic and copies ran while one was open for 5% -> 6% of each run, Pallas kernels for 7% -> 26%
where the time goes in v5:
time: 104 us
  Pallas kernels  39 us (38%)
  starting transfers between devices  27.8 us (27%)
  waiting for transfers between devices  22 us (21%)
  local copies, waits for them, and re-layouts  10.8 us (10%)
  matrix products  3.22 us (3%)
    pallas_call x3, Pallas kernels, stencil_stage(): pl.pallas_call(interior_kernel(planes, ny, nz), out_shape=jax.ShapeDtypeS...  21.7 us
    pallas_call x3, Pallas kernels, stencil_stage(): pl.pallas_call(finish_kernel(stage, planes, ny), out_shape=jax.ShapeDtype...  17.3 us
    ppermute x8, waiting for transfers between devices, butterfly_sum(): values = values + lax.ppermute(values, axis, pairs)  16.8 us
    ppermute x8, starting transfers between devices, butterfly_sum(): values = values + lax.ppermute(values, axis, pairs)  11.9 us
    ppermute x3, starting transfers between devices, halos(): lax.ppermute(lax.slice_in_dim(block, 0, width, axis=0), axis, backward)  8.13 us
    ppermute x3, starting transfers between devices, halos(): lax.ppermute(lax.slice_in_dim(block, block.shape[0] - width, None, axis=0...  5.99 us
    ppermute x3, waiting for transfers between devices, halos(): lax.ppermute(lax.slice_in_dim(block, block.shape[0] - width, None, axis=0...  5.19 us
    slice x3, local copies, waits for them, and re-layouts, halos(): lax.slice_in_dim(block, 0, width, axis=0)  4.89 us
  transfers between devices with their start and end apart: 15, of which 9 were waited for; matrix products, arithmetic and copies ran while one was open for 6% of the time, Pallas kernels for 26%

profile of v5, /device:TPU:0, one launch (start us, length us, event | category | flops | bytes accessed | tf_op | source)
XLA Modules:
  0.0 103.7 jit_solution(11905885955706479410)
XLA Ops:
  0.6 1.3 %fusion.2 = (bf16[4,16,32,128]{3,2,1,0:T(8,128)(2,1)S(1)}, bf16[4,16,32,128]{3,2,1,0:T(8,128)(2,1)S(1)}) fusion(bf16[8,16,32,128]{3,2,1,0:T(8,128)(2,1)} %refs_5_.1), kind=kLoop, calls=%fused_computation.8 | loop fusion | bytes 2097152 | tf_op jit(solution)/shard_map/slice | solution.py:23
  2.5 5.0 %collective-permute-start.1 = (bf16[4,16,32,128]{3,2,1,0:T(8,128)(2,1)S(1)}, bf16[4,16,32,128]{3,2,1,0:T(8,128)(2,1)S(1)}, u32[]{:S(2)}, u32[]{:S(2)}) collective-permute-start(bf16[4,16,32,128]{3,2,1,0:T(8,128)(2,1)S(1)} %get-tuple-element.10), channel_id=1, source_target_pairs={{1,0},{2,1},{3,2},{4,3},{5,4},{6,5},{7,6},{8,7},{9,8},{10,9},{11,1... | collective-permute-start | bytes 1572872 | tf_op jit(solution)/shard_map/ppermute | solution.py:23
  7.5 7.2 %interior_first.1.refs_3_ = f32[8,16,32,128]{3,2,1,0:T(8,128)} custom-call(bf16[8,16,32,128]{3,2,1,0:T(8,128)(2,1)} %refs_5_.1), custom_call_target="tpu_custom_call" | custom-call | tf_op jit(solution)/shard_map/interior_first/pallas_call | solution.py:91
  14.7 1.9 %broadcast_in_dim.2.refs_4_ = f32[8,16,32,128]{3,2,1,0:T(8,128)} broadcast(f32[8,16,32]{2,1,0:T(8,128)S(1)} %copy-done.9), dimensions={0,1,2} | broadcast | bytes 2113536 | tf_op jit(solution)/shard_map/broadcast_in_dim | solution.py:118
  16.7 5.7 %finish_first.1.own.refs_2_ = bf16[8,16,32,128]{3,2,1,0:T(8,128)(2,1)} custom-call(bf16[4,16,32,128]{3,2,1,0:T(8,128)(2,1)} %copy-done.5, bf16[4,16,32,128]{3,2,1,0:T(8,128)(2,1)} %copy-done.6, bf16[8,16,32,128]{3,2,1,0:T(8,128)(2,1)} %refs_5_.1, f32[8,16,32,128]{3,2,1,0:T(8,128)} %interior_first.1.refs_3_, f32[8,16,32,128]{3,2,1,0:T(8,128)} %broadcast_in_dim.2.refs_4_), custom_call_target="tpu_custom_call" | custom-call | tf_op jit(solution)/shard_map/finish_first/pallas_call | solution.py:99
  22.4 1.3 %fusion.1 = (bf16[4,16,32,128]{3,2,1,0:T(8,128)(2,1)S(1)}, bf16[4,16,32,128]{3,2,1,0:T(8,128)(2,1)S(1)}) fusion(bf16[8,16,32,128]{3,2,1,0:T(8,128)(2,1)} %finish_first.1.own.refs_2_), kind=kLoop, calls=%fused_computation.7 | loop fusion | bytes 2097152 | tf_op jit(solution)/shard_map/slice | solution.py:23
  23.7 4.6 %collective-permute-start.2 = (bf16[4,16,32,128]{3,2,1,0:T(8,128)(2,1)S(1)}, bf16[4,16,32,128]{3,2,1,0:T(8,128)(2,1)S(1)}, u32[]{:S(2)}, u32[]{:S(2)}) collective-permute-start(bf16[4,16,32,128]{3,2,1,0:T(8,128)(2,1)S(1)} %get-tuple-element.9), channel_id=1, source_target_pairs={{0,1},{1,2},{2,3},{3,4},{4,5},{5,6},{6,7},{7,8},{8,9},{9,10},{10,1... | collective-permute-start | bytes 1572872 | tf_op jit(solution)/shard_map/ppermute | solution.py:22
  28.3 7.2 %interior_filtered.1.refs_3_ = f32[8,16,32,128]{3,2,1,0:T(8,128)} custom-call(bf16[8,16,32,128]{3,2,1,0:T(8,128)(2,1)} %finish_first.1.own.refs_2_), custom_call_target="tpu_custom_call" | custom-call | tf_op jit(solution)/shard_map/interior_filtered/pallas_call | solution.py:91
  35.6 0.8 copy-done.7
  36.4 0.8 copy-done.8
  37.1 6.1 %finish_filtered.1.own.refs_2_ = bf16[8,16,32,128]{3,2,1,0:T(8,128)(2,1)} custom-call(bf16[4,16,32,128]{3,2,1,0:T(8,128)(2,1)} %copy-done.7, bf16[4,16,32,128]{3,2,1,0:T(8,128)(2,1)} %copy-done.8, bf16[8,16,32,128]{3,2,1,0:T(8,128)(2,1)} %finish_first.1.own.refs_2_, f32[8,16,32,128]{3,2,1,0:T(8,128)} %interior_filtered.1.refs_3_, ...), custom_call_target="tpu_custom_call" | custom-call | tf_op jit(solution)/shard_map/finish_filtered/pallas_call | solution.py:99
  43.3 1.8 %collective-permute-start.4 = (bf16[4096,128]{1,0:T(8,128)(2,1)}, bf16[4096,128]{1,0:T(8,128)(2,1)S(1)}, u32[]{:S(2)}, u32[]{:S(2)}) collective-permute-start(bf16[4096,128]{1,0:T(8,128)(2,1)} %bitcast.18), channel_id=1, source_target_pairs={{0,16},{16,0},{1,17},{17,1},{2,18},{18,2},{3,19},{19,3},{4,20},{20... | collective-permute-start | bytes 3145736 | tf_op jit(solution)/shard_map/ppermute | solution.py:133
  45.1 2.3 %fusion = (bf16[4,16,32,128]{3,2,1,0:T(8,128)(2,1)}, bf16[4,16,32,128]{3,2,1,0:T(8,128)(2,1)}) fusion(bf16[8,16,32,128]{3,2,1,0:T(8,128)(2,1)} %finish_filtered.1.own.refs_2_), kind=kLoop, calls=%fused_computation.6 | loop fusion | bytes 2097152 | tf_op jit(solution)/shard_map/slice | solution.py:23
  47.4 3.1 %collective-permute-start.10 = (bf16[4,16,32,128]{3,2,1,0:T(8,128)(2,1)}, bf16[4,16,32,128]{3,2,1,0:T(8,128)(2,1)S(1)}, u32[]{:S(2)}, u32[]{:S(2)}) collective-permute-start(bf16[4,16,32,128]{3,2,1,0:T(8,128)(2,1)} %get-tuple-element.6), channel_id=1, source_target_pairs={{1,0},{2,1},{3,2},{4,3},{5,4},{6,5},{7,6},{8,7},{9,8},{10,9},{11,1... | collective-permute-start | bytes 1572872 | tf_op jit(solution)/shard_map/ppermute | solution.py:23
  50.5 0.9 collective-permute-start.9
  51.4 7.2 %interior_applied.1.refs_3_ = f32[8,16,32,128]{3,2,1,0:T(8,128)} custom-call(bf16[8,16,32,128]{3,2,1,0:T(8,128)(2,1)} %finish_filtered.1.own.refs_2_), custom_call_target="tpu_custom_call" | custom-call | tf_op jit(solution)/shard_map/interior_applied/pallas_call | solution.py:91
  59.1 5.2 %collective-permute-done.9.refs_0_ = bf16[4,16,32,128]{3,2,1,0:T(8,128)(2,1)S(1)} collective-permute-done((bf16[4,16,32,128]{3,2,1,0:T(8,128)(2,1)}, bf16[4,16,32,128]{3,2,1,0:T(8,128)(2,1)S(1)}, u32[]{:S(2)}, u32[]{:S(2)}) %collective-permute-start.9) | collective-permute-done | bytes 524320 | tf_op jit(solution)/shard_map/ppermute | solution.py:22
  64.3 0.8 copy-done.4
  65.1 5.5 %finish_applied.1 = bf16[8,16,32,128]{3,2,1,0:T(8,128)(2,1)} custom-call(bf16[4,16,32,128]{3,2,1,0:T(8,128)(2,1)} %copy-done.4, bf16[4,16,32,128]{3,2,1,0:T(8,128)(2,1)} %copy-done.3, bf16[8,16,32,128]{3,2,1,0:T(8,128)(2,1)} %finish_filtered.1.own.refs_2_, f32[8,16,32,128]{3,2,1,0:T(8,128)} %interior_applied.1.refs_3_, ...), custom_call_target="tpu_custom_call" | custom-call | tf_op jit(solution)/shard_map/finish_applied/pallas_call | solution.py:99
  70.6 1.8 %convolution_bitcast_fusion = f32[128,128]{0,1:T(8,128)S(1)} fusion(bf16[8,16,32,128]{3,2,1,0:T(8,128)(2,1)} %finish_applied.1, bf16[8,16,32,128]{3,2,1,0:T(8,128)(2,1)S(1)} %copy-done.1), kind=kOutput, calls=%fused_computation | convolution fusion | flops 134217728 | bytes 2162688 | tf_op jit(solution)/shard_map/cb,ck->bk/dot_general | solution.py:122
  72.9 3.3 %collective-permute-start.11 = (f32[128,256]{0,1:T(8,128)S(1)}, f32[128,256]{0,1:T(8,128)S(1)}, u32[]{:S(2)}, u32[]{:S(2)}) collective-permute-start(f32[128,256]{0,1:T(8,128)S(1)} %maximum_select_fusion.1), channel_id=1, source_target_pairs={{0,1},{1,0},{2,3},{3,2},{4,5},{5,4},{6,7},{7,6},{8,9},{9,8},{10,11... | collective-permute-start | bytes 393224 | tf_op jit(solution)/shard_map/ppermute | solution.py:111
  78.1 1.3 %collective-permute-start.6 = (f32[128,256]{0,1:T(8,128)S(1)}, f32[128,256]{0,1:T(8,128)S(1)}, u32[]{:S(2)}, u32[]{:S(2)}) collective-permute-start(f32[128,256]{0,1:T(8,128)S(1)} %add.24), channel_id=1, source_target_pairs={{0,2},{1,3},{2,0},{3,1},{4,6},{5,7},{6,4},{7,5},{8,10},{9,11},{10,... | collective-permute-start | bytes 393224 | tf_op jit(solution)/shard_map/ppermute | solution.py:111
  79.4 4.2 %collective-permute-done.12 = f32[128,256]{0,1:T(8,128)S(1)} collective-permute-done((f32[128,256]{0,1:T(8,128)S(1)}, f32[128,256]{0,1:T(8,128)S(1)}, u32[]{:S(2)}, u32[]{:S(2)}) %collective-permute-start.12) | collective-permute-done | bytes 131104 | tf_op jit(solution)/shard_map/ppermute | solution.py:111
  83.6 1.4 %collective-permute-start.13 = (f32[128,256]{0,1:T(8,128)S(1)}, f32[128,256]{0,1:T(8,128)S(1)}, u32[]{:S(2)}, u32[]{:S(2)}) collective-permute-start(f32[128,256]{0,1:T(8,128)S(1)} %add.29), channel_id=1, source_target_pairs={{0,4},{1,5},{2,6},{3,7},{4,0},{5,1},{6,2},{7,3},{8,12},{9,13},{10,... | collective-permute-start | bytes 393224 | tf_op jit(solution)/shard_map/ppermute | solution.py:111
  85.0 0.9 collective-permute-done.6
  85.9 1.4 %collective-permute-start.7 = (f32[128,256]{0,1:T(8,128)S(1)}, f32[128,256]{0,1:T(8,128)S(1)}, u32[]{:S(2)}, u32[]{:S(2)}) collective-permute-start(f32[128,256]{0,1:T(8,128)S(1)} %add.25), channel_id=1, source_target_pairs={{0,4},{1,5},{2,6},{3,7},{4,0},{5,1},{6,2},{7,3},{8,12},{9,13},{10,... | collective-permute-start | bytes 393224 | tf_op jit(solution)/shard_map/ppermute | solution.py:111
  87.2 2.0 %collective-permute-done.13 = f32[128,256]{0,1:T(8,128)S(1)} collective-permute-done((f32[128,256]{0,1:T(8,128)S(1)}, f32[128,256]{0,1:T(8,128)S(1)}, u32[]{:S(2)}, u32[]{:S(2)}) %collective-permute-start.13) | collective-permute-done | bytes 131104 | tf_op jit(solution)/shard_map/ppermute | solution.py:111
  89.3 2.4 %collective-permute-start.14 = (f32[128,256]{0,1:T(8,128)S(1)}, f32[128,256]{0,1:T(8,128)S(1)}, u32[]{:S(2)}, u32[]{:S(2)}) collective-permute-start(f32[128,256]{0,1:T(8,128)S(1)} %add.30), channel_id=1, source_target_pairs={{0,8},{1,9},{2,10},{3,11},{4,12},{5,13},{6,14},{7,15},{8,0},{9,1},... | collective-permute-start | bytes 393224 | tf_op jit(solution)/shard_map/ppermute | solution.py:111
  91.6 1.2 %collective-permute-done.7 = f32[128,256]{0,1:T(8,128)S(1)} collective-permute-done((f32[128,256]{0,1:T(8,128)S(1)}, f32[128,256]{0,1:T(8,128)S(1)}, u32[]{:S(2)}, u32[]{:S(2)}) %collective-permute-start.7) | collective-permute-done | bytes 131104 | tf_op jit(solution)/shard_map/ppermute | solution.py:111
  92.9 1.8 %collective-permute-start.8 = (f32[128,256]{0,1:T(8,128)S(1)}, f32[128,256]{0,1:T(8,128)S(1)}, u32[]{:S(2)}, u32[]{:S(2)}) collective-permute-start(f32[128,256]{0,1:T(8,128)S(1)} %add.26), channel_id=1, source_target_pairs={{0,8},{1,9},{2,10},{3,11},{4,12},{5,13},{6,14},{7,15},{8,0},{9,1},... | collective-permute-start | bytes 393224 | tf_op jit(solution)/shard_map/ppermute | solution.py:111
  94.7 6.5 %collective-permute-done.14 = f32[128,256]{0,1:T(8,128)S(1)} collective-permute-done((f32[128,256]{0,1:T(8,128)S(1)}, f32[128,256]{0,1:T(8,128)S(1)}, u32[]{:S(2)}, u32[]{:S(2)}) %collective-permute-start.14) | collective-permute-done | bytes 131104 | tf_op jit(solution)/shard_map/ppermute | solution.py:111
  102.0 0.9 collective-permute-done.8
  (44 shorter events, 5.1 us)
Async XLA Ops:
  1.9 12.8 %copy-start.9 = (f32[8,16,32]{2,1,0:T(8,128)S(1)}, f32[8,16,32]{2,1,0:T(8,128)}, u32[]{:S(2)}) copy-start(f32[8,16,32]{2,1,0:T(8,128)} %param.3) | copy-start | bytes 49156
  2.0 12.8 %collective-permute-start = (bf16[4,16,32,128]{3,2,1,0:T(8,128)(2,1)S(1)}, bf16[4,16,32,128]{3,2,1,0:T(8,128)(2,1)S(1)}, u32[]{:S(2)}, u32[]{:S(2)}) collective-permute-start(bf16[4,16,32,128]{3,2,1,0:T(8,128)(2,1)S(1)} %get-tuple-element.11), channel_id=1, source_target_pairs={{0,1},{1,2},{2,3},{3,4},{4,5},{5,6},{6,7},{7,8},{8,9},{9,10},{10,1... | collective-permute-start | bytes 1572872 | tf_op jit(solution)/shard_map/ppermute | solution.py:22
  2.5 12.3 %collective-permute-start.1 = (bf16[4,16,32,128]{3,2,1,0:T(8,128)(2,1)S(1)}, bf16[4,16,32,128]{3,2,1,0:T(8,128)(2,1)S(1)}, u32[]{:S(2)}, u32[]{:S(2)}) collective-permute-start(bf16[4,16,32,128]{3,2,1,0:T(8,128)(2,1)S(1)} %get-tuple-element.10), channel_id=1, source_target_pairs={{1,0},{2,1},{3,2},{4,3},{5,4},{6,5},{7,6},{8,7},{9,8},{10,9},{11,1... | collective-permute-start | bytes 1572872 | tf_op jit(solution)/shard_map/ppermute | solution.py:23
  14.7 2.0 %copy-start.5 = (bf16[4,16,32,128]{3,2,1,0:T(8,128)(2,1)}, bf16[4,16,32,128]{3,2,1,0:T(8,128)(2,1)S(1)}, u32[]{:S(2)}) copy-start(bf16[4,16,32,128]{3,2,1,0:T(8,128)(2,1)S(1)} %collective-permute-done.refs_0_) | copy-start | bytes 1572868
  14.7 2.0 %copy-start.6 = (bf16[4,16,32,128]{3,2,1,0:T(8,128)(2,1)}, bf16[4,16,32,128]{3,2,1,0:T(8,128)(2,1)S(1)}, u32[]{:S(2)}) copy-start(bf16[4,16,32,128]{3,2,1,0:T(8,128)(2,1)S(1)} %collective-permute-done.1.refs_1_) | copy-start | bytes 1572868
  23.7 11.8 %collective-permute-start.2 = (bf16[4,16,32,128]{3,2,1,0:T(8,128)(2,1)S(1)}, bf16[4,16,32,128]{3,2,1,0:T(8,128)(2,1)S(1)}, u32[]{:S(2)}, u32[]{:S(2)}) collective-permute-start(bf16[4,16,32,128]{3,2,1,0:T(8,128)(2,1)S(1)} %get-tuple-element.9), channel_id=1, source_target_pairs={{0,1},{1,2},{2,3},{3,4},{4,5},{5,6},{6,7},{7,8},{8,9},{9,10},{10,1... | collective-permute-start | bytes 1572872 | tf_op jit(solution)/shard_map/ppermute | solution.py:22
  28.3 7.2 %collective-permute-start.3 = (bf16[4,16,32,128]{3,2,1,0:T(8,128)(2,1)S(1)}, bf16[4,16,32,128]{3,2,1,0:T(8,128)(2,1)S(1)}, u32[]{:S(2)}, u32[]{:S(2)}) collective-permute-start(bf16[4,16,32,128]{3,2,1,0:T(8,128)(2,1)S(1)} %get-tuple-element.8), channel_id=1, source_target_pairs={{1,0},{2,1},{3,2},{4,3},{5,4},{6,5},{7,6},{8,7},{9,8},{10,9},{11,1... | collective-permute-start | bytes 1572872 | tf_op jit(solution)/shard_map/ppermute | solution.py:23
  35.5 0.8 copy-start.7
  36.3 0.8 copy-start.8
  43.3 29.1 %collective-permute-start.4 = (bf16[4096,128]{1,0:T(8,128)(2,1)}, bf16[4096,128]{1,0:T(8,128)(2,1)S(1)}, u32[]{:S(2)}, u32[]{:S(2)}) collective-permute-start(bf16[4096,128]{1,0:T(8,128)(2,1)} %bitcast.18), channel_id=1, source_target_pairs={{0,16},{16,0},{1,17},{17,1},{2,18},{18,2},{3,19},{19,3},{4,20},{20... | collective-permute-start | bytes 3145736 | tf_op jit(solution)/shard_map/ppermute | solution.py:133
  47.4 11.2 %copy-start = (bf16[8,16,32,128]{3,2,1,0:T(8,128)(2,1)S(1)}, bf16[8,16,32,128]{3,2,1,0:T(8,128)(2,1)}, u32[]{:S(2)}) copy-start(bf16[8,16,32,128]{3,2,1,0:T(8,128)(2,1)} %finish_filtered.1.own.refs_2_) | copy-start | bytes 3145732
  47.4 11.7 %collective-permute-start.10 = (bf16[4,16,32,128]{3,2,1,0:T(8,128)(2,1)}, bf16[4,16,32,128]{3,2,1,0:T(8,128)(2,1)S(1)}, u32[]{:S(2)}, u32[]{:S(2)}) collective-permute-start(bf16[4,16,32,128]{3,2,1,0:T(8,128)(2,1)} %get-tuple-element.6), channel_id=1, source_target_pairs={{1,0},{2,1},{3,2},{4,3},{5,4},{6,5},{7,6},{8,7},{9,8},{10,9},{11,1... | collective-permute-start | bytes 1572872 | tf_op jit(solution)/shard_map/ppermute | solution.py:23
  50.5 13.8 %collective-permute-start.9 = (bf16[4,16,32,128]{3,2,1,0:T(8,128)(2,1)}, bf16[4,16,32,128]{3,2,1,0:T(8,128)(2,1)S(1)}, u32[]{:S(2)}, u32[]{:S(2)}) collective-permute-start(bf16[4,16,32,128]{3,2,1,0:T(8,128)(2,1)} %get-tuple-element.7), channel_id=1, source_target_pairs={{0,1},{1,2},{2,3},{3,4},{4,5},{5,6},{6,7},{7,8},{8,9},{9,10},{10,1... | collective-permute-start | bytes 1572872 | tf_op jit(solution)/shard_map/ppermute | solution.py:22
  59.1 11.5 %copy-start.1 = (bf16[8,16,32,128]{3,2,1,0:T(8,128)(2,1)S(1)}, bf16[8,16,32,128]{3,2,1,0:T(8,128)(2,1)}, u32[]{:S(2)}) copy-start(bf16[8,16,32,128]{3,2,1,0:T(8,128)(2,1)} %finish_filtered.1.own.refs_2_) | copy-start | bytes 3145732
  59.1 5.2 %copy-start.3 = (bf16[4,16,32,128]{3,2,1,0:T(8,128)(2,1)}, bf16[4,16,32,128]{3,2,1,0:T(8,128)(2,1)S(1)}, u32[]{:S(2)}) copy-start(bf16[4,16,32,128]{3,2,1,0:T(8,128)(2,1)S(1)} %collective-permute-done.10.refs_1_) | copy-start | bytes 1572868
  64.3 0.8 copy-start.4
  70.6 1.8 %copy-start.2 = (bf16[8,16,32,128]{3,2,1,0:T(8,128)(2,1)S(1)}, bf16[8,16,32,128]{3,2,1,0:T(8,128)(2,1)}, u32[]{:S(2)}) copy-start(bf16[8,16,32,128]{3,2,1,0:T(8,128)(2,1)} %finish_applied.1) | copy-start | bytes 3145732
  72.9 4.3 %collective-permute-start.11 = (f32[128,256]{0,1:T(8,128)S(1)}, f32[128,256]{0,1:T(8,128)S(1)}, u32[]{:S(2)}, u32[]{:S(2)}) collective-permute-start(f32[128,256]{0,1:T(8,128)S(1)} %maximum_select_fusion.1), channel_id=1, source_target_pairs={{0,1},{1,0},{2,3},{3,2},{4,5},{5,4},{6,7},{7,6},{8,9},{9,8},{10,11... | collective-permute-start | bytes 393224 | tf_op jit(solution)/shard_map/ppermute | solution.py:111
  76.7 1.4 %collective-permute-start.5 = (f32[128,256]{0,1:T(8,128)S(1)}, f32[128,256]{0,1:T(8,128)S(1)}, u32[]{:S(2)}, u32[]{:S(2)}) collective-permute-start(f32[128,256]{0,1:T(8,128)S(1)} %maximum_select_fusion), channel_id=1, source_target_pairs={{0,1},{1,0},{2,3},{3,2},{4,5},{5,4},{6,7},{7,6},{8,9},{9,8},{10,11... | collective-permute-start | bytes 393224 | tf_op jit(solution)/shard_map/ppermute | solution.py:111
  77.2 6.4 %collective-permute-start.12 = (f32[128,256]{0,1:T(8,128)S(1)}, f32[128,256]{0,1:T(8,128)S(1)}, u32[]{:S(2)}, u32[]{:S(2)}) collective-permute-start(f32[128,256]{0,1:T(8,128)S(1)} %add.28), channel_id=1, source_target_pairs={{0,2},{1,3},{2,0},{3,1},{4,6},{5,7},{6,4},{7,5},{8,10},{9,11},{10,... | collective-permute-start | bytes 393224 | tf_op jit(solution)/shard_map/ppermute | solution.py:111
  78.1 7.7 %collective-permute-start.6 = (f32[128,256]{0,1:T(8,128)S(1)}, f32[128,256]{0,1:T(8,128)S(1)}, u32[]{:S(2)}, u32[]{:S(2)}) collective-permute-start(f32[128,256]{0,1:T(8,128)S(1)} %add.24), channel_id=1, source_target_pairs={{0,2},{1,3},{2,0},{3,1},{4,6},{5,7},{6,4},{7,5},{8,10},{9,11},{10,... | collective-permute-start | bytes 393224 | tf_op jit(solution)/shard_map/ppermute | solution.py:111
  83.6 5.6 %collective-permute-start.13 = (f32[128,256]{0,1:T(8,128)S(1)}, f32[128,256]{0,1:T(8,128)S(1)}, u32[]{:S(2)}, u32[]{:S(2)}) collective-permute-start(f32[128,256]{0,1:T(8,128)S(1)} %add.29), channel_id=1, source_target_pairs={{0,4},{1,5},{2,6},{3,7},{4,0},{5,1},{6,2},{7,3},{8,12},{9,13},{10,... | collective-permute-start | bytes 393224 | tf_op jit(solution)/shard_map/ppermute | solution.py:111
  85.9 7.0 %collective-permute-start.7 = (f32[128,256]{0,1:T(8,128)S(1)}, f32[128,256]{0,1:T(8,128)S(1)}, u32[]{:S(2)}, u32[]{:S(2)}) collective-permute-start(f32[128,256]{0,1:T(8,128)S(1)} %add.25), channel_id=1, source_target_pairs={{0,4},{1,5},{2,6},{3,7},{4,0},{5,1},{6,2},{7,3},{8,12},{9,13},{10,... | collective-permute-start | bytes 393224 | tf_op jit(solution)/shard_map/ppermute | solution.py:111
  89.3 12.0 %collective-permute-start.14 = (f32[128,256]{0,1:T(8,128)S(1)}, f32[128,256]{0,1:T(8,128)S(1)}, u32[]{:S(2)}, u32[]{:S(2)}) collective-permute-start(f32[128,256]{0,1:T(8,128)S(1)} %add.30), channel_id=1, source_target_pairs={{0,8},{1,9},{2,10},{3,11},{4,12},{5,13},{6,14},{7,15},{8,0},{9,1},... | collective-permute-start | bytes 393224 | tf_op jit(solution)/shard_map/ppermute | solution.py:111
  92.9 10.0 %collective-permute-start.8 = (f32[128,256]{0,1:T(8,128)S(1)}, f32[128,256]{0,1:T(8,128)S(1)}, u32[]{:S(2)}, u32[]{:S(2)}) collective-permute-start(f32[128,256]{0,1:T(8,128)S(1)} %add.26), channel_id=1, source_target_pairs={{0,8},{1,9},{2,10},{3,11},{4,12},{5,13},{6,14},{7,15},{8,0},{9,1},... | collective-permute-start | bytes 393224 | tf_op jit(solution)/shard_map/ppermute | solution.py:111

commit v6 on v5

--- a/solution.py
+++ b/solution.py
@@ -15,17 +15,10 @@
 memory_factor = -1.0 / 7.0
 
 
-def halos(block, axis, width):
-    count = lax.axis_size(axis)
-    forward = [(i, (i + 1) % count) for i in range(count)]
-    backward = [(target, source) for source, target in forward]
-    low = lax.ppermute(lax.slice_in_dim(block, block.shape[0] - width, None, axis=0), axis, forward)
-    high = lax.ppermute(lax.slice_in_dim(block, 0, width, axis=0), axis, backward)
-    return low, high
+def interior_kernel(stage, planes, ny, nz):
+    shift = 0.0 if stage == "applied" else spectrum_centre
 
-
-def interior_kernel(planes, ny, nz):
-    def kernel(own, out):
+    def kernel(own, pot, out):
         for x in range(planes):
             def row(y, carry, x=x):
                 centre = own[x, y].astype(jnp.float32)
@@ -41,7 +34,10 @@
                     if x - k >= 0:
                         beside = beside + own[x - k, y].astype(jnp.float32)
                     summed = summed + stencil_weights[k] * beside
-                out[x, y] = summed
+                applied = -0.5 * summed + pot[x, y] * centre
+                if shift:
+                    applied = applied - shift * centre
+                out[x, y] = applied
                 return carry
 
             lax.fori_loop(0, ny, row, 0)
@@ -51,10 +47,11 @@
 
 def finish_kernel(stage, planes, ny):
     def kernel(*refs):
-        if stage == "filtered":
-            low, high, own, partial, pot, initial, out = refs
-        else:
-            low, high, own, partial, pot, out = refs
+        refs = list(refs)
+        low, high, partial = refs[:3]
+        initial = refs[3] if stage == "filtered" else None
+        outs = refs[4:] if stage == "filtered" else refs[3:]
+        out = outs[0]
         for x in range(planes):
             def row(y, carry, x=x):
                 summed = partial[x, y]
@@ -66,18 +63,22 @@
                         outside.append(low[x - k + RADIUS, y].astype(jnp.float32))
                     if outside:
                         term = outside[0] if len(outside) == 1 else outside[0] + outside[1]
-                        summed = summed + stencil_weights[k] * term
-                centre = own[x, y].astype(jnp.float32)
-                applied = -0.5 * summed + pot[x, y] * centre
+                        summed = summed + (-0.5 * stencil_weights[k]) * term
                 if stage == "first":
-                    result = (applied - spectrum_centre * centre) * first_factor
+                    result = summed * first_factor
                 elif stage == "filtered":
-                    result = (applied - spectrum_centre * centre) * second_factor + (
+                    result = summed * second_factor + (
                         memory_factor * initial[x, y].astype(jnp.float32)
                     )
                 else:
-                    result = applied
-                out[x, y] = result.astype(out.dtype)
+                    result = summed
+                result = result.astype(out.dtype)
+                out[x, y] = result
+                if len(outs) == 3:
+                    if x >= planes - RADIUS:
+                        outs[1][x - planes + RADIUS, y] = result
+                    if x < RADIUS:
+                        outs[2][x, y] = result
                 return carry
 
             lax.fori_loop(0, ny, row, 0)
@@ -85,22 +86,33 @@
     return kernel
 
 
-def stencil_stage(stage, block, potential_wide, initial=None):
+def stencil_stage(stage, block, sends, potential_wide, initial=None, keep_sends=True):
     planes, ny, nz, nb = block.shape
-    low, high = halos(block, "domain", RADIUS)
+    low, high = exchange(sends, "domain")
     partial = pl.pallas_call(
-        interior_kernel(planes, ny, nz),
+        interior_kernel(stage, planes, ny, nz),
         out_shape=jax.ShapeDtypeStruct(block.shape, jnp.float32),
         name=f"interior_{stage}",
-    )(block)
-    operands = [low, high, block, partial, potential_wide]
+    )(block, potential_wide)
+    operands = [low, high, partial]
     if initial is not None:
         operands.append(initial)
+    shapes = [jax.ShapeDtypeStruct(block.shape, jnp.bfloat16)]
+    if keep_sends:
+        edge = jax.ShapeDtypeStruct((RADIUS, ny, nz, nb), jnp.bfloat16)
+        shapes += [edge, edge]
     return pl.pallas_call(
         finish_kernel(stage, planes, ny),
-        out_shape=jax.ShapeDtypeStruct(block.shape, jnp.bfloat16),
+        out_shape=tuple(shapes),
         name=f"finish_{stage}",
     )(*operands)
+
+
+def exchange(sends, axis):
+    count = lax.axis_size(axis)
+    forward = [(i, (i + 1) % count) for i in range(count)]
+    backward = [(target, source) for source, target in forward]
+    return lax.ppermute(sends[0], axis, forward), lax.ppermute(sends[1], axis, backward)
 
 
 def butterfly_sum(values, axis):
@@ -127,13 +139,22 @@
         jnp.concatenate([mine, theirs], axis=1),
         jnp.concatenate([theirs, mine], axis=1),
     )
-    first = stencil_stage("first", orbitals, potential_wide)
-    filtered = stencil_stage("filtered", first, potential_wide, orbitals)
+    planes_sent = (
+        lax.slice_in_dim(orbitals, planes - RADIUS, None, axis=0),
+        lax.slice_in_dim(orbitals, 0, RADIUS, axis=0),
+    )
+    first, *first_sent = stencil_stage("first", orbitals, planes_sent, potential_wide)
+    filtered, *filtered_sent = stencil_stage(
+        "filtered", first, first_sent, potential_wide, orbitals
+    )
     own_block = filtered.reshape(cell_count, nb)
     partner = lax.ppermute(own_block, "band", [(0, 1), (1, 0)])
     correlation_piece = placed(gram(own_block, own_block), gram(own_block, partner))
     correlation = butterfly_sum(correlation_piece, "domain") * cell_weight
-    applied = stencil_stage("applied", filtered, potential_wide).reshape(cell_count, nb)
+    (applied_grid,) = stencil_stage(
+        "applied", filtered, filtered_sent, potential_wide, keep_sends=False
+    )
+    applied = applied_grid.reshape(cell_count, nb)
     energy_piece = placed(gram(applied, own_block), gram(applied, partner))
     projected = butterfly_sum(energy_piece, "domain") * cell_weight
     return (filtered, correlation, projected)

time: 104 us -> 97.1 us (0.934)
  starting transfers between devices: 27.8 us -> 19.8 us
  waiting for transfers between devices: 22 us -> 25.2 us
  local copies, waits for them, and re-layouts: 10.8 us -> 8.79 us
    ppermute x8, starting transfers between devices: 11.9 us -> 5.79 us  [butterfly_sum(): values = values + lax.ppermute(values, axis, pairs)]
    slice x3 -> x1, local copies, waits for them, and re-layouts: 4.89 us -> 1.33 us  [shards(): lax.slice_in_dim(orbitals, 0, RADIUS, axis=0)]
    ppermute x8, waiting for transfers between devices: 16.8 us -> 19.9 us  [butterfly_sum(): values = values + lax.ppermute(values, axis, pairs)]
    ppermute x1, waiting for transfers between devices: 0.01 us -> 2.52 us  [shards(): partner = lax.ppermute(own_block, 'band', [(0, 1), (1, 0)])]
    ppermute x6, waiting for transfers between devices: 5.2 us -> 2.8 us  [the longest x3 2.79 us: exchange(): lax.ppermute(sends[0], axis, forward)]
    ppermute x6, starting transfers between devices: 14.1 us -> 12.1 us  [the longest x3 11 us: exchange(): lax.ppermute(sends[1], axis, backward)]
    unnamed x22 -> x20, local copies, waits for them, and re-layouts: 3.94 us -> 5.52 us
  transfers between devices with their start and end apart: 15 -> 15, of which waited for: 9 -> 10; matrix products, arithmetic and copies ran while one was open for 6% -> 6% of each run, Pallas kernels for 26% -> 30%
where the time goes in v6:
time: 97.1 us; the launch traced here: 96.9 us
  Pallas kernels  39 us (40%)
  waiting for transfers between devices  25.2 us (26%)
  starting transfers between devices  19.8 us (20%)
  local copies, waits for them, and re-layouts  8.79 us (9%)
  matrix products  3.22 us (3%)
    pallas_call x3, Pallas kernels, stencil_stage(): pl.pallas_call(interior_kernel(stage, planes, ny, nz), out_shape=jax.Shap...  25.1 us
    ppermute x8, waiting for transfers between devices, butterfly_sum(): values = values + lax.ppermute(values, axis, pairs)  19.9 us
    pallas_call x3, Pallas kernels, stencil_stage(): pl.pallas_call(finish_kernel(stage, planes, ny), out_shape=tuple(shapes),...  13.8 us
    ppermute x3, starting transfers between devices, exchange(): lax.ppermute(sends[1], axis, backward)  11 us
    ppermute x8, starting transfers between devices, butterfly_sum(): values = values + lax.ppermute(values, axis, pairs)  5.79 us
    unnamed x20, local copies, waits for them, and re-layouts  5.52 us
    dot_general x4, matrix products, shards(): jnp.einsum('cb,ck->bk', rows, cols, preferred_element_type=jnp.float32)  3.22 us
    ppermute x3, waiting for transfers between devices, exchange(): lax.ppermute(sends[0], axis, forward)  2.79 us
  transfers between devices with their start and end apart: 15, of which 10 were waited for; matrix products, arithmetic and copies ran while one was open for 6% of the time, Pallas kernels for 30%

profile of v6, /device:TPU:0, one launch (start us, length us, event | category | flops | bytes accessed | tf_op | source)
XLA Modules:
  0.0 96.9 jit_solution(6904628123206924270)
XLA Ops:
  0.6 1.3 %fusion = (bf16[4,16,32,128]{3,2,1,0:T(8,128)(2,1)S(1)}, bf16[4,16,32,128]{3,2,1,0:T(8,128)(2,1)S(1)}) fusion(bf16[8,16,32,128]{3,2,1,0:T(8,128)(2,1)} %refs_3_.1), kind=kLoop, calls=%fused_computation.6 | loop fusion | bytes 2097152 | tf_op jit(solution)/shard_map/slice | solution.py:144
  2.5 5.0 %collective-permute-start.1 = (bf16[4,16,32,128]{3,2,1,0:T(8,128)(2,1)S(1)}, bf16[4,16,32,128]{3,2,1,0:T(8,128)(2,1)S(1)}, u32[]{:S(2)}, u32[]{:S(2)}) collective-permute-start(bf16[4,16,32,128]{3,2,1,0:T(8,128)(2,1)S(1)} %get-tuple-element.18), channel_id=1, source_target_pairs={{1,0},{2,1},{3,2},{4,3},{5,4},{6,5},{7,6},{8,7},{9,8},{10,9},{11,1... | collective-permute-start | bytes 1572872 | tf_op jit(solution)/shard_map/ppermute | solution.py:115
  7.5 1.9 %broadcast_in_dim.2.pot = f32[8,16,32,128]{3,2,1,0:T(8,128)} broadcast(f32[8,16,32]{2,1,0:T(8,128)S(1)} %copy-done.8), dimensions={0,1,2} | broadcast | bytes 2113536 | tf_op jit(solution)/shard_map/broadcast_in_dim | solution.py:130
  9.5 8.4 %interior_first.1.refs_2_ = f32[8,16,32,128]{3,2,1,0:T(8,128)} custom-call(bf16[8,16,32,128]{3,2,1,0:T(8,128)(2,1)} %refs_3_.1, f32[8,16,32,128]{3,2,1,0:T(8,128)} %broadcast_in_dim.2.pot), custom_call_target="tpu_custom_call" | custom-call | tf_op jit(solution)/shard_map/interior_first/pallas_call | solution.py:92
  17.9 0.8 copy-done.2
  18.7 0.8 copy-done.3
  19.5 4.6 %finish_first.1 = (bf16[8,16,32,128]{3,2,1,0:T(8,128)(2,1)}, bf16[4,16,32,128]{3,2,1,0:T(8,128)(2,1)}, bf16[4,16,32,128]{3,2,1,0:T(8,128)(2,1)}) custom-call(bf16[4,16,32,128]{3,2,1,0:T(8,128)(2,1)} %copy-done.2, bf16[4,16,32,128]{3,2,1,0:T(8,128)(2,1)} %copy-done.3, f32[8,16,32,128]{3,2,1,0:T(8,128)} %interior_first.1.refs_2_), custom_call_target="tpu_custom_call" | custom-call | tf_op jit(solution)/shard_map/finish_first/pallas_call | solution.py:104
  24.7 3.8 %collective-permute-start.3 = (bf16[4,16,32,128]{3,2,1,0:T(8,128)(2,1)}, bf16[4,16,32,128]{3,2,1,0:T(8,128)(2,1)S(1)}, u32[]{:S(2)}, u32[]{:S(2)}) collective-permute-start(bf16[4,16,32,128]{3,2,1,0:T(8,128)(2,1)} %get-tuple-element.10), channel_id=1, source_target_pairs={{1,0},{2,1},{3,2},{4,3},{5,4},{6,5},{7,6},{8,7},{9,8},{10,9},{11,1... | collective-permute-start | bytes 1572872 | tf_op jit(solution)/shard_map/ppermute | solution.py:115
  28.5 8.4 %interior_filtered.1.refs_2_ = f32[8,16,32,128]{3,2,1,0:T(8,128)} custom-call(bf16[8,16,32,128]{3,2,1,0:T(8,128)(2,1)} %get-tuple-element.11.own, f32[8,16,32,128]{3,2,1,0:T(8,128)} %broadcast_in_dim.2.pot), custom_call_target="tpu_custom_call" | custom-call | tf_op jit(solution)/shard_map/interior_filtered/pallas_call | solution.py:92
  36.9 0.8 copy-done.6
  37.7 0.8 copy-done.7
  38.5 5.0 %finish_filtered.1 = (bf16[8,16,32,128]{3,2,1,0:T(8,128)(2,1)}, bf16[4,16,32,128]{3,2,1,0:T(8,128)(2,1)}, bf16[4,16,32,128]{3,2,1,0:T(8,128)(2,1)}) custom-call(bf16[4,16,32,128]{3,2,1,0:T(8,128)(2,1)} %copy-done.6, bf16[4,16,32,128]{3,2,1,0:T(8,128)(2,1)} %copy-done.7, f32[8,16,32,128]{3,2,1,0:T(8,128)} %interior_filtered.1.refs_2_, ...), custom_call_target="tpu_custom_call" | custom-call | tf_op jit(solution)/shard_map/finish_filtered/pallas_call | solution.py:104
  43.6 1.9 %collective-permute-start.4 = (bf16[4096,128]{1,0:T(8,128)(2,1)}, bf16[4096,128]{1,0:T(8,128)(2,1)S(1)}, u32[]{:S(2)}, u32[]{:S(2)}) collective-permute-start(bf16[4096,128]{1,0:T(8,128)(2,1)} %bitcast.18), channel_id=1, source_target_pairs={{0,16},{16,0},{1,17},{17,1},{2,18},{18,2},{3,19},{19,3},{4,20},{20... | collective-permute-start | bytes 3145736 | tf_op jit(solution)/shard_map/ppermute | solution.py:151
  45.5 2.1 %collective-permute-start.10 = (bf16[4,16,32,128]{3,2,1,0:T(8,128)(2,1)}, bf16[4,16,32,128]{3,2,1,0:T(8,128)(2,1)S(1)}, u32[]{:S(2)}, u32[]{:S(2)}) collective-permute-start(bf16[4,16,32,128]{3,2,1,0:T(8,128)(2,1)} %get-tuple-element.14), channel_id=1, source_target_pairs={{1,0},{2,1},{3,2},{4,3},{5,4},{6,5},{7,6},{8,7},{9,8},{10,9},{11,1... | collective-permute-start | bytes 1572872 | tf_op jit(solution)/shard_map/ppermute | solution.py:115
  47.6 8.3 %interior_applied.1.refs_2_ = f32[8,16,32,128]{3,2,1,0:T(8,128)} custom-call(bf16[8,16,32,128]{3,2,1,0:T(8,128)(2,1)} %get-tuple-element.15.own, f32[8,16,32,128]{3,2,1,0:T(8,128)} %broadcast_in_dim.2.pot), custom_call_target="tpu_custom_call" | custom-call | tf_op jit(solution)/shard_map/interior_applied/pallas_call | solution.py:92
  56.5 2.8 %collective-permute-done.9.refs_0_ = bf16[4,16,32,128]{3,2,1,0:T(8,128)(2,1)S(1)} collective-permute-done((bf16[4,16,32,128]{3,2,1,0:T(8,128)(2,1)}, bf16[4,16,32,128]{3,2,1,0:T(8,128)(2,1)S(1)}, u32[]{:S(2)}, u32[]{:S(2)}) %collective-permute-start.9) | collective-permute-done | bytes 524320 | tf_op jit(solution)/shard_map/ppermute | solution.py:115
  59.2 0.8 copy-done.5
  60.0 4.2 %finish_applied.1 = bf16[8,16,32,128]{3,2,1,0:T(8,128)(2,1)} custom-call(bf16[4,16,32,128]{3,2,1,0:T(8,128)(2,1)} %copy-done.5, bf16[4,16,32,128]{3,2,1,0:T(8,128)(2,1)} %copy-done.4, f32[8,16,32,128]{3,2,1,0:T(8,128)} %interior_applied.1.refs_2_), custom_call_target="tpu_custom_call" | custom-call | tf_op jit(solution)/shard_map/finish_applied/pallas_call | solution.py:104
  64.2 1.8 %convolution_bitcast_fusion = f32[128,128]{0,1:T(8,128)S(1)} fusion(bf16[8,16,32,128]{3,2,1,0:T(8,128)(2,1)} %finish_applied.1, bf16[8,16,32,128]{3,2,1,0:T(8,128)(2,1)S(1)} %copy-done), kind=kOutput, calls=%fused_computation | convolution fusion | flops 134217728 | bytes 2162688 | tf_op jit(solution)/shard_map/cb,ck->bk/dot_general | solution.py:134
  66.0 2.5 %collective-permute-done.4 = bf16[4096,128]{1,0:T(8,128)(2,1)S(1)} collective-permute-done((bf16[4096,128]{1,0:T(8,128)(2,1)}, bf16[4096,128]{1,0:T(8,128)(2,1)S(1)}, u32[]{:S(2)}, u32[]{:S(2)}) %collective-permute-start.4) | collective-permute-done | bytes 1048608 | tf_op jit(solution)/shard_map/ppermute | solution.py:151
  69.1 1.1 %collective-permute-start.11 = (f32[128,256]{0,1:T(8,128)S(1)}, f32[128,256]{0,1:T(8,128)S(1)}, u32[]{:S(2)}, u32[]{:S(2)}) collective-permute-start(f32[128,256]{0,1:T(8,128)S(1)} %maximum_select_fusion.1), channel_id=1, source_target_pairs={{0,1},{1,0},{2,3},{3,2},{4,5},{5,4},{6,7},{7,6},{8,9},{9,8},{10,11... | collective-permute-start | bytes 393224 | tf_op jit(solution)/shard_map/ppermute | solution.py:123
  71.3 0.8 collective-permute-done.5
  72.1 1.3 %collective-permute-start.6 = (f32[128,256]{0,1:T(8,128)S(1)}, f32[128,256]{0,1:T(8,128)S(1)}, u32[]{:S(2)}, u32[]{:S(2)}) collective-permute-start(f32[128,256]{0,1:T(8,128)S(1)} %add.24), channel_id=1, source_target_pairs={{0,2},{1,3},{2,0},{3,1},{4,6},{5,7},{6,4},{7,5},{8,10},{9,11},{10,... | collective-permute-start | bytes 393224 | tf_op jit(solution)/shard_map/ppermute | solution.py:123
  73.4 4.2 %collective-permute-done.12 = f32[128,256]{0,1:T(8,128)S(1)} collective-permute-done((f32[128,256]{0,1:T(8,128)S(1)}, f32[128,256]{0,1:T(8,128)S(1)}, u32[]{:S(2)}, u32[]{:S(2)}) %collective-permute-start.12) | collective-permute-done | bytes 131104 | tf_op jit(solution)/shard_map/ppermute | solution.py:123
  78.1 1.8 %collective-permute-done.6 = f32[128,256]{0,1:T(8,128)S(1)} collective-permute-done((f32[128,256]{0,1:T(8,128)S(1)}, f32[128,256]{0,1:T(8,128)S(1)}, u32[]{:S(2)}, u32[]{:S(2)}) %collective-permute-start.6) | collective-permute-done | bytes 131104 | tf_op jit(solution)/shard_map/ppermute | solution.py:123
  80.3 3.0 %collective-permute-done.13 = f32[128,256]{0,1:T(8,128)S(1)} collective-permute-done((f32[128,256]{0,1:T(8,128)S(1)}, f32[128,256]{0,1:T(8,128)S(1)}, u32[]{:S(2)}, u32[]{:S(2)}) %collective-permute-start.13) | collective-permute-done | bytes 131104 | tf_op jit(solution)/shard_map/ppermute | solution.py:123
  83.3 1.4 %collective-permute-start.14 = (f32[128,256]{0,1:T(8,128)S(1)}, f32[128,256]{0,1:T(8,128)S(1)}, u32[]{:S(2)}, u32[]{:S(2)}) collective-permute-start(f32[128,256]{0,1:T(8,128)S(1)} %add.30), channel_id=1, source_target_pairs={{0,8},{1,9},{2,10},{3,11},{4,12},{5,13},{6,14},{7,15},{8,0},{9,1},... | collective-permute-start | bytes 393224 | tf_op jit(solution)/shard_map/ppermute | solution.py:123
  84.7 2.1 %collective-permute-done.7 = f32[128,256]{0,1:T(8,128)S(1)} collective-permute-done((f32[128,256]{0,1:T(8,128)S(1)}, f32[128,256]{0,1:T(8,128)S(1)}, u32[]{:S(2)}, u32[]{:S(2)}) %collective-permute-start.7) | collective-permute-done | bytes 131104 | tf_op jit(solution)/shard_map/ppermute | solution.py:123
  86.9 0.9 collective-permute-start.8
  87.8 6.8 %collective-permute-done.14 = f32[128,256]{0,1:T(8,128)S(1)} collective-permute-done((f32[128,256]{0,1:T(8,128)S(1)}, f32[128,256]{0,1:T(8,128)S(1)}, u32[]{:S(2)}, u32[]{:S(2)}) %collective-permute-start.14) | collective-permute-done | bytes 131104 | tf_op jit(solution)/shard_map/ppermute | solution.py:123
  94.6 0.8 copy.6
  96.1 0.8 copy.5
  (40 shorter events, 4.9 us)
Async XLA Ops:
  0.6 6.9 %copy-start.8 = (f32[8,16,32]{2,1,0:T(8,128)S(1)}, f32[8,16,32]{2,1,0:T(8,128)}, u32[]{:S(2)}) copy-start(f32[8,16,32]{2,1,0:T(8,128)} %param.3) | copy-start | bytes 49156
  2.0 15.9 %collective-permute-start = (bf16[4,16,32,128]{3,2,1,0:T(8,128)(2,1)S(1)}, bf16[4,16,32,128]{3,2,1,0:T(8,128)(2,1)S(1)}, u32[]{:S(2)}, u32[]{:S(2)}) collective-permute-start(bf16[4,16,32,128]{3,2,1,0:T(8,128)(2,1)S(1)} %get-tuple-element.19), channel_id=1, source_target_pairs={{0,1},{1,2},{2,3},{3,4},{4,5},{5,6},{6,7},{7,8},{8,9},{9,10},{10,1... | collective-permute-start | bytes 1572872 | tf_op jit(solution)/shard_map/ppermute | solution.py:115
  2.5 15.4 %collective-permute-start.1 = (bf16[4,16,32,128]{3,2,1,0:T(8,128)(2,1)S(1)}, bf16[4,16,32,128]{3,2,1,0:T(8,128)(2,1)S(1)}, u32[]{:S(2)}, u32[]{:S(2)}) collective-permute-start(bf16[4,16,32,128]{3,2,1,0:T(8,128)(2,1)S(1)} %get-tuple-element.18), channel_id=1, source_target_pairs={{1,0},{2,1},{3,2},{4,3},{5,4},{6,5},{7,6},{8,7},{9,8},{10,9},{11,1... | collective-permute-start | bytes 1572872 | tf_op jit(solution)/shard_map/ppermute | solution.py:115
  17.9 0.8 copy-start.2
  18.7 0.8 copy-start.3
  24.1 12.9 %collective-permute-start.2 = (bf16[4,16,32,128]{3,2,1,0:T(8,128)(2,1)}, bf16[4,16,32,128]{3,2,1,0:T(8,128)(2,1)S(1)}, u32[]{:S(2)}, u32[]{:S(2)}) collective-permute-start(bf16[4,16,32,128]{3,2,1,0:T(8,128)(2,1)} %get-tuple-element.9), channel_id=1, source_target_pairs={{0,1},{1,2},{2,3},{3,4},{4,5},{5,6},{6,7},{7,8},{8,9},{9,10},{10,1... | collective-permute-start | bytes 1572872 | tf_op jit(solution)/shard_map/ppermute | solution.py:115
  24.7 12.2 %collective-permute-start.3 = (bf16[4,16,32,128]{3,2,1,0:T(8,128)(2,1)}, bf16[4,16,32,128]{3,2,1,0:T(8,128)(2,1)S(1)}, u32[]{:S(2)}, u32[]{:S(2)}) collective-permute-start(bf16[4,16,32,128]{3,2,1,0:T(8,128)(2,1)} %get-tuple-element.10), channel_id=1, source_target_pairs={{1,0},{2,1},{3,2},{4,3},{5,4},{6,5},{7,6},{8,7},{9,8},{10,9},{11,1... | collective-permute-start | bytes 1572872 | tf_op jit(solution)/shard_map/ppermute | solution.py:115
  36.9 0.8 copy-start.6
  37.7 0.8 copy-start.7
  43.6 25.0 %collective-permute-start.4 = (bf16[4096,128]{1,0:T(8,128)(2,1)}, bf16[4096,128]{1,0:T(8,128)(2,1)S(1)}, u32[]{:S(2)}, u32[]{:S(2)}) collective-permute-start(bf16[4096,128]{1,0:T(8,128)(2,1)} %bitcast.18), channel_id=1, source_target_pairs={{0,16},{16,0},{1,17},{17,1},{2,18},{18,2},{3,19},{19,3},{4,20},{20... | collective-permute-start | bytes 3145736 | tf_op jit(solution)/shard_map/ppermute | solution.py:151
  45.5 10.9 %collective-permute-start.10 = (bf16[4,16,32,128]{3,2,1,0:T(8,128)(2,1)}, bf16[4,16,32,128]{3,2,1,0:T(8,128)(2,1)S(1)}, u32[]{:S(2)}, u32[]{:S(2)}) collective-permute-start(bf16[4,16,32,128]{3,2,1,0:T(8,128)(2,1)} %get-tuple-element.14), channel_id=1, source_target_pairs={{1,0},{2,1},{3,2},{4,3},{5,4},{6,5},{7,6},{8,7},{9,8},{10,9},{11,1... | collective-permute-start | bytes 1572872 | tf_op jit(solution)/shard_map/ppermute | solution.py:115
  47.6 11.6 %collective-permute-start.9 = (bf16[4,16,32,128]{3,2,1,0:T(8,128)(2,1)}, bf16[4,16,32,128]{3,2,1,0:T(8,128)(2,1)S(1)}, u32[]{:S(2)}, u32[]{:S(2)}) collective-permute-start(bf16[4,16,32,128]{3,2,1,0:T(8,128)(2,1)} %get-tuple-element.13), channel_id=1, source_target_pairs={{0,1},{1,2},{2,3},{3,4},{4,5},{5,6},{6,7},{7,8},{8,9},{9,10},{10,1... | collective-permute-start | bytes 1572872 | tf_op jit(solution)/shard_map/ppermute | solution.py:115
  47.6 8.3 %copy-start = (bf16[8,16,32,128]{3,2,1,0:T(8,128)(2,1)S(1)}, bf16[8,16,32,128]{3,2,1,0:T(8,128)(2,1)}, u32[]{:S(2)}) copy-start(bf16[8,16,32,128]{3,2,1,0:T(8,128)(2,1)} %get-tuple-element.15.own) | copy-start | bytes 3145732
  56.4 2.8 %copy-start.4 = (bf16[4,16,32,128]{3,2,1,0:T(8,128)(2,1)}, bf16[4,16,32,128]{3,2,1,0:T(8,128)(2,1)S(1)}, u32[]{:S(2)}) copy-start(bf16[4,16,32,128]{3,2,1,0:T(8,128)(2,1)S(1)} %collective-permute-done.10.refs_1_) | copy-start | bytes 1572868
  59.2 0.8 copy-start.5
  64.2 4.3 %copy-start.1 = (bf16[8,16,32,128]{3,2,1,0:T(8,128)(2,1)S(1)}, bf16[8,16,32,128]{3,2,1,0:T(8,128)(2,1)}, u32[]{:S(2)}) copy-start(bf16[8,16,32,128]{3,2,1,0:T(8,128)(2,1)} %finish_applied.1) | copy-start | bytes 3145732
  69.1 2.1 %collective-permute-start.11 = (f32[128,256]{0,1:T(8,128)S(1)}, f32[128,256]{0,1:T(8,128)S(1)}, u32[]{:S(2)}, u32[]{:S(2)}) collective-permute-start(f32[128,256]{0,1:T(8,128)S(1)} %maximum_select_fusion.1), channel_id=1, source_target_pairs={{0,1},{1,0},{2,3},{3,2},{4,5},{5,4},{6,7},{7,6},{8,9},{9,8},{10,11... | collective-permute-start | bytes 393224 | tf_op jit(solution)/shard_map/ppermute | solution.py:123
  70.7 1.4 %collective-permute-start.5 = (f32[128,256]{0,1:T(8,128)S(1)}, f32[128,256]{0,1:T(8,128)S(1)}, u32[]{:S(2)}, u32[]{:S(2)}) collective-permute-start(f32[128,256]{0,1:T(8,128)S(1)} %maximum_select_fusion), channel_id=1, source_target_pairs={{0,1},{1,0},{2,3},{3,2},{4,5},{5,4},{6,7},{7,6},{8,9},{9,8},{10,11... | collective-permute-start | bytes 393224 | tf_op jit(solution)/shard_map/ppermute | solution.py:123
  71.2 6.4 %collective-permute-start.12 = (f32[128,256]{0,1:T(8,128)S(1)}, f32[128,256]{0,1:T(8,128)S(1)}, u32[]{:S(2)}, u32[]{:S(2)}) collective-permute-start(f32[128,256]{0,1:T(8,128)S(1)} %add.28), channel_id=1, source_target_pairs={{0,2},{1,3},{2,0},{3,1},{4,6},{5,7},{6,4},{7,5},{8,10},{9,11},{10,... | collective-permute-start | bytes 393224 | tf_op jit(solution)/shard_map/ppermute | solution.py:123
  72.1 7.7 %collective-permute-start.6 = (f32[128,256]{0,1:T(8,128)S(1)}, f32[128,256]{0,1:T(8,128)S(1)}, u32[]{:S(2)}, u32[]{:S(2)}) collective-permute-start(f32[128,256]{0,1:T(8,128)S(1)} %add.24), channel_id=1, source_target_pairs={{0,2},{1,3},{2,0},{3,1},{4,6},{5,7},{6,4},{7,5},{8,10},{9,11},{10,... | collective-permute-start | bytes 393224 | tf_op jit(solution)/shard_map/ppermute | solution.py:123
  77.6 5.6 %collective-permute-start.13 = (f32[128,256]{0,1:T(8,128)S(1)}, f32[128,256]{0,1:T(8,128)S(1)}, u32[]{:S(2)}, u32[]{:S(2)}) collective-permute-start(f32[128,256]{0,1:T(8,128)S(1)} %add.29), channel_id=1, source_target_pairs={{0,4},{1,5},{2,6},{3,7},{4,0},{5,1},{6,2},{7,3},{8,12},{9,13},{10,... | collective-permute-start | bytes 393224 | tf_op jit(solution)/shard_map/ppermute | solution.py:123
  79.9 7.0 %collective-permute-start.7 = (f32[128,256]{0,1:T(8,128)S(1)}, f32[128,256]{0,1:T(8,128)S(1)}, u32[]{:S(2)}, u32[]{:S(2)}) collective-permute-start(f32[128,256]{0,1:T(8,128)S(1)} %add.25), channel_id=1, source_target_pairs={{0,4},{1,5},{2,6},{3,7},{4,0},{5,1},{6,2},{7,3},{8,12},{9,13},{10,... | collective-permute-start | bytes 393224 | tf_op jit(solution)/shard_map/ppermute | solution.py:123
  83.3 11.3 %collective-permute-start.14 = (f32[128,256]{0,1:T(8,128)S(1)}, f32[128,256]{0,1:T(8,128)S(1)}, u32[]{:S(2)}, u32[]{:S(2)}) collective-permute-start(f32[128,256]{0,1:T(8,128)S(1)} %add.30), channel_id=1, source_target_pairs={{0,8},{1,9},{2,10},{3,11},{4,12},{5,13},{6,14},{7,15},{8,0},{9,1},... | collective-permute-start | bytes 393224 | tf_op jit(solution)/shard_map/ppermute | solution.py:123
  86.9 9.2 %collective-permute-start.8 = (f32[128,256]{0,1:T(8,128)S(1)}, f32[128,256]{0,1:T(8,128)S(1)}, u32[]{:S(2)}, u32[]{:S(2)}) collective-permute-start(f32[128,256]{0,1:T(8,128)S(1)} %add.26), channel_id=1, source_target_pairs={{0,8},{1,9},{2,10},{3,11},{4,12},{5,13},{6,14},{7,15},{8,0},{9,1},... | collective-permute-start | bytes 393224 | tf_op jit(solution)/shard_map/ppermute | solution.py:123

commit v7 on v6

--- a/solution.py
+++ b/solution.py
@@ -18,21 +18,22 @@
 def interior_kernel(stage, planes, ny, nz):
     shift = 0.0 if stage == "applied" else spectrum_centre
 
-    def kernel(own, pot, out):
+    def kernel(own_narrow, pot, out, own):
+        for x in range(planes):
+            own[x] = own_narrow[x].astype(jnp.float32)
         for x in range(planes):
             def row(y, carry, x=x):
-                centre = own[x, y].astype(jnp.float32)
+                centre = own[x, y]
                 summed = (3.0 * stencil_weights[0]) * centre
                 for k in range(1, RADIUS + 1):
-                    beside = own[x, (y + k) % ny].astype(jnp.float32)
-                    beside = beside + own[x, (y + ny - k) % ny].astype(jnp.float32)
+                    beside = own[x, (y + k) % ny] + own[x, (y + ny - k) % ny]
                     beside = beside + (
                         pltpu.roll(centre, k, 0) + pltpu.roll(centre, nz - k, 0)
                     )
                     if x + k < planes:
-                        beside = beside + own[x + k, y].astype(jnp.float32)
+                        beside = beside + own[x + k, y]
                     if x - k >= 0:
-                        beside = beside + own[x - k, y].astype(jnp.float32)
+                        beside = beside + own[x - k, y]
                     summed = summed + stencil_weights[k] * beside
                 applied = -0.5 * summed + pot[x, y] * centre
                 if shift:
@@ -92,6 +93,7 @@
     partial = pl.pallas_call(
         interior_kernel(stage, planes, ny, nz),
         out_shape=jax.ShapeDtypeStruct(block.shape, jnp.float32),
+        scratch_shapes=[pltpu.VMEM(block.shape, jnp.float32)],
         name=f"interior_{stage}",
     )(block, potential_wide)
     operands = [low, high, partial]

time: 97.1 us -> 97.1 us (level)
  starting transfers between devices: 19.8 us -> 21.7 us
  waiting for transfers between devices: 25.2 us -> 23.9 us
    ppermute x8, starting transfers between devices: 5.79 us -> 7.47 us  [butterfly_sum(): values = values + lax.ppermute(values, axis, pairs)]
where the time goes in v7:
time: 97.1 us; the launch traced here: 96.9 us
  Pallas kernels  38.4 us (40%)
  waiting for transfers between devices  23.9 us (25%)
  starting transfers between devices  21.7 us (22%)
  local copies, waits for them, and re-layouts  8.79 us (9%)
  matrix products  3.21 us (3%)
    pallas_call x3, Pallas kernels, stencil_stage(): pl.pallas_call(interior_kernel(stage, planes, ny, nz), out_shape=jax.Shap...  24.5 us
    ppermute x8, waiting for transfers between devices, butterfly_sum(): values = values + lax.ppermute(values, axis, pairs)  19.1 us
    pallas_call x3, Pallas kernels, stencil_stage(): pl.pallas_call(finish_kernel(stage, planes, ny), out_shape=tuple(shapes),...  13.8 us
    ppermute x3, starting transfers between devices, exchange(): lax.ppermute(sends[1], axis, backward)  11 us
    ppermute x8, starting transfers between devices, butterfly_sum(): values = values + lax.ppermute(values, axis, pairs)  7.47 us
    unnamed x20, local copies, waits for them, and re-layouts  5.52 us
    dot_general x4, matrix products, shards(): jnp.einsum('cb,ck->bk', rows, cols, preferred_element_type=jnp.float32)  3.21 us
    ppermute x3, waiting for transfers between devices, exchange(): lax.ppermute(sends[0], axis, forward)  2.97 us
  transfers between devices with their start and end apart: 15, of which 10 were waited for; matrix products, arithmetic and copies ran while one was open for 6% of the time, Pallas kernels for 30%

profile of v7, /device:TPU:0, one launch (start us, length us, event | category | flops | bytes accessed | tf_op | source)
XLA Modules:
  0.0 96.9 jit_solution(7198990792959953131)
XLA Ops:
  0.6 1.3 %fusion = (bf16[4,16,32,128]{3,2,1,0:T(8,128)(2,1)S(1)}, bf16[4,16,32,128]{3,2,1,0:T(8,128)(2,1)S(1)}) fusion(bf16[8,16,32,128]{3,2,1,0:T(8,128)(2,1)} %refs_3_.1), kind=kLoop, calls=%fused_computation.6 | loop fusion | bytes 2097152 | tf_op jit(solution)/shard_map/slice | solution.py:146
  2.5 5.0 %collective-permute-start.1 = (bf16[4,16,32,128]{3,2,1,0:T(8,128)(2,1)S(1)}, bf16[4,16,32,128]{3,2,1,0:T(8,128)(2,1)S(1)}, u32[]{:S(2)}, u32[]{:S(2)}) collective-permute-start(bf16[4,16,32,128]{3,2,1,0:T(8,128)(2,1)S(1)} %get-tuple-element.18), channel_id=1, source_target_pairs={{1,0},{2,1},{3,2},{4,3},{5,4},{6,5},{7,6},{8,7},{9,8},{10,9},{11,1... | collective-permute-start | bytes 1572872 | tf_op jit(solution)/shard_map/ppermute | solution.py:117
  7.5 1.9 %broadcast_in_dim.2.pot = f32[8,16,32,128]{3,2,1,0:T(8,128)} broadcast(f32[8,16,32]{2,1,0:T(8,128)S(1)} %copy-done.8), dimensions={0,1,2} | broadcast | bytes 2113536 | tf_op jit(solution)/shard_map/broadcast_in_dim | solution.py:132
  9.5 8.2 %interior_first.1.refs_2_ = f32[8,16,32,128]{3,2,1,0:T(8,128)} custom-call(bf16[8,16,32,128]{3,2,1,0:T(8,128)(2,1)} %refs_3_.1, f32[8,16,32,128]{3,2,1,0:T(8,128)} %broadcast_in_dim.2.pot), custom_call_target="tpu_custom_call" | custom-call | tf_op jit(solution)/shard_map/interior_first/pallas_call | solution.py:93
  17.7 0.8 copy-done.2
  18.5 0.8 copy-done.3
  19.3 4.6 %finish_first.1 = (bf16[8,16,32,128]{3,2,1,0:T(8,128)(2,1)}, bf16[4,16,32,128]{3,2,1,0:T(8,128)(2,1)}, bf16[4,16,32,128]{3,2,1,0:T(8,128)(2,1)}) custom-call(bf16[4,16,32,128]{3,2,1,0:T(8,128)(2,1)} %copy-done.2, bf16[4,16,32,128]{3,2,1,0:T(8,128)(2,1)} %copy-done.3, f32[8,16,32,128]{3,2,1,0:T(8,128)} %interior_first.1.refs_2_), custom_call_target="tpu_custom_call" | custom-call | tf_op jit(solution)/shard_map/finish_first/pallas_call | solution.py:106
  23.8 0.9 collective-permute-start.2
  24.7 3.6 %collective-permute-start.3 = (bf16[4,16,32,128]{3,2,1,0:T(8,128)(2,1)}, bf16[4,16,32,128]{3,2,1,0:T(8,128)(2,1)S(1)}, u32[]{:S(2)}, u32[]{:S(2)}) collective-permute-start(bf16[4,16,32,128]{3,2,1,0:T(8,128)(2,1)} %get-tuple-element.10), channel_id=1, source_target_pairs={{1,0},{2,1},{3,2},{4,3},{5,4},{6,5},{7,6},{8,7},{9,8},{10,9},{11,1... | collective-permute-start | bytes 1572872 | tf_op jit(solution)/shard_map/ppermute | solution.py:117
  28.3 8.2 %interior_filtered.1.refs_2_ = f32[8,16,32,128]{3,2,1,0:T(8,128)} custom-call(bf16[8,16,32,128]{3,2,1,0:T(8,128)(2,1)} %get-tuple-element.11.own_narrow, f32[8,16,32,128]{3,2,1,0:T(8,128)} %broadcast_in_dim.2.pot), custom_call_target="tpu_custom_call" | custom-call | tf_op jit(solution)/shard_map/interior_filtered/pallas_call | solution.py:93
  36.5 0.8 copy-done.6
  37.3 0.8 copy-done.7
  38.1 5.0 %finish_filtered.1 = (bf16[8,16,32,128]{3,2,1,0:T(8,128)(2,1)}, bf16[4,16,32,128]{3,2,1,0:T(8,128)(2,1)}, bf16[4,16,32,128]{3,2,1,0:T(8,128)(2,1)}) custom-call(bf16[4,16,32,128]{3,2,1,0:T(8,128)(2,1)} %copy-done.6, bf16[4,16,32,128]{3,2,1,0:T(8,128)(2,1)} %copy-done.7, f32[8,16,32,128]{3,2,1,0:T(8,128)} %interior_filtered.1.refs_2_, ...), custom_call_target="tpu_custom_call" | custom-call | tf_op jit(solution)/shard_map/finish_filtered/pallas_call | solution.py:106
  43.1 1.9 %collective-permute-start.4 = (bf16[4096,128]{1,0:T(8,128)(2,1)}, bf16[4096,128]{1,0:T(8,128)(2,1)S(1)}, u32[]{:S(2)}, u32[]{:S(2)}) collective-permute-start(bf16[4096,128]{1,0:T(8,128)(2,1)} %bitcast.18), channel_id=1, source_target_pairs={{0,16},{16,0},{1,17},{17,1},{2,18},{18,2},{3,19},{19,3},{4,20},{20... | collective-permute-start | bytes 3145736 | tf_op jit(solution)/shard_map/ppermute | solution.py:153
  45.1 2.3 %collective-permute-start.10 = (bf16[4,16,32,128]{3,2,1,0:T(8,128)(2,1)}, bf16[4,16,32,128]{3,2,1,0:T(8,128)(2,1)S(1)}, u32[]{:S(2)}, u32[]{:S(2)}) collective-permute-start(bf16[4,16,32,128]{3,2,1,0:T(8,128)(2,1)} %get-tuple-element.14), channel_id=1, source_target_pairs={{1,0},{2,1},{3,2},{4,3},{5,4},{6,5},{7,6},{8,7},{9,8},{10,9},{11,1... | collective-permute-start | bytes 1572872 | tf_op jit(solution)/shard_map/ppermute | solution.py:117
  47.4 8.1 %interior_applied.1.refs_2_ = f32[8,16,32,128]{3,2,1,0:T(8,128)} custom-call(bf16[8,16,32,128]{3,2,1,0:T(8,128)(2,1)} %get-tuple-element.15.own_narrow, f32[8,16,32,128]{3,2,1,0:T(8,128)} %broadcast_in_dim.2.pot), custom_call_target="tpu_custom_call" | custom-call | tf_op jit(solution)/shard_map/interior_applied/pallas_call | solution.py:93
  56.1 3.0 %collective-permute-done.9.refs_0_ = bf16[4,16,32,128]{3,2,1,0:T(8,128)(2,1)S(1)} collective-permute-done((bf16[4,16,32,128]{3,2,1,0:T(8,128)(2,1)}, bf16[4,16,32,128]{3,2,1,0:T(8,128)(2,1)S(1)}, u32[]{:S(2)}, u32[]{:S(2)}) %collective-permute-start.9) | collective-permute-done | bytes 524320 | tf_op jit(solution)/shard_map/ppermute | solution.py:117
  59.0 0.8 copy-done.5
  59.8 4.2 %finish_applied.1 = bf16[8,16,32,128]{3,2,1,0:T(8,128)(2,1)} custom-call(bf16[4,16,32,128]{3,2,1,0:T(8,128)(2,1)} %copy-done.5, bf16[4,16,32,128]{3,2,1,0:T(8,128)(2,1)} %copy-done.4, f32[8,16,32,128]{3,2,1,0:T(8,128)} %interior_applied.1.refs_2_), custom_call_target="tpu_custom_call" | custom-call | tf_op jit(solution)/shard_map/finish_applied/pallas_call | solution.py:106
  64.0 1.8 %convolution_bitcast_fusion = f32[128,128]{0,1:T(8,128)S(1)} fusion(bf16[8,16,32,128]{3,2,1,0:T(8,128)(2,1)} %finish_applied.1, bf16[8,16,32,128]{3,2,1,0:T(8,128)(2,1)S(1)} %copy-done), kind=kOutput, calls=%fused_computation | convolution fusion | flops 134217728 | bytes 2162688 | tf_op jit(solution)/shard_map/cb,ck->bk/dot_general | solution.py:136
  65.8 1.8 %collective-permute-done.4 = bf16[4096,128]{1,0:T(8,128)(2,1)S(1)} collective-permute-done((bf16[4096,128]{1,0:T(8,128)(2,1)}, bf16[4096,128]{1,0:T(8,128)(2,1)S(1)}, u32[]{:S(2)}, u32[]{:S(2)}) %collective-permute-start.4) | collective-permute-done | bytes 1048608 | tf_op jit(solution)/shard_map/ppermute | solution.py:153
  68.2 1.8 %collective-permute-start.11 = (f32[128,256]{0,1:T(8,128)S(1)}, f32[128,256]{0,1:T(8,128)S(1)}, u32[]{:S(2)}, u32[]{:S(2)}) collective-permute-start(f32[128,256]{0,1:T(8,128)S(1)} %maximum_select_fusion.1), channel_id=1, source_target_pairs={{0,1},{1,0},{2,3},{3,2},{4,5},{5,4},{6,7},{7,6},{8,9},{9,8},{10,11... | collective-permute-start | bytes 393224 | tf_op jit(solution)/shard_map/ppermute | solution.py:125
  71.0 0.8 collective-permute-done.5
  71.9 1.3 %collective-permute-start.6 = (f32[128,256]{0,1:T(8,128)S(1)}, f32[128,256]{0,1:T(8,128)S(1)}, u32[]{:S(2)}, u32[]{:S(2)}) collective-permute-start(f32[128,256]{0,1:T(8,128)S(1)} %add.24), channel_id=1, source_target_pairs={{0,2},{1,3},{2,0},{3,1},{4,6},{5,7},{6,4},{7,5},{8,10},{9,11},{10,... | collective-permute-start | bytes 393224 | tf_op jit(solution)/shard_map/ppermute | solution.py:125
  73.1 4.2 %collective-permute-done.12 = f32[128,256]{0,1:T(8,128)S(1)} collective-permute-done((f32[128,256]{0,1:T(8,128)S(1)}, f32[128,256]{0,1:T(8,128)S(1)}, u32[]{:S(2)}, u32[]{:S(2)}) %collective-permute-start.12) | collective-permute-done | bytes 131104 | tf_op jit(solution)/shard_map/ppermute | solution.py:125
  78.1 1.5 %collective-permute-done.6 = f32[128,256]{0,1:T(8,128)S(1)} collective-permute-done((f32[128,256]{0,1:T(8,128)S(1)}, f32[128,256]{0,1:T(8,128)S(1)}, u32[]{:S(2)}, u32[]{:S(2)}) %collective-permute-start.6) | collective-permute-done | bytes 131104 | tf_op jit(solution)/shard_map/ppermute | solution.py:125
  80.3 2.7 %collective-permute-done.13 = f32[128,256]{0,1:T(8,128)S(1)} collective-permute-done((f32[128,256]{0,1:T(8,128)S(1)}, f32[128,256]{0,1:T(8,128)S(1)}, u32[]{:S(2)}, u32[]{:S(2)}) %collective-permute-start.13) | collective-permute-done | bytes 131104 | tf_op jit(solution)/shard_map/ppermute | solution.py:125
  83.0 1.7 %collective-permute-start.14 = (f32[128,256]{0,1:T(8,128)S(1)}, f32[128,256]{0,1:T(8,128)S(1)}, u32[]{:S(2)}, u32[]{:S(2)}) collective-permute-start(f32[128,256]{0,1:T(8,128)S(1)} %add.30), channel_id=1, source_target_pairs={{0,8},{1,9},{2,10},{3,11},{4,12},{5,13},{6,14},{7,15},{8,0},{9,1},... | collective-permute-start | bytes 393224 | tf_op jit(solution)/shard_map/ppermute | solution.py:125
  84.7 1.9 %collective-permute-done.7 = f32[128,256]{0,1:T(8,128)S(1)} collective-permute-done((f32[128,256]{0,1:T(8,128)S(1)}, f32[128,256]{0,1:T(8,128)S(1)}, u32[]{:S(2)}, u32[]{:S(2)}) %collective-permute-start.7) | collective-permute-done | bytes 131104 | tf_op jit(solution)/shard_map/ppermute | solution.py:125
  86.6 1.2 %collective-permute-start.8 = (f32[128,256]{0,1:T(8,128)S(1)}, f32[128,256]{0,1:T(8,128)S(1)}, u32[]{:S(2)}, u32[]{:S(2)}) collective-permute-start(f32[128,256]{0,1:T(8,128)S(1)} %add.26), channel_id=1, source_target_pairs={{0,8},{1,9},{2,10},{3,11},{4,12},{5,13},{6,14},{7,15},{8,0},{9,1},... | collective-permute-start | bytes 393224 | tf_op jit(solution)/shard_map/ppermute | solution.py:125
  87.8 6.8 %collective-permute-done.14 = f32[128,256]{0,1:T(8,128)S(1)} collective-permute-done((f32[128,256]{0,1:T(8,128)S(1)}, f32[128,256]{0,1:T(8,128)S(1)}, u32[]{:S(2)}, u32[]{:S(2)}) %collective-permute-start.14) | collective-permute-done | bytes 131104 | tf_op jit(solution)/shard_map/ppermute | solution.py:125
  94.6 0.8 copy.6
  (40 shorter events, 5.5 us)
Async XLA Ops:
  0.6 6.9 %copy-start.8 = (f32[8,16,32]{2,1,0:T(8,128)S(1)}, f32[8,16,32]{2,1,0:T(8,128)}, u32[]{:S(2)}) copy-start(f32[8,16,32]{2,1,0:T(8,128)} %param.3) | copy-start | bytes 49156
  2.0 15.7 %collective-permute-start = (bf16[4,16,32,128]{3,2,1,0:T(8,128)(2,1)S(1)}, bf16[4,16,32,128]{3,2,1,0:T(8,128)(2,1)S(1)}, u32[]{:S(2)}, u32[]{:S(2)}) collective-permute-start(bf16[4,16,32,128]{3,2,1,0:T(8,128)(2,1)S(1)} %get-tuple-element.19), channel_id=1, source_target_pairs={{0,1},{1,2},{2,3},{3,4},{4,5},{5,6},{6,7},{7,8},{8,9},{9,10},{10,1... | collective-permute-start | bytes 1572872 | tf_op jit(solution)/shard_map/ppermute | solution.py:117
  2.5 15.2 %collective-permute-start.1 = (bf16[4,16,32,128]{3,2,1,0:T(8,128)(2,1)S(1)}, bf16[4,16,32,128]{3,2,1,0:T(8,128)(2,1)S(1)}, u32[]{:S(2)}, u32[]{:S(2)}) collective-permute-start(bf16[4,16,32,128]{3,2,1,0:T(8,128)(2,1)S(1)} %get-tuple-element.18), channel_id=1, source_target_pairs={{1,0},{2,1},{3,2},{4,3},{5,4},{6,5},{7,6},{8,7},{9,8},{10,9},{11,1... | collective-permute-start | bytes 1572872 | tf_op jit(solution)/shard_map/ppermute | solution.py:117
  17.7 0.8 copy-start.2
  18.5 0.8 copy-start.3
  23.8 12.6 %collective-permute-start.2 = (bf16[4,16,32,128]{3,2,1,0:T(8,128)(2,1)}, bf16[4,16,32,128]{3,2,1,0:T(8,128)(2,1)S(1)}, u32[]{:S(2)}, u32[]{:S(2)}) collective-permute-start(bf16[4,16,32,128]{3,2,1,0:T(8,128)(2,1)} %get-tuple-element.9), channel_id=1, source_target_pairs={{0,1},{1,2},{2,3},{3,4},{4,5},{5,6},{6,7},{7,8},{8,9},{9,10},{10,1... | collective-permute-start | bytes 1572872 | tf_op jit(solution)/shard_map/ppermute | solution.py:117
  24.7 11.8 %collective-permute-start.3 = (bf16[4,16,32,128]{3,2,1,0:T(8,128)(2,1)}, bf16[4,16,32,128]{3,2,1,0:T(8,128)(2,1)S(1)}, u32[]{:S(2)}, u32[]{:S(2)}) collective-permute-start(bf16[4,16,32,128]{3,2,1,0:T(8,128)(2,1)} %get-tuple-element.10), channel_id=1, source_target_pairs={{1,0},{2,1},{3,2},{4,3},{5,4},{6,5},{7,6},{8,7},{9,8},{10,9},{11,1... | collective-permute-start | bytes 1572872 | tf_op jit(solution)/shard_map/ppermute | solution.py:117
  36.5 0.8 copy-start.6
  37.3 0.8 copy-start.7
  43.1 24.5 %collective-permute-start.4 = (bf16[4096,128]{1,0:T(8,128)(2,1)}, bf16[4096,128]{1,0:T(8,128)(2,1)S(1)}, u32[]{:S(2)}, u32[]{:S(2)}) collective-permute-start(bf16[4096,128]{1,0:T(8,128)(2,1)} %bitcast.18), channel_id=1, source_target_pairs={{0,16},{16,0},{1,17},{17,1},{2,18},{18,2},{3,19},{19,3},{4,20},{20... | collective-permute-start | bytes 3145736 | tf_op jit(solution)/shard_map/ppermute | solution.py:153
  45.1 11.0 %collective-permute-start.10 = (bf16[4,16,32,128]{3,2,1,0:T(8,128)(2,1)}, bf16[4,16,32,128]{3,2,1,0:T(8,128)(2,1)S(1)}, u32[]{:S(2)}, u32[]{:S(2)}) collective-permute-start(bf16[4,16,32,128]{3,2,1,0:T(8,128)(2,1)} %get-tuple-element.14), channel_id=1, source_target_pairs={{1,0},{2,1},{3,2},{4,3},{5,4},{6,5},{7,6},{8,7},{9,8},{10,9},{11,1... | collective-permute-start | bytes 1572872 | tf_op jit(solution)/shard_map/ppermute | solution.py:117
  47.4 11.6 %collective-permute-start.9 = (bf16[4,16,32,128]{3,2,1,0:T(8,128)(2,1)}, bf16[4,16,32,128]{3,2,1,0:T(8,128)(2,1)S(1)}, u32[]{:S(2)}, u32[]{:S(2)}) collective-permute-start(bf16[4,16,32,128]{3,2,1,0:T(8,128)(2,1)} %get-tuple-element.13), channel_id=1, source_target_pairs={{0,1},{1,2},{2,3},{3,4},{4,5},{5,6},{6,7},{7,8},{8,9},{9,10},{10,1... | collective-permute-start | bytes 1572872 | tf_op jit(solution)/shard_map/ppermute | solution.py:117
  47.4 8.1 %copy-start = (bf16[8,16,32,128]{3,2,1,0:T(8,128)(2,1)S(1)}, bf16[8,16,32,128]{3,2,1,0:T(8,128)(2,1)}, u32[]{:S(2)}) copy-start(bf16[8,16,32,128]{3,2,1,0:T(8,128)(2,1)} %get-tuple-element.15.own_narrow) | copy-start | bytes 3145732
  56.0 3.0 %copy-start.4 = (bf16[4,16,32,128]{3,2,1,0:T(8,128)(2,1)}, bf16[4,16,32,128]{3,2,1,0:T(8,128)(2,1)S(1)}, u32[]{:S(2)}) copy-start(bf16[4,16,32,128]{3,2,1,0:T(8,128)(2,1)S(1)} %collective-permute-done.10.refs_1_) | copy-start | bytes 1572868
  59.0 0.8 copy-start.5
  64.0 3.6 %copy-start.1 = (bf16[8,16,32,128]{3,2,1,0:T(8,128)(2,1)S(1)}, bf16[8,16,32,128]{3,2,1,0:T(8,128)(2,1)}, u32[]{:S(2)}) copy-start(bf16[8,16,32,128]{3,2,1,0:T(8,128)(2,1)} %finish_applied.1) | copy-start | bytes 3145732
  68.2 2.8 %collective-permute-start.11 = (f32[128,256]{0,1:T(8,128)S(1)}, f32[128,256]{0,1:T(8,128)S(1)}, u32[]{:S(2)}, u32[]{:S(2)}) collective-permute-start(f32[128,256]{0,1:T(8,128)S(1)} %maximum_select_fusion.1), channel_id=1, source_target_pairs={{0,1},{1,0},{2,3},{3,2},{4,5},{5,4},{6,7},{7,6},{8,9},{9,8},{10,11... | collective-permute-start | bytes 393224 | tf_op jit(solution)/shard_map/ppermute | solution.py:125
  70.4 1.4 %collective-permute-start.5 = (f32[128,256]{0,1:T(8,128)S(1)}, f32[128,256]{0,1:T(8,128)S(1)}, u32[]{:S(2)}, u32[]{:S(2)}) collective-permute-start(f32[128,256]{0,1:T(8,128)S(1)} %maximum_select_fusion), channel_id=1, source_target_pairs={{0,1},{1,0},{2,3},{3,2},{4,5},{5,4},{6,7},{7,6},{8,9},{9,8},{10,11... | collective-permute-start | bytes 393224 | tf_op jit(solution)/shard_map/ppermute | solution.py:125
  71.0 6.4 %collective-permute-start.12 = (f32[128,256]{0,1:T(8,128)S(1)}, f32[128,256]{0,1:T(8,128)S(1)}, u32[]{:S(2)}, u32[]{:S(2)}) collective-permute-start(f32[128,256]{0,1:T(8,128)S(1)} %add.28), channel_id=1, source_target_pairs={{0,2},{1,3},{2,0},{3,1},{4,6},{5,7},{6,4},{7,5},{8,10},{9,11},{10,... | collective-permute-start | bytes 393224 | tf_op jit(solution)/shard_map/ppermute | solution.py:125
  71.9 7.7 %collective-permute-start.6 = (f32[128,256]{0,1:T(8,128)S(1)}, f32[128,256]{0,1:T(8,128)S(1)}, u32[]{:S(2)}, u32[]{:S(2)}) collective-permute-start(f32[128,256]{0,1:T(8,128)S(1)} %add.24), channel_id=1, source_target_pairs={{0,2},{1,3},{2,0},{3,1},{4,6},{5,7},{6,4},{7,5},{8,10},{9,11},{10,... | collective-permute-start | bytes 393224 | tf_op jit(solution)/shard_map/ppermute | solution.py:125
  77.4 5.6 %collective-permute-start.13 = (f32[128,256]{0,1:T(8,128)S(1)}, f32[128,256]{0,1:T(8,128)S(1)}, u32[]{:S(2)}, u32[]{:S(2)}) collective-permute-start(f32[128,256]{0,1:T(8,128)S(1)} %add.29), channel_id=1, source_target_pairs={{0,4},{1,5},{2,6},{3,7},{4,0},{5,1},{6,2},{7,3},{8,12},{9,13},{10,... | collective-permute-start | bytes 393224 | tf_op jit(solution)/shard_map/ppermute | solution.py:125
  79.6 7.0 %collective-permute-start.7 = (f32[128,256]{0,1:T(8,128)S(1)}, f32[128,256]{0,1:T(8,128)S(1)}, u32[]{:S(2)}, u32[]{:S(2)}) collective-permute-start(f32[128,256]{0,1:T(8,128)S(1)} %add.25), channel_id=1, source_target_pairs={{0,4},{1,5},{2,6},{3,7},{4,0},{5,1},{6,2},{7,3},{8,12},{9,13},{10,... | collective-permute-start | bytes 393224 | tf_op jit(solution)/shard_map/ppermute | solution.py:125
  83.0 11.6 %collective-permute-start.14 = (f32[128,256]{0,1:T(8,128)S(1)}, f32[128,256]{0,1:T(8,128)S(1)}, u32[]{:S(2)}, u32[]{:S(2)}) collective-permute-start(f32[128,256]{0,1:T(8,128)S(1)} %add.30), channel_id=1, source_target_pairs={{0,8},{1,9},{2,10},{3,11},{4,12},{5,13},{6,14},{7,15},{8,0},{9,1},... | collective-permute-start | bytes 393224 | tf_op jit(solution)/shard_map/ppermute | solution.py:125
  86.6 9.5 %collective-permute-start.8 = (f32[128,256]{0,1:T(8,128)S(1)}, f32[128,256]{0,1:T(8,128)S(1)}, u32[]{:S(2)}, u32[]{:S(2)}) collective-permute-start(f32[128,256]{0,1:T(8,128)S(1)} %add.26), channel_id=1, source_target_pairs={{0,8},{1,9},{2,10},{3,11},{4,12},{5,13},{6,14},{7,15},{8,0},{9,1},... | collective-permute-start | bytes 393224 | tf_op jit(solution)/shard_map/ppermute | solution.py:125

commit v8 on v7

--- a/solution.py
+++ b/solution.py
@@ -119,12 +119,23 @@
 
 def butterfly_sum(values, axis):
     count = lax.axis_size(axis)
-    bit = 1
+    index = lax.axis_index(axis)
+    pairs_of = lambda bit: [(i, i ^ bit) for i in range(count)]
+    half = values.shape[0] // 2
+    upper = index % 2
+    keep = lax.dynamic_slice_in_dim(values, upper * half, half, axis=0)
+    send = lax.dynamic_slice_in_dim(values, (1 - upper) * half, half, axis=0)
+    values = keep + lax.ppermute(send, axis, pairs_of(1))
+    bit = 2
     while bit < count:
-        pairs = [(i, i ^ bit) for i in range(count)]
-        values = values + lax.ppermute(values, axis, pairs)
+        values = values + lax.ppermute(values, axis, pairs_of(bit))
         bit *= 2
-    return values
+    other = lax.ppermute(values, axis, pairs_of(1))
+    return jnp.where(
+        upper == 0,
+        jnp.concatenate([values, other], axis=0),
+        jnp.concatenate([other, values], axis=0),
+    )
 
 
 def shards(orbitals, potential):

time: 97.1 us -> 98.4 us (1.013)
  local copies, waits for them, and re-layouts: 8.79 us -> 9.81 us
    ppermute x3, waiting for transfers between devices: 2.97 us -> 0.01 us  [exchange(): lax.ppermute(sends[0], axis, forward)]
    ppermute x8 -> x10, waiting for transfers between devices: 19.1 us -> 22 us  [the longest x6 20.6 us: butterfly_sum(): values = values + lax.ppermute(values, axis, pairs_of(bit))]
    ppermute x8 -> x10, starting transfers between devices: 7.47 us -> 5.01 us  [the longest x6 3.21 us: butterfly_sum(): values = values + lax.ppermute(values, axis, pairs_of(bit))]
    ppermute x3, starting transfers between devices: 1.36 us -> 3.22 us  [exchange(): lax.ppermute(sends[0], axis, forward)]
  transfers between devices with their start and end apart: 15 -> 17, of which waited for: 10 -> 10; matrix products, arithmetic and copies ran while one was open for 6% -> 6% of each run, Pallas kernels for 30% -> 29%
where the time goes in v8:
time: 98.4 us; the launch traced here: 98.2 us
  Pallas kernels  38.4 us (39%)
  waiting for transfers between devices  23.9 us (24%)
  starting transfers between devices  21.4 us (22%)
  local copies, waits for them, and re-layouts  9.81 us (10%)
  matrix products  3.22 us (3%)
    pallas_call x3, Pallas kernels, stencil_stage(): pl.pallas_call(interior_kernel(stage, planes, ny, nz), out_shape=jax.Shap...  24.6 us
    ppermute x6, waiting for transfers between devices, butterfly_sum(): values = values + lax.ppermute(values, axis, pairs_of(bit))  20.6 us
    pallas_call x3, Pallas kernels, stencil_stage(): pl.pallas_call(finish_kernel(stage, planes, ny), out_shape=tuple(shapes),...  13.8 us
    ppermute x3, starting transfers between devices, exchange(): lax.ppermute(sends[1], axis, backward)  11.2 us
    unnamed x20, local copies, waits for them, and re-layouts  6.34 us
    ppermute x3, starting transfers between devices, exchange(): lax.ppermute(sends[0], axis, forward)  3.22 us
    dot_general x4, matrix products, shards(): jnp.einsum('cb,ck->bk', rows, cols, preferred_element_type=jnp.float32)  3.22 us
    ppermute x6, starting transfers between devices, butterfly_sum(): values = values + lax.ppermute(values, axis, pairs_of(bit))  3.21 us
  transfers between devices with their start and end apart: 17, of which 10 were waited for; matrix products, arithmetic and copies ran while one was open for 6% of the time, Pallas kernels for 29%

profile of v8, /device:TPU:0, one launch (start us, length us, event | category | flops | bytes accessed | tf_op | source)
XLA Modules:
  0.0 98.2 jit_solution(6562353443141539676)
XLA Ops:
  0.6 1.3 %fusion.2 = (bf16[4,16,32,128]{3,2,1,0:T(8,128)(2,1)S(1)}, bf16[4,16,32,128]{3,2,1,0:T(8,128)(2,1)S(1)}) fusion(bf16[8,16,32,128]{3,2,1,0:T(8,128)(2,1)} %refs_3_.1), kind=kLoop, calls=%fused_computation.12 | loop fusion | bytes 2097152 | tf_op jit(solution)/shard_map/slice | solution.py:157
  2.5 5.0 %collective-permute-start.1 = (bf16[4,16,32,128]{3,2,1,0:T(8,128)(2,1)S(1)}, bf16[4,16,32,128]{3,2,1,0:T(8,128)(2,1)S(1)}, u32[]{:S(2)}, u32[]{:S(2)}) collective-permute-start(bf16[4,16,32,128]{3,2,1,0:T(8,128)(2,1)S(1)} %get-tuple-element.18), channel_id=1, source_target_pairs={{1,0},{2,1},{3,2},{4,3},{5,4},{6,5},{7,6},{8,7},{9,8},{10,9},{11,1... | collective-permute-start | bytes 1572872 | tf_op jit(solution)/shard_map/ppermute | solution.py:117
  7.5 1.9 %broadcast_in_dim.2.pot = f32[8,16,32,128]{3,2,1,0:T(8,128)} broadcast(f32[8,16,32]{2,1,0:T(8,128)S(1)} %copy-done.8), dimensions={0,1,2} | broadcast | bytes 2113536 | tf_op jit(solution)/shard_map/broadcast_in_dim | solution.py:143
  9.5 8.2 %interior_first.1.refs_2_ = f32[8,16,32,128]{3,2,1,0:T(8,128)} custom-call(bf16[8,16,32,128]{3,2,1,0:T(8,128)(2,1)} %refs_3_.1, f32[8,16,32,128]{3,2,1,0:T(8,128)} %broadcast_in_dim.2.pot), custom_call_target="tpu_custom_call" | custom-call | tf_op jit(solution)/shard_map/interior_first/pallas_call | solution.py:93
  17.7 0.8 copy-done.2
  18.5 0.8 copy-done.3
  19.3 4.6 %finish_first.1 = (bf16[8,16,32,128]{3,2,1,0:T(8,128)(2,1)}, bf16[4,16,32,128]{3,2,1,0:T(8,128)(2,1)}, bf16[4,16,32,128]{3,2,1,0:T(8,128)(2,1)}) custom-call(bf16[4,16,32,128]{3,2,1,0:T(8,128)(2,1)} %copy-done.2, bf16[4,16,32,128]{3,2,1,0:T(8,128)(2,1)} %copy-done.3, f32[8,16,32,128]{3,2,1,0:T(8,128)} %interior_first.1.refs_2_), custom_call_target="tpu_custom_call" | custom-call | tf_op jit(solution)/shard_map/finish_first/pallas_call | solution.py:106
  23.9 0.8 collective-permute-start.2
  24.7 3.6 %collective-permute-start.3 = (bf16[4,16,32,128]{3,2,1,0:T(8,128)(2,1)}, bf16[4,16,32,128]{3,2,1,0:T(8,128)(2,1)S(1)}, u32[]{:S(2)}, u32[]{:S(2)}) collective-permute-start(bf16[4,16,32,128]{3,2,1,0:T(8,128)(2,1)} %get-tuple-element.10), channel_id=1, source_target_pairs={{1,0},{2,1},{3,2},{4,3},{5,4},{6,5},{7,6},{8,7},{9,8},{10,9},{11,1... | collective-permute-start | bytes 1572872 | tf_op jit(solution)/shard_map/ppermute | solution.py:117
  28.3 8.2 %interior_filtered.1.refs_2_ = f32[8,16,32,128]{3,2,1,0:T(8,128)} custom-call(bf16[8,16,32,128]{3,2,1,0:T(8,128)(2,1)} %get-tuple-element.11.own_narrow, f32[8,16,32,128]{3,2,1,0:T(8,128)} %broadcast_in_dim.2.pot), custom_call_target="tpu_custom_call" | custom-call | tf_op jit(solution)/shard_map/interior_filtered/pallas_call | solution.py:93
  36.6 0.8 copy-done.6
  37.4 0.8 copy-done.7
  38.2 5.1 %finish_filtered.1 = (bf16[8,16,32,128]{3,2,1,0:T(8,128)(2,1)}, bf16[4,16,32,128]{3,2,1,0:T(8,128)(2,1)}, bf16[4,16,32,128]{3,2,1,0:T(8,128)(2,1)}) custom-call(bf16[4,16,32,128]{3,2,1,0:T(8,128)(2,1)} %copy-done.6, bf16[4,16,32,128]{3,2,1,0:T(8,128)(2,1)} %copy-done.7, f32[8,16,32,128]{3,2,1,0:T(8,128)} %interior_filtered.1.refs_2_, ...), custom_call_target="tpu_custom_call" | custom-call | tf_op jit(solution)/shard_map/finish_filtered/pallas_call | solution.py:106
  43.2 1.9 %collective-permute-start.4 = (bf16[4096,128]{1,0:T(8,128)(2,1)}, bf16[4096,128]{1,0:T(8,128)(2,1)S(1)}, u32[]{:S(2)}, u32[]{:S(2)}) collective-permute-start(bf16[4096,128]{1,0:T(8,128)(2,1)} %bitcast.18), channel_id=1, source_target_pairs={{0,16},{16,0},{1,17},{17,1},{2,18},{18,2},{3,19},{19,3},{4,20},{20... | collective-permute-start | bytes 3145736 | tf_op jit(solution)/shard_map/ppermute | solution.py:164
  45.2 1.9 %collective-permute-start.10 = (bf16[4,16,32,128]{3,2,1,0:T(8,128)(2,1)}, bf16[4,16,32,128]{3,2,1,0:T(8,128)(2,1)S(1)}, u32[]{:S(2)}, u32[]{:S(2)}) collective-permute-start(bf16[4,16,32,128]{3,2,1,0:T(8,128)(2,1)} %get-tuple-element.13), channel_id=1, source_target_pairs={{0,1},{1,2},{2,3},{3,4},{4,5},{5,6},{6,7},{7,8},{8,9},{9,10},{10,1... | collective-permute-start | bytes 1572872 | tf_op jit(solution)/shard_map/ppermute | solution.py:117
  47.1 2.5 %collective-permute-start.11 = (bf16[4,16,32,128]{3,2,1,0:T(8,128)(2,1)}, bf16[4,16,32,128]{3,2,1,0:T(8,128)(2,1)S(1)}, u32[]{:S(2)}, u32[]{:S(2)}) collective-permute-start(bf16[4,16,32,128]{3,2,1,0:T(8,128)(2,1)} %get-tuple-element.14), channel_id=1, source_target_pairs={{1,0},{2,1},{3,2},{4,3},{5,4},{6,5},{7,6},{8,7},{9,8},{10,9},{11,1... | collective-permute-start | bytes 1572872 | tf_op jit(solution)/shard_map/ppermute | solution.py:117
  49.6 8.2 %interior_applied.1.refs_2_ = f32[8,16,32,128]{3,2,1,0:T(8,128)} custom-call(bf16[8,16,32,128]{3,2,1,0:T(8,128)(2,1)} %get-tuple-element.15.own_narrow, f32[8,16,32,128]{3,2,1,0:T(8,128)} %broadcast_in_dim.2.pot), custom_call_target="tpu_custom_call" | custom-call | tf_op jit(solution)/shard_map/interior_applied/pallas_call | solution.py:93
  58.3 0.8 copy-done.4
  59.1 0.8 copy-done.5
  59.8 4.2 %finish_applied.1 = bf16[8,16,32,128]{3,2,1,0:T(8,128)(2,1)} custom-call(bf16[4,16,32,128]{3,2,1,0:T(8,128)(2,1)} %copy-done.4, bf16[4,16,32,128]{3,2,1,0:T(8,128)(2,1)} %copy-done.5, f32[8,16,32,128]{3,2,1,0:T(8,128)} %interior_applied.1.refs_2_), custom_call_target="tpu_custom_call" | custom-call | tf_op jit(solution)/shard_map/finish_applied/pallas_call | solution.py:106
  64.0 1.8 %convolution_bitcast_fusion = f32[128,128]{0,1:T(8,128)S(1)} fusion(bf16[8,16,32,128]{3,2,1,0:T(8,128)(2,1)} %finish_applied.1, bf16[8,16,32,128]{3,2,1,0:T(8,128)(2,1)S(1)} %copy-done), kind=kOutput, calls=%fused_computation | convolution fusion | flops 134217728 | bytes 2162688 | tf_op jit(solution)/shard_map/cb,ck->bk/dot_general | solution.py:147
  65.8 2.0 %collective-permute-done.4 = bf16[4096,128]{1,0:T(8,128)(2,1)S(1)} collective-permute-done((bf16[4096,128]{1,0:T(8,128)(2,1)}, bf16[4096,128]{1,0:T(8,128)(2,1)S(1)}, u32[]{:S(2)}, u32[]{:S(2)}) %collective-permute-start.4) | collective-permute-done | bytes 1048608 | tf_op jit(solution)/shard_map/ppermute | solution.py:164
  68.4 1.6 %collective-permute-start.12 = (f32[64,256]{0,1:T(8,128)S(1)}, f32[64,256]{0,1:T(8,128)S(1)}, u32[]{:S(2)}, u32[]{:S(2)}) collective-permute-start(f32[64,256]{0,1:T(8,128)S(1)} %constant_dynamic-slice_fusion), channel_id=1, source_target_pairs={{0,1},{1,0},{2,3},{3,2},{4,5},{5,4},{6,7},{7,6},{8,9},{9,8},{10,11... | collective-permute-start | bytes 196616 | tf_op jit(solution)/shard_map/ppermute | solution.py:128
  72.1 1.2 %collective-permute-start.6 = (f32[64,256]{0,1:T(8,128)S(1)}, f32[64,256]{0,1:T(8,128)S(1)}, u32[]{:S(2)}, u32[]{:S(2)}) collective-permute-start(f32[64,256]{0,1:T(8,128)S(1)} %dynamic-slice_add_fusion.1), channel_id=1, source_target_pairs={{0,2},{1,3},{2,0},{3,1},{4,6},{5,7},{6,4},{7,5},{8,10},{9,11},{10,... | collective-permute-start | bytes 196616 | tf_op jit(solution)/shard_map/ppermute | solution.py:131
  73.4 4.1 %collective-permute-done.13 = f32[64,256]{0,1:T(8,128)S(1)} collective-permute-done((f32[64,256]{0,1:T(8,128)S(1)}, f32[64,256]{0,1:T(8,128)S(1)}, u32[]{:S(2)}, u32[]{:S(2)}) %collective-permute-start.13) | collective-permute-done | bytes 65568 | tf_op jit(solution)/shard_map/ppermute | solution.py:131
  77.6 2.1 %collective-permute-done.6 = f32[64,256]{0,1:T(8,128)S(1)} collective-permute-done((f32[64,256]{0,1:T(8,128)S(1)}, f32[64,256]{0,1:T(8,128)S(1)}, u32[]{:S(2)}, u32[]{:S(2)}) %collective-permute-start.6) | collective-permute-done | bytes 65568 | tf_op jit(solution)/shard_map/ppermute | solution.py:131
  79.8 3.3 %collective-permute-done.14 = f32[64,256]{0,1:T(8,128)S(1)} collective-permute-done((f32[64,256]{0,1:T(8,128)S(1)}, f32[64,256]{0,1:T(8,128)S(1)}, u32[]{:S(2)}, u32[]{:S(2)}) %collective-permute-start.14) | collective-permute-done | bytes 65568 | tf_op jit(solution)/shard_map/ppermute | solution.py:131
  83.2 0.8 collective-permute-start.15
  83.9 2.8 %collective-permute-done.7 = f32[64,256]{0,1:T(8,128)S(1)} collective-permute-done((f32[64,256]{0,1:T(8,128)S(1)}, f32[64,256]{0,1:T(8,128)S(1)}, u32[]{:S(2)}, u32[]{:S(2)}) %collective-permute-start.7) | collective-permute-done | bytes 65568 | tf_op jit(solution)/shard_map/ppermute | solution.py:131
  86.8 0.8 collective-permute-start.8
  87.6 6.7 %collective-permute-done.15 = f32[64,256]{0,1:T(8,128)S(1)} collective-permute-done((f32[64,256]{0,1:T(8,128)S(1)}, f32[64,256]{0,1:T(8,128)S(1)}, u32[]{:S(2)}, u32[]{:S(2)}) %collective-permute-start.15) | collective-permute-done | bytes 65568 | tf_op jit(solution)/shard_map/ppermute | solution.py:131
  94.4 1.4 %collective-permute-done.8 = f32[64,256]{0,1:T(8,128)S(1)} collective-permute-done((f32[64,256]{0,1:T(8,128)S(1)}, f32[64,256]{0,1:T(8,128)S(1)}, u32[]{:S(2)}, u32[]{:S(2)}) %collective-permute-start.8) | collective-permute-done | bytes 65568 | tf_op jit(solution)/shard_map/ppermute | solution.py:131
  (48 shorter events, 6.3 us)
Async XLA Ops:
  0.6 6.9 %copy-start.8 = (f32[8,16,32]{2,1,0:T(8,128)S(1)}, f32[8,16,32]{2,1,0:T(8,128)}, u32[]{:S(2)}) copy-start(f32[8,16,32]{2,1,0:T(8,128)} %param.3) | copy-start | bytes 49156
  2.0 15.7 %collective-permute-start = (bf16[4,16,32,128]{3,2,1,0:T(8,128)(2,1)S(1)}, bf16[4,16,32,128]{3,2,1,0:T(8,128)(2,1)S(1)}, u32[]{:S(2)}, u32[]{:S(2)}) collective-permute-start(bf16[4,16,32,128]{3,2,1,0:T(8,128)(2,1)S(1)} %get-tuple-element.19), channel_id=1, source_target_pairs={{0,1},{1,2},{2,3},{3,4},{4,5},{5,6},{6,7},{7,8},{8,9},{9,10},{10,1... | collective-permute-start | bytes 1572872 | tf_op jit(solution)/shard_map/ppermute | solution.py:117
  2.5 15.2 %collective-permute-start.1 = (bf16[4,16,32,128]{3,2,1,0:T(8,128)(2,1)S(1)}, bf16[4,16,32,128]{3,2,1,0:T(8,128)(2,1)S(1)}, u32[]{:S(2)}, u32[]{:S(2)}) collective-permute-start(bf16[4,16,32,128]{3,2,1,0:T(8,128)(2,1)S(1)} %get-tuple-element.18), channel_id=1, source_target_pairs={{1,0},{2,1},{3,2},{4,3},{5,4},{6,5},{7,6},{8,7},{9,8},{10,9},{11,1... | collective-permute-start | bytes 1572872 | tf_op jit(solution)/shard_map/ppermute | solution.py:117
  17.7 0.8 copy-start.2
  18.5 0.8 copy-start.3
  23.9 12.7 %collective-permute-start.2 = (bf16[4,16,32,128]{3,2,1,0:T(8,128)(2,1)}, bf16[4,16,32,128]{3,2,1,0:T(8,128)(2,1)S(1)}, u32[]{:S(2)}, u32[]{:S(2)}) collective-permute-start(bf16[4,16,32,128]{3,2,1,0:T(8,128)(2,1)} %get-tuple-element.9), channel_id=1, source_target_pairs={{0,1},{1,2},{2,3},{3,4},{4,5},{5,6},{6,7},{7,8},{8,9},{9,10},{10,1... | collective-permute-start | bytes 1572872 | tf_op jit(solution)/shard_map/ppermute | solution.py:117
  24.7 11.8 %collective-permute-start.3 = (bf16[4,16,32,128]{3,2,1,0:T(8,128)(2,1)}, bf16[4,16,32,128]{3,2,1,0:T(8,128)(2,1)S(1)}, u32[]{:S(2)}, u32[]{:S(2)}) collective-permute-start(bf16[4,16,32,128]{3,2,1,0:T(8,128)(2,1)} %get-tuple-element.10), channel_id=1, source_target_pairs={{1,0},{2,1},{3,2},{4,3},{5,4},{6,5},{7,6},{8,7},{9,8},{10,9},{11,1... | collective-permute-start | bytes 1572872 | tf_op jit(solution)/shard_map/ppermute | solution.py:117
  36.6 0.8 copy-start.6
  37.4 0.8 copy-start.7
  43.2 24.6 %collective-permute-start.4 = (bf16[4096,128]{1,0:T(8,128)(2,1)}, bf16[4096,128]{1,0:T(8,128)(2,1)S(1)}, u32[]{:S(2)}, u32[]{:S(2)}) collective-permute-start(bf16[4096,128]{1,0:T(8,128)(2,1)} %bitcast.18), channel_id=1, source_target_pairs={{0,16},{16,0},{1,17},{17,1},{2,18},{18,2},{3,19},{19,3},{4,20},{20... | collective-permute-start | bytes 3145736 | tf_op jit(solution)/shard_map/ppermute | solution.py:164
  45.2 13.1 %collective-permute-start.10 = (bf16[4,16,32,128]{3,2,1,0:T(8,128)(2,1)}, bf16[4,16,32,128]{3,2,1,0:T(8,128)(2,1)S(1)}, u32[]{:S(2)}, u32[]{:S(2)}) collective-permute-start(bf16[4,16,32,128]{3,2,1,0:T(8,128)(2,1)} %get-tuple-element.13), channel_id=1, source_target_pairs={{0,1},{1,2},{2,3},{3,4},{4,5},{5,6},{6,7},{7,8},{8,9},{9,10},{10,1... | collective-permute-start | bytes 1572872 | tf_op jit(solution)/shard_map/ppermute | solution.py:117
  47.1 11.2 %collective-permute-start.11 = (bf16[4,16,32,128]{3,2,1,0:T(8,128)(2,1)}, bf16[4,16,32,128]{3,2,1,0:T(8,128)(2,1)S(1)}, u32[]{:S(2)}, u32[]{:S(2)}) collective-permute-start(bf16[4,16,32,128]{3,2,1,0:T(8,128)(2,1)} %get-tuple-element.14), channel_id=1, source_target_pairs={{1,0},{2,1},{3,2},{4,3},{5,4},{6,5},{7,6},{8,7},{9,8},{10,9},{11,1... | collective-permute-start | bytes 1572872 | tf_op jit(solution)/shard_map/ppermute | solution.py:117
  49.6 8.2 %copy-start = (bf16[8,16,32,128]{3,2,1,0:T(8,128)(2,1)S(1)}, bf16[8,16,32,128]{3,2,1,0:T(8,128)(2,1)}, u32[]{:S(2)}) copy-start(bf16[8,16,32,128]{3,2,1,0:T(8,128)(2,1)} %get-tuple-element.15.own_narrow) | copy-start | bytes 3145732
  58.3 0.8 copy-start.4
  59.1 0.8 copy-start.5
  64.0 3.8 %copy-start.1 = (bf16[8,16,32,128]{3,2,1,0:T(8,128)(2,1)S(1)}, bf16[8,16,32,128]{3,2,1,0:T(8,128)(2,1)}, u32[]{:S(2)}) copy-start(bf16[8,16,32,128]{3,2,1,0:T(8,128)(2,1)} %finish_applied.1) | copy-start | bytes 3145732
  68.4 2.6 %collective-permute-start.12 = (f32[64,256]{0,1:T(8,128)S(1)}, f32[64,256]{0,1:T(8,128)S(1)}, u32[]{:S(2)}, u32[]{:S(2)}) collective-permute-start(f32[64,256]{0,1:T(8,128)S(1)} %constant_dynamic-slice_fusion), channel_id=1, source_target_pairs={{0,1},{1,0},{2,3},{3,2},{4,5},{5,4},{6,7},{7,6},{8,9},{9,8},{10,11... | collective-permute-start | bytes 196616 | tf_op jit(solution)/shard_map/ppermute | solution.py:128
  70.6 1.4 %collective-permute-start.5 = (f32[64,256]{0,1:T(8,128)S(1)}, f32[64,256]{0,1:T(8,128)S(1)}, u32[]{:S(2)}, u32[]{:S(2)}) collective-permute-start(f32[64,256]{0,1:T(8,128)S(1)} %constant_dynamic-slice_fusion.1), channel_id=1, source_target_pairs={{0,1},{1,0},{2,3},{3,2},{4,5},{5,4},{6,7},{7,6},{8,9},{9,8},{10,11... | collective-permute-start | bytes 196616 | tf_op jit(solution)/shard_map/ppermute | solution.py:128
  71.1 6.4 %collective-permute-start.13 = (f32[64,256]{0,1:T(8,128)S(1)}, f32[64,256]{0,1:T(8,128)S(1)}, u32[]{:S(2)}, u32[]{:S(2)}) collective-permute-start(f32[64,256]{0,1:T(8,128)S(1)} %dynamic-slice_add_fusion), channel_id=1, source_target_pairs={{0,2},{1,3},{2,0},{3,1},{4,6},{5,7},{6,4},{7,5},{8,10},{9,11},{10,... | collective-permute-start | bytes 196616 | tf_op jit(solution)/shard_map/ppermute | solution.py:131
  72.1 7.6 %collective-permute-start.6 = (f32[64,256]{0,1:T(8,128)S(1)}, f32[64,256]{0,1:T(8,128)S(1)}, u32[]{:S(2)}, u32[]{:S(2)}) collective-permute-start(f32[64,256]{0,1:T(8,128)S(1)} %dynamic-slice_add_fusion.1), channel_id=1, source_target_pairs={{0,2},{1,3},{2,0},{3,1},{4,6},{5,7},{6,4},{7,5},{8,10},{9,11},{10,... | collective-permute-start | bytes 196616 | tf_op jit(solution)/shard_map/ppermute | solution.py:131
  77.5 5.6 %collective-permute-start.14 = (f32[64,256]{0,1:T(8,128)S(1)}, f32[64,256]{0,1:T(8,128)S(1)}, u32[]{:S(2)}, u32[]{:S(2)}) collective-permute-start(f32[64,256]{0,1:T(8,128)S(1)} %add.45), channel_id=1, source_target_pairs={{0,4},{1,5},{2,6},{3,7},{4,0},{5,1},{6,2},{7,3},{8,12},{9,13},{10,... | collective-permute-start | bytes 196616 | tf_op jit(solution)/shard_map/ppermute | solution.py:131
  79.7 7.0 %collective-permute-start.7 = (f32[64,256]{0,1:T(8,128)S(1)}, f32[64,256]{0,1:T(8,128)S(1)}, u32[]{:S(2)}, u32[]{:S(2)}) collective-permute-start(f32[64,256]{0,1:T(8,128)S(1)} %add.41), channel_id=1, source_target_pairs={{0,4},{1,5},{2,6},{3,7},{4,0},{5,1},{6,2},{7,3},{8,12},{9,13},{10,... | collective-permute-start | bytes 196616 | tf_op jit(solution)/shard_map/ppermute | solution.py:131
  83.2 11.2 %collective-permute-start.15 = (f32[64,256]{0,1:T(8,128)S(1)}, f32[64,256]{0,1:T(8,128)S(1)}, u32[]{:S(2)}, u32[]{:S(2)}) collective-permute-start(f32[64,256]{0,1:T(8,128)S(1)} %add.46), channel_id=1, source_target_pairs={{0,8},{1,9},{2,10},{3,11},{4,12},{5,13},{6,14},{7,15},{8,0},{9,1},... | collective-permute-start | bytes 196616 | tf_op jit(solution)/shard_map/ppermute | solution.py:131
  86.8 9.1 %collective-permute-start.8 = (f32[64,256]{0,1:T(8,128)S(1)}, f32[64,256]{0,1:T(8,128)S(1)}, u32[]{:S(2)}, u32[]{:S(2)}) collective-permute-start(f32[64,256]{0,1:T(8,128)S(1)} %add.42), channel_id=1, source_target_pairs={{0,8},{1,9},{2,10},{3,11},{4,12},{5,13},{6,14},{7,15},{8,0},{9,1},... | collective-permute-start | bytes 196616 | tf_op jit(solution)/shard_map/ppermute | solution.py:131
  94.3 1.6 %collective-permute-start.16 = (f32[64,256]{0,1:T(8,128)S(1)}, f32[64,256]{0,1:T(8,128)S(1)}, u32[]{:S(2)}, u32[]{:S(2)}) collective-permute-start(f32[64,256]{0,1:T(8,128)S(1)} %add.47), channel_id=1, source_target_pairs={{0,1},{1,0},{2,3},{3,2},{4,5},{5,4},{6,7},{7,6},{8,9},{9,8},{10,11... | collective-permute-start | bytes 196616 | tf_op jit(solution)/shard_map/ppermute | solution.py:133
  95.8 1.4 %collective-permute-start.9 = (f32[64,256]{0,1:T(8,128)S(1)}, f32[64,256]{0,1:T(8,128)S(1)}, u32[]{:S(2)}, u32[]{:S(2)}) collective-permute-start(f32[64,256]{0,1:T(8,128)S(1)} %add.43), channel_id=1, source_target_pairs={{0,1},{1,0},{2,3},{3,2},{4,5},{5,4},{6,7},{7,6},{8,9},{9,8},{10,11... | collective-permute-start | bytes 196616 | tf_op jit(solution)/shard_map/ppermute | solution.py:133

commit v9 on v8

--- a/solution.py
+++ b/solution.py
@@ -126,10 +126,20 @@
     keep = lax.dynamic_slice_in_dim(values, upper * half, half, axis=0)
     send = lax.dynamic_slice_in_dim(values, (1 - upper) * half, half, axis=0)
     values = keep + lax.ppermute(send, axis, pairs_of(1))
+    bits = []
     bit = 2
     while bit < count:
-        values = values + lax.ppermute(values, axis, pairs_of(bit))
+        bits.append(bit)
         bit *= 2
+    while bits:
+        if len(bits) == 1:
+            values = values + lax.ppermute(values, axis, pairs_of(bits.pop(0)))
+            continue
+        a, b = bits.pop(0), bits.pop(0)
+        near = lax.ppermute(values, axis, pairs_of(a))
+        far = lax.ppermute(values, axis, pairs_of(b))
+        across = lax.ppermute(values, axis, pairs_of(a | b))
+        values = (values + near) + (far + across)
     other = lax.ppermute(values, axis, pairs_of(1))
     return jnp.where(
         upper == 0,

time: 98.4 us -> 99.1 us (level)
  starting transfers between devices: 21.4 us -> 27.2 us
  waiting for transfers between devices: 23.9 us -> 18.9 us
    ppermute x6 -> x8, starting transfers between devices: 3.21 us -> 9.01 us  [the longest x2 3.16 us: butterfly_sum(): far = lax.ppermute(values, axis, pairs_of(b))]
    ppermute x6 -> x8, waiting for transfers between devices: 20.6 us -> 16.2 us  [the longest x2 8.95 us: butterfly_sum(): across = lax.ppermute(values, axis, pairs_of(a | b))]
  transfers between devices with their start and end apart: 17 -> 19, of which waited for: 10 -> 7; matrix products, arithmetic and copies ran while one was open for 6% -> 6% of each run, Pallas kernels for 29% -> 29%
where the time goes in v9:
time: 99.1 us; the launch traced here: 98.9 us
  Pallas kernels  38.4 us (39%)
  starting transfers between devices  27.2 us (27%)
  waiting for transfers between devices  18.9 us (19%)
  local copies, waits for them, and re-layouts  9.8 us (10%)
  matrix products  3.21 us (3%)
    pallas_call x3, Pallas kernels, stencil_stage(): pl.pallas_call(interior_kernel(stage, planes, ny, nz), out_shape=jax.Shap...  24.5 us
    pallas_call x3, Pallas kernels, stencil_stage(): pl.pallas_call(finish_kernel(stage, planes, ny), out_shape=tuple(shapes),...  13.8 us
    ppermute x3, starting transfers between devices, exchange(): lax.ppermute(sends[1], axis, backward)  11.1 us
    ppermute x2, waiting for transfers between devices, butterfly_sum(): across = lax.ppermute(values, axis, pairs_of(a | b))  8.95 us
    ppermute x2, waiting for transfers between devices, butterfly_sum(): values = values + lax.ppermute(values, axis, pairs_of(bits.pop(0)))  6.96 us
    unnamed x20, local copies, waits for them, and re-layouts  6.32 us
    ppermute x3, starting transfers between devices, exchange(): lax.ppermute(sends[0], axis, forward)  3.28 us
    dot_general x4, matrix products, shards(): jnp.einsum('cb,ck->bk', rows, cols, preferred_element_type=jnp.float32)  3.21 us
  transfers between devices with their start and end apart: 19, of which 7 were waited for; matrix products, arithmetic and copies ran while one was open for 6% of the time, Pallas kernels for 29%

profile of v9, /device:TPU:0, one launch (start us, length us, event | category | flops | bytes accessed | tf_op | source)
XLA Modules:
  0.0 98.9 jit_solution(14764662494426258247)
XLA Ops:
  0.6 1.3 %fusion.2 = (bf16[4,16,32,128]{3,2,1,0:T(8,128)(2,1)S(1)}, bf16[4,16,32,128]{3,2,1,0:T(8,128)(2,1)S(1)}) fusion(bf16[8,16,32,128]{3,2,1,0:T(8,128)(2,1)} %refs_3_.1), kind=kLoop, calls=%fused_computation.14 | loop fusion | bytes 2097152 | tf_op jit(solution)/shard_map/slice | solution.py:167
  2.5 5.0 %collective-permute-start.1 = (bf16[4,16,32,128]{3,2,1,0:T(8,128)(2,1)S(1)}, bf16[4,16,32,128]{3,2,1,0:T(8,128)(2,1)S(1)}, u32[]{:S(2)}, u32[]{:S(2)}) collective-permute-start(bf16[4,16,32,128]{3,2,1,0:T(8,128)(2,1)S(1)} %get-tuple-element.18), channel_id=1, source_target_pairs={{1,0},{2,1},{3,2},{4,3},{5,4},{6,5},{7,6},{8,7},{9,8},{10,9},{11,1... | collective-permute-start | bytes 1572872 | tf_op jit(solution)/shard_map/ppermute | solution.py:117
  7.5 2.0 %broadcast_in_dim.2.pot = f32[8,16,32,128]{3,2,1,0:T(8,128)} broadcast(f32[8,16,32]{2,1,0:T(8,128)S(1)} %copy-done.8), dimensions={0,1,2} | broadcast | bytes 2113536 | tf_op jit(solution)/shard_map/broadcast_in_dim | solution.py:153
  9.5 8.2 %interior_first.1.refs_2_ = f32[8,16,32,128]{3,2,1,0:T(8,128)} custom-call(bf16[8,16,32,128]{3,2,1,0:T(8,128)(2,1)} %refs_3_.1, f32[8,16,32,128]{3,2,1,0:T(8,128)} %broadcast_in_dim.2.pot), custom_call_target="tpu_custom_call" | custom-call | tf_op jit(solution)/shard_map/interior_first/pallas_call | solution.py:93
  17.7 0.8 copy-done.2
  18.5 0.8 copy-done.3
  19.3 4.6 %finish_first.1 = (bf16[8,16,32,128]{3,2,1,0:T(8,128)(2,1)}, bf16[4,16,32,128]{3,2,1,0:T(8,128)(2,1)}, bf16[4,16,32,128]{3,2,1,0:T(8,128)(2,1)}) custom-call(bf16[4,16,32,128]{3,2,1,0:T(8,128)(2,1)} %copy-done.2, bf16[4,16,32,128]{3,2,1,0:T(8,128)(2,1)} %copy-done.3, f32[8,16,32,128]{3,2,1,0:T(8,128)} %interior_first.1.refs_2_), custom_call_target="tpu_custom_call" | custom-call | tf_op jit(solution)/shard_map/finish_first/pallas_call | solution.py:106
  23.9 0.8 collective-permute-start.2
  24.7 3.6 %collective-permute-start.3 = (bf16[4,16,32,128]{3,2,1,0:T(8,128)(2,1)}, bf16[4,16,32,128]{3,2,1,0:T(8,128)(2,1)S(1)}, u32[]{:S(2)}, u32[]{:S(2)}) collective-permute-start(bf16[4,16,32,128]{3,2,1,0:T(8,128)(2,1)} %get-tuple-element.10), channel_id=1, source_target_pairs={{1,0},{2,1},{3,2},{4,3},{5,4},{6,5},{7,6},{8,7},{9,8},{10,9},{11,1... | collective-permute-start | bytes 1572872 | tf_op jit(solution)/shard_map/ppermute | solution.py:117
  28.3 8.2 %interior_filtered.1.refs_2_ = f32[8,16,32,128]{3,2,1,0:T(8,128)} custom-call(bf16[8,16,32,128]{3,2,1,0:T(8,128)(2,1)} %get-tuple-element.11.own_narrow, f32[8,16,32,128]{3,2,1,0:T(8,128)} %broadcast_in_dim.2.pot), custom_call_target="tpu_custom_call" | custom-call | tf_op jit(solution)/shard_map/interior_filtered/pallas_call | solution.py:93
  36.5 0.8 copy-done.6
  37.3 0.8 copy-done.7
  38.1 5.1 %finish_filtered.1 = (bf16[8,16,32,128]{3,2,1,0:T(8,128)(2,1)}, bf16[4,16,32,128]{3,2,1,0:T(8,128)(2,1)}, bf16[4,16,32,128]{3,2,1,0:T(8,128)(2,1)}) custom-call(bf16[4,16,32,128]{3,2,1,0:T(8,128)(2,1)} %copy-done.6, bf16[4,16,32,128]{3,2,1,0:T(8,128)(2,1)} %copy-done.7, f32[8,16,32,128]{3,2,1,0:T(8,128)} %interior_filtered.1.refs_2_, ...), custom_call_target="tpu_custom_call" | custom-call | tf_op jit(solution)/shard_map/finish_filtered/pallas_call | solution.py:106
  43.2 1.9 %collective-permute-start.4 = (bf16[4096,128]{1,0:T(8,128)(2,1)}, bf16[4096,128]{1,0:T(8,128)(2,1)S(1)}, u32[]{:S(2)}, u32[]{:S(2)}) collective-permute-start(bf16[4096,128]{1,0:T(8,128)(2,1)} %bitcast.18), channel_id=1, source_target_pairs={{0,16},{16,0},{1,17},{17,1},{2,18},{18,2},{3,19},{19,3},{4,20},{20... | collective-permute-start | bytes 3145736 | tf_op jit(solution)/shard_map/ppermute | solution.py:174
  45.1 1.9 %collective-permute-start.11 = (bf16[4,16,32,128]{3,2,1,0:T(8,128)(2,1)}, bf16[4,16,32,128]{3,2,1,0:T(8,128)(2,1)S(1)}, u32[]{:S(2)}, u32[]{:S(2)}) collective-permute-start(bf16[4,16,32,128]{3,2,1,0:T(8,128)(2,1)} %get-tuple-element.13), channel_id=1, source_target_pairs={{0,1},{1,2},{2,3},{3,4},{4,5},{5,6},{6,7},{7,8},{8,9},{9,10},{10,1... | collective-permute-start | bytes 1572872 | tf_op jit(solution)/shard_map/ppermute | solution.py:117
  47.1 2.5 %collective-permute-start.12 = (bf16[4,16,32,128]{3,2,1,0:T(8,128)(2,1)}, bf16[4,16,32,128]{3,2,1,0:T(8,128)(2,1)S(1)}, u32[]{:S(2)}, u32[]{:S(2)}) collective-permute-start(bf16[4,16,32,128]{3,2,1,0:T(8,128)(2,1)} %get-tuple-element.14), channel_id=1, source_target_pairs={{1,0},{2,1},{3,2},{4,3},{5,4},{6,5},{7,6},{8,7},{9,8},{10,9},{11,1... | collective-permute-start | bytes 1572872 | tf_op jit(solution)/shard_map/ppermute | solution.py:117
  49.6 8.1 %interior_applied.1.refs_2_ = f32[8,16,32,128]{3,2,1,0:T(8,128)} custom-call(bf16[8,16,32,128]{3,2,1,0:T(8,128)(2,1)} %get-tuple-element.15.own_narrow, f32[8,16,32,128]{3,2,1,0:T(8,128)} %broadcast_in_dim.2.pot), custom_call_target="tpu_custom_call" | custom-call | tf_op jit(solution)/shard_map/interior_applied/pallas_call | solution.py:93
  58.2 0.8 copy-done.4
  59.0 0.8 copy-done.5
  59.8 4.2 %finish_applied.1 = bf16[8,16,32,128]{3,2,1,0:T(8,128)(2,1)} custom-call(bf16[4,16,32,128]{3,2,1,0:T(8,128)(2,1)} %copy-done.4, bf16[4,16,32,128]{3,2,1,0:T(8,128)(2,1)} %copy-done.5, f32[8,16,32,128]{3,2,1,0:T(8,128)} %interior_applied.1.refs_2_), custom_call_target="tpu_custom_call" | custom-call | tf_op jit(solution)/shard_map/finish_applied/pallas_call | solution.py:106
  64.0 1.8 %convolution_bitcast_fusion = f32[128,128]{0,1:T(8,128)S(1)} fusion(bf16[8,16,32,128]{3,2,1,0:T(8,128)(2,1)} %finish_applied.1, bf16[8,16,32,128]{3,2,1,0:T(8,128)(2,1)S(1)} %copy-done), kind=kOutput, calls=%fused_computation | convolution fusion | flops 134217728 | bytes 2162688 | tf_op jit(solution)/shard_map/cb,ck->bk/dot_general | solution.py:157
  65.8 1.9 %collective-permute-done.4 = bf16[4096,128]{1,0:T(8,128)(2,1)S(1)} collective-permute-done((bf16[4096,128]{1,0:T(8,128)(2,1)}, bf16[4096,128]{1,0:T(8,128)(2,1)S(1)}, u32[]{:S(2)}, u32[]{:S(2)}) %collective-permute-start.4) | collective-permute-done | bytes 1048608 | tf_op jit(solution)/shard_map/ppermute | solution.py:174
  68.3 1.6 %collective-permute-start.13 = (f32[64,256]{0,1:T(8,128)S(1)}, f32[64,256]{0,1:T(8,128)S(1)}, u32[]{:S(2)}, u32[]{:S(2)}) collective-permute-start(f32[64,256]{0,1:T(8,128)S(1)} %constant_dynamic-slice_fusion), channel_id=1, source_target_pairs={{0,1},{1,0},{2,3},{3,2},{4,5},{5,4},{6,7},{7,6},{8,9},{9,8},{10,11... | collective-permute-start | bytes 196616 | tf_op jit(solution)/shard_map/ppermute | solution.py:128
  71.3 1.6 %collective-permute-start.15 = (f32[64,256]{0,1:T(8,128)S(1)}, f32[64,256]{0,1:T(8,128)S(1)}, u32[]{:S(2)}, u32[]{:S(2)}) collective-permute-start(f32[64,256]{0,1:T(8,128)S(1)} %dynamic-slice_add_fusion), channel_id=1, source_target_pairs={{0,4},{1,5},{2,6},{3,7},{4,0},{5,1},{6,2},{7,3},{8,12},{9,13},{10,... | collective-permute-start | bytes 196616 | tf_op jit(solution)/shard_map/ppermute | solution.py:140
  72.9 1.7 %collective-permute-start.16 = (f32[64,256]{0,1:T(8,128)S(1)}, f32[64,256]{0,1:T(8,128)S(1)}, u32[]{:S(2)}, u32[]{:S(2)}) collective-permute-start(f32[64,256]{0,1:T(8,128)S(1)} %dynamic-slice_add_fusion), channel_id=1, source_target_pairs={{0,6},{1,7},{2,4},{3,5},{4,2},{5,3},{6,0},{7,1},{8,14},{9,15},{10,... | collective-permute-start | bytes 196616 | tf_op jit(solution)/shard_map/ppermute | solution.py:141
  75.0 1.6 %collective-permute-start.7 = (f32[64,256]{0,1:T(8,128)S(1)}, f32[64,256]{0,1:T(8,128)S(1)}, u32[]{:S(2)}, u32[]{:S(2)}) collective-permute-start(f32[64,256]{0,1:T(8,128)S(1)} %dynamic-slice_add_fusion.1), channel_id=1, source_target_pairs={{0,4},{1,5},{2,6},{3,7},{4,0},{5,1},{6,2},{7,3},{8,12},{9,13},{10,... | collective-permute-start | bytes 196616 | tf_op jit(solution)/shard_map/ppermute | solution.py:140
  76.9 1.4 %collective-permute-start.8 = (f32[64,256]{0,1:T(8,128)S(1)}, f32[64,256]{0,1:T(8,128)S(1)}, u32[]{:S(2)}, u32[]{:S(2)}) collective-permute-start(f32[64,256]{0,1:T(8,128)S(1)} %dynamic-slice_add_fusion.1), channel_id=1, source_target_pairs={{0,6},{1,7},{2,4},{3,5},{4,2},{5,3},{6,0},{7,1},{8,14},{9,15},{10,... | collective-permute-start | bytes 196616 | tf_op jit(solution)/shard_map/ppermute | solution.py:141
  78.3 3.5 %collective-permute-done.16 = f32[64,256]{0,1:T(8,128)S(1)} collective-permute-done((f32[64,256]{0,1:T(8,128)S(1)}, f32[64,256]{0,1:T(8,128)S(1)}, u32[]{:S(2)}, u32[]{:S(2)}) %collective-permute-start.16) | collective-permute-done | bytes 65568 | tf_op jit(solution)/shard_map/ppermute | solution.py:141
  81.8 2.1 %collective-permute-start.17 = (f32[64,256]{0,1:T(8,128)S(1)}, f32[64,256]{0,1:T(8,128)S(1)}, u32[]{:S(2)}, u32[]{:S(2)}) collective-permute-start(f32[64,256]{0,1:T(8,128)S(1)} %add_add_fusion), channel_id=1, source_target_pairs={{0,8},{1,9},{2,10},{3,11},{4,12},{5,13},{6,14},{7,15},{8,0},{9,1},... | collective-permute-start | bytes 196616 | tf_op jit(solution)/shard_map/ppermute | solution.py:136
  83.9 5.4 %collective-permute-done.8 = f32[64,256]{0,1:T(8,128)S(1)} collective-permute-done((f32[64,256]{0,1:T(8,128)S(1)}, f32[64,256]{0,1:T(8,128)S(1)}, u32[]{:S(2)}, u32[]{:S(2)}) %collective-permute-start.8) | collective-permute-done | bytes 65568 | tf_op jit(solution)/shard_map/ppermute | solution.py:141
  89.6 7.0 %collective-permute-done.9 = f32[64,256]{0,1:T(8,128)S(1)} collective-permute-done((f32[64,256]{0,1:T(8,128)S(1)}, f32[64,256]{0,1:T(8,128)S(1)}, u32[]{:S(2)}, u32[]{:S(2)}) %collective-permute-start.9) | collective-permute-done | bytes 65568 | tf_op jit(solution)/shard_map/ppermute | solution.py:136
  98.1 0.8 copy.5
  (50 shorter events, 5.4 us)
Async XLA Ops:
  0.6 6.9 %copy-start.8 = (f32[8,16,32]{2,1,0:T(8,128)S(1)}, f32[8,16,32]{2,1,0:T(8,128)}, u32[]{:S(2)}) copy-start(f32[8,16,32]{2,1,0:T(8,128)} %param.3) | copy-start | bytes 49156
  2.0 15.7 %collective-permute-start = (bf16[4,16,32,128]{3,2,1,0:T(8,128)(2,1)S(1)}, bf16[4,16,32,128]{3,2,1,0:T(8,128)(2,1)S(1)}, u32[]{:S(2)}, u32[]{:S(2)}) collective-permute-start(bf16[4,16,32,128]{3,2,1,0:T(8,128)(2,1)S(1)} %get-tuple-element.19), channel_id=1, source_target_pairs={{0,1},{1,2},{2,3},{3,4},{4,5},{5,6},{6,7},{7,8},{8,9},{9,10},{10,1... | collective-permute-start | bytes 1572872 | tf_op jit(solution)/shard_map/ppermute | solution.py:117
  2.5 15.2 %collective-permute-start.1 = (bf16[4,16,32,128]{3,2,1,0:T(8,128)(2,1)S(1)}, bf16[4,16,32,128]{3,2,1,0:T(8,128)(2,1)S(1)}, u32[]{:S(2)}, u32[]{:S(2)}) collective-permute-start(bf16[4,16,32,128]{3,2,1,0:T(8,128)(2,1)S(1)} %get-tuple-element.18), channel_id=1, source_target_pairs={{1,0},{2,1},{3,2},{4,3},{5,4},{6,5},{7,6},{8,7},{9,8},{10,9},{11,1... | collective-permute-start | bytes 1572872 | tf_op jit(solution)/shard_map/ppermute | solution.py:117
  17.7 0.8 copy-start.2
  18.5 0.8 copy-start.3
  23.9 12.6 %collective-permute-start.2 = (bf16[4,16,32,128]{3,2,1,0:T(8,128)(2,1)}, bf16[4,16,32,128]{3,2,1,0:T(8,128)(2,1)S(1)}, u32[]{:S(2)}, u32[]{:S(2)}) collective-permute-start(bf16[4,16,32,128]{3,2,1,0:T(8,128)(2,1)} %get-tuple-element.9), channel_id=1, source_target_pairs={{0,1},{1,2},{2,3},{3,4},{4,5},{5,6},{6,7},{7,8},{8,9},{9,10},{10,1... | collective-permute-start | bytes 1572872 | tf_op jit(solution)/shard_map/ppermute | solution.py:117
  24.7 11.8 %collective-permute-start.3 = (bf16[4,16,32,128]{3,2,1,0:T(8,128)(2,1)}, bf16[4,16,32,128]{3,2,1,0:T(8,128)(2,1)S(1)}, u32[]{:S(2)}, u32[]{:S(2)}) collective-permute-start(bf16[4,16,32,128]{3,2,1,0:T(8,128)(2,1)} %get-tuple-element.10), channel_id=1, source_target_pairs={{1,0},{2,1},{3,2},{4,3},{5,4},{6,5},{7,6},{8,7},{9,8},{10,9},{11,1... | collective-permute-start | bytes 1572872 | tf_op jit(solution)/shard_map/ppermute | solution.py:117
  36.5 0.8 copy-start.6
  37.3 0.8 copy-start.7
  43.2 24.5 %collective-permute-start.4 = (bf16[4096,128]{1,0:T(8,128)(2,1)}, bf16[4096,128]{1,0:T(8,128)(2,1)S(1)}, u32[]{:S(2)}, u32[]{:S(2)}) collective-permute-start(bf16[4096,128]{1,0:T(8,128)(2,1)} %bitcast.18), channel_id=1, source_target_pairs={{0,16},{16,0},{1,17},{17,1},{2,18},{18,2},{3,19},{19,3},{4,20},{20... | collective-permute-start | bytes 3145736 | tf_op jit(solution)/shard_map/ppermute | solution.py:174
  45.1 13.1 %collective-permute-start.11 = (bf16[4,16,32,128]{3,2,1,0:T(8,128)(2,1)}, bf16[4,16,32,128]{3,2,1,0:T(8,128)(2,1)S(1)}, u32[]{:S(2)}, u32[]{:S(2)}) collective-permute-start(bf16[4,16,32,128]{3,2,1,0:T(8,128)(2,1)} %get-tuple-element.13), channel_id=1, source_target_pairs={{0,1},{1,2},{2,3},{3,4},{4,5},{5,6},{6,7},{7,8},{8,9},{9,10},{10,1... | collective-permute-start | bytes 1572872 | tf_op jit(solution)/shard_map/ppermute | solution.py:117
  47.1 11.2 %collective-permute-start.12 = (bf16[4,16,32,128]{3,2,1,0:T(8,128)(2,1)}, bf16[4,16,32,128]{3,2,1,0:T(8,128)(2,1)S(1)}, u32[]{:S(2)}, u32[]{:S(2)}) collective-permute-start(bf16[4,16,32,128]{3,2,1,0:T(8,128)(2,1)} %get-tuple-element.14), channel_id=1, source_target_pairs={{1,0},{2,1},{3,2},{4,3},{5,4},{6,5},{7,6},{8,7},{9,8},{10,9},{11,1... | collective-permute-start | bytes 1572872 | tf_op jit(solution)/shard_map/ppermute | solution.py:117
  49.6 8.1 %copy-start = (bf16[8,16,32,128]{3,2,1,0:T(8,128)(2,1)S(1)}, bf16[8,16,32,128]{3,2,1,0:T(8,128)(2,1)}, u32[]{:S(2)}) copy-start(bf16[8,16,32,128]{3,2,1,0:T(8,128)(2,1)} %get-tuple-element.15.own_narrow) | copy-start | bytes 3145732
  58.2 0.8 copy-start.4
  59.0 0.8 copy-start.5
  64.0 3.7 %copy-start.1 = (bf16[8,16,32,128]{3,2,1,0:T(8,128)(2,1)S(1)}, bf16[8,16,32,128]{3,2,1,0:T(8,128)(2,1)}, u32[]{:S(2)}) copy-start(bf16[8,16,32,128]{3,2,1,0:T(8,128)(2,1)} %finish_applied.1) | copy-start | bytes 3145732
  68.3 2.6 %collective-permute-start.13 = (f32[64,256]{0,1:T(8,128)S(1)}, f32[64,256]{0,1:T(8,128)S(1)}, u32[]{:S(2)}, u32[]{:S(2)}) collective-permute-start(f32[64,256]{0,1:T(8,128)S(1)} %constant_dynamic-slice_fusion), channel_id=1, source_target_pairs={{0,1},{1,0},{2,3},{3,2},{4,5},{5,4},{6,7},{7,6},{8,9},{9,8},{10,11... | collective-permute-start | bytes 196616 | tf_op jit(solution)/shard_map/ppermute | solution.py:128
  70.5 4.1 %collective-permute-start.5 = (f32[64,256]{0,1:T(8,128)S(1)}, f32[64,256]{0,1:T(8,128)S(1)}, u32[]{:S(2)}, u32[]{:S(2)}) collective-permute-start(f32[64,256]{0,1:T(8,128)S(1)} %constant_dynamic-slice_fusion.1), channel_id=1, source_target_pairs={{0,1},{1,0},{2,3},{3,2},{4,5},{5,4},{6,7},{7,6},{8,9},{9,8},{10,11... | collective-permute-start | bytes 196616 | tf_op jit(solution)/shard_map/ppermute | solution.py:128
  71.0 5.8 %collective-permute-start.14 = (f32[64,256]{0,1:T(8,128)S(1)}, f32[64,256]{0,1:T(8,128)S(1)}, u32[]{:S(2)}, u32[]{:S(2)}) collective-permute-start(f32[64,256]{0,1:T(8,128)S(1)} %dynamic-slice_add_fusion), channel_id=1, source_target_pairs={{0,2},{1,3},{2,0},{3,1},{4,6},{5,7},{6,4},{7,5},{8,10},{9,11},{10,... | collective-permute-start | bytes 196616 | tf_op jit(solution)/shard_map/ppermute | solution.py:139
  71.3 7.0 %collective-permute-start.15 = (f32[64,256]{0,1:T(8,128)S(1)}, f32[64,256]{0,1:T(8,128)S(1)}, u32[]{:S(2)}, u32[]{:S(2)}) collective-permute-start(f32[64,256]{0,1:T(8,128)S(1)} %dynamic-slice_add_fusion), channel_id=1, source_target_pairs={{0,4},{1,5},{2,6},{3,7},{4,0},{5,1},{6,2},{7,3},{8,12},{9,13},{10,... | collective-permute-start | bytes 196616 | tf_op jit(solution)/shard_map/ppermute | solution.py:140
  72.9 8.9 %collective-permute-start.16 = (f32[64,256]{0,1:T(8,128)S(1)}, f32[64,256]{0,1:T(8,128)S(1)}, u32[]{:S(2)}, u32[]{:S(2)}) collective-permute-start(f32[64,256]{0,1:T(8,128)S(1)} %dynamic-slice_add_fusion), channel_id=1, source_target_pairs={{0,6},{1,7},{2,4},{3,5},{4,2},{5,3},{6,0},{7,1},{8,14},{9,15},{10,... | collective-permute-start | bytes 196616 | tf_op jit(solution)/shard_map/ppermute | solution.py:141
  74.7 9.2 %collective-permute-start.6 = (f32[64,256]{0,1:T(8,128)S(1)}, f32[64,256]{0,1:T(8,128)S(1)}, u32[]{:S(2)}, u32[]{:S(2)}) collective-permute-start(f32[64,256]{0,1:T(8,128)S(1)} %dynamic-slice_add_fusion.1), channel_id=1, source_target_pairs={{0,2},{1,3},{2,0},{3,1},{4,6},{5,7},{6,4},{7,5},{8,10},{9,11},{10,... | collective-permute-start | bytes 196616 | tf_op jit(solution)/shard_map/ppermute | solution.py:139
  75.0 8.9 %collective-permute-start.7 = (f32[64,256]{0,1:T(8,128)S(1)}, f32[64,256]{0,1:T(8,128)S(1)}, u32[]{:S(2)}, u32[]{:S(2)}) collective-permute-start(f32[64,256]{0,1:T(8,128)S(1)} %dynamic-slice_add_fusion.1), channel_id=1, source_target_pairs={{0,4},{1,5},{2,6},{3,7},{4,0},{5,1},{6,2},{7,3},{8,12},{9,13},{10,... | collective-permute-start | bytes 196616 | tf_op jit(solution)/shard_map/ppermute | solution.py:140
  76.9 12.5 %collective-permute-start.8 = (f32[64,256]{0,1:T(8,128)S(1)}, f32[64,256]{0,1:T(8,128)S(1)}, u32[]{:S(2)}, u32[]{:S(2)}) collective-permute-start(f32[64,256]{0,1:T(8,128)S(1)} %dynamic-slice_add_fusion.1), channel_id=1, source_target_pairs={{0,6},{1,7},{2,4},{3,5},{4,2},{5,3},{6,0},{7,1},{8,14},{9,15},{10,... | collective-permute-start | bytes 196616 | tf_op jit(solution)/shard_map/ppermute | solution.py:141
  81.8 7.7 %collective-permute-start.17 = (f32[64,256]{0,1:T(8,128)S(1)}, f32[64,256]{0,1:T(8,128)S(1)}, u32[]{:S(2)}, u32[]{:S(2)}) collective-permute-start(f32[64,256]{0,1:T(8,128)S(1)} %add_add_fusion), channel_id=1, source_target_pairs={{0,8},{1,9},{2,10},{3,11},{4,12},{5,13},{6,14},{7,15},{8,0},{9,1},... | collective-permute-start | bytes 196616 | tf_op jit(solution)/shard_map/ppermute | solution.py:136
  89.4 7.2 %collective-permute-start.9 = (f32[64,256]{0,1:T(8,128)S(1)}, f32[64,256]{0,1:T(8,128)S(1)}, u32[]{:S(2)}, u32[]{:S(2)}) collective-permute-start(f32[64,256]{0,1:T(8,128)S(1)} %add_add_fusion.1), channel_id=1, source_target_pairs={{0,8},{1,9},{2,10},{3,11},{4,12},{5,13},{6,14},{7,15},{8,0},{9,1},... | collective-permute-start | bytes 196616 | tf_op jit(solution)/shard_map/ppermute | solution.py:136
  89.5 7.1 %collective-permute-start.18 = (f32[64,256]{0,1:T(8,128)S(1)}, f32[64,256]{0,1:T(8,128)S(1)}, u32[]{:S(2)}, u32[]{:S(2)}) collective-permute-start(f32[64,256]{0,1:T(8,128)S(1)} %add.55), channel_id=1, source_target_pairs={{0,1},{1,0},{2,3},{3,2},{4,5},{5,4},{6,7},{7,6},{8,9},{9,8},{10,11... | collective-permute-start | bytes 196616 | tf_op jit(solution)/shard_map/ppermute | solution.py:143
  96.6 1.4 %collective-permute-start.10 = (f32[64,256]{0,1:T(8,128)S(1)}, f32[64,256]{0,1:T(8,128)S(1)}, u32[]{:S(2)}, u32[]{:S(2)}) collective-permute-start(f32[64,256]{0,1:T(8,128)S(1)} %add.50), channel_id=1, source_target_pairs={{0,1},{1,0},{2,3},{3,2},{4,5},{5,4},{6,7},{7,6},{8,9},{9,8},{10,11... | collective-permute-start | bytes 196616 | tf_op jit(solution)/shard_map/ppermute | solution.py:143

commit v10 on v7

--- a/solution.py
+++ b/solution.py
@@ -15,96 +15,133 @@
 memory_factor = -1.0 / 7.0
 
 
+def plane_blocks(planes):
+    return (planes // RADIUS, RADIUS) if planes % RADIUS == 0 else (1, planes)
+
+
 def interior_kernel(stage, planes, ny, nz):
     shift = 0.0 if stage == "applied" else spectrum_centre
+    blocks, depth = plane_blocks(planes)
 
     def kernel(own_narrow, pot, out, own):
-        for x in range(planes):
-            own[x] = own_narrow[x].astype(jnp.float32)
-        for x in range(planes):
-            def row(y, carry, x=x):
-                centre = own[x, y]
-                summed = (3.0 * stencil_weights[0]) * centre
-                for k in range(1, RADIUS + 1):
-                    beside = own[x, (y + k) % ny] + own[x, (y + ny - k) % ny]
-                    beside = beside + (
-                        pltpu.roll(centre, k, 0) + pltpu.roll(centre, nz - k, 0)
-                    )
-                    if x + k < planes:
-                        beside = beside + own[x + k, y]
-                    if x - k >= 0:
-                        beside = beside + own[x - k, y]
-                    summed = summed + stencil_weights[k] * beside
-                applied = -0.5 * summed + pot[x, y] * centre
-                if shift:
-                    applied = applied - shift * centre
-                out[x, y] = applied
-                return carry
-
-            lax.fori_loop(0, ny, row, 0)
+        step = pl.program_id(0)
+
+        @pl.when(step == 0)
+        def _():
+            for x in range(planes):
+                own[x] = own_narrow[x].astype(jnp.float32)
+
+        for block in range(blocks):
+            @pl.when(step == block)
+            def _(block=block):
+                for j in range(depth):
+                    x = block * depth + j
+
+                    def row(y, carry, x=x, j=j):
+                        centre = own[x, y]
+                        summed = (3.0 * stencil_weights[0]) * centre
+                        for k in range(1, RADIUS + 1):
+                            beside = own[x, (y + k) % ny] + own[x, (y + ny - k) % ny]
+                            beside = beside + (
+                                pltpu.roll(centre, k, 0) + pltpu.roll(centre, nz - k, 0)
+                            )
+                            if x + k < planes:
+                                beside = beside + own[x + k, y]
+                            if x - k >= 0:
+                                beside = beside + own[x - k, y]
+                            summed = summed + stencil_weights[k] * beside
+                        applied = -0.5 * summed + pot[j, y] * centre
+                        if shift:
+                            applied = applied - shift * centre
+                        out[j, y] = applied
+                        return carry
+
+                    lax.fori_loop(0, ny, row, 0)
 
     return kernel
 
 
 def finish_kernel(stage, planes, ny):
+    blocks, depth = plane_blocks(planes)
+
     def kernel(*refs):
         refs = list(refs)
         low, high, partial = refs[:3]
         initial = refs[3] if stage == "filtered" else None
         outs = refs[4:] if stage == "filtered" else refs[3:]
         out = outs[0]
-        for x in range(planes):
-            def row(y, carry, x=x):
-                summed = partial[x, y]
-                for k in range(1, RADIUS + 1):
-                    outside = []
-                    if x + k >= planes:
-                        outside.append(high[x + k - planes, y].astype(jnp.float32))
-                    if x - k < 0:
-                        outside.append(low[x - k + RADIUS, y].astype(jnp.float32))
-                    if outside:
-                        term = outside[0] if len(outside) == 1 else outside[0] + outside[1]
-                        summed = summed + (-0.5 * stencil_weights[k]) * term
-                if stage == "first":
-                    result = summed * first_factor
-                elif stage == "filtered":
-                    result = summed * second_factor + (
-                        memory_factor * initial[x, y].astype(jnp.float32)
-                    )
-                else:
-                    result = summed
-                result = result.astype(out.dtype)
-                out[x, y] = result
-                if len(outs) == 3:
-                    if x >= planes - RADIUS:
-                        outs[1][x - planes + RADIUS, y] = result
-                    if x < RADIUS:
-                        outs[2][x, y] = result
-                return carry
-
-            lax.fori_loop(0, ny, row, 0)
+        step = pl.program_id(0)
+        for block in range(blocks):
+            @pl.when(step == block)
+            def _(block=block):
+                for j in range(depth):
+                    x = block * depth + j
+
+                    def row(y, carry, x=x, j=j):
+                        summed = partial[j, y]
+                        for k in range(1, RADIUS + 1):
+                            outside = []
+                            if x + k >= planes:
+                                outside.append(high[x + k - planes, y].astype(jnp.float32))
+                            if x - k < 0:
+                                outside.append(low[x - k + RADIUS, y].astype(jnp.float32))
+                            if outside:
+                                term = outside[0] if len(outside) == 1 else outside[0] + outside[1]
+                                summed = summed + (-0.5 * stencil_weights[k]) * term
+                        if stage == "first":
+                            result = summed * first_factor
+                        elif stage == "filtered":
+                            result = summed * second_factor + (
+                                memory_factor * initial[j, y].astype(jnp.float32)
+                            )
+                        else:
+                            result = summed
+                        result = result.astype(out.dtype)
+                        out[j, y] = result
+                        if len(outs) == 3:
+                            if x >= planes - RADIUS:
+                                outs[1][x - planes + RADIUS, y] = result
+                            if x < RADIUS:
+                                outs[2][x, y] = result
+                        return carry
+
+                    lax.fori_loop(0, ny, row, 0)
 
     return kernel
 
 
 def stencil_stage(stage, block, sends, potential_wide, initial=None, keep_sends=True):
     planes, ny, nz, nb = block.shape
+    blocks, depth = plane_blocks(planes)
+    whole = pl.BlockSpec(block.shape, lambda i: (0, 0, 0, 0))
+    edge = pl.BlockSpec((RADIUS, ny, nz, nb), lambda i: (0, 0, 0, 0))
+    part = pl.BlockSpec((depth, ny, nz, nb), lambda i: (i, 0, 0, 0))
     low, high = exchange(sends, "domain")
     partial = pl.pallas_call(
         interior_kernel(stage, planes, ny, nz),
+        grid=(blocks,),
+        in_specs=[whole, part],
+        out_specs=part,
         out_shape=jax.ShapeDtypeStruct(block.shape, jnp.float32),
         scratch_shapes=[pltpu.VMEM(block.shape, jnp.float32)],
         name=f"interior_{stage}",
     )(block, potential_wide)
     operands = [low, high, partial]
+    in_specs = [edge, edge, part]
     if initial is not None:
         operands.append(initial)
+        in_specs.append(part)
     shapes = [jax.ShapeDtypeStruct(block.shape, jnp.bfloat16)]
+    out_specs = [part]
     if keep_sends:
-        edge = jax.ShapeDtypeStruct((RADIUS, ny, nz, nb), jnp.bfloat16)
-        shapes += [edge, edge]
+        edge_shape = jax.ShapeDtypeStruct((RADIUS, ny, nz, nb), jnp.bfloat16)
+        shapes += [edge_shape, edge_shape]
+        out_specs += [edge, edge]
     return pl.pallas_call(
         finish_kernel(stage, planes, ny),
+        grid=(blocks,),
+        in_specs=in_specs,
+        out_specs=tuple(out_specs),
         out_shape=tuple(shapes),
         name=f"finish_{stage}",
     )(*operands)

time: 97.1 us -> 95.1 us (0.979)
  Pallas kernels: 38.4 us -> 34.5 us
  starting transfers between devices: 21.7 us -> 23.8 us
    pallas_call x6, Pallas kernels: 38.4 us -> 34.5 us  [the longest x3 22.5 us: stencil_stage(): pl.pallas_call(interior_kernel(stage, planes, ny, nz), grid=(blocks,), in...]
    ppermute x1, waiting for transfers between devices: 1.84 us -> 0.29 us  [shards(): partner = lax.ppermute(own_block, 'band', [(0, 1), (1, 0)])]
    ppermute x8, starting transfers between devices: 7.47 us -> 8.53 us  [butterfly_sum(): values = values + lax.ppermute(values, axis, pairs)]
    ppermute x3, starting transfers between devices: 1.36 us -> 2.4 us  [exchange(): lax.ppermute(sends[0], axis, forward)]
  transfers between devices with their start and end apart: 15 -> 15, of which waited for: 10 -> 10; matrix products, arithmetic and copies ran while one was open for 6% -> 6% of each run, Pallas kernels for 30% -> 27%
where the time goes in v10:
time: 95.1 us; the launch traced here: 94.9 us
  Pallas kernels  34.5 us (36%)
  starting transfers between devices  23.8 us (25%)
  waiting for transfers between devices  23.6 us (25%)
  local copies, waits for them, and re-layouts  8.79 us (9%)
  matrix products  3.22 us (3%)
    pallas_call x3, Pallas kernels, stencil_stage(): pl.pallas_call(interior_kernel(stage, planes, ny, nz), grid=(blocks,), in...  22.5 us
    ppermute x8, waiting for transfers between devices, butterfly_sum(): values = values + lax.ppermute(values, axis, pairs)  20 us
    pallas_call x3, Pallas kernels, stencil_stage(): pl.pallas_call(finish_kernel(stage, planes, ny), grid=(blocks,), in_specs...  12.1 us
    ppermute x3, starting transfers between devices, exchange(): lax.ppermute(sends[1], axis, backward)  11 us
    ppermute x8, starting transfers between devices, butterfly_sum(): values = values + lax.ppermute(values, axis, pairs)  8.53 us
    unnamed x20, local copies, waits for them, and re-layouts  5.52 us
    ppermute x3, waiting for transfers between devices, exchange(): lax.ppermute(sends[0], axis, forward)  3.31 us
    dot_general x4, matrix products, shards(): jnp.einsum('cb,ck->bk', rows, cols, preferred_element_type=jnp.float32)  3.22 us
  transfers between devices with their start and end apart: 15, of which 10 were waited for; matrix products, arithmetic and copies ran while one was open for 6% of the time, Pallas kernels for 27%

profile of v10, /device:TPU:0, one launch (start us, length us, event | category | flops | bytes accessed | tf_op | source)
XLA Modules:
  0.0 94.9 jit_solution(8728875768877320787)
XLA Ops:
  0.6 1.3 %fusion = (bf16[4,16,32,128]{3,2,1,0:T(8,128)(2,1)S(1)}, bf16[4,16,32,128]{3,2,1,0:T(8,128)(2,1)S(1)}) fusion(bf16[8,16,32,128]{3,2,1,0:T(8,128)(2,1)} %refs_3_.1), kind=kLoop, calls=%fused_computation.6 | loop fusion | bytes 2097152 | tf_op jit(solution)/shard_map/slice | solution.py:183
  2.5 5.0 %collective-permute-start.1 = (bf16[4,16,32,128]{3,2,1,0:T(8,128)(2,1)S(1)}, bf16[4,16,32,128]{3,2,1,0:T(8,128)(2,1)S(1)}, u32[]{:S(2)}, u32[]{:S(2)}) collective-permute-start(bf16[4,16,32,128]{3,2,1,0:T(8,128)(2,1)S(1)} %get-tuple-element.18), channel_id=1, source_target_pairs={{1,0},{2,1},{3,2},{4,3},{5,4},{6,5},{7,6},{8,7},{9,8},{10,9},{11,1... | collective-permute-start | bytes 1572872 | tf_op jit(solution)/shard_map/ppermute | solution.py:154
  7.5 1.9 %broadcast_in_dim.2.pot = f32[8,16,32,128]{3,2,1,0:T(8,128)} broadcast(f32[8,16,32]{2,1,0:T(8,128)S(1)} %copy-done.8), dimensions={0,1,2} | broadcast | bytes 2113536 | tf_op jit(solution)/shard_map/broadcast_in_dim | solution.py:169
  9.5 7.5 %interior_first.1.refs_2_ = f32[8,16,32,128]{3,2,1,0:T(8,128)} custom-call(bf16[8,16,32,128]{3,2,1,0:T(8,128)(2,1)} %refs_3_.1, f32[8,16,32,128]{3,2,1,0:T(8,128)} %broadcast_in_dim.2.pot), custom_call_target="tpu_custom_call" | custom-call | tf_op jit(solution)/shard_map/interior_first/pallas_call | solution.py:120
  17.0 0.8 copy-done.2
  17.8 0.8 copy-done.3
  18.6 4.0 %finish_first.1 = (bf16[8,16,32,128]{3,2,1,0:T(8,128)(2,1)}, bf16[4,16,32,128]{3,2,1,0:T(8,128)(2,1)}, bf16[4,16,32,128]{3,2,1,0:T(8,128)(2,1)}) custom-call(bf16[4,16,32,128]{3,2,1,0:T(8,128)(2,1)} %copy-done.2, bf16[4,16,32,128]{3,2,1,0:T(8,128)(2,1)} %copy-done.3, f32[8,16,32,128]{3,2,1,0:T(8,128)} %interior_first.1.refs_2_), custom_call_target="tpu_custom_call" | custom-call | tf_op jit(solution)/shard_map/finish_first/pallas_call | solution.py:140
  22.6 1.6 %collective-permute-start.2 = (bf16[4,16,32,128]{3,2,1,0:T(8,128)(2,1)}, bf16[4,16,32,128]{3,2,1,0:T(8,128)(2,1)S(1)}, u32[]{:S(2)}, u32[]{:S(2)}) collective-permute-start(bf16[4,16,32,128]{3,2,1,0:T(8,128)(2,1)} %get-tuple-element.9), channel_id=1, source_target_pairs={{0,1},{1,2},{2,3},{3,4},{4,5},{5,6},{6,7},{7,8},{8,9},{9,10},{10,1... | collective-permute-start | bytes 1572872 | tf_op jit(solution)/shard_map/ppermute | solution.py:154
  24.2 2.9 %collective-permute-start.3 = (bf16[4,16,32,128]{3,2,1,0:T(8,128)(2,1)}, bf16[4,16,32,128]{3,2,1,0:T(8,128)(2,1)S(1)}, u32[]{:S(2)}, u32[]{:S(2)}) collective-permute-start(bf16[4,16,32,128]{3,2,1,0:T(8,128)(2,1)} %get-tuple-element.10), channel_id=1, source_target_pairs={{1,0},{2,1},{3,2},{4,3},{5,4},{6,5},{7,6},{8,7},{9,8},{10,9},{11,1... | collective-permute-start | bytes 1572872 | tf_op jit(solution)/shard_map/ppermute | solution.py:154
  27.0 7.5 %interior_filtered.1.refs_2_ = f32[8,16,32,128]{3,2,1,0:T(8,128)} custom-call(bf16[8,16,32,128]{3,2,1,0:T(8,128)(2,1)} %get-tuple-element.11.own_narrow, f32[8,16,32,128]{3,2,1,0:T(8,128)} %broadcast_in_dim.2.pot), custom_call_target="tpu_custom_call" | custom-call | tf_op jit(solution)/shard_map/interior_filtered/pallas_call | solution.py:120
  34.5 0.8 copy-done.6
  35.3 0.8 copy-done.7
  36.1 4.4 %finish_filtered.1 = (bf16[8,16,32,128]{3,2,1,0:T(8,128)(2,1)}, bf16[4,16,32,128]{3,2,1,0:T(8,128)(2,1)}, bf16[4,16,32,128]{3,2,1,0:T(8,128)(2,1)}) custom-call(bf16[4,16,32,128]{3,2,1,0:T(8,128)(2,1)} %copy-done.6, bf16[4,16,32,128]{3,2,1,0:T(8,128)(2,1)} %copy-done.7, f32[8,16,32,128]{3,2,1,0:T(8,128)} %interior_filtered.1.refs_2_, ...), custom_call_target="tpu_custom_call" | custom-call | tf_op jit(solution)/shard_map/finish_filtered/pallas_call | solution.py:140
  40.6 1.9 %collective-permute-start.4 = (bf16[4096,128]{1,0:T(8,128)(2,1)}, bf16[4096,128]{1,0:T(8,128)(2,1)S(1)}, u32[]{:S(2)}, u32[]{:S(2)}) collective-permute-start(bf16[4096,128]{1,0:T(8,128)(2,1)} %bitcast.18), channel_id=1, source_target_pairs={{0,16},{16,0},{1,17},{17,1},{2,18},{18,2},{3,19},{19,3},{4,20},{20... | collective-permute-start | bytes 3145736 | tf_op jit(solution)/shard_map/ppermute | solution.py:190
  42.5 3.0 %collective-permute-start.10 = (bf16[4,16,32,128]{3,2,1,0:T(8,128)(2,1)}, bf16[4,16,32,128]{3,2,1,0:T(8,128)(2,1)S(1)}, u32[]{:S(2)}, u32[]{:S(2)}) collective-permute-start(bf16[4,16,32,128]{3,2,1,0:T(8,128)(2,1)} %get-tuple-element.14), channel_id=1, source_target_pairs={{1,0},{2,1},{3,2},{4,3},{5,4},{6,5},{7,6},{8,7},{9,8},{10,9},{11,1... | collective-permute-start | bytes 1572872 | tf_op jit(solution)/shard_map/ppermute | solution.py:154
  45.9 7.5 %interior_applied.1.refs_2_ = f32[8,16,32,128]{3,2,1,0:T(8,128)} custom-call(bf16[8,16,32,128]{3,2,1,0:T(8,128)(2,1)} %get-tuple-element.15.own_narrow, f32[8,16,32,128]{3,2,1,0:T(8,128)} %broadcast_in_dim.2.pot), custom_call_target="tpu_custom_call" | custom-call | tf_op jit(solution)/shard_map/interior_applied/pallas_call | solution.py:120
  53.9 3.3 %collective-permute-done.9.refs_0_ = bf16[4,16,32,128]{3,2,1,0:T(8,128)(2,1)S(1)} collective-permute-done((bf16[4,16,32,128]{3,2,1,0:T(8,128)(2,1)}, bf16[4,16,32,128]{3,2,1,0:T(8,128)(2,1)S(1)}, u32[]{:S(2)}, u32[]{:S(2)}) %collective-permute-start.9) | collective-permute-done | bytes 524320 | tf_op jit(solution)/shard_map/ppermute | solution.py:154
  57.2 0.8 copy-done.5
  58.0 3.6 %finish_applied.1 = bf16[8,16,32,128]{3,2,1,0:T(8,128)(2,1)} custom-call(bf16[4,16,32,128]{3,2,1,0:T(8,128)(2,1)} %copy-done.5, bf16[4,16,32,128]{3,2,1,0:T(8,128)(2,1)} %copy-done.4, f32[8,16,32,128]{3,2,1,0:T(8,128)} %interior_applied.1.refs_2_), custom_call_target="tpu_custom_call" | custom-call | tf_op jit(solution)/shard_map/finish_applied/pallas_call | solution.py:140
  61.6 1.8 %convolution_bitcast_fusion = f32[128,128]{0,1:T(8,128)S(1)} fusion(bf16[8,16,32,128]{3,2,1,0:T(8,128)(2,1)} %finish_applied.1, bf16[8,16,32,128]{3,2,1,0:T(8,128)(2,1)S(1)} %copy-done), kind=kOutput, calls=%fused_computation | convolution fusion | flops 134217728 | bytes 2162688 | tf_op jit(solution)/shard_map/cb,ck->bk/dot_general | solution.py:173
  64.2 4.0 %collective-permute-start.11 = (f32[128,256]{0,1:T(8,128)S(1)}, f32[128,256]{0,1:T(8,128)S(1)}, u32[]{:S(2)}, u32[]{:S(2)}) collective-permute-start(f32[128,256]{0,1:T(8,128)S(1)} %maximum_select_fusion.1), channel_id=1, source_target_pairs={{0,1},{1,0},{2,3},{3,2},{4,5},{5,4},{6,7},{7,6},{8,9},{9,8},{10,11... | collective-permute-start | bytes 393224 | tf_op jit(solution)/shard_map/ppermute | solution.py:162
  69.3 0.8 collective-permute-done.5
  70.2 1.3 %collective-permute-start.6 = (f32[128,256]{0,1:T(8,128)S(1)}, f32[128,256]{0,1:T(8,128)S(1)}, u32[]{:S(2)}, u32[]{:S(2)}) collective-permute-start(f32[128,256]{0,1:T(8,128)S(1)} %add.24), channel_id=1, source_target_pairs={{0,2},{1,3},{2,0},{3,1},{4,6},{5,7},{6,4},{7,5},{8,10},{9,11},{10,... | collective-permute-start | bytes 393224 | tf_op jit(solution)/shard_map/ppermute | solution.py:162
  71.4 4.2 %collective-permute-done.12 = f32[128,256]{0,1:T(8,128)S(1)} collective-permute-done((f32[128,256]{0,1:T(8,128)S(1)}, f32[128,256]{0,1:T(8,128)S(1)}, u32[]{:S(2)}, u32[]{:S(2)}) %collective-permute-start.12) | collective-permute-done | bytes 131104 | tf_op jit(solution)/shard_map/ppermute | solution.py:162
  76.0 1.8 %collective-permute-done.6 = f32[128,256]{0,1:T(8,128)S(1)} collective-permute-done((f32[128,256]{0,1:T(8,128)S(1)}, f32[128,256]{0,1:T(8,128)S(1)}, u32[]{:S(2)}, u32[]{:S(2)}) %collective-permute-start.6) | collective-permute-done | bytes 131104 | tf_op jit(solution)/shard_map/ppermute | solution.py:162
  78.3 3.0 %collective-permute-done.13 = f32[128,256]{0,1:T(8,128)S(1)} collective-permute-done((f32[128,256]{0,1:T(8,128)S(1)}, f32[128,256]{0,1:T(8,128)S(1)}, u32[]{:S(2)}, u32[]{:S(2)}) %collective-permute-start.13) | collective-permute-done | bytes 131104 | tf_op jit(solution)/shard_map/ppermute | solution.py:162
  81.3 1.4 %collective-permute-start.14 = (f32[128,256]{0,1:T(8,128)S(1)}, f32[128,256]{0,1:T(8,128)S(1)}, u32[]{:S(2)}, u32[]{:S(2)}) collective-permute-start(f32[128,256]{0,1:T(8,128)S(1)} %add.30), channel_id=1, source_target_pairs={{0,8},{1,9},{2,10},{3,11},{4,12},{5,13},{6,14},{7,15},{8,0},{9,1},... | collective-permute-start | bytes 393224 | tf_op jit(solution)/shard_map/ppermute | solution.py:162
  82.7 2.2 %collective-permute-done.7 = f32[128,256]{0,1:T(8,128)S(1)} collective-permute-done((f32[128,256]{0,1:T(8,128)S(1)}, f32[128,256]{0,1:T(8,128)S(1)}, u32[]{:S(2)}, u32[]{:S(2)}) %collective-permute-start.7) | collective-permute-done | bytes 131104 | tf_op jit(solution)/shard_map/ppermute | solution.py:162
  84.9 0.9 collective-permute-start.8
  85.8 6.8 %collective-permute-done.14 = f32[128,256]{0,1:T(8,128)S(1)} collective-permute-done((f32[128,256]{0,1:T(8,128)S(1)}, f32[128,256]{0,1:T(8,128)S(1)}, u32[]{:S(2)}, u32[]{:S(2)}) %collective-permute-start.14) | collective-permute-done | bytes 131104 | tf_op jit(solution)/shard_map/ppermute | solution.py:162
  92.6 0.8 copy.6
  94.1 0.8 copy.5
  (40 shorter events, 4.8 us)
Async XLA Ops:
  0.6 6.9 %copy-start.8 = (f32[8,16,32]{2,1,0:T(8,128)S(1)}, f32[8,16,32]{2,1,0:T(8,128)}, u32[]{:S(2)}) copy-start(f32[8,16,32]{2,1,0:T(8,128)} %param.3) | copy-start | bytes 49156
  2.0 15.0 %collective-permute-start = (bf16[4,16,32,128]{3,2,1,0:T(8,128)(2,1)S(1)}, bf16[4,16,32,128]{3,2,1,0:T(8,128)(2,1)S(1)}, u32[]{:S(2)}, u32[]{:S(2)}) collective-permute-start(bf16[4,16,32,128]{3,2,1,0:T(8,128)(2,1)S(1)} %get-tuple-element.19), channel_id=1, source_target_pairs={{0,1},{1,2},{2,3},{3,4},{4,5},{5,6},{6,7},{7,8},{8,9},{9,10},{10,1... | collective-permute-start | bytes 1572872 | tf_op jit(solution)/shard_map/ppermute | solution.py:154
  2.5 14.5 %collective-permute-start.1 = (bf16[4,16,32,128]{3,2,1,0:T(8,128)(2,1)S(1)}, bf16[4,16,32,128]{3,2,1,0:T(8,128)(2,1)S(1)}, u32[]{:S(2)}, u32[]{:S(2)}) collective-permute-start(bf16[4,16,32,128]{3,2,1,0:T(8,128)(2,1)S(1)} %get-tuple-element.18), channel_id=1, source_target_pairs={{1,0},{2,1},{3,2},{4,3},{5,4},{6,5},{7,6},{8,7},{9,8},{10,9},{11,1... | collective-permute-start | bytes 1572872 | tf_op jit(solution)/shard_map/ppermute | solution.py:154
  16.9 0.8 copy-start.2
  17.8 0.8 copy-start.3
  22.6 11.9 %collective-permute-start.2 = (bf16[4,16,32,128]{3,2,1,0:T(8,128)(2,1)}, bf16[4,16,32,128]{3,2,1,0:T(8,128)(2,1)S(1)}, u32[]{:S(2)}, u32[]{:S(2)}) collective-permute-start(bf16[4,16,32,128]{3,2,1,0:T(8,128)(2,1)} %get-tuple-element.9), channel_id=1, source_target_pairs={{0,1},{1,2},{2,3},{3,4},{4,5},{5,6},{6,7},{7,8},{8,9},{9,10},{10,1... | collective-permute-start | bytes 1572872 | tf_op jit(solution)/shard_map/ppermute | solution.py:154
  24.2 10.4 %collective-permute-start.3 = (bf16[4,16,32,128]{3,2,1,0:T(8,128)(2,1)}, bf16[4,16,32,128]{3,2,1,0:T(8,128)(2,1)S(1)}, u32[]{:S(2)}, u32[]{:S(2)}) collective-permute-start(bf16[4,16,32,128]{3,2,1,0:T(8,128)(2,1)} %get-tuple-element.10), channel_id=1, source_target_pairs={{1,0},{2,1},{3,2},{4,3},{5,4},{6,5},{7,6},{8,7},{9,8},{10,9},{11,1... | collective-permute-start | bytes 1572872 | tf_op jit(solution)/shard_map/ppermute | solution.py:154
  34.5 0.8 copy-start.6
  35.3 0.8 copy-start.7
  40.6 23.1 %collective-permute-start.4 = (bf16[4096,128]{1,0:T(8,128)(2,1)}, bf16[4096,128]{1,0:T(8,128)(2,1)S(1)}, u32[]{:S(2)}, u32[]{:S(2)}) collective-permute-start(bf16[4096,128]{1,0:T(8,128)(2,1)} %bitcast.18), channel_id=1, source_target_pairs={{0,16},{16,0},{1,17},{17,1},{2,18},{18,2},{3,19},{19,3},{4,20},{20... | collective-permute-start | bytes 3145736 | tf_op jit(solution)/shard_map/ppermute | solution.py:190
  42.5 11.4 %collective-permute-start.10 = (bf16[4,16,32,128]{3,2,1,0:T(8,128)(2,1)}, bf16[4,16,32,128]{3,2,1,0:T(8,128)(2,1)S(1)}, u32[]{:S(2)}, u32[]{:S(2)}) collective-permute-start(bf16[4,16,32,128]{3,2,1,0:T(8,128)(2,1)} %get-tuple-element.14), channel_id=1, source_target_pairs={{1,0},{2,1},{3,2},{4,3},{5,4},{6,5},{7,6},{8,7},{9,8},{10,9},{11,1... | collective-permute-start | bytes 1572872 | tf_op jit(solution)/shard_map/ppermute | solution.py:154
  45.6 11.6 %collective-permute-start.9 = (bf16[4,16,32,128]{3,2,1,0:T(8,128)(2,1)}, bf16[4,16,32,128]{3,2,1,0:T(8,128)(2,1)S(1)}, u32[]{:S(2)}, u32[]{:S(2)}) collective-permute-start(bf16[4,16,32,128]{3,2,1,0:T(8,128)(2,1)} %get-tuple-element.13), channel_id=1, source_target_pairs={{0,1},{1,2},{2,3},{3,4},{4,5},{5,6},{6,7},{7,8},{8,9},{9,10},{10,1... | collective-permute-start | bytes 1572872 | tf_op jit(solution)/shard_map/ppermute | solution.py:154
  45.9 7.5 %copy-start = (bf16[8,16,32,128]{3,2,1,0:T(8,128)(2,1)S(1)}, bf16[8,16,32,128]{3,2,1,0:T(8,128)(2,1)}, u32[]{:S(2)}) copy-start(bf16[8,16,32,128]{3,2,1,0:T(8,128)(2,1)} %get-tuple-element.15.own_narrow) | copy-start | bytes 3145732
  53.9 3.3 %copy-start.4 = (bf16[4,16,32,128]{3,2,1,0:T(8,128)(2,1)}, bf16[4,16,32,128]{3,2,1,0:T(8,128)(2,1)S(1)}, u32[]{:S(2)}) copy-start(bf16[4,16,32,128]{3,2,1,0:T(8,128)(2,1)S(1)} %collective-permute-done.10.refs_1_) | copy-start | bytes 1572868
  57.2 0.8 copy-start.5
  61.6 2.1 %copy-start.1 = (bf16[8,16,32,128]{3,2,1,0:T(8,128)(2,1)S(1)}, bf16[8,16,32,128]{3,2,1,0:T(8,128)(2,1)}, u32[]{:S(2)}) copy-start(bf16[8,16,32,128]{3,2,1,0:T(8,128)(2,1)} %finish_applied.1) | copy-start | bytes 3145732
  64.2 5.0 %collective-permute-start.11 = (f32[128,256]{0,1:T(8,128)S(1)}, f32[128,256]{0,1:T(8,128)S(1)}, u32[]{:S(2)}, u32[]{:S(2)}) collective-permute-start(f32[128,256]{0,1:T(8,128)S(1)} %maximum_select_fusion.1), channel_id=1, source_target_pairs={{0,1},{1,0},{2,3},{3,2},{4,5},{5,4},{6,7},{7,6},{8,9},{9,8},{10,11... | collective-permute-start | bytes 393224 | tf_op jit(solution)/shard_map/ppermute | solution.py:162
  68.7 1.4 %collective-permute-start.5 = (f32[128,256]{0,1:T(8,128)S(1)}, f32[128,256]{0,1:T(8,128)S(1)}, u32[]{:S(2)}, u32[]{:S(2)}) collective-permute-start(f32[128,256]{0,1:T(8,128)S(1)} %maximum_select_fusion), channel_id=1, source_target_pairs={{0,1},{1,0},{2,3},{3,2},{4,5},{5,4},{6,7},{7,6},{8,9},{9,8},{10,11... | collective-permute-start | bytes 393224 | tf_op jit(solution)/shard_map/ppermute | solution.py:162
  69.2 6.4 %collective-permute-start.12 = (f32[128,256]{0,1:T(8,128)S(1)}, f32[128,256]{0,1:T(8,128)S(1)}, u32[]{:S(2)}, u32[]{:S(2)}) collective-permute-start(f32[128,256]{0,1:T(8,128)S(1)} %add.28), channel_id=1, source_target_pairs={{0,2},{1,3},{2,0},{3,1},{4,6},{5,7},{6,4},{7,5},{8,10},{9,11},{10,... | collective-permute-start | bytes 393224 | tf_op jit(solution)/shard_map/ppermute | solution.py:162
  70.2 7.7 %collective-permute-start.6 = (f32[128,256]{0,1:T(8,128)S(1)}, f32[128,256]{0,1:T(8,128)S(1)}, u32[]{:S(2)}, u32[]{:S(2)}) collective-permute-start(f32[128,256]{0,1:T(8,128)S(1)} %add.24), channel_id=1, source_target_pairs={{0,2},{1,3},{2,0},{3,1},{4,6},{5,7},{6,4},{7,5},{8,10},{9,11},{10,... | collective-permute-start | bytes 393224 | tf_op jit(solution)/shard_map/ppermute | solution.py:162
  75.6 5.6 %collective-permute-start.13 = (f32[128,256]{0,1:T(8,128)S(1)}, f32[128,256]{0,1:T(8,128)S(1)}, u32[]{:S(2)}, u32[]{:S(2)}) collective-permute-start(f32[128,256]{0,1:T(8,128)S(1)} %add.29), channel_id=1, source_target_pairs={{0,4},{1,5},{2,6},{3,7},{4,0},{5,1},{6,2},{7,3},{8,12},{9,13},{10,... | collective-permute-start | bytes 393224 | tf_op jit(solution)/shard_map/ppermute | solution.py:162
  77.9 7.0 %collective-permute-start.7 = (f32[128,256]{0,1:T(8,128)S(1)}, f32[128,256]{0,1:T(8,128)S(1)}, u32[]{:S(2)}, u32[]{:S(2)}) collective-permute-start(f32[128,256]{0,1:T(8,128)S(1)} %add.25), channel_id=1, source_target_pairs={{0,4},{1,5},{2,6},{3,7},{4,0},{5,1},{6,2},{7,3},{8,12},{9,13},{10,... | collective-permute-start | bytes 393224 | tf_op jit(solution)/shard_map/ppermute | solution.py:162
  81.3 11.3 %collective-permute-start.14 = (f32[128,256]{0,1:T(8,128)S(1)}, f32[128,256]{0,1:T(8,128)S(1)}, u32[]{:S(2)}, u32[]{:S(2)}) collective-permute-start(f32[128,256]{0,1:T(8,128)S(1)} %add.30), channel_id=1, source_target_pairs={{0,8},{1,9},{2,10},{3,11},{4,12},{5,13},{6,14},{7,15},{8,0},{9,1},... | collective-permute-start | bytes 393224 | tf_op jit(solution)/shard_map/ppermute | solution.py:162
  84.9 9.2 %collective-permute-start.8 = (f32[128,256]{0,1:T(8,128)S(1)}, f32[128,256]{0,1:T(8,128)S(1)}, u32[]{:S(2)}, u32[]{:S(2)}) collective-permute-start(f32[128,256]{0,1:T(8,128)S(1)} %add.26), channel_id=1, source_target_pairs={{0,8},{1,9},{2,10},{3,11},{4,12},{5,13},{6,14},{7,15},{8,0},{9,1},... | collective-permute-start | bytes 393224 | tf_op jit(solution)/shard_map/ppermute | solution.py:162

commit v11 on v10

--- a/solution.py
+++ b/solution.py
@@ -50,7 +50,11 @@
                             if x - k >= 0:
                                 beside = beside + own[x - k, y]
                             summed = summed + stencil_weights[k] * beside
-                        applied = -0.5 * summed + pot[j, y] * centre
+                        chosen = lax.broadcasted_iota(jnp.int32, (nz, ny), 1) == y
+                        column = jnp.sum(
+                            jnp.where(chosen, pot[x], 0.0), axis=1, keepdims=True
+                        )
+                        applied = -0.5 * summed + column * centre
                         if shift:
                             applied = applied - shift * centre
                         out[j, y] = applied
@@ -117,10 +121,11 @@
     edge = pl.BlockSpec((RADIUS, ny, nz, nb), lambda i: (0, 0, 0, 0))
     part = pl.BlockSpec((depth, ny, nz, nb), lambda i: (i, 0, 0, 0))
     low, high = exchange(sends, "domain")
+    potential_whole = pl.BlockSpec(potential_wide.shape, lambda i: (0, 0, 0))
     partial = pl.pallas_call(
         interior_kernel(stage, planes, ny, nz),
         grid=(blocks,),
-        in_specs=[whole, part],
+        in_specs=[whole, potential_whole],
         out_specs=part,
         out_shape=jax.ShapeDtypeStruct(block.shape, jnp.float32),
         scratch_shapes=[pltpu.VMEM(block.shape, jnp.float32)],
@@ -166,7 +171,7 @@
 
 def shards(orbitals, potential):
     planes, ny, nz, nb = orbitals.shape
-    potential_wide = jnp.broadcast_to(potential[:, :, :, None], (planes, ny, nz, nb))
+    potential_wide = jnp.swapaxes(potential, 1, 2)
     cell_count = planes * ny * nz
     cell_weight = 1.0 / (cell_count * lax.axis_size("domain"))
     band = lax.axis_index("band")

time: 95.1 us -> 101 us (1.062)
  Pallas kernels: 34.5 us -> 50.8 us
  starting transfers between devices: 23.8 us -> 15.9 us
  waiting for transfers between devices: 23.6 us -> 21.4 us
    pallas_call x3, Pallas kernels: 22.5 us -> 38.7 us  [stencil_stage(): pl.pallas_call(interior_kernel(stage, planes, ny, nz), grid=(blocks,), in...]
    ppermute x8, starting transfers between devices: 8.53 us -> 3.38 us  [butterfly_sum(): values = values + lax.ppermute(values, axis, pairs)]
    ppermute x3, waiting for transfers between devices: 3.31 us -> 0.01 us  [exchange(): lax.ppermute(sends[0], axis, forward)]
    broadcast_in_dim x1 -> x0, local copies, waits for them, and re-layouts: 1.93 us -> none  [shards(): jnp.broadcast_to(potential[:, :, :, None], (planes, ny, nz, nb))]
    ppermute x3, starting transfers between devices: 11 us -> 9.47 us  [exchange(): lax.ppermute(sends[1], axis, backward)]
    ppermute x8, waiting for transfers between devices: 20 us -> 21.4 us  [butterfly_sum(): values = values + lax.ppermute(values, axis, pairs)]
    unnamed x20 -> x21, local copies, waits for them, and re-layouts: 5.52 us -> 6.98 us
    ppermute x3, starting transfers between devices: 2.4 us -> 1.01 us  [exchange(): lax.ppermute(sends[0], axis, forward)]
  transfers between devices with their start and end apart: 15 -> 15, of which waited for: 10 -> 8; matrix products, arithmetic and copies ran while one was open for 6% -> 4% of each run, Pallas kernels for 27% -> 42%
where the time goes in v11:
time: 101 us
  Pallas kernels  50.8 us (50%)
  waiting for transfers between devices  21.4 us (21%)
  starting transfers between devices  15.9 us (16%)
  local copies, waits for them, and re-layouts  8.31 us (8%)
  matrix products  3.23 us (3%)
    pallas_call x3, Pallas kernels, stencil_stage(): pl.pallas_call(interior_kernel(stage, planes, ny, nz), grid=(blocks,), in...  38.7 us
    ppermute x8, waiting for transfers between devices, butterfly_sum(): values = values + lax.ppermute(values, axis, pairs)  21.4 us
    pallas_call x3, Pallas kernels, stencil_stage(): pl.pallas_call(finish_kernel(stage, planes, ny), grid=(blocks,), in_specs...  12.1 us
    ppermute x3, starting transfers between devices, exchange(): lax.ppermute(sends[1], axis, backward)  9.47 us
    unnamed x21, local copies, waits for them, and re-layouts  6.98 us
    ppermute x8, starting transfers between devices, butterfly_sum(): values = values + lax.ppermute(values, axis, pairs)  3.38 us
    dot_general x4, matrix products, shards(): jnp.einsum('cb,ck->bk', rows, cols, preferred_element_type=jnp.float32)  3.23 us
  transfers between devices with their start and end apart: 15, of which 8 were waited for; matrix products, arithmetic and copies ran while one was open for 4% of the time, Pallas kernels for 42%

profile of v11, /device:TPU:0, one launch (start us, length us, event | category | flops | bytes accessed | tf_op | source)
XLA Modules:
  0.0 100.6 jit_solution(9894710869785863817)
XLA Ops:
  0.6 1.3 %fusion = (bf16[4,16,32,128]{3,2,1,0:T(8,128)(2,1)S(1)}, bf16[4,16,32,128]{3,2,1,0:T(8,128)(2,1)S(1)}) fusion(bf16[8,16,32,128]{3,2,1,0:T(8,128)(2,1)} %refs_3_.1), kind=kLoop, calls=%fused_computation.6 | loop fusion | bytes 2097152 | tf_op jit(solution)/shard_map/slice | solution.py:188
  2.0 0.5 collective-permute-start
  2.5 5.0 %collective-permute-start.1 = (bf16[4,16,32,128]{3,2,1,0:T(8,128)(2,1)S(1)}, bf16[4,16,32,128]{3,2,1,0:T(8,128)(2,1)S(1)}, u32[]{:S(2)}, u32[]{:S(2)}) collective-permute-start(bf16[4,16,32,128]{3,2,1,0:T(8,128)(2,1)S(1)} %get-tuple-element.18), channel_id=1, source_target_pairs={{1,0},{2,1},{3,2},{4,3},{5,4},{6,5},{7,6},{8,7},{9,8},{10,9},{11,1... | collective-permute-start | bytes 1572872 | tf_op jit(solution)/shard_map/ppermute | solution.py:159
  7.5 0.8 copy.5
  8.3 13.0 %interior_first.1.refs_2_ = f32[8,16,32,128]{3,2,1,0:T(8,128)} custom-call(bf16[8,16,32,128]{3,2,1,0:T(8,128)(2,1)} %refs_3_.1, f32[8,32,16]{2,1,0:T(8,128)} %bitcast.22), custom_call_target="tpu_custom_call" | custom-call | tf_op jit(solution)/shard_map/interior_first/pallas_call | solution.py:125
  21.3 0.8 copy-done.2
  22.1 0.8 copy-done.3
  22.8 4.0 %finish_first.1 = (bf16[8,16,32,128]{3,2,1,0:T(8,128)(2,1)}, bf16[4,16,32,128]{3,2,1,0:T(8,128)(2,1)}, bf16[4,16,32,128]{3,2,1,0:T(8,128)(2,1)}) custom-call(bf16[4,16,32,128]{3,2,1,0:T(8,128)(2,1)} %copy-done.2, bf16[4,16,32,128]{3,2,1,0:T(8,128)(2,1)} %copy-done.3, f32[8,16,32,128]{3,2,1,0:T(8,128)} %interior_first.1.refs_2_), custom_call_target="tpu_custom_call" | custom-call | tf_op jit(solution)/shard_map/finish_first/pallas_call | solution.py:145
  26.9 4.4 %collective-permute-start.3 = (bf16[4,16,32,128]{3,2,1,0:T(8,128)(2,1)}, bf16[4,16,32,128]{3,2,1,0:T(8,128)(2,1)S(1)}, u32[]{:S(2)}, u32[]{:S(2)}) collective-permute-start(bf16[4,16,32,128]{3,2,1,0:T(8,128)(2,1)} %get-tuple-element.10), channel_id=1, source_target_pairs={{1,0},{2,1},{3,2},{4,3},{5,4},{6,5},{7,6},{8,7},{9,8},{10,9},{11,1... | collective-permute-start | bytes 1572872 | tf_op jit(solution)/shard_map/ppermute | solution.py:159
  31.3 13.0 %interior_filtered.1.refs_2_ = f32[8,16,32,128]{3,2,1,0:T(8,128)} custom-call(bf16[8,16,32,128]{3,2,1,0:T(8,128)(2,1)} %get-tuple-element.11.own_narrow, f32[8,32,16]{2,1,0:T(8,128)} %bitcast.23), custom_call_target="tpu_custom_call" | custom-call | tf_op jit(solution)/shard_map/interior_filtered/pallas_call | solution.py:125
  44.3 0.8 copy-done.6
  45.1 0.8 copy-done.7
  45.9 4.4 %finish_filtered.1 = (bf16[8,16,32,128]{3,2,1,0:T(8,128)(2,1)}, bf16[4,16,32,128]{3,2,1,0:T(8,128)(2,1)}, bf16[4,16,32,128]{3,2,1,0:T(8,128)(2,1)}) custom-call(bf16[4,16,32,128]{3,2,1,0:T(8,128)(2,1)} %copy-done.6, bf16[4,16,32,128]{3,2,1,0:T(8,128)(2,1)} %copy-done.7, f32[8,16,32,128]{3,2,1,0:T(8,128)} %interior_filtered.1.refs_2_, ...), custom_call_target="tpu_custom_call" | custom-call | tf_op jit(solution)/shard_map/finish_filtered/pallas_call | solution.py:145
  50.3 2.0 %collective-permute-start.4 = (bf16[4096,128]{1,0:T(8,128)(2,1)}, bf16[4096,128]{1,0:T(8,128)(2,1)S(1)}, u32[]{:S(2)}, u32[]{:S(2)}) collective-permute-start(bf16[4096,128]{1,0:T(8,128)(2,1)} %bitcast.19), channel_id=1, source_target_pairs={{0,16},{16,0},{1,17},{17,1},{2,18},{18,2},{3,19},{19,3},{4,20},{20... | collective-permute-start | bytes 3145736 | tf_op jit(solution)/shard_map/ppermute | solution.py:195
  52.3 0.5 collective-permute-start.9
  52.8 12.8 %interior_applied.1.refs_2_ = f32[8,16,32,128]{3,2,1,0:T(8,128)} custom-call(bf16[8,16,32,128]{3,2,1,0:T(8,128)(2,1)} %get-tuple-element.15.own_narrow, f32[8,32,16]{2,1,0:T(8,128)} %bitcast.24), custom_call_target="tpu_custom_call" | custom-call | tf_op jit(solution)/shard_map/interior_applied/pallas_call | solution.py:125
  66.1 0.8 copy-done.4
  66.9 0.8 copy-done.5
  67.7 3.6 %finish_applied.1 = bf16[8,16,32,128]{3,2,1,0:T(8,128)(2,1)} custom-call(bf16[4,16,32,128]{3,2,1,0:T(8,128)(2,1)} %copy-done.5, bf16[4,16,32,128]{3,2,1,0:T(8,128)(2,1)} %copy-done.4, f32[8,16,32,128]{3,2,1,0:T(8,128)} %interior_applied.1.refs_2_), custom_call_target="tpu_custom_call" | custom-call | tf_op jit(solution)/shard_map/finish_applied/pallas_call | solution.py:145
  71.3 1.8 %convolution_bitcast_fusion = f32[128,128]{0,1:T(8,128)S(1)} fusion(bf16[8,16,32,128]{3,2,1,0:T(8,128)(2,1)} %finish_applied.1, bf16[8,16,32,128]{3,2,1,0:T(8,128)(2,1)S(1)} %copy-done), kind=kOutput, calls=%fused_computation | convolution fusion | flops 134217728 | bytes 2162688 | tf_op jit(solution)/shard_map/cb,ck->bk/dot_general | solution.py:178
  74.2 0.6 collective-permute-start.5
  75.1 0.6 collective-permute-done.5
  75.8 1.5 %collective-permute-start.6 = (f32[128,256]{0,1:T(8,128)S(1)}, f32[128,256]{0,1:T(8,128)S(1)}, u32[]{:S(2)}, u32[]{:S(2)}) collective-permute-start(f32[128,256]{0,1:T(8,128)S(1)} %add.24), channel_id=1, source_target_pairs={{0,2},{1,3},{2,0},{3,1},{4,6},{5,7},{6,4},{7,5},{8,10},{9,11},{10,... | collective-permute-start | bytes 393224 | tf_op jit(solution)/shard_map/ppermute | solution.py:167
  77.2 4.2 %collective-permute-done.12 = f32[128,256]{0,1:T(8,128)S(1)} collective-permute-done((f32[128,256]{0,1:T(8,128)S(1)}, f32[128,256]{0,1:T(8,128)S(1)}, u32[]{:S(2)}, u32[]{:S(2)}) %collective-permute-start.12) | collective-permute-done | bytes 131104 | tf_op jit(solution)/shard_map/ppermute | solution.py:167
  81.5 1.9 %collective-permute-done.6 = f32[128,256]{0,1:T(8,128)S(1)} collective-permute-done((f32[128,256]{0,1:T(8,128)S(1)}, f32[128,256]{0,1:T(8,128)S(1)}, u32[]{:S(2)}, u32[]{:S(2)}) %collective-permute-start.6) | collective-permute-done | bytes 131104 | tf_op jit(solution)/shard_map/ppermute | solution.py:167
  83.7 4.0 %collective-permute-done.13 = f32[128,256]{0,1:T(8,128)S(1)} collective-permute-done((f32[128,256]{0,1:T(8,128)S(1)}, f32[128,256]{0,1:T(8,128)S(1)}, u32[]{:S(2)}, u32[]{:S(2)}) %collective-permute-start.13) | collective-permute-done | bytes 131104 | tf_op jit(solution)/shard_map/ppermute | solution.py:167
  87.8 2.9 %collective-permute-done.7 = f32[128,256]{0,1:T(8,128)S(1)} collective-permute-done((f32[128,256]{0,1:T(8,128)S(1)}, f32[128,256]{0,1:T(8,128)S(1)}, u32[]{:S(2)}, u32[]{:S(2)}) %collective-permute-start.7) | collective-permute-done | bytes 131104 | tf_op jit(solution)/shard_map/ppermute | solution.py:167
  90.7 0.8 collective-permute-start.8
  91.5 6.8 %collective-permute-done.14 = f32[128,256]{0,1:T(8,128)S(1)} collective-permute-done((f32[128,256]{0,1:T(8,128)S(1)}, f32[128,256]{0,1:T(8,128)S(1)}, u32[]{:S(2)}, u32[]{:S(2)}) %collective-permute-start.14) | collective-permute-done | bytes 131104 | tf_op jit(solution)/shard_map/ppermute | solution.py:167
  98.4 0.8 copy.7
  99.1 0.7 collective-permute-done.8
  99.9 0.8 copy.6
  (40 shorter events, 2.5 us)
Async XLA Ops:
  0.6 6.9 %copy-start.8 = (f32[8,16,32]{2,1,0:T(8,128)S(1)}, f32[8,16,32]{2,1,0:T(8,128)}, u32[]{:S(2)}) copy-start(f32[8,16,32]{2,1,0:T(8,128)} %param.3) | copy-start | bytes 49156
  2.0 19.3 %collective-permute-start = (bf16[4,16,32,128]{3,2,1,0:T(8,128)(2,1)S(1)}, bf16[4,16,32,128]{3,2,1,0:T(8,128)(2,1)S(1)}, u32[]{:S(2)}, u32[]{:S(2)}) collective-permute-start(bf16[4,16,32,128]{3,2,1,0:T(8,128)(2,1)S(1)} %get-tuple-element.19), channel_id=1, source_target_pairs={{0,1},{1,2},{2,3},{3,4},{4,5},{5,6},{6,7},{7,8},{8,9},{9,10},{10,1... | collective-permute-start | bytes 1572872 | tf_op jit(solution)/shard_map/ppermute | solution.py:159
  2.5 18.8 %collective-permute-start.1 = (bf16[4,16,32,128]{3,2,1,0:T(8,128)(2,1)S(1)}, bf16[4,16,32,128]{3,2,1,0:T(8,128)(2,1)S(1)}, u32[]{:S(2)}, u32[]{:S(2)}) collective-permute-start(bf16[4,16,32,128]{3,2,1,0:T(8,128)(2,1)S(1)} %get-tuple-element.18), channel_id=1, source_target_pairs={{1,0},{2,1},{3,2},{4,3},{5,4},{6,5},{7,6},{8,7},{9,8},{10,9},{11,1... | collective-permute-start | bytes 1572872 | tf_op jit(solution)/shard_map/ppermute | solution.py:159
  21.2 0.8 copy-start.2
  22.0 0.8 copy-start.3
  26.9 17.4 %collective-permute-start.2 = (bf16[4,16,32,128]{3,2,1,0:T(8,128)(2,1)}, bf16[4,16,32,128]{3,2,1,0:T(8,128)(2,1)S(1)}, u32[]{:S(2)}, u32[]{:S(2)}) collective-permute-start(bf16[4,16,32,128]{3,2,1,0:T(8,128)(2,1)} %get-tuple-element.9), channel_id=1, source_target_pairs={{0,1},{1,2},{2,3},{3,4},{4,5},{5,6},{6,7},{7,8},{8,9},{9,10},{10,1... | collective-permute-start | bytes 1572872 | tf_op jit(solution)/shard_map/ppermute | solution.py:159
  26.9 17.4 %collective-permute-start.3 = (bf16[4,16,32,128]{3,2,1,0:T(8,128)(2,1)}, bf16[4,16,32,128]{3,2,1,0:T(8,128)(2,1)S(1)}, u32[]{:S(2)}, u32[]{:S(2)}) collective-permute-start(bf16[4,16,32,128]{3,2,1,0:T(8,128)(2,1)} %get-tuple-element.10), channel_id=1, source_target_pairs={{1,0},{2,1},{3,2},{4,3},{5,4},{6,5},{7,6},{8,7},{9,8},{10,9},{11,1... | collective-permute-start | bytes 1572872 | tf_op jit(solution)/shard_map/ppermute | solution.py:159
  44.3 0.8 copy-start.6
  45.1 0.8 copy-start.7
  50.3 15.3 %copy-start = (bf16[8,16,32,128]{3,2,1,0:T(8,128)(2,1)S(1)}, bf16[8,16,32,128]{3,2,1,0:T(8,128)(2,1)}, u32[]{:S(2)}) copy-start(bf16[8,16,32,128]{3,2,1,0:T(8,128)(2,1)} %get-tuple-element.15.own_narrow) | copy-start | bytes 3145732
  50.3 22.8 %collective-permute-start.4 = (bf16[4096,128]{1,0:T(8,128)(2,1)}, bf16[4096,128]{1,0:T(8,128)(2,1)S(1)}, u32[]{:S(2)}, u32[]{:S(2)}) collective-permute-start(bf16[4096,128]{1,0:T(8,128)(2,1)} %bitcast.19), channel_id=1, source_target_pairs={{0,16},{16,0},{1,17},{17,1},{2,18},{18,2},{3,19},{19,3},{4,20},{20... | collective-permute-start | bytes 3145736 | tf_op jit(solution)/shard_map/ppermute | solution.py:195
  52.3 13.8 %collective-permute-start.10 = (bf16[4,16,32,128]{3,2,1,0:T(8,128)(2,1)}, bf16[4,16,32,128]{3,2,1,0:T(8,128)(2,1)S(1)}, u32[]{:S(2)}, u32[]{:S(2)}) collective-permute-start(bf16[4,16,32,128]{3,2,1,0:T(8,128)(2,1)} %get-tuple-element.14), channel_id=1, source_target_pairs={{1,0},{2,1},{3,2},{4,3},{5,4},{6,5},{7,6},{8,7},{9,8},{10,9},{11,1... | collective-permute-start | bytes 1572872 | tf_op jit(solution)/shard_map/ppermute | solution.py:159
  52.3 13.8 %collective-permute-start.9 = (bf16[4,16,32,128]{3,2,1,0:T(8,128)(2,1)}, bf16[4,16,32,128]{3,2,1,0:T(8,128)(2,1)S(1)}, u32[]{:S(2)}, u32[]{:S(2)}) collective-permute-start(bf16[4,16,32,128]{3,2,1,0:T(8,128)(2,1)} %get-tuple-element.13), channel_id=1, source_target_pairs={{0,1},{1,2},{2,3},{3,4},{4,5},{5,6},{6,7},{7,8},{8,9},{9,10},{10,1... | collective-permute-start | bytes 1572872 | tf_op jit(solution)/shard_map/ppermute | solution.py:159
  66.1 0.8 copy-start.4
  66.9 0.8 copy-start.5
  71.3 1.8 %copy-start.1 = (bf16[8,16,32,128]{3,2,1,0:T(8,128)(2,1)S(1)}, bf16[8,16,32,128]{3,2,1,0:T(8,128)(2,1)}, u32[]{:S(2)}) copy-start(bf16[8,16,32,128]{3,2,1,0:T(8,128)(2,1)} %finish_applied.1) | copy-start | bytes 3145732
  73.6 1.4 %collective-permute-start.11 = (f32[128,256]{0,1:T(8,128)S(1)}, f32[128,256]{0,1:T(8,128)S(1)}, u32[]{:S(2)}, u32[]{:S(2)}) collective-permute-start(f32[128,256]{0,1:T(8,128)S(1)} %maximum_select_fusion.1), channel_id=1, source_target_pairs={{0,1},{1,0},{2,3},{3,2},{4,5},{5,4},{6,7},{7,6},{8,9},{9,8},{10,11... | collective-permute-start | bytes 393224 | tf_op jit(solution)/shard_map/ppermute | solution.py:167
  74.2 1.5 %collective-permute-start.5 = (f32[128,256]{0,1:T(8,128)S(1)}, f32[128,256]{0,1:T(8,128)S(1)}, u32[]{:S(2)}, u32[]{:S(2)}) collective-permute-start(f32[128,256]{0,1:T(8,128)S(1)} %maximum_select_fusion), channel_id=1, source_target_pairs={{0,1},{1,0},{2,3},{3,2},{4,5},{5,4},{6,7},{7,6},{8,9},{9,8},{10,11... | collective-permute-start | bytes 393224 | tf_op jit(solution)/shard_map/ppermute | solution.py:167
  75.0 6.4 %collective-permute-start.12 = (f32[128,256]{0,1:T(8,128)S(1)}, f32[128,256]{0,1:T(8,128)S(1)}, u32[]{:S(2)}, u32[]{:S(2)}) collective-permute-start(f32[128,256]{0,1:T(8,128)S(1)} %add.28), channel_id=1, source_target_pairs={{0,2},{1,3},{2,0},{3,1},{4,6},{5,7},{6,4},{7,5},{8,10},{9,11},{10,... | collective-permute-start | bytes 393224 | tf_op jit(solution)/shard_map/ppermute | solution.py:167
  75.8 7.7 %collective-permute-start.6 = (f32[128,256]{0,1:T(8,128)S(1)}, f32[128,256]{0,1:T(8,128)S(1)}, u32[]{:S(2)}, u32[]{:S(2)}) collective-permute-start(f32[128,256]{0,1:T(8,128)S(1)} %add.24), channel_id=1, source_target_pairs={{0,2},{1,3},{2,0},{3,1},{4,6},{5,7},{6,4},{7,5},{8,10},{9,11},{10,... | collective-permute-start | bytes 393224 | tf_op jit(solution)/shard_map/ppermute | solution.py:167
  81.5 6.2 %collective-permute-start.13 = (f32[128,256]{0,1:T(8,128)S(1)}, f32[128,256]{0,1:T(8,128)S(1)}, u32[]{:S(2)}, u32[]{:S(2)}) collective-permute-start(f32[128,256]{0,1:T(8,128)S(1)} %add.29), channel_id=1, source_target_pairs={{0,4},{1,5},{2,6},{3,7},{4,0},{5,1},{6,2},{7,3},{8,12},{9,13},{10,... | collective-permute-start | bytes 393224 | tf_op jit(solution)/shard_map/ppermute | solution.py:167
  83.5 7.2 %collective-permute-start.7 = (f32[128,256]{0,1:T(8,128)S(1)}, f32[128,256]{0,1:T(8,128)S(1)}, u32[]{:S(2)}, u32[]{:S(2)}) collective-permute-start(f32[128,256]{0,1:T(8,128)S(1)} %add.25), channel_id=1, source_target_pairs={{0,4},{1,5},{2,6},{3,7},{4,0},{5,1},{6,2},{7,3},{8,12},{9,13},{10,... | collective-permute-start | bytes 393224 | tf_op jit(solution)/shard_map/ppermute | solution.py:167
  87.7 10.7 %collective-permute-start.14 = (f32[128,256]{0,1:T(8,128)S(1)}, f32[128,256]{0,1:T(8,128)S(1)}, u32[]{:S(2)}, u32[]{:S(2)}) collective-permute-start(f32[128,256]{0,1:T(8,128)S(1)} %add.30), channel_id=1, source_target_pairs={{0,8},{1,9},{2,10},{3,11},{4,12},{5,13},{6,14},{7,15},{8,0},{9,1},... | collective-permute-start | bytes 393224 | tf_op jit(solution)/shard_map/ppermute | solution.py:167
  90.7 9.1 %collective-permute-start.8 = (f32[128,256]{0,1:T(8,128)S(1)}, f32[128,256]{0,1:T(8,128)S(1)}, u32[]{:S(2)}, u32[]{:S(2)}) collective-permute-start(f32[128,256]{0,1:T(8,128)S(1)} %add.26), channel_id=1, source_target_pairs={{0,8},{1,9},{2,10},{3,11},{4,12},{5,13},{6,14},{7,15},{8,0},{9,1},... | collective-permute-start | bytes 393224 | tf_op jit(solution)/shard_map/ppermute | solution.py:167

commit v12 on v10

--- a/solution.py
+++ b/solution.py
@@ -154,6 +154,137 @@
     return lax.ppermute(sends[0], axis, forward), lax.ppermute(sends[1], axis, backward)
 
 
+def interior_halves_kernel(stage, planes, ny, nz, parts):
+    shift = 0.0 if stage == "applied" else spectrum_centre
+    blocks, depth = plane_blocks(planes)
+
+    def kernel(*refs):
+        narrow = refs[:parts]
+        pot, out, own = refs[parts:]
+        step = pl.program_id(0)
+
+        @pl.when(step == 0)
+        def _():
+            for x in range(planes):
+                if parts == 1:
+                    own[x] = narrow[0][x].astype(jnp.float32)
+                else:
+                    own[x] = narrow[x // depth][x % depth].astype(jnp.float32)
+
+        for block in range(blocks):
+            @pl.when(step == block)
+            def _(block=block):
+                for j in range(depth):
+                    x = block * depth + j
+
+                    def row(y, carry, x=x, j=j):
+                        centre = own[x, y]
+                        summed = (3.0 * stencil_weights[0]) * centre
+                        for k in range(1, RADIUS + 1):
+                            beside = own[x, (y + k) % ny] + own[x, (y + ny - k) % ny]
+                            beside = beside + (
+                                pltpu.roll(centre, k, 0) + pltpu.roll(centre, nz - k, 0)
+                            )
+                            if x + k < planes:
+                                beside = beside + own[x + k, y]
+                            if x - k >= 0:
+                                beside = beside + own[x - k, y]
+                            summed = summed + stencil_weights[k] * beside
+                        applied = -0.5 * summed + pot[j, y] * centre
+                        if shift:
+                            applied = applied - shift * centre
+                        out[j, y] = applied
+                        return carry
+
+                    lax.fori_loop(0, ny, row, 0)
+
+    return kernel
+
+
+def finish_half_kernel(stage, planes, ny, half):
+    def kernel(*refs):
+        halo, partial = refs[:2]
+        initial = refs[2] if stage == "filtered" else None
+        out = refs[-1]
+        for j in range(RADIUS):
+            x = half * RADIUS + j
+
+            def row(y, carry, x=x, j=j):
+                summed = partial[j, y]
+                for k in range(1, RADIUS + 1):
+                    if x + k >= planes:
+                        summed = summed + (-0.5 * stencil_weights[k]) * halo[
+                            x + k - planes, y
+                        ].astype(jnp.float32)
+                    if x - k < 0:
+                        summed = summed + (-0.5 * stencil_weights[k]) * halo[
+                            x - k + RADIUS, y
+                        ].astype(jnp.float32)
+                if stage == "first":
+                    result = summed * first_factor
+                elif stage == "filtered":
+                    result = summed * second_factor + (
+                        memory_factor * initial[j, y].astype(jnp.float32)
+                    )
+                else:
+                    result = summed
+                out[j, y] = result.astype(out.dtype)
+                return carry
+
+            lax.fori_loop(0, ny, row, 0)
+
+    return kernel
+
+
+def stencil_halves(stage, halves, potential_wide, initial=None):
+    parts = len(halves)
+    if parts == 1:
+        planes, ny, nz, nb = halves[0].shape
+        lower = lax.slice_in_dim(halves[0], 0, RADIUS, axis=0)
+        upper = lax.slice_in_dim(halves[0], RADIUS, None, axis=0)
+    else:
+        lower, upper = halves
+        ny, nz, nb = lower.shape[1:]
+        planes = 2 * RADIUS
+    blocks, depth = plane_blocks(planes)
+    count = lax.axis_size("domain")
+    forward = [(i, (i + 1) % count) for i in range(count)]
+    backward = [(target, source) for source, target in forward]
+    below = lax.ppermute(upper, "domain", forward)
+    above = lax.ppermute(lower, "domain", backward)
+    part = pl.BlockSpec((depth, ny, nz, nb), lambda i: (i, 0, 0, 0))
+    narrow_specs = [pl.BlockSpec(h.shape, lambda i: (0, 0, 0, 0)) for h in halves]
+    partial = pl.pallas_call(
+        interior_halves_kernel(stage, planes, ny, nz, parts),
+        grid=(blocks,),
+        in_specs=narrow_specs + [part],
+        out_specs=part,
+        out_shape=jax.ShapeDtypeStruct((planes, ny, nz, nb), jnp.float32),
+        scratch_shapes=[pltpu.VMEM((planes, ny, nz, nb), jnp.float32)],
+        name=f"interior_{stage}",
+    )(*halves, potential_wide)
+    results = []
+    for half, halo in ((0, below), (1, above)):
+        chosen = pl.BlockSpec((RADIUS, ny, nz, nb), lambda i, half=half: (half, 0, 0, 0))
+        edge = pl.BlockSpec((RADIUS, ny, nz, nb), lambda i: (0, 0, 0, 0))
+        operands = [halo, partial]
+        in_specs = [edge, chosen]
+        if initial is not None:
+            operands.append(initial)
+            in_specs.append(chosen)
+        results.append(
+            pl.pallas_call(
+                finish_half_kernel(stage, planes, ny, half),
+                grid=(1,),
+                in_specs=in_specs,
+                out_specs=edge,
+                out_shape=jax.ShapeDtypeStruct((RADIUS, ny, nz, nb), jnp.bfloat16),
+                name=f"finish_{stage}_{half}",
+            )(*operands)
+        )
+    return results
+
+
 def butterfly_sum(values, axis):
     count = lax.axis_size(axis)
     bit = 1
@@ -178,21 +309,31 @@
         jnp.concatenate([mine, theirs], axis=1),
         jnp.concatenate([theirs, mine], axis=1),
     )
-    planes_sent = (
-        lax.slice_in_dim(orbitals, planes - RADIUS, None, axis=0),
-        lax.slice_in_dim(orbitals, 0, RADIUS, axis=0),
-    )
-    first, *first_sent = stencil_stage("first", orbitals, planes_sent, potential_wide)
-    filtered, *filtered_sent = stencil_stage(
-        "filtered", first, first_sent, potential_wide, orbitals
-    )
+    if planes == 2 * RADIUS:
+        first_halves = stencil_halves("first", [orbitals], potential_wide)
+        filtered_halves = stencil_halves("filtered", first_halves, potential_wide, orbitals)
+        filtered = jnp.concatenate(filtered_halves, axis=0)
+    else:
+        planes_sent = (
+            lax.slice_in_dim(orbitals, planes - RADIUS, None, axis=0),
+            lax.slice_in_dim(orbitals, 0, RADIUS, axis=0),
+        )
+        first, *first_sent = stencil_stage("first", orbitals, planes_sent, potential_wide)
+        filtered, *filtered_sent = stencil_stage(
+            "filtered", first, first_sent, potential_wide, orbitals
+        )
     own_block = filtered.reshape(cell_count, nb)
     partner = lax.ppermute(own_block, "band", [(0, 1), (1, 0)])
     correlation_piece = placed(gram(own_block, own_block), gram(own_block, partner))
     correlation = butterfly_sum(correlation_piece, "domain") * cell_weight
-    (applied_grid,) = stencil_stage(
-        "applied", filtered, filtered_sent, potential_wide, keep_sends=False
-    )
+    if planes == 2 * RADIUS:
+        applied_grid = jnp.concatenate(
+            stencil_halves("applied", filtered_halves, potential_wide), axis=0
+        )
+    else:
+        (applied_grid,) = stencil_stage(
+            "applied", filtered, filtered_sent, potential_wide, keep_sends=False
+        )
     applied = applied_grid.reshape(cell_count, nb)
     energy_piece = placed(gram(applied, own_block), gram(applied, partner))
     projected = butterfly_sum(energy_piece, "domain") * cell_weight

time: 95.1 us -> 97 us (1.020)
  Pallas kernels: 34.5 us -> 39.9 us
  waiting for transfers between devices: 23.6 us -> 19.5 us
  other arithmetic: 0.15 us -> 2.56 us
  matrix products: 3.22 us -> 1.93 us
    pallas_call x6 -> x9, Pallas kernels: 34.5 us -> 39.9 us  [the longest x3 22.3 us: stencil_halves(): pl.pallas_call(interior_halves_kernel(stage, planes, ny, nz, parts), grid...]
    ppermute x6, waiting for transfers between devices: 3.32 us -> 0.02 us  [the longest x3 0.01 us: stencil_halves(): above = lax.ppermute(lower, 'domain', backward)]
    concatenate x0 -> x2, other arithmetic: none -> 2.41 us  [the longest x1 1.21 us: shards(): filtered = jnp.concatenate(filtered_halves, axis=0)]
    ppermute x8, waiting for transfers between devices: 20 us -> 18.6 us  [butterfly_sum(): values = values + lax.ppermute(values, axis, pairs)]
    dot_general x4, matrix products: 3.22 us -> 1.93 us  [shards(): jnp.einsum('cb,ck->bk', rows, cols, preferred_element_type=jnp.float32)]
    ppermute x6, starting transfers between devices: 13.4 us -> 14.4 us  [the longest x3 14.3 us: stencil_halves(): above = lax.ppermute(lower, 'domain', backward)]
    unnamed x20 -> x22, local copies, waits for them, and re-layouts: 5.52 us -> 4.7 us
  transfers between devices with their start and end apart: 15 -> 15, of which waited for: 10 -> 9; matrix products, arithmetic and copies ran while one was open for 6% -> 6% of each run, Pallas kernels for 27% -> 38%
where the time goes in v12:
time: 97 us; the launch traced here: 96.6 us
  Pallas kernels  39.9 us (41%)
  starting transfers between devices  24 us (25%)
  waiting for transfers between devices  19.5 us (20%)
  local copies, waits for them, and re-layouts  7.98 us (8%)
  other arithmetic  2.56 us (3%)
  matrix products  1.93 us (2%)
    pallas_call x3, Pallas kernels, stencil_halves(): pl.pallas_call(interior_halves_kernel(stage, planes, ny, nz, parts), grid...  22.3 us
    ppermute x8, waiting for transfers between devices, butterfly_sum(): values = values + lax.ppermute(values, axis, pairs)  18.6 us
    pallas_call x6, Pallas kernels, stencil_halves(): pl.pallas_call(finish_half_kernel(stage, planes, ny, half), grid=(1,), in...  17.6 us
    ppermute x3, starting transfers between devices, stencil_halves(): above = lax.ppermute(lower, 'domain', backward)  14.3 us
    ppermute x8, starting transfers between devices, butterfly_sum(): values = values + lax.ppermute(values, axis, pairs)  8.06 us
    unnamed x22, local copies, waits for them, and re-layouts  4.7 us
    broadcast_in_dim x1, local copies, waits for them, and re-layouts, shards(): jnp.broadcast_to(potential[:, :, :, None], (planes, ny, nz, nb))  1.94 us
  transfers between devices with their start and end apart: 15, of which 9 were waited for; matrix products, arithmetic and copies ran while one was open for 6% of the time, Pallas kernels for 38%

profile of v12, /device:TPU:0, one launch (start us, length us, event | category | flops | bytes accessed | tf_op | source)
XLA Modules:
  0.0 96.6 jit_solution(2626224326772643917)
XLA Ops:
  0.6 1.3 %fusion = (bf16[4,16,32,128]{3,2,1,0:T(8,128)(2,1)S(1)}, bf16[4,16,32,128]{3,2,1,0:T(8,128)(2,1)S(1)}) fusion(bf16[8,16,32,128]{3,2,1,0:T(8,128)(2,1)} %refs_2_.3), kind=kLoop, calls=%fused_computation.8 | loop fusion | bytes 2097152 | tf_op jit(solution)/shard_map/slice | solution.py:243
  2.0 5.5 %collective-permute-start = (bf16[4,16,32,128]{3,2,1,0:T(8,128)(2,1)S(1)}, bf16[4,16,32,128]{3,2,1,0:T(8,128)(2,1)S(1)}, u32[]{:S(2)}, u32[]{:S(2)}) collective-permute-start(bf16[4,16,32,128]{3,2,1,0:T(8,128)(2,1)S(1)} %get-tuple-element.6), channel_id=1, source_target_pairs={{1,0},{2,1},{3,2},{4,3},{5,4},{6,5},{7,6},{8,7},{9,8},{10,9},{11,1... | collective-permute-start | bytes 1572872 | tf_op jit(solution)/shard_map/ppermute | solution.py:254
  7.5 1.9 %broadcast_in_dim.2.refs_1_.refs_2_ = f32[8,16,32,128]{3,2,1,0:T(8,128)} broadcast(f32[8,16,32]{2,1,0:T(8,128)S(1)} %copy-done.9), dimensions={0,1,2} | broadcast | bytes 2113536 | tf_op jit(solution)/shard_map/broadcast_in_dim | solution.py:300
  9.4 7.5 %interior_first.1.refs_1_ = f32[8,16,32,128]{3,2,1,0:T(8,128)} custom-call(bf16[8,16,32,128]{3,2,1,0:T(8,128)(2,1)} %refs_2_.3, f32[8,16,32,128]{3,2,1,0:T(8,128)} %broadcast_in_dim.2.refs_1_.refs_2_), custom_call_target="tpu_custom_call" | custom-call | tf_op jit(solution)/shard_map/interior_first/pallas_call | solution.py:257
  16.9 0.8 copy-done.6
  17.7 2.9 %finish_first_1.1.refs_1_ = bf16[4,16,32,128]{3,2,1,0:T(8,128)(2,1)} custom-call(bf16[4,16,32,128]{3,2,1,0:T(8,128)(2,1)} %copy-done.6, f32[8,16,32,128]{3,2,1,0:T(8,128)} %interior_first.1.refs_1_), custom_call_target="tpu_custom_call" | custom-call | tf_op jit(solution)/shard_map/finish_first_1/pallas_call | solution.py:276
  20.6 0.8 copy-done.5
  21.4 2.9 %finish_first_0.1.refs_0_ = bf16[4,16,32,128]{3,2,1,0:T(8,128)(2,1)} custom-call(bf16[4,16,32,128]{3,2,1,0:T(8,128)(2,1)} %copy-done.5, f32[8,16,32,128]{3,2,1,0:T(8,128)} %interior_first.1.refs_1_), custom_call_target="tpu_custom_call" | custom-call | tf_op jit(solution)/shard_map/finish_first_0/pallas_call | solution.py:276
  24.2 4.4 %collective-permute-start.3 = (bf16[4,16,32,128]{3,2,1,0:T(8,128)(2,1)}, bf16[4,16,32,128]{3,2,1,0:T(8,128)(2,1)S(1)}, u32[]{:S(2)}, u32[]{:S(2)}) collective-permute-start(bf16[4,16,32,128]{3,2,1,0:T(8,128)(2,1)} %finish_first_0.1.refs_0_), channel_id=1, source_target_pairs={{1,0},{2,1},{3,2},{4,3},{5,4},{6,5},{7,6},{8,7},{9,8},{10,9},{11,1... | collective-permute-start | bytes 1572872 | tf_op jit(solution)/shard_map/ppermute | solution.py:254
  28.7 7.5 %interior_filtered.1.refs_1_ = f32[8,16,32,128]{3,2,1,0:T(8,128)} custom-call(bf16[4,16,32,128]{3,2,1,0:T(8,128)(2,1)} %finish_first_0.1.refs_0_, bf16[4,16,32,128]{3,2,1,0:T(8,128)(2,1)} %finish_first_1.1.refs_1_, f32[8,16,32,128]{3,2,1,0:T(8,128)} %broadcast_in_dim.2.refs_1_.refs_2_), custom_call_target="tpu_custom_call" | custom-call | tf_op jit(solution)/shard_map/interior_filtered/pallas_call | solution.py:257
  36.2 0.8 copy-done.7
  36.9 3.1 %finish_filtered_0.1.refs_0_ = bf16[4,16,32,128]{3,2,1,0:T(8,128)(2,1)} custom-call(bf16[4,16,32,128]{3,2,1,0:T(8,128)(2,1)} %copy-done.7, f32[8,16,32,128]{3,2,1,0:T(8,128)} %interior_filtered.1.refs_1_, bf16[8,16,32,128]{3,2,1,0:T(8,128)(2,1)} %refs_2_.3), custom_call_target="tpu_custom_call" | custom-call | tf_op jit(solution)/shard_map/finish_filtered_0/pallas_call | solution.py:276
  40.1 0.8 copy-done.8
  40.8 3.1 %finish_filtered_1.1.refs_1_ = bf16[4,16,32,128]{3,2,1,0:T(8,128)(2,1)} custom-call(bf16[4,16,32,128]{3,2,1,0:T(8,128)(2,1)} %copy-done.8, f32[8,16,32,128]{3,2,1,0:T(8,128)} %interior_filtered.1.refs_1_, bf16[8,16,32,128]{3,2,1,0:T(8,128)(2,1)} %refs_2_.3), custom_call_target="tpu_custom_call" | custom-call | tf_op jit(solution)/shard_map/finish_filtered_1/pallas_call | solution.py:276
  43.9 1.2 %pad_maximum_fusion = bf16[8,16,32,128]{3,2,1,0:T(8,128)(2,1)S(1)} fusion(bf16[4,16,32,128]{3,2,1,0:T(8,128)(2,1)} %finish_filtered_1.1.refs_1_, bf16[4,16,32,128]{3,2,1,0:T(8,128)(2,1)S(1)} %copy-done.1), kind=kLoop, calls=%fused_computation.2 | loop fusion | flops 524288 | bytes 2097152 | tf_op jit(solution)/shard_map/concatenate | solution.py:315
  45.2 1.6 %collective-permute-start.4 = (bf16[4096,128]{1,0:T(8,128)(2,1)S(1)}, bf16[4096,128]{1,0:T(8,128)(2,1)S(1)}, u32[]{:S(2)}, u32[]{:S(2)}) collective-permute-start(bf16[4096,128]{1,0:T(8,128)(2,1)S(1)} %bitcast.17), channel_id=1, source_target_pairs={{0,16},{16,0},{1,17},{17,1},{2,18},{18,2},{3,19},{19,3},{4,20},{20... | collective-permute-start | bytes 3145736 | tf_op jit(solution)/shard_map/ppermute | solution.py:326
  46.7 4.4 %collective-permute-start.10 = (bf16[4,16,32,128]{3,2,1,0:T(8,128)(2,1)S(1)}, bf16[4,16,32,128]{3,2,1,0:T(8,128)(2,1)}, u32[]{:S(2)}, u32[]{:S(2)}) collective-permute-start(bf16[4,16,32,128]{3,2,1,0:T(8,128)(2,1)S(1)} %copy-done.1), channel_id=1, source_target_pairs={{1,0},{2,1},{3,2},{4,3},{5,4},{6,5},{7,6},{8,7},{9,8},{10,9},{11,1... | collective-permute-start | bytes 1572872 | tf_op jit(solution)/shard_map/ppermute | solution.py:254
  51.2 7.3 %interior_applied.1.refs_1_ = f32[8,16,32,128]{3,2,1,0:T(8,128)} custom-call(bf16[4,16,32,128]{3,2,1,0:T(8,128)(2,1)} %finish_filtered_0.1.refs_0_, bf16[4,16,32,128]{3,2,1,0:T(8,128)(2,1)} %finish_filtered_1.1.refs_1_, f32[8,16,32,128]{3,2,1,0:T(8,128)} %broadcast_in_dim.2.refs_1_.refs_2_), custom_call_target="tpu_custom_call" | custom-call | tf_op jit(solution)/shard_map/interior_applied/pallas_call | solution.py:257
  59.0 2.8 %finish_applied_0.1 = bf16[4,16,32,128]{3,2,1,0:T(8,128)(2,1)} custom-call(bf16[4,16,32,128]{3,2,1,0:T(8,128)(2,1)} %collective-permute-done.9.refs_0_, f32[8,16,32,128]{3,2,1,0:T(8,128)} %interior_applied.1.refs_1_), custom_call_target="tpu_custom_call" | custom-call | tf_op jit(solution)/shard_map/finish_applied_0/pallas_call | solution.py:276
  61.8 2.9 %finish_applied_1.1 = bf16[4,16,32,128]{3,2,1,0:T(8,128)(2,1)} custom-call(bf16[4,16,32,128]{3,2,1,0:T(8,128)(2,1)} %collective-permute-done.10.refs_0_, f32[8,16,32,128]{3,2,1,0:T(8,128)} %interior_applied.1.refs_1_), custom_call_target="tpu_custom_call" | custom-call | tf_op jit(solution)/shard_map/finish_applied_1/pallas_call | solution.py:276
  64.7 1.2 %pad_maximum_fusion.1 = bf16[8,16,32,128]{3,2,1,0:T(8,128)(2,1)S(1)} fusion(bf16[4,16,32,128]{3,2,1,0:T(8,128)(2,1)} %finish_applied_1.1, bf16[4,16,32,128]{3,2,1,0:T(8,128)(2,1)S(1)} %copy-done.3), kind=kLoop, calls=%fused_computation.3 | loop fusion | flops 524288 | bytes 2097152 | tf_op jit(solution)/shard_map/concatenate | solution.py:330
  66.4 0.9 collective-permute-done.4
  69.9 1.5 %collective-permute-start.6 = (f32[128,256]{0,1:T(8,128)S(1)}, f32[128,256]{0,1:T(8,128)S(1)}, u32[]{:S(2)}, u32[]{:S(2)}) collective-permute-start(f32[128,256]{0,1:T(8,128)S(1)} %add.24), channel_id=1, source_target_pairs={{0,2},{1,3},{2,0},{3,1},{4,6},{5,7},{6,4},{7,5},{8,10},{9,11},{10,... | collective-permute-start | bytes 393224 | tf_op jit(solution)/shard_map/ppermute | solution.py:293
  71.4 4.2 %collective-permute-done.12 = f32[128,256]{0,1:T(8,128)S(1)} collective-permute-done((f32[128,256]{0,1:T(8,128)S(1)}, f32[128,256]{0,1:T(8,128)S(1)}, u32[]{:S(2)}, u32[]{:S(2)}) %collective-permute-start.12) | collective-permute-done | bytes 131104 | tf_op jit(solution)/shard_map/ppermute | solution.py:293
  75.6 1.4 %collective-permute-start.13 = (f32[128,256]{0,1:T(8,128)S(1)}, f32[128,256]{0,1:T(8,128)S(1)}, u32[]{:S(2)}, u32[]{:S(2)}) collective-permute-start(f32[128,256]{0,1:T(8,128)S(1)} %add.29), channel_id=1, source_target_pairs={{0,4},{1,5},{2,6},{3,7},{4,0},{5,1},{6,2},{7,3},{8,12},{9,13},{10,... | collective-permute-start | bytes 393224 | tf_op jit(solution)/shard_map/ppermute | solution.py:293
  77.7 1.4 %collective-permute-start.7 = (f32[128,256]{0,1:T(8,128)S(1)}, f32[128,256]{0,1:T(8,128)S(1)}, u32[]{:S(2)}, u32[]{:S(2)}) collective-permute-start(f32[128,256]{0,1:T(8,128)S(1)} %add.25), channel_id=1, source_target_pairs={{0,4},{1,5},{2,6},{3,7},{4,0},{5,1},{6,2},{7,3},{8,12},{9,13},{10,... | collective-permute-start | bytes 393224 | tf_op jit(solution)/shard_map/ppermute | solution.py:293
  79.1 4.2 %collective-permute-done.13 = f32[128,256]{0,1:T(8,128)S(1)} collective-permute-done((f32[128,256]{0,1:T(8,128)S(1)}, f32[128,256]{0,1:T(8,128)S(1)}, u32[]{:S(2)}, u32[]{:S(2)}) %collective-permute-start.13) | collective-permute-done | bytes 131104 | tf_op jit(solution)/shard_map/ppermute | solution.py:293
  83.2 1.0 %collective-permute-start.14 = (f32[128,256]{0,1:T(8,128)S(1)}, f32[128,256]{0,1:T(8,128)S(1)}, u32[]{:S(2)}, u32[]{:S(2)}) collective-permute-start(f32[128,256]{0,1:T(8,128)S(1)} %add.30), channel_id=1, source_target_pairs={{0,8},{1,9},{2,10},{3,11},{4,12},{5,13},{6,14},{7,15},{8,0},{9,1},... | collective-permute-start | bytes 393224 | tf_op jit(solution)/shard_map/ppermute | solution.py:293
  84.9 2.1 %collective-permute-start.8 = (f32[128,256]{0,1:T(8,128)S(1)}, f32[128,256]{0,1:T(8,128)S(1)}, u32[]{:S(2)}, u32[]{:S(2)}) collective-permute-start(f32[128,256]{0,1:T(8,128)S(1)} %add.26), channel_id=1, source_target_pairs={{0,8},{1,9},{2,10},{3,11},{4,12},{5,13},{6,14},{7,15},{8,0},{9,1},... | collective-permute-start | bytes 393224 | tf_op jit(solution)/shard_map/ppermute | solution.py:293
  87.0 7.4 %collective-permute-done.14 = f32[128,256]{0,1:T(8,128)S(1)} collective-permute-done((f32[128,256]{0,1:T(8,128)S(1)}, f32[128,256]{0,1:T(8,128)S(1)}, u32[]{:S(2)}, u32[]{:S(2)}) %collective-permute-start.14) | collective-permute-done | bytes 131104 | tf_op jit(solution)/shard_map/ppermute | solution.py:293
  94.5 0.8 copy.6
  95.9 0.8 copy.5
  (47 shorter events, 5.6 us)
Async XLA Ops:
  0.6 6.8 %copy-start.9 = (f32[8,16,32]{2,1,0:T(8,128)S(1)}, f32[8,16,32]{2,1,0:T(8,128)}, u32[]{:S(2)}) copy-start(f32[8,16,32]{2,1,0:T(8,128)} %param.3) | copy-start | bytes 49156
  2.0 14.9 %collective-permute-start = (bf16[4,16,32,128]{3,2,1,0:T(8,128)(2,1)S(1)}, bf16[4,16,32,128]{3,2,1,0:T(8,128)(2,1)S(1)}, u32[]{:S(2)}, u32[]{:S(2)}) collective-permute-start(bf16[4,16,32,128]{3,2,1,0:T(8,128)(2,1)S(1)} %get-tuple-element.6), channel_id=1, source_target_pairs={{1,0},{2,1},{3,2},{4,3},{5,4},{6,5},{7,6},{8,7},{9,8},{10,9},{11,1... | collective-permute-start | bytes 1572872 | tf_op jit(solution)/shard_map/ppermute | solution.py:254
  7.5 13.1 %collective-permute-start.2 = (bf16[4,16,32,128]{3,2,1,0:T(8,128)(2,1)S(1)}, bf16[4,16,32,128]{3,2,1,0:T(8,128)(2,1)S(1)}, u32[]{:S(2)}, u32[]{:S(2)}) collective-permute-start(bf16[4,16,32,128]{3,2,1,0:T(8,128)(2,1)S(1)} %get-tuple-element.7), channel_id=1, source_target_pairs={{0,1},{1,2},{2,3},{3,4},{4,5},{5,6},{6,7},{7,8},{8,9},{9,10},{10,1... | collective-permute-start | bytes 1572872 | tf_op jit(solution)/shard_map/ppermute | solution.py:253
  16.9 0.8 copy-start.6
  20.6 15.6 %collective-permute-start.1 = (bf16[4,16,32,128]{3,2,1,0:T(8,128)(2,1)}, bf16[4,16,32,128]{3,2,1,0:T(8,128)(2,1)S(1)}, u32[]{:S(2)}, u32[]{:S(2)}) collective-permute-start(bf16[4,16,32,128]{3,2,1,0:T(8,128)(2,1)} %finish_first_1.1.refs_1_), channel_id=1, source_target_pairs={{0,1},{1,2},{2,3},{3,4},{4,5},{5,6},{6,7},{7,8},{8,9},{9,10},{10,1... | collective-permute-start | bytes 1572872 | tf_op jit(solution)/shard_map/ppermute | solution.py:253
  20.6 0.8 copy-start.5
  24.2 15.8 %collective-permute-start.3 = (bf16[4,16,32,128]{3,2,1,0:T(8,128)(2,1)}, bf16[4,16,32,128]{3,2,1,0:T(8,128)(2,1)S(1)}, u32[]{:S(2)}, u32[]{:S(2)}) collective-permute-start(bf16[4,16,32,128]{3,2,1,0:T(8,128)(2,1)} %finish_first_0.1.refs_0_), channel_id=1, source_target_pairs={{1,0},{2,1},{3,2},{4,3},{5,4},{6,5},{7,6},{8,7},{9,8},{10,9},{11,1... | collective-permute-start | bytes 1572872 | tf_op jit(solution)/shard_map/ppermute | solution.py:254
  36.2 0.8 copy-start.7
  40.0 3.9 %copy-start.1 = (bf16[4,16,32,128]{3,2,1,0:T(8,128)(2,1)S(1)}, bf16[4,16,32,128]{3,2,1,0:T(8,128)(2,1)}, u32[]{:S(2)}) copy-start(bf16[4,16,32,128]{3,2,1,0:T(8,128)(2,1)} %finish_filtered_0.1.refs_0_) | copy-start | bytes 1572868
  40.0 0.8 copy-start.8
  43.9 2.8 %copy-start.2 = (bf16[4,16,32,128]{3,2,1,0:T(8,128)(2,1)S(1)}, bf16[4,16,32,128]{3,2,1,0:T(8,128)(2,1)}, u32[]{:S(2)}) copy-start(bf16[4,16,32,128]{3,2,1,0:T(8,128)(2,1)} %finish_filtered_1.1.refs_1_) | copy-start | bytes 1572868
  45.1 22.7 %copy-start = (bf16[8,16,32,128]{3,2,1,0:T(8,128)(2,1)}, bf16[8,16,32,128]{3,2,1,0:T(8,128)(2,1)S(1)}, u32[]{:S(2)}) copy-start(bf16[8,16,32,128]{3,2,1,0:T(8,128)(2,1)S(1)} %pad_maximum_fusion) | copy-start | bytes 3145732
  45.2 22.1 %collective-permute-start.4 = (bf16[4096,128]{1,0:T(8,128)(2,1)S(1)}, bf16[4096,128]{1,0:T(8,128)(2,1)S(1)}, u32[]{:S(2)}, u32[]{:S(2)}) collective-permute-start(bf16[4096,128]{1,0:T(8,128)(2,1)S(1)} %bitcast.17), channel_id=1, source_target_pairs={{0,16},{16,0},{1,17},{17,1},{2,18},{18,2},{3,19},{19,3},{4,20},{20... | collective-permute-start | bytes 3145736 | tf_op jit(solution)/shard_map/ppermute | solution.py:326
  46.7 12.2 %collective-permute-start.9 = (bf16[4,16,32,128]{3,2,1,0:T(8,128)(2,1)S(1)}, bf16[4,16,32,128]{3,2,1,0:T(8,128)(2,1)}, u32[]{:S(2)}, u32[]{:S(2)}) collective-permute-start(bf16[4,16,32,128]{3,2,1,0:T(8,128)(2,1)S(1)} %copy-done.2), channel_id=1, source_target_pairs={{0,1},{1,2},{2,3},{3,4},{4,5},{5,6},{6,7},{7,8},{8,9},{9,10},{10,1... | collective-permute-start | bytes 1572872 | tf_op jit(solution)/shard_map/ppermute | solution.py:253
  46.7 15.1 %collective-permute-start.10 = (bf16[4,16,32,128]{3,2,1,0:T(8,128)(2,1)S(1)}, bf16[4,16,32,128]{3,2,1,0:T(8,128)(2,1)}, u32[]{:S(2)}, u32[]{:S(2)}) collective-permute-start(bf16[4,16,32,128]{3,2,1,0:T(8,128)(2,1)S(1)} %copy-done.1), channel_id=1, source_target_pairs={{1,0},{2,1},{3,2},{4,3},{5,4},{6,5},{7,6},{8,7},{9,8},{10,9},{11,1... | collective-permute-start | bytes 1572872 | tf_op jit(solution)/shard_map/ppermute | solution.py:254
  61.8 2.9 %copy-start.3 = (bf16[4,16,32,128]{3,2,1,0:T(8,128)(2,1)S(1)}, bf16[4,16,32,128]{3,2,1,0:T(8,128)(2,1)}, u32[]{:S(2)}) copy-start(bf16[4,16,32,128]{3,2,1,0:T(8,128)(2,1)} %finish_applied_0.1) | copy-start | bytes 1572868
  64.7 1.2 %copy-start.4 = (bf16[4,16,32,128]{3,2,1,0:T(8,128)(2,1)S(1)}, bf16[4,16,32,128]{3,2,1,0:T(8,128)(2,1)}, u32[]{:S(2)}) copy-start(bf16[4,16,32,128]{3,2,1,0:T(8,128)(2,1)} %finish_applied_1.1) | copy-start | bytes 1572868
  67.8 1.4 %collective-permute-start.11 = (f32[128,256]{0,1:T(8,128)S(1)}, f32[128,256]{0,1:T(8,128)S(1)}, u32[]{:S(2)}, u32[]{:S(2)}) collective-permute-start(f32[128,256]{0,1:T(8,128)S(1)} %maximum_select_fusion.1), channel_id=1, source_target_pairs={{0,1},{1,0},{2,3},{3,2},{4,5},{5,4},{6,7},{7,6},{8,9},{9,8},{10,11... | collective-permute-start | bytes 393224 | tf_op jit(solution)/shard_map/ppermute | solution.py:293
  68.4 1.5 %collective-permute-start.5 = (f32[128,256]{0,1:T(8,128)S(1)}, f32[128,256]{0,1:T(8,128)S(1)}, u32[]{:S(2)}, u32[]{:S(2)}) collective-permute-start(f32[128,256]{0,1:T(8,128)S(1)} %maximum_select_fusion), channel_id=1, source_target_pairs={{0,1},{1,0},{2,3},{3,2},{4,5},{5,4},{6,7},{7,6},{8,9},{9,8},{10,11... | collective-permute-start | bytes 393224 | tf_op jit(solution)/shard_map/ppermute | solution.py:293
  69.2 6.4 %collective-permute-start.12 = (f32[128,256]{0,1:T(8,128)S(1)}, f32[128,256]{0,1:T(8,128)S(1)}, u32[]{:S(2)}, u32[]{:S(2)}) collective-permute-start(f32[128,256]{0,1:T(8,128)S(1)} %add.28), channel_id=1, source_target_pairs={{0,2},{1,3},{2,0},{3,1},{4,6},{5,7},{6,4},{7,5},{8,10},{9,11},{10,... | collective-permute-start | bytes 393224 | tf_op jit(solution)/shard_map/ppermute | solution.py:293
  69.9 7.7 %collective-permute-start.6 = (f32[128,256]{0,1:T(8,128)S(1)}, f32[128,256]{0,1:T(8,128)S(1)}, u32[]{:S(2)}, u32[]{:S(2)}) collective-permute-start(f32[128,256]{0,1:T(8,128)S(1)} %add.24), channel_id=1, source_target_pairs={{0,2},{1,3},{2,0},{3,1},{4,6},{5,7},{6,4},{7,5},{8,10},{9,11},{10,... | collective-permute-start | bytes 393224 | tf_op jit(solution)/shard_map/ppermute | solution.py:293
  75.6 7.6 %collective-permute-start.13 = (f32[128,256]{0,1:T(8,128)S(1)}, f32[128,256]{0,1:T(8,128)S(1)}, u32[]{:S(2)}, u32[]{:S(2)}) collective-permute-start(f32[128,256]{0,1:T(8,128)S(1)} %add.29), channel_id=1, source_target_pairs={{0,4},{1,5},{2,6},{3,7},{4,0},{5,1},{6,2},{7,3},{8,12},{9,13},{10,... | collective-permute-start | bytes 393224 | tf_op jit(solution)/shard_map/ppermute | solution.py:293
  77.7 7.2 %collective-permute-start.7 = (f32[128,256]{0,1:T(8,128)S(1)}, f32[128,256]{0,1:T(8,128)S(1)}, u32[]{:S(2)}, u32[]{:S(2)}) collective-permute-start(f32[128,256]{0,1:T(8,128)S(1)} %add.25), channel_id=1, source_target_pairs={{0,4},{1,5},{2,6},{3,7},{4,0},{5,1},{6,2},{7,3},{8,12},{9,13},{10,... | collective-permute-start | bytes 393224 | tf_op jit(solution)/shard_map/ppermute | solution.py:293
  83.2 11.2 %collective-permute-start.14 = (f32[128,256]{0,1:T(8,128)S(1)}, f32[128,256]{0,1:T(8,128)S(1)}, u32[]{:S(2)}, u32[]{:S(2)}) collective-permute-start(f32[128,256]{0,1:T(8,128)S(1)} %add.30), channel_id=1, source_target_pairs={{0,8},{1,9},{2,10},{3,11},{4,12},{5,13},{6,14},{7,15},{8,0},{9,1},... | collective-permute-start | bytes 393224 | tf_op jit(solution)/shard_map/ppermute | solution.py:293
  84.9 11.0 %collective-permute-start.8 = (f32[128,256]{0,1:T(8,128)S(1)}, f32[128,256]{0,1:T(8,128)S(1)}, u32[]{:S(2)}, u32[]{:S(2)}) collective-permute-start(f32[128,256]{0,1:T(8,128)S(1)} %add.26), channel_id=1, source_target_pairs={{0,8},{1,9},{2,10},{3,11},{4,12},{5,13},{6,14},{7,15},{8,0},{9,1},... | collective-permute-start | bytes 393224 | tf_op jit(solution)/shard_map/ppermute | solution.py:293

commit v13 on v10

--- a/solution.py
+++ b/solution.py
@@ -66,9 +66,10 @@
 
     def kernel(*refs):
         refs = list(refs)
-        low, high, partial = refs[:3]
-        initial = refs[3] if stage == "filtered" else None
-        outs = refs[4:] if stage == "filtered" else refs[3:]
+        low, partial = refs[:2]
+        high = low
+        initial = refs[2] if stage == "filtered" else None
+        outs = refs[3:] if stage == "filtered" else refs[2:]
         out = outs[0]
         step = pl.program_id(0)
         for block in range(blocks):
@@ -113,6 +114,96 @@
 def stencil_stage(stage, block, sends, potential_wide, initial=None, keep_sends=True):
     planes, ny, nz, nb = block.shape
     blocks, depth = plane_blocks(planes)
+    if blocks < 2:
+        return stencil_stage_whole(stage, block, sends, potential_wide, initial, keep_sends)
+    whole = pl.BlockSpec(block.shape, lambda i: (0, 0, 0, 0))
+    edge = pl.BlockSpec((RADIUS, ny, nz, nb), lambda i: (0, 0, 0, 0))
+    part = pl.BlockSpec((depth, ny, nz, nb), lambda i: (i, 0, 0, 0))
+    low, high = exchange(sends, "domain")
+    partial = pl.pallas_call(
+        interior_kernel(stage, planes, ny, nz),
+        grid=(blocks,),
+        in_specs=[whole, part],
+        out_specs=part,
+        out_shape=jax.ShapeDtypeStruct(block.shape, jnp.float32),
+        scratch_shapes=[pltpu.VMEM(block.shape, jnp.float32)],
+        name=f"interior_{stage}",
+    )(block, potential_wide)
+    halos = jnp.concatenate([low, high], axis=0)
+    halo_block = pl.BlockSpec((RADIUS, ny, nz, nb), lambda i: (jnp.minimum(i, 1), 0, 0, 0))
+    operands = [halos, partial]
+    in_specs = [halo_block, part]
+    if initial is not None:
+        operands.append(initial)
+        in_specs.append(part)
+    shapes = [jax.ShapeDtypeStruct(block.shape, jnp.bfloat16)]
+    out_specs = [part]
+    if keep_sends:
+        edge_shape = jax.ShapeDtypeStruct((RADIUS, ny, nz, nb), jnp.bfloat16)
+        shapes += [edge_shape, edge_shape]
+        out_specs += [edge, edge]
+    return pl.pallas_call(
+        finish_kernel(stage, planes, ny),
+        grid=(blocks,),
+        in_specs=in_specs,
+        out_specs=tuple(out_specs),
+        out_shape=tuple(shapes),
+        name=f"finish_{stage}",
+    )(*operands)
+
+
+def finish_kernel_whole(stage, planes, ny):
+    blocks, depth = plane_blocks(planes)
+
+    def kernel(*refs):
+        refs = list(refs)
+        low, high, partial = refs[:3]
+        initial = refs[3] if stage == "filtered" else None
+        outs = refs[4:] if stage == "filtered" else refs[3:]
+        out = outs[0]
+        step = pl.program_id(0)
+        for block in range(blocks):
+            @pl.when(step == block)
+            def _(block=block):
+                for j in range(depth):
+                    x = block * depth + j
+
+                    def row(y, carry, x=x, j=j):
+                        summed = partial[j, y]
+                        for k in range(1, RADIUS + 1):
+                            outside = []
+                            if x + k >= planes:
+                                outside.append(high[x + k - planes, y].astype(jnp.float32))
+                            if x - k < 0:
+                                outside.append(low[x - k + RADIUS, y].astype(jnp.float32))
+                            if outside:
+                                term = outside[0] if len(outside) == 1 else outside[0] + outside[1]
+                                summed = summed + (-0.5 * stencil_weights[k]) * term
+                        if stage == "first":
+                            result = summed * first_factor
+                        elif stage == "filtered":
+                            result = summed * second_factor + (
+                                memory_factor * initial[j, y].astype(jnp.float32)
+                            )
+                        else:
+                            result = summed
+                        result = result.astype(out.dtype)
+                        out[j, y] = result
+                        if len(outs) == 3:
+                            if x >= planes - RADIUS:
+                                outs[1][x - planes + RADIUS, y] = result
+                            if x < RADIUS:
+                                outs[2][x, y] = result
+                        return carry
+
+                    lax.fori_loop(0, ny, row, 0)
+
+    return kernel
+
+
+def stencil_stage_whole(stage, block, sends, potential_wide, initial=None, keep_sends=True):
+    planes, ny, nz, nb = block.shape
+    blocks, depth = plane_blocks(planes)
     whole = pl.BlockSpec(block.shape, lambda i: (0, 0, 0, 0))
     edge = pl.BlockSpec((RADIUS, ny, nz, nb), lambda i: (0, 0, 0, 0))
     part = pl.BlockSpec((depth, ny, nz, nb), lambda i: (i, 0, 0, 0))
@@ -138,7 +229,7 @@
         shapes += [edge_shape, edge_shape]
         out_specs += [edge, edge]
     return pl.pallas_call(
-        finish_kernel(stage, planes, ny),
+        finish_kernel_whole(stage, planes, ny),
         grid=(blocks,),
         in_specs=in_specs,
         out_specs=tuple(out_specs),

time: 95.1 us -> 93.2 us (0.980)
  local copies, waits for them, and re-layouts: 8.79 us -> 4.8 us
  other arithmetic: 0.15 us -> 3.37 us
  starting transfers between devices: 23.8 us -> 22 us
  waiting for transfers between devices: 23.6 us -> 24.6 us
    unnamed x20 -> x8, local copies, waits for them, and re-layouts: 5.52 us -> 1.52 us
    concatenate x0 -> x3, other arithmetic: none -> 3.22 us  [stencil_stage(): halos = jnp.concatenate([low, high], axis=0)]
    ppermute x8, starting transfers between devices: 8.53 us -> 5.92 us  [butterfly_sum(): values = values + lax.ppermute(values, axis, pairs)]
    ppermute x8, waiting for transfers between devices: 20 us -> 21.3 us  [butterfly_sum(): values = values + lax.ppermute(values, axis, pairs)]
  transfers between devices with their start and end apart: 15 -> 15, of which waited for: 10 -> 9; matrix products, arithmetic and copies ran while one was open for 6% -> 7% of each run, Pallas kernels for 27% -> 28%
where the time goes in v13:
time: 93.2 us; the launch traced here: 93 us
  Pallas kernels  34.3 us (37%)
  waiting for transfers between devices  24.6 us (26%)
  starting transfers between devices  22 us (24%)
  local copies, waits for them, and re-layouts  4.8 us (5%)
  other arithmetic  3.37 us (4%)
  matrix products  3.22 us (3%)
    pallas_call x3, Pallas kernels, stencil_stage(): pl.pallas_call(interior_kernel(stage, planes, ny, nz), grid=(blocks,), in...  22.6 us
    ppermute x8, waiting for transfers between devices, butterfly_sum(): values = values + lax.ppermute(values, axis, pairs)  21.3 us
    pallas_call x3, Pallas kernels, stencil_stage(): pl.pallas_call(finish_kernel(stage, planes, ny), grid=(blocks,), in_specs...  11.7 us
    ppermute x3, starting transfers between devices, exchange(): lax.ppermute(sends[1], axis, backward)  11 us
    ppermute x8, starting transfers between devices, butterfly_sum(): values = values + lax.ppermute(values, axis, pairs)  5.92 us
    ppermute x3, waiting for transfers between devices, exchange(): lax.ppermute(sends[0], axis, forward)  3.26 us
    dot_general x4, matrix products, shards(): jnp.einsum('cb,ck->bk', rows, cols, preferred_element_type=jnp.float32)  3.22 us
    concatenate x3, other arithmetic, stencil_stage(): halos = jnp.concatenate([low, high], axis=0)  3.22 us
  transfers between devices with their start and end apart: 15, of which 9 were waited for; matrix products, arithmetic and copies ran while one was open for 7% of the time, Pallas kernels for 28%

profile of v13, /device:TPU:0, one launch (start us, length us, event | category | flops | bytes accessed | tf_op | source)
XLA Modules:
  0.0 93.0 jit_solution(18089753465053644273)
XLA Ops:
  0.6 1.3 %fusion = (bf16[4,16,32,128]{3,2,1,0:T(8,128)(2,1)S(1)}, bf16[4,16,32,128]{3,2,1,0:T(8,128)(2,1)S(1)}) fusion(bf16[8,16,32,128]{3,2,1,0:T(8,128)(2,1)} %refs_2_.1), kind=kLoop, calls=%fused_computation.9 | loop fusion | bytes 2097152 | tf_op jit(solution)/shard_map/slice | solution.py:273
  2.0 0.5 collective-permute-start
  2.5 5.0 %collective-permute-start.1 = (bf16[4,16,32,128]{3,2,1,0:T(8,128)(2,1)S(1)}, bf16[4,16,32,128]{3,2,1,0:T(8,128)(2,1)S(1)}, u32[]{:S(2)}, u32[]{:S(2)}) collective-permute-start(bf16[4,16,32,128]{3,2,1,0:T(8,128)(2,1)S(1)} %get-tuple-element.19), channel_id=1, source_target_pairs={{1,0},{2,1},{3,2},{4,3},{5,4},{6,5},{7,6},{8,7},{9,8},{10,9},{11,1... | collective-permute-start | bytes 1572872 | tf_op jit(solution)/shard_map/ppermute | solution.py:245
  7.5 1.9 %broadcast_in_dim.2.pot = f32[8,16,32,128]{3,2,1,0:T(8,128)} broadcast(f32[8,16,32]{2,1,0:T(8,128)S(1)} %copy-done.2), dimensions={0,1,2} | broadcast | bytes 2113536 | tf_op jit(solution)/shard_map/broadcast_in_dim | solution.py:260
  9.5 7.5 %interior_first.1.refs_1_ = f32[8,16,32,128]{3,2,1,0:T(8,128)} custom-call(bf16[8,16,32,128]{3,2,1,0:T(8,128)(2,1)} %refs_2_.1, f32[8,16,32,128]{3,2,1,0:T(8,128)} %broadcast_in_dim.2.pot), custom_call_target="tpu_custom_call" | custom-call | tf_op jit(solution)/shard_map/interior_first/pallas_call | solution.py:123
  17.0 1.1 %pad_maximum_fusion.refs_0_ = bf16[8,16,32,128]{3,2,1,0:T(8,128)(2,1)} fusion(bf16[4,16,32,128]{3,2,1,0:T(8,128)(2,1)S(1)} %collective-permute-done.1, bf16[4,16,32,128]{3,2,1,0:T(8,128)(2,1)S(1)} %collective-permute-done), kind=kLoop, calls=%fused_computation.2 | loop fusion | flops 524288 | bytes 2097152 | tf_op jit(solution)/shard_map/concatenate | solution.py:132
  18.1 4.0 %finish_first.1 = (bf16[8,16,32,128]{3,2,1,0:T(8,128)(2,1)}, bf16[4,16,32,128]{3,2,1,0:T(8,128)(2,1)}, bf16[4,16,32,128]{3,2,1,0:T(8,128)(2,1)}) custom-call(bf16[8,16,32,128]{3,2,1,0:T(8,128)(2,1)} %pad_maximum_fusion.refs_0_, f32[8,16,32,128]{3,2,1,0:T(8,128)} %interior_first.1.refs_1_), custom_call_target="tpu_custom_call" | custom-call | tf_op jit(solution)/shard_map/finish_first/pallas_call | solution.py:145
  22.0 2.3 %collective-permute-start.2 = (bf16[4,16,32,128]{3,2,1,0:T(8,128)(2,1)}, bf16[4,16,32,128]{3,2,1,0:T(8,128)(2,1)S(1)}, u32[]{:S(2)}, u32[]{:S(2)}) collective-permute-start(bf16[4,16,32,128]{3,2,1,0:T(8,128)(2,1)} %get-tuple-element.9), channel_id=1, source_target_pairs={{0,1},{1,2},{2,3},{3,4},{4,5},{5,6},{6,7},{7,8},{8,9},{9,10},{10,1... | collective-permute-start | bytes 1572872 | tf_op jit(solution)/shard_map/ppermute | solution.py:245
  24.3 2.1 %collective-permute-start.3 = (bf16[4,16,32,128]{3,2,1,0:T(8,128)(2,1)}, bf16[4,16,32,128]{3,2,1,0:T(8,128)(2,1)S(1)}, u32[]{:S(2)}, u32[]{:S(2)}) collective-permute-start(bf16[4,16,32,128]{3,2,1,0:T(8,128)(2,1)} %get-tuple-element.10), channel_id=1, source_target_pairs={{1,0},{2,1},{3,2},{4,3},{5,4},{6,5},{7,6},{8,7},{9,8},{10,9},{11,1... | collective-permute-start | bytes 1572872 | tf_op jit(solution)/shard_map/ppermute | solution.py:245
  26.5 7.5 %interior_filtered.1.refs_1_ = f32[8,16,32,128]{3,2,1,0:T(8,128)} custom-call(bf16[8,16,32,128]{3,2,1,0:T(8,128)(2,1)} %get-tuple-element.11.own_narrow, f32[8,16,32,128]{3,2,1,0:T(8,128)} %broadcast_in_dim.2.pot), custom_call_target="tpu_custom_call" | custom-call | tf_op jit(solution)/shard_map/interior_filtered/pallas_call | solution.py:123
  34.0 1.1 %pad_maximum_fusion.1.refs_0_ = bf16[8,16,32,128]{3,2,1,0:T(8,128)(2,1)} fusion(bf16[4,16,32,128]{3,2,1,0:T(8,128)(2,1)S(1)} %collective-permute-done.3, bf16[4,16,32,128]{3,2,1,0:T(8,128)(2,1)S(1)} %collective-permute-done.2), kind=kLoop, calls=%fused_computation.3 | loop fusion | flops 524288 | bytes 2097152 | tf_op jit(solution)/shard_map/concatenate | solution.py:132
  35.1 4.3 %finish_filtered.1 = (bf16[8,16,32,128]{3,2,1,0:T(8,128)(2,1)}, bf16[4,16,32,128]{3,2,1,0:T(8,128)(2,1)}, bf16[4,16,32,128]{3,2,1,0:T(8,128)(2,1)}) custom-call(bf16[8,16,32,128]{3,2,1,0:T(8,128)(2,1)} %pad_maximum_fusion.1.refs_0_, f32[8,16,32,128]{3,2,1,0:T(8,128)} %interior_filtered.1.refs_1_, bf16[8,16,32,128]{3,2,1,0:T(8,128)(2,1)} %refs_2_.1), custom_call_target="tpu_custom_call" | custom-call | tf_op jit(solution)/shard_map/finish_filtered/pallas_call | solution.py:145
  39.3 1.9 %collective-permute-start.4 = (bf16[4096,128]{1,0:T(8,128)(2,1)}, bf16[4096,128]{1,0:T(8,128)(2,1)S(1)}, u32[]{:S(2)}, u32[]{:S(2)}) collective-permute-start(bf16[4096,128]{1,0:T(8,128)(2,1)} %bitcast.18), channel_id=1, source_target_pairs={{0,16},{16,0},{1,17},{17,1},{2,18},{18,2},{3,19},{19,3},{4,20},{20... | collective-permute-start | bytes 3145736 | tf_op jit(solution)/shard_map/ppermute | solution.py:281
  41.3 3.8 %collective-permute-start.10 = (bf16[4,16,32,128]{3,2,1,0:T(8,128)(2,1)}, bf16[4,16,32,128]{3,2,1,0:T(8,128)(2,1)S(1)}, u32[]{:S(2)}, u32[]{:S(2)}) collective-permute-start(bf16[4,16,32,128]{3,2,1,0:T(8,128)(2,1)} %get-tuple-element.14), channel_id=1, source_target_pairs={{1,0},{2,1},{3,2},{4,3},{5,4},{6,5},{7,6},{8,7},{9,8},{10,9},{11,1... | collective-permute-start | bytes 1572872 | tf_op jit(solution)/shard_map/ppermute | solution.py:245
  45.4 7.5 %interior_applied.1.refs_1_ = f32[8,16,32,128]{3,2,1,0:T(8,128)} custom-call(bf16[8,16,32,128]{3,2,1,0:T(8,128)(2,1)} %get-tuple-element.15.own_narrow, f32[8,16,32,128]{3,2,1,0:T(8,128)} %broadcast_in_dim.2.pot), custom_call_target="tpu_custom_call" | custom-call | tf_op jit(solution)/shard_map/interior_applied/pallas_call | solution.py:123
  53.4 3.3 %collective-permute-done.9 = bf16[4,16,32,128]{3,2,1,0:T(8,128)(2,1)S(1)} collective-permute-done((bf16[4,16,32,128]{3,2,1,0:T(8,128)(2,1)}, bf16[4,16,32,128]{3,2,1,0:T(8,128)(2,1)S(1)}, u32[]{:S(2)}, u32[]{:S(2)}) %collective-permute-start.9) | collective-permute-done | bytes 524320 | tf_op jit(solution)/shard_map/ppermute | solution.py:245
  56.7 1.1 %pad_maximum_fusion.2.refs_0_ = bf16[8,16,32,128]{3,2,1,0:T(8,128)(2,1)} fusion(bf16[4,16,32,128]{3,2,1,0:T(8,128)(2,1)S(1)} %collective-permute-done.10, bf16[4,16,32,128]{3,2,1,0:T(8,128)(2,1)S(1)} %collective-permute-done.9), kind=kLoop, calls=%fused_computation.4 | loop fusion | flops 524288 | bytes 2097152 | tf_op jit(solution)/shard_map/concatenate | solution.py:132
  57.8 3.5 %finish_applied.1 = bf16[8,16,32,128]{3,2,1,0:T(8,128)(2,1)} custom-call(bf16[8,16,32,128]{3,2,1,0:T(8,128)(2,1)} %pad_maximum_fusion.2.refs_0_, f32[8,16,32,128]{3,2,1,0:T(8,128)} %interior_applied.1.refs_1_), custom_call_target="tpu_custom_call" | custom-call | tf_op jit(solution)/shard_map/finish_applied/pallas_call | solution.py:145
  61.3 1.8 %convolution_bitcast_fusion = f32[128,128]{0,1:T(8,128)S(1)} fusion(bf16[8,16,32,128]{3,2,1,0:T(8,128)(2,1)} %finish_applied.1, bf16[8,16,32,128]{3,2,1,0:T(8,128)(2,1)S(1)} %copy-done), kind=kOutput, calls=%fused_computation | convolution fusion | flops 134217728 | bytes 2162688 | tf_op jit(solution)/shard_map/cb,ck->bk/dot_general | solution.py:264
  63.1 0.5 fusion.2
  63.6 3.5 %collective-permute-start.11 = (f32[128,256]{0,1:T(8,128)S(1)}, f32[128,256]{0,1:T(8,128)S(1)}, u32[]{:S(2)}, u32[]{:S(2)}) collective-permute-start(f32[128,256]{0,1:T(8,128)S(1)} %maximum_select_fusion.1), channel_id=1, source_target_pairs={{0,1},{1,0},{2,3},{3,2},{4,5},{5,4},{6,7},{7,6},{8,9},{9,8},{10,11... | collective-permute-start | bytes 393224 | tf_op jit(solution)/shard_map/ppermute | solution.py:253
  68.2 0.8 collective-permute-done.5
  69.0 1.3 %collective-permute-start.6 = (f32[128,256]{0,1:T(8,128)S(1)}, f32[128,256]{0,1:T(8,128)S(1)}, u32[]{:S(2)}, u32[]{:S(2)}) collective-permute-start(f32[128,256]{0,1:T(8,128)S(1)} %add.24), channel_id=1, source_target_pairs={{0,2},{1,3},{2,0},{3,1},{4,6},{5,7},{6,4},{7,5},{8,10},{9,11},{10,... | collective-permute-start | bytes 393224 | tf_op jit(solution)/shard_map/ppermute | solution.py:253
  70.3 4.2 %collective-permute-done.12 = f32[128,256]{0,1:T(8,128)S(1)} collective-permute-done((f32[128,256]{0,1:T(8,128)S(1)}, f32[128,256]{0,1:T(8,128)S(1)}, u32[]{:S(2)}, u32[]{:S(2)}) %collective-permute-start.12) | collective-permute-done | bytes 131104 | tf_op jit(solution)/shard_map/ppermute | solution.py:253
  74.6 2.1 %collective-permute-done.6 = f32[128,256]{0,1:T(8,128)S(1)} collective-permute-done((f32[128,256]{0,1:T(8,128)S(1)}, f32[128,256]{0,1:T(8,128)S(1)}, u32[]{:S(2)}, u32[]{:S(2)}) %collective-permute-start.6) | collective-permute-done | bytes 131104 | tf_op jit(solution)/shard_map/ppermute | solution.py:253
  76.8 3.3 %collective-permute-done.13 = f32[128,256]{0,1:T(8,128)S(1)} collective-permute-done((f32[128,256]{0,1:T(8,128)S(1)}, f32[128,256]{0,1:T(8,128)S(1)}, u32[]{:S(2)}, u32[]{:S(2)}) %collective-permute-start.13) | collective-permute-done | bytes 131104 | tf_op jit(solution)/shard_map/ppermute | solution.py:253
  80.2 0.7 collective-permute-start.14
  80.9 2.9 %collective-permute-done.7 = f32[128,256]{0,1:T(8,128)S(1)} collective-permute-done((f32[128,256]{0,1:T(8,128)S(1)}, f32[128,256]{0,1:T(8,128)S(1)}, u32[]{:S(2)}, u32[]{:S(2)}) %collective-permute-start.7) | collective-permute-done | bytes 131104 | tf_op jit(solution)/shard_map/ppermute | solution.py:253
  84.0 6.8 %collective-permute-done.14 = f32[128,256]{0,1:T(8,128)S(1)} collective-permute-done((f32[128,256]{0,1:T(8,128)S(1)}, f32[128,256]{0,1:T(8,128)S(1)}, u32[]{:S(2)}, u32[]{:S(2)}) %collective-permute-start.14) | collective-permute-done | bytes 131104 | tf_op jit(solution)/shard_map/ppermute | solution.py:253
  90.8 0.8 copy.6
  91.5 0.7 collective-permute-done.8
  92.3 0.8 copy.5
  (31 shorter events, 2.3 us)
Async XLA Ops:
  0.6 6.9 %copy-start.2 = (f32[8,16,32]{2,1,0:T(8,128)S(1)}, f32[8,16,32]{2,1,0:T(8,128)}, u32[]{:S(2)}) copy-start(f32[8,16,32]{2,1,0:T(8,128)} %param.3) | copy-start | bytes 49156
  2.0 15.0 %collective-permute-start = (bf16[4,16,32,128]{3,2,1,0:T(8,128)(2,1)S(1)}, bf16[4,16,32,128]{3,2,1,0:T(8,128)(2,1)S(1)}, u32[]{:S(2)}, u32[]{:S(2)}) collective-permute-start(bf16[4,16,32,128]{3,2,1,0:T(8,128)(2,1)S(1)} %get-tuple-element.18), channel_id=1, source_target_pairs={{0,1},{1,2},{2,3},{3,4},{4,5},{5,6},{6,7},{7,8},{8,9},{9,10},{10,1... | collective-permute-start | bytes 1572872 | tf_op jit(solution)/shard_map/ppermute | solution.py:245
  2.5 14.5 %collective-permute-start.1 = (bf16[4,16,32,128]{3,2,1,0:T(8,128)(2,1)S(1)}, bf16[4,16,32,128]{3,2,1,0:T(8,128)(2,1)S(1)}, u32[]{:S(2)}, u32[]{:S(2)}) collective-permute-start(bf16[4,16,32,128]{3,2,1,0:T(8,128)(2,1)S(1)} %get-tuple-element.19), channel_id=1, source_target_pairs={{1,0},{2,1},{3,2},{4,3},{5,4},{6,5},{7,6},{8,7},{9,8},{10,9},{11,1... | collective-permute-start | bytes 1572872 | tf_op jit(solution)/shard_map/ppermute | solution.py:245
  22.0 12.0 %collective-permute-start.2 = (bf16[4,16,32,128]{3,2,1,0:T(8,128)(2,1)}, bf16[4,16,32,128]{3,2,1,0:T(8,128)(2,1)S(1)}, u32[]{:S(2)}, u32[]{:S(2)}) collective-permute-start(bf16[4,16,32,128]{3,2,1,0:T(8,128)(2,1)} %get-tuple-element.9), channel_id=1, source_target_pairs={{0,1},{1,2},{2,3},{3,4},{4,5},{5,6},{6,7},{7,8},{8,9},{9,10},{10,1... | collective-permute-start | bytes 1572872 | tf_op jit(solution)/shard_map/ppermute | solution.py:245
  24.3 9.7 %collective-permute-start.3 = (bf16[4,16,32,128]{3,2,1,0:T(8,128)(2,1)}, bf16[4,16,32,128]{3,2,1,0:T(8,128)(2,1)S(1)}, u32[]{:S(2)}, u32[]{:S(2)}) collective-permute-start(bf16[4,16,32,128]{3,2,1,0:T(8,128)(2,1)} %get-tuple-element.10), channel_id=1, source_target_pairs={{1,0},{2,1},{3,2},{4,3},{5,4},{6,5},{7,6},{8,7},{9,8},{10,9},{11,1... | collective-permute-start | bytes 1572872 | tf_op jit(solution)/shard_map/ppermute | solution.py:245
  39.3 23.7 %collective-permute-start.4 = (bf16[4096,128]{1,0:T(8,128)(2,1)}, bf16[4096,128]{1,0:T(8,128)(2,1)S(1)}, u32[]{:S(2)}, u32[]{:S(2)}) collective-permute-start(bf16[4096,128]{1,0:T(8,128)(2,1)} %bitcast.18), channel_id=1, source_target_pairs={{0,16},{16,0},{1,17},{17,1},{2,18},{18,2},{3,19},{19,3},{4,20},{20... | collective-permute-start | bytes 3145736 | tf_op jit(solution)/shard_map/ppermute | solution.py:281
  41.3 12.2 %collective-permute-start.10 = (bf16[4,16,32,128]{3,2,1,0:T(8,128)(2,1)}, bf16[4,16,32,128]{3,2,1,0:T(8,128)(2,1)S(1)}, u32[]{:S(2)}, u32[]{:S(2)}) collective-permute-start(bf16[4,16,32,128]{3,2,1,0:T(8,128)(2,1)} %get-tuple-element.14), channel_id=1, source_target_pairs={{1,0},{2,1},{3,2},{4,3},{5,4},{6,5},{7,6},{8,7},{9,8},{10,9},{11,1... | collective-permute-start | bytes 1572872 | tf_op jit(solution)/shard_map/ppermute | solution.py:245
  45.1 11.6 %collective-permute-start.9 = (bf16[4,16,32,128]{3,2,1,0:T(8,128)(2,1)}, bf16[4,16,32,128]{3,2,1,0:T(8,128)(2,1)S(1)}, u32[]{:S(2)}, u32[]{:S(2)}) collective-permute-start(bf16[4,16,32,128]{3,2,1,0:T(8,128)(2,1)} %get-tuple-element.13), channel_id=1, source_target_pairs={{0,1},{1,2},{2,3},{3,4},{4,5},{5,6},{6,7},{7,8},{8,9},{9,10},{10,1... | collective-permute-start | bytes 1572872 | tf_op jit(solution)/shard_map/ppermute | solution.py:245
  45.4 7.5 %copy-start = (bf16[8,16,32,128]{3,2,1,0:T(8,128)(2,1)S(1)}, bf16[8,16,32,128]{3,2,1,0:T(8,128)(2,1)}, u32[]{:S(2)}) copy-start(bf16[8,16,32,128]{3,2,1,0:T(8,128)(2,1)} %get-tuple-element.15.own_narrow) | copy-start | bytes 3145732
  61.3 1.8 %copy-start.1 = (bf16[8,16,32,128]{3,2,1,0:T(8,128)(2,1)S(1)}, bf16[8,16,32,128]{3,2,1,0:T(8,128)(2,1)}, u32[]{:S(2)}) copy-start(bf16[8,16,32,128]{3,2,1,0:T(8,128)(2,1)} %finish_applied.1) | copy-start | bytes 3145732
  63.6 4.5 %collective-permute-start.11 = (f32[128,256]{0,1:T(8,128)S(1)}, f32[128,256]{0,1:T(8,128)S(1)}, u32[]{:S(2)}, u32[]{:S(2)}) collective-permute-start(f32[128,256]{0,1:T(8,128)S(1)} %maximum_select_fusion.1), channel_id=1, source_target_pairs={{0,1},{1,0},{2,3},{3,2},{4,5},{5,4},{6,7},{7,6},{8,9},{9,8},{10,11... | collective-permute-start | bytes 393224 | tf_op jit(solution)/shard_map/ppermute | solution.py:253
  67.6 1.4 %collective-permute-start.5 = (f32[128,256]{0,1:T(8,128)S(1)}, f32[128,256]{0,1:T(8,128)S(1)}, u32[]{:S(2)}, u32[]{:S(2)}) collective-permute-start(f32[128,256]{0,1:T(8,128)S(1)} %maximum_select_fusion), channel_id=1, source_target_pairs={{0,1},{1,0},{2,3},{3,2},{4,5},{5,4},{6,7},{7,6},{8,9},{9,8},{10,11... | collective-permute-start | bytes 393224 | tf_op jit(solution)/shard_map/ppermute | solution.py:253
  68.1 6.4 %collective-permute-start.12 = (f32[128,256]{0,1:T(8,128)S(1)}, f32[128,256]{0,1:T(8,128)S(1)}, u32[]{:S(2)}, u32[]{:S(2)}) collective-permute-start(f32[128,256]{0,1:T(8,128)S(1)} %add.28), channel_id=1, source_target_pairs={{0,2},{1,3},{2,0},{3,1},{4,6},{5,7},{6,4},{7,5},{8,10},{9,11},{10,... | collective-permute-start | bytes 393224 | tf_op jit(solution)/shard_map/ppermute | solution.py:253
  69.0 7.7 %collective-permute-start.6 = (f32[128,256]{0,1:T(8,128)S(1)}, f32[128,256]{0,1:T(8,128)S(1)}, u32[]{:S(2)}, u32[]{:S(2)}) collective-permute-start(f32[128,256]{0,1:T(8,128)S(1)} %add.24), channel_id=1, source_target_pairs={{0,2},{1,3},{2,0},{3,1},{4,6},{5,7},{6,4},{7,5},{8,10},{9,11},{10,... | collective-permute-start | bytes 393224 | tf_op jit(solution)/shard_map/ppermute | solution.py:253
  74.5 5.6 %collective-permute-start.13 = (f32[128,256]{0,1:T(8,128)S(1)}, f32[128,256]{0,1:T(8,128)S(1)}, u32[]{:S(2)}, u32[]{:S(2)}) collective-permute-start(f32[128,256]{0,1:T(8,128)S(1)} %add.29), channel_id=1, source_target_pairs={{0,4},{1,5},{2,6},{3,7},{4,0},{5,1},{6,2},{7,3},{8,12},{9,13},{10,... | collective-permute-start | bytes 393224 | tf_op jit(solution)/shard_map/ppermute | solution.py:253
  76.8 7.0 %collective-permute-start.7 = (f32[128,256]{0,1:T(8,128)S(1)}, f32[128,256]{0,1:T(8,128)S(1)}, u32[]{:S(2)}, u32[]{:S(2)}) collective-permute-start(f32[128,256]{0,1:T(8,128)S(1)} %add.25), channel_id=1, source_target_pairs={{0,4},{1,5},{2,6},{3,7},{4,0},{5,1},{6,2},{7,3},{8,12},{9,13},{10,... | collective-permute-start | bytes 393224 | tf_op jit(solution)/shard_map/ppermute | solution.py:253
  80.2 10.6 %collective-permute-start.14 = (f32[128,256]{0,1:T(8,128)S(1)}, f32[128,256]{0,1:T(8,128)S(1)}, u32[]{:S(2)}, u32[]{:S(2)}) collective-permute-start(f32[128,256]{0,1:T(8,128)S(1)} %add.30), channel_id=1, source_target_pairs={{0,8},{1,9},{2,10},{3,11},{4,12},{5,13},{6,14},{7,15},{8,0},{9,1},... | collective-permute-start | bytes 393224 | tf_op jit(solution)/shard_map/ppermute | solution.py:253
  83.8 8.5 %collective-permute-start.8 = (f32[128,256]{0,1:T(8,128)S(1)}, f32[128,256]{0,1:T(8,128)S(1)}, u32[]{:S(2)}, u32[]{:S(2)}) collective-permute-start(f32[128,256]{0,1:T(8,128)S(1)} %add.26), channel_id=1, source_target_pairs={{0,8},{1,9},{2,10},{3,11},{4,12},{5,13},{6,14},{7,15},{8,0},{9,1},... | collective-permute-start | bytes 393224 | tf_op jit(solution)/shard_map/ppermute | solution.py:253

commit v14 on v13

--- a/solution.py
+++ b/solution.py
@@ -3,6 +3,7 @@
 from jax import lax
 from jax.experimental import pallas as pl
 from jax.experimental.pallas import tpu as pltpu
+from jax.experimental.layout import Layout, with_layout_constraint
 from jax.sharding import PartitionSpec as P
 
 RADIUS = 4
@@ -261,8 +262,9 @@
     cell_count = planes * ny * nz
     cell_weight = 1.0 / (cell_count * lax.axis_size("domain"))
     band = lax.axis_index("band")
-    gram = lambda rows, cols: jnp.einsum(
-        "cb,ck->bk", rows, cols, preferred_element_type=jnp.float32
+    gram = lambda rows, cols: with_layout_constraint(
+        jnp.einsum("cb,ck->bk", rows, cols, preferred_element_type=jnp.float32),
+        Layout((0, 1)),
     )
     placed = lambda mine, theirs: jnp.where(
         band == 0,

time: 93.2 us -> 93.1 us (level)
  local copies, waits for them, and re-layouts: 4.8 us -> 3.29 us
  other arithmetic: 3.37 us -> 4.7 us
    unnamed x8 -> x6, local copies, waits for them, and re-layouts: 1.52 us -> 0.01 us
where the time goes in v14:
time: 93.1 us; the launch traced here: 92.9 us
  Pallas kernels  34.3 us (37%)
  waiting for transfers between devices  24.7 us (27%)
  starting transfers between devices  22 us (24%)
  other arithmetic  4.7 us (5%)
  local copies, waits for them, and re-layouts  3.29 us (4%)
  matrix products  3.22 us (3%)
    pallas_call x3, Pallas kernels, stencil_stage(): pl.pallas_call(interior_kernel(stage, planes, ny, nz), grid=(blocks,), in...  22.6 us
    ppermute x8, waiting for transfers between devices, butterfly_sum(): values = values + lax.ppermute(values, axis, pairs)  21.4 us
    pallas_call x3, Pallas kernels, stencil_stage(): pl.pallas_call(finish_kernel(stage, planes, ny), grid=(blocks,), in_specs...  11.7 us
    ppermute x3, starting transfers between devices, exchange(): lax.ppermute(sends[1], axis, backward)  11 us
    ppermute x8, starting transfers between devices, butterfly_sum(): values = values + lax.ppermute(values, axis, pairs)  5.92 us
    ppermute x3, waiting for transfers between devices, exchange(): lax.ppermute(sends[0], axis, forward)  3.26 us
    concatenate x3, other arithmetic, stencil_stage(): halos = jnp.concatenate([low, high], axis=0)  3.22 us
    dot_general x4, matrix products, shards(): jnp.einsum('cb,ck->bk', rows, cols, preferred_element_type=jnp.float32)  3.22 us
  transfers between devices with their start and end apart: 15, of which 9 were waited for; matrix products, arithmetic and copies ran while one was open for 7% of the time, Pallas kernels for 28%

profile of v14, /device:TPU:0, one launch (start us, length us, event | category | flops | bytes accessed | tf_op | source)
XLA Modules:
  0.0 92.9 jit_solution(8590596120029624865)
XLA Ops:
  0.6 1.3 %fusion = (bf16[4,16,32,128]{3,2,1,0:T(8,128)(2,1)S(1)}, bf16[4,16,32,128]{3,2,1,0:T(8,128)(2,1)S(1)}) fusion(bf16[8,16,32,128]{3,2,1,0:T(8,128)(2,1)} %refs_2_.1), kind=kLoop, calls=%fused_computation.9 | loop fusion | bytes 2097152 | tf_op jit(solution)/shard_map/slice | solution.py:275
  2.0 0.5 collective-permute-start
  2.5 5.0 %collective-permute-start.1 = (bf16[4,16,32,128]{3,2,1,0:T(8,128)(2,1)S(1)}, bf16[4,16,32,128]{3,2,1,0:T(8,128)(2,1)S(1)}, u32[]{:S(2)}, u32[]{:S(2)}) collective-permute-start(bf16[4,16,32,128]{3,2,1,0:T(8,128)(2,1)S(1)} %get-tuple-element.16), channel_id=1, source_target_pairs={{1,0},{2,1},{3,2},{4,3},{5,4},{6,5},{7,6},{8,7},{9,8},{10,9},{11,1... | collective-permute-start | bytes 1572872 | tf_op jit(solution)/shard_map/ppermute | solution.py:246
  7.5 1.9 %broadcast_in_dim.2.pot = f32[8,16,32,128]{3,2,1,0:T(8,128)} broadcast(f32[8,16,32]{2,1,0:T(8,128)S(1)} %copy-done.2), dimensions={0,1,2} | broadcast | bytes 2113536 | tf_op jit(solution)/shard_map/broadcast_in_dim | solution.py:261
  9.5 7.5 %interior_first.1.refs_1_ = f32[8,16,32,128]{3,2,1,0:T(8,128)} custom-call(bf16[8,16,32,128]{3,2,1,0:T(8,128)(2,1)} %refs_2_.1, f32[8,16,32,128]{3,2,1,0:T(8,128)} %broadcast_in_dim.2.pot), custom_call_target="tpu_custom_call" | custom-call | tf_op jit(solution)/shard_map/interior_first/pallas_call | solution.py:124
  17.0 1.1 %pad_maximum_fusion.refs_0_ = bf16[8,16,32,128]{3,2,1,0:T(8,128)(2,1)} fusion(bf16[4,16,32,128]{3,2,1,0:T(8,128)(2,1)S(1)} %collective-permute-done.1, bf16[4,16,32,128]{3,2,1,0:T(8,128)(2,1)S(1)} %collective-permute-done), kind=kLoop, calls=%fused_computation.2 | loop fusion | flops 524288 | bytes 2097152 | tf_op jit(solution)/shard_map/concatenate | solution.py:133
  18.1 4.0 %finish_first.1 = (bf16[8,16,32,128]{3,2,1,0:T(8,128)(2,1)}, bf16[4,16,32,128]{3,2,1,0:T(8,128)(2,1)}, bf16[4,16,32,128]{3,2,1,0:T(8,128)(2,1)}) custom-call(bf16[8,16,32,128]{3,2,1,0:T(8,128)(2,1)} %pad_maximum_fusion.refs_0_, f32[8,16,32,128]{3,2,1,0:T(8,128)} %interior_first.1.refs_1_), custom_call_target="tpu_custom_call" | custom-call | tf_op jit(solution)/shard_map/finish_first/pallas_call | solution.py:146
  22.0 2.3 %collective-permute-start.2 = (bf16[4,16,32,128]{3,2,1,0:T(8,128)(2,1)}, bf16[4,16,32,128]{3,2,1,0:T(8,128)(2,1)S(1)}, u32[]{:S(2)}, u32[]{:S(2)}) collective-permute-start(bf16[4,16,32,128]{3,2,1,0:T(8,128)(2,1)} %get-tuple-element.9), channel_id=1, source_target_pairs={{0,1},{1,2},{2,3},{3,4},{4,5},{5,6},{6,7},{7,8},{8,9},{9,10},{10,1... | collective-permute-start | bytes 1572872 | tf_op jit(solution)/shard_map/ppermute | solution.py:246
  24.3 2.1 %collective-permute-start.3 = (bf16[4,16,32,128]{3,2,1,0:T(8,128)(2,1)}, bf16[4,16,32,128]{3,2,1,0:T(8,128)(2,1)S(1)}, u32[]{:S(2)}, u32[]{:S(2)}) collective-permute-start(bf16[4,16,32,128]{3,2,1,0:T(8,128)(2,1)} %get-tuple-element.10), channel_id=1, source_target_pairs={{1,0},{2,1},{3,2},{4,3},{5,4},{6,5},{7,6},{8,7},{9,8},{10,9},{11,1... | collective-permute-start | bytes 1572872 | tf_op jit(solution)/shard_map/ppermute | solution.py:246
  26.5 7.5 %interior_filtered.1.refs_1_ = f32[8,16,32,128]{3,2,1,0:T(8,128)} custom-call(bf16[8,16,32,128]{3,2,1,0:T(8,128)(2,1)} %get-tuple-element.11.own_narrow, f32[8,16,32,128]{3,2,1,0:T(8,128)} %broadcast_in_dim.2.pot), custom_call_target="tpu_custom_call" | custom-call | tf_op jit(solution)/shard_map/interior_filtered/pallas_call | solution.py:124
  34.0 1.1 %pad_maximum_fusion.1.refs_0_ = bf16[8,16,32,128]{3,2,1,0:T(8,128)(2,1)} fusion(bf16[4,16,32,128]{3,2,1,0:T(8,128)(2,1)S(1)} %collective-permute-done.3, bf16[4,16,32,128]{3,2,1,0:T(8,128)(2,1)S(1)} %collective-permute-done.2), kind=kLoop, calls=%fused_computation.3 | loop fusion | flops 524288 | bytes 2097152 | tf_op jit(solution)/shard_map/concatenate | solution.py:133
  35.1 4.3 %finish_filtered.1 = (bf16[8,16,32,128]{3,2,1,0:T(8,128)(2,1)}, bf16[4,16,32,128]{3,2,1,0:T(8,128)(2,1)}, bf16[4,16,32,128]{3,2,1,0:T(8,128)(2,1)}) custom-call(bf16[8,16,32,128]{3,2,1,0:T(8,128)(2,1)} %pad_maximum_fusion.1.refs_0_, f32[8,16,32,128]{3,2,1,0:T(8,128)} %interior_filtered.1.refs_1_, bf16[8,16,32,128]{3,2,1,0:T(8,128)(2,1)} %refs_2_.1), custom_call_target="tpu_custom_call" | custom-call | tf_op jit(solution)/shard_map/finish_filtered/pallas_call | solution.py:146
  39.3 1.9 %collective-permute-start.4 = (bf16[4096,128]{1,0:T(8,128)(2,1)}, bf16[4096,128]{1,0:T(8,128)(2,1)S(1)}, u32[]{:S(2)}, u32[]{:S(2)}) collective-permute-start(bf16[4096,128]{1,0:T(8,128)(2,1)} %bitcast.18), channel_id=1, source_target_pairs={{0,16},{16,0},{1,17},{17,1},{2,18},{18,2},{3,19},{19,3},{4,20},{20... | collective-permute-start | bytes 3145736 | tf_op jit(solution)/shard_map/ppermute | solution.py:283
  41.3 3.8 %collective-permute-start.10 = (bf16[4,16,32,128]{3,2,1,0:T(8,128)(2,1)}, bf16[4,16,32,128]{3,2,1,0:T(8,128)(2,1)S(1)}, u32[]{:S(2)}, u32[]{:S(2)}) collective-permute-start(bf16[4,16,32,128]{3,2,1,0:T(8,128)(2,1)} %get-tuple-element.14), channel_id=1, source_target_pairs={{1,0},{2,1},{3,2},{4,3},{5,4},{6,5},{7,6},{8,7},{9,8},{10,9},{11,1... | collective-permute-start | bytes 1572872 | tf_op jit(solution)/shard_map/ppermute | solution.py:246
  45.4 7.5 %interior_applied.1.refs_1_ = f32[8,16,32,128]{3,2,1,0:T(8,128)} custom-call(bf16[8,16,32,128]{3,2,1,0:T(8,128)(2,1)} %get-tuple-element.6.own_narrow, f32[8,16,32,128]{3,2,1,0:T(8,128)} %broadcast_in_dim.2.pot), custom_call_target="tpu_custom_call" | custom-call | tf_op jit(solution)/shard_map/interior_applied/pallas_call | solution.py:124
  53.4 3.3 %collective-permute-done.9 = bf16[4,16,32,128]{3,2,1,0:T(8,128)(2,1)S(1)} collective-permute-done((bf16[4,16,32,128]{3,2,1,0:T(8,128)(2,1)}, bf16[4,16,32,128]{3,2,1,0:T(8,128)(2,1)S(1)}, u32[]{:S(2)}, u32[]{:S(2)}) %collective-permute-start.9) | collective-permute-done | bytes 524320 | tf_op jit(solution)/shard_map/ppermute | solution.py:246
  56.7 1.1 %pad_maximum_fusion.2.refs_0_ = bf16[8,16,32,128]{3,2,1,0:T(8,128)(2,1)} fusion(bf16[4,16,32,128]{3,2,1,0:T(8,128)(2,1)S(1)} %collective-permute-done.10, bf16[4,16,32,128]{3,2,1,0:T(8,128)(2,1)S(1)} %collective-permute-done.9), kind=kLoop, calls=%fused_computation.4 | loop fusion | flops 524288 | bytes 2097152 | tf_op jit(solution)/shard_map/concatenate | solution.py:133
  57.8 3.5 %finish_applied.1 = bf16[8,16,32,128]{3,2,1,0:T(8,128)(2,1)} custom-call(bf16[8,16,32,128]{3,2,1,0:T(8,128)(2,1)} %pad_maximum_fusion.2.refs_0_, f32[8,16,32,128]{3,2,1,0:T(8,128)} %interior_applied.1.refs_1_), custom_call_target="tpu_custom_call" | custom-call | tf_op jit(solution)/shard_map/finish_applied/pallas_call | solution.py:146
  61.3 1.8 %convolution_bitcast_fusion = f32[128,128]{1,0:T(8,128)S(1)} fusion(bf16[8,16,32,128]{3,2,1,0:T(8,128)(2,1)} %finish_applied.1, bf16[8,16,32,128]{3,2,1,0:T(8,128)(2,1)S(1)} %copy-done), kind=kOutput, calls=%fused_computation | convolution fusion | flops 134217728 | bytes 2162688 | tf_op jit(solution)/shard_map/cb,ck->bk/dot_general | solution.py:266
  63.1 0.5 fusion.2
  63.6 3.5 %collective-permute-start.11 = (f32[128,256]{1,0:T(8,128)S(1)}, f32[128,256]{1,0:T(8,128)S(1)}, u32[]{:S(2)}, u32[]{:S(2)}) collective-permute-start(f32[128,256]{1,0:T(8,128)S(1)} %maximum_select_fusion.1), channel_id=1, source_target_pairs={{0,1},{1,0},{2,3},{3,2},{4,5},{5,4},{6,7},{7,6},{8,9},{9,8},{10,11... | collective-permute-start | bytes 393224 | tf_op jit(solution)/shard_map/ppermute | solution.py:254
  68.2 0.8 collective-permute-done.5
  69.0 1.3 %collective-permute-start.6 = (f32[128,256]{1,0:T(8,128)S(1)}, f32[128,256]{1,0:T(8,128)S(1)}, u32[]{:S(2)}, u32[]{:S(2)}) collective-permute-start(f32[128,256]{1,0:T(8,128)S(1)} %add.24), channel_id=1, source_target_pairs={{0,2},{1,3},{2,0},{3,1},{4,6},{5,7},{6,4},{7,5},{8,10},{9,11},{10,... | collective-permute-start | bytes 393224 | tf_op jit(solution)/shard_map/ppermute | solution.py:254
  70.3 4.2 %collective-permute-done.12 = f32[128,256]{1,0:T(8,128)S(1)} collective-permute-done((f32[128,256]{1,0:T(8,128)S(1)}, f32[128,256]{1,0:T(8,128)S(1)}, u32[]{:S(2)}, u32[]{:S(2)}) %collective-permute-start.12) | collective-permute-done | bytes 131104 | tf_op jit(solution)/shard_map/ppermute | solution.py:254
  74.6 2.1 %collective-permute-done.6 = f32[128,256]{1,0:T(8,128)S(1)} collective-permute-done((f32[128,256]{1,0:T(8,128)S(1)}, f32[128,256]{1,0:T(8,128)S(1)}, u32[]{:S(2)}, u32[]{:S(2)}) %collective-permute-start.6) | collective-permute-done | bytes 131104 | tf_op jit(solution)/shard_map/ppermute | solution.py:254
  76.9 3.3 %collective-permute-done.13 = f32[128,256]{1,0:T(8,128)S(1)} collective-permute-done((f32[128,256]{1,0:T(8,128)S(1)}, f32[128,256]{1,0:T(8,128)S(1)}, u32[]{:S(2)}, u32[]{:S(2)}) %collective-permute-start.13) | collective-permute-done | bytes 131104 | tf_op jit(solution)/shard_map/ppermute | solution.py:254
  80.2 0.7 collective-permute-start.14
  80.9 2.9 %collective-permute-done.7 = f32[128,256]{1,0:T(8,128)S(1)} collective-permute-done((f32[128,256]{1,0:T(8,128)S(1)}, f32[128,256]{1,0:T(8,128)S(1)}, u32[]{:S(2)}, u32[]{:S(2)}) %collective-permute-start.7) | collective-permute-done | bytes 131104 | tf_op jit(solution)/shard_map/ppermute | solution.py:254
  84.0 6.8 %collective-permute-done.14 = f32[128,256]{1,0:T(8,128)S(1)} collective-permute-done((f32[128,256]{1,0:T(8,128)S(1)}, f32[128,256]{1,0:T(8,128)S(1)}, u32[]{:S(2)}, u32[]{:S(2)}) %collective-permute-start.14) | collective-permute-done | bytes 131104 | tf_op jit(solution)/shard_map/ppermute | solution.py:254
  90.8 0.7 add_multiply_fusion
  91.4 0.8 collective-permute-done.8
  92.3 0.7 add_multiply_fusion.1
  (29 shorter events, 2.3 us)
Async XLA Ops:
  0.6 6.9 %copy-start.2 = (f32[8,16,32]{2,1,0:T(8,128)S(1)}, f32[8,16,32]{2,1,0:T(8,128)}, u32[]{:S(2)}) copy-start(f32[8,16,32]{2,1,0:T(8,128)} %param.3) | copy-start | bytes 49156
  2.0 15.0 %collective-permute-start = (bf16[4,16,32,128]{3,2,1,0:T(8,128)(2,1)S(1)}, bf16[4,16,32,128]{3,2,1,0:T(8,128)(2,1)S(1)}, u32[]{:S(2)}, u32[]{:S(2)}) collective-permute-start(bf16[4,16,32,128]{3,2,1,0:T(8,128)(2,1)S(1)} %get-tuple-element.15), channel_id=1, source_target_pairs={{0,1},{1,2},{2,3},{3,4},{4,5},{5,6},{6,7},{7,8},{8,9},{9,10},{10,1... | collective-permute-start | bytes 1572872 | tf_op jit(solution)/shard_map/ppermute | solution.py:246
  2.5 14.5 %collective-permute-start.1 = (bf16[4,16,32,128]{3,2,1,0:T(8,128)(2,1)S(1)}, bf16[4,16,32,128]{3,2,1,0:T(8,128)(2,1)S(1)}, u32[]{:S(2)}, u32[]{:S(2)}) collective-permute-start(bf16[4,16,32,128]{3,2,1,0:T(8,128)(2,1)S(1)} %get-tuple-element.16), channel_id=1, source_target_pairs={{1,0},{2,1},{3,2},{4,3},{5,4},{6,5},{7,6},{8,7},{9,8},{10,9},{11,1... | collective-permute-start | bytes 1572872 | tf_op jit(solution)/shard_map/ppermute | solution.py:246
  22.0 12.0 %collective-permute-start.2 = (bf16[4,16,32,128]{3,2,1,0:T(8,128)(2,1)}, bf16[4,16,32,128]{3,2,1,0:T(8,128)(2,1)S(1)}, u32[]{:S(2)}, u32[]{:S(2)}) collective-permute-start(bf16[4,16,32,128]{3,2,1,0:T(8,128)(2,1)} %get-tuple-element.9), channel_id=1, source_target_pairs={{0,1},{1,2},{2,3},{3,4},{4,5},{5,6},{6,7},{7,8},{8,9},{9,10},{10,1... | collective-permute-start | bytes 1572872 | tf_op jit(solution)/shard_map/ppermute | solution.py:246
  24.3 9.7 %collective-permute-start.3 = (bf16[4,16,32,128]{3,2,1,0:T(8,128)(2,1)}, bf16[4,16,32,128]{3,2,1,0:T(8,128)(2,1)S(1)}, u32[]{:S(2)}, u32[]{:S(2)}) collective-permute-start(bf16[4,16,32,128]{3,2,1,0:T(8,128)(2,1)} %get-tuple-element.10), channel_id=1, source_target_pairs={{1,0},{2,1},{3,2},{4,3},{5,4},{6,5},{7,6},{8,7},{9,8},{10,9},{11,1... | collective-permute-start | bytes 1572872 | tf_op jit(solution)/shard_map/ppermute | solution.py:246
  39.3 23.7 %collective-permute-start.4 = (bf16[4096,128]{1,0:T(8,128)(2,1)}, bf16[4096,128]{1,0:T(8,128)(2,1)S(1)}, u32[]{:S(2)}, u32[]{:S(2)}) collective-permute-start(bf16[4096,128]{1,0:T(8,128)(2,1)} %bitcast.18), channel_id=1, source_target_pairs={{0,16},{16,0},{1,17},{17,1},{2,18},{18,2},{3,19},{19,3},{4,20},{20... | collective-permute-start | bytes 3145736 | tf_op jit(solution)/shard_map/ppermute | solution.py:283
  41.3 12.2 %collective-permute-start.10 = (bf16[4,16,32,128]{3,2,1,0:T(8,128)(2,1)}, bf16[4,16,32,128]{3,2,1,0:T(8,128)(2,1)S(1)}, u32[]{:S(2)}, u32[]{:S(2)}) collective-permute-start(bf16[4,16,32,128]{3,2,1,0:T(8,128)(2,1)} %get-tuple-element.14), channel_id=1, source_target_pairs={{1,0},{2,1},{3,2},{4,3},{5,4},{6,5},{7,6},{8,7},{9,8},{10,9},{11,1... | collective-permute-start | bytes 1572872 | tf_op jit(solution)/shard_map/ppermute | solution.py:246
  45.1 11.6 %collective-permute-start.9 = (bf16[4,16,32,128]{3,2,1,0:T(8,128)(2,1)}, bf16[4,16,32,128]{3,2,1,0:T(8,128)(2,1)S(1)}, u32[]{:S(2)}, u32[]{:S(2)}) collective-permute-start(bf16[4,16,32,128]{3,2,1,0:T(8,128)(2,1)} %get-tuple-element.13), channel_id=1, source_target_pairs={{0,1},{1,2},{2,3},{3,4},{4,5},{5,6},{6,7},{7,8},{8,9},{9,10},{10,1... | collective-permute-start | bytes 1572872 | tf_op jit(solution)/shard_map/ppermute | solution.py:246
  45.4 7.5 %copy-start = (bf16[8,16,32,128]{3,2,1,0:T(8,128)(2,1)S(1)}, bf16[8,16,32,128]{3,2,1,0:T(8,128)(2,1)}, u32[]{:S(2)}) copy-start(bf16[8,16,32,128]{3,2,1,0:T(8,128)(2,1)} %get-tuple-element.6.own_narrow) | copy-start | bytes 3145732
  61.3 1.8 %copy-start.1 = (bf16[8,16,32,128]{3,2,1,0:T(8,128)(2,1)S(1)}, bf16[8,16,32,128]{3,2,1,0:T(8,128)(2,1)}, u32[]{:S(2)}) copy-start(bf16[8,16,32,128]{3,2,1,0:T(8,128)(2,1)} %finish_applied.1) | copy-start | bytes 3145732
  63.6 4.5 %collective-permute-start.11 = (f32[128,256]{1,0:T(8,128)S(1)}, f32[128,256]{1,0:T(8,128)S(1)}, u32[]{:S(2)}, u32[]{:S(2)}) collective-permute-start(f32[128,256]{1,0:T(8,128)S(1)} %maximum_select_fusion.1), channel_id=1, source_target_pairs={{0,1},{1,0},{2,3},{3,2},{4,5},{5,4},{6,7},{7,6},{8,9},{9,8},{10,11... | collective-permute-start | bytes 393224 | tf_op jit(solution)/shard_map/ppermute | solution.py:254
  67.6 1.4 %collective-permute-start.5 = (f32[128,256]{1,0:T(8,128)S(1)}, f32[128,256]{1,0:T(8,128)S(1)}, u32[]{:S(2)}, u32[]{:S(2)}) collective-permute-start(f32[128,256]{1,0:T(8,128)S(1)} %maximum_select_fusion), channel_id=1, source_target_pairs={{0,1},{1,0},{2,3},{3,2},{4,5},{5,4},{6,7},{7,6},{8,9},{9,8},{10,11... | collective-permute-start | bytes 393224 | tf_op jit(solution)/shard_map/ppermute | solution.py:254
  68.1 6.4 %collective-permute-start.12 = (f32[128,256]{1,0:T(8,128)S(1)}, f32[128,256]{1,0:T(8,128)S(1)}, u32[]{:S(2)}, u32[]{:S(2)}) collective-permute-start(f32[128,256]{1,0:T(8,128)S(1)} %add.28), channel_id=1, source_target_pairs={{0,2},{1,3},{2,0},{3,1},{4,6},{5,7},{6,4},{7,5},{8,10},{9,11},{10,... | collective-permute-start | bytes 393224 | tf_op jit(solution)/shard_map/ppermute | solution.py:254
  69.0 7.7 %collective-permute-start.6 = (f32[128,256]{1,0:T(8,128)S(1)}, f32[128,256]{1,0:T(8,128)S(1)}, u32[]{:S(2)}, u32[]{:S(2)}) collective-permute-start(f32[128,256]{1,0:T(8,128)S(1)} %add.24), channel_id=1, source_target_pairs={{0,2},{1,3},{2,0},{3,1},{4,6},{5,7},{6,4},{7,5},{8,10},{9,11},{10,... | collective-permute-start | bytes 393224 | tf_op jit(solution)/shard_map/ppermute | solution.py:254
  74.5 5.6 %collective-permute-start.13 = (f32[128,256]{1,0:T(8,128)S(1)}, f32[128,256]{1,0:T(8,128)S(1)}, u32[]{:S(2)}, u32[]{:S(2)}) collective-permute-start(f32[128,256]{1,0:T(8,128)S(1)} %add.29), channel_id=1, source_target_pairs={{0,4},{1,5},{2,6},{3,7},{4,0},{5,1},{6,2},{7,3},{8,12},{9,13},{10,... | collective-permute-start | bytes 393224 | tf_op jit(solution)/shard_map/ppermute | solution.py:254
  76.8 7.0 %collective-permute-start.7 = (f32[128,256]{1,0:T(8,128)S(1)}, f32[128,256]{1,0:T(8,128)S(1)}, u32[]{:S(2)}, u32[]{:S(2)}) collective-permute-start(f32[128,256]{1,0:T(8,128)S(1)} %add.25), channel_id=1, source_target_pairs={{0,4},{1,5},{2,6},{3,7},{4,0},{5,1},{6,2},{7,3},{8,12},{9,13},{10,... | collective-permute-start | bytes 393224 | tf_op jit(solution)/shard_map/ppermute | solution.py:254
  80.2 10.6 %collective-permute-start.14 = (f32[128,256]{1,0:T(8,128)S(1)}, f32[128,256]{1,0:T(8,128)S(1)}, u32[]{:S(2)}, u32[]{:S(2)}) collective-permute-start(f32[128,256]{1,0:T(8,128)S(1)} %add.30), channel_id=1, source_target_pairs={{0,8},{1,9},{2,10},{3,11},{4,12},{5,13},{6,14},{7,15},{8,0},{9,1},... | collective-permute-start | bytes 393224 | tf_op jit(solution)/shard_map/ppermute | solution.py:254
  83.8 8.5 %collective-permute-start.8 = (f32[128,256]{1,0:T(8,128)S(1)}, f32[128,256]{1,0:T(8,128)S(1)}, u32[]{:S(2)}, u32[]{:S(2)}) collective-permute-start(f32[128,256]{1,0:T(8,128)S(1)} %add.26), channel_id=1, source_target_pairs={{0,8},{1,9},{2,10},{3,11},{4,12},{5,13},{6,14},{7,15},{8,0},{9,1},... | collective-permute-start | bytes 393224 | tf_op jit(solution)/shard_map/ppermute | solution.py:254

commit v15 on v14

--- a/solution.py
+++ b/solution.py
@@ -24,8 +24,12 @@
     shift = 0.0 if stage == "applied" else spectrum_centre
     blocks, depth = plane_blocks(planes)
 
-    def kernel(own_narrow, pot, out, own):
+    def kernel(own_narrow, pot_t, out, own, pot):
         step = pl.program_id(0)
+        nb = out.shape[-1]
+        lanes = lax.broadcasted_iota(jnp.int32, (ny, ny * nb), 1)
+        rows = lax.broadcasted_iota(jnp.int32, (ny, ny * nb), 0)
+        select = (lanes // nb == rows).astype(jnp.float32)
 
         @pl.when(step == 0)
         def _():
@@ -37,6 +41,14 @@
             def _(block=block):
                 for j in range(depth):
                     x = block * depth + j
+                    spread = jnp.dot(
+                        pot_t[x],
+                        select,
+                        precision=lax.Precision.HIGHEST,
+                        preferred_element_type=jnp.float32,
+                    )
+                    for y in range(ny):
+                        pot[y] = spread[:, y * nb:(y + 1) * nb]
 
                     def row(y, carry, x=x, j=j):
                         centre = own[x, y]
@@ -51,7 +63,7 @@
                             if x - k >= 0:
                                 beside = beside + own[x - k, y]
                             summed = summed + stencil_weights[k] * beside
-                        applied = -0.5 * summed + pot[j, y] * centre
+                        applied = -0.5 * summed + pot[y] * centre
                         if shift:
                             applied = applied - shift * centre
                         out[j, y] = applied
@@ -124,10 +136,13 @@
     partial = pl.pallas_call(
         interior_kernel(stage, planes, ny, nz),
         grid=(blocks,),
-        in_specs=[whole, part],
+        in_specs=[whole, pl.BlockSpec(potential_wide.shape, lambda i: (0, 0, 0))],
         out_specs=part,
         out_shape=jax.ShapeDtypeStruct(block.shape, jnp.float32),
-        scratch_shapes=[pltpu.VMEM(block.shape, jnp.float32)],
+        scratch_shapes=[
+            pltpu.VMEM(block.shape, jnp.float32),
+            pltpu.VMEM((ny, nz, nb), jnp.float32),
+        ],
         name=f"interior_{stage}",
     )(block, potential_wide)
     halos = jnp.concatenate([low, high], axis=0)
@@ -212,10 +227,13 @@
     partial = pl.pallas_call(
         interior_kernel(stage, planes, ny, nz),
         grid=(blocks,),
-        in_specs=[whole, part],
+        in_specs=[whole, pl.BlockSpec(potential_wide.shape, lambda i: (0, 0, 0))],
         out_specs=part,
         out_shape=jax.ShapeDtypeStruct(block.shape, jnp.float32),
-        scratch_shapes=[pltpu.VMEM(block.shape, jnp.float32)],
+        scratch_shapes=[
+            pltpu.VMEM(block.shape, jnp.float32),
+            pltpu.VMEM((ny, nz, nb), jnp.float32),
+        ],
         name=f"interior_{stage}",
     )(block, potential_wide)
     operands = [low, high, partial]
@@ -258,7 +276,7 @@
 
 def shards(orbitals, potential):
     planes, ny, nz, nb = orbitals.shape
-    potential_wide = jnp.broadcast_to(potential[:, :, :, None], (planes, ny, nz, nb))
+    potential_wide = jnp.swapaxes(potential, 1, 2)
     cell_count = planes * ny * nz
     cell_weight = 1.0 / (cell_count * lax.axis_size("domain"))
     band = lax.axis_index("band")

time: 93.1 us -> 97 us (1.042)
  Pallas kernels: 34.3 us -> 41.8 us
  starting transfers between devices: 22 us -> 16 us
  waiting for transfers between devices: 24.7 us -> 28.1 us
  local copies, waits for them, and re-layouts: 3.29 us -> 2.1 us
    pallas_call x3, Pallas kernels: 22.6 us -> 30.2 us  [stencil_stage(): pl.pallas_call(interior_kernel(stage, planes, ny, nz), grid=(blocks,), in...]
    ppermute x1, waiting for transfers between devices: 0.01 us -> 5.01 us  [shards(): partner = lax.ppermute(own_block, 'band', [(0, 1), (1, 0)])]
    ppermute x8, starting transfers between devices: 5.92 us -> 2.81 us  [butterfly_sum(): values = values + lax.ppermute(values, axis, pairs)]
    ppermute x3, waiting for transfers between devices: 3.26 us -> 1.15 us  [exchange(): lax.ppermute(sends[0], axis, forward)]
    broadcast_in_dim x1 -> x0, local copies, waits for them, and re-layouts: 1.94 us -> none  [shards(): jnp.broadcast_to(potential[:, :, :, None], (planes, ny, nz, nb))]
    ppermute x3, starting transfers between devices: 3.16 us -> 1.43 us  [exchange(): lax.ppermute(sends[0], axis, forward)]
    ppermute x3, starting transfers between devices: 11 us -> 9.77 us  [exchange(): lax.ppermute(sends[1], axis, backward)]
  transfers between devices with their start and end apart: 15 -> 15, of which waited for: 9 -> 10; matrix products, arithmetic and copies ran while one was open for 7% -> 6% of each run, Pallas kernels for 28% -> 35%
where the time goes in v15:
time: 97 us; the launch traced here: 96.7 us
  Pallas kernels  41.8 us (43%)
  waiting for transfers between devices  28.1 us (29%)
  starting transfers between devices  16 us (16%)
  other arithmetic  4.68 us (5%)
  matrix products  3.22 us (3%)
  local copies, waits for them, and re-layouts  2.1 us (2%)
    pallas_call x3, Pallas kernels, stencil_stage(): pl.pallas_call(interior_kernel(stage, planes, ny, nz), grid=(blocks,), in...  30.2 us
    ppermute x8, waiting for transfers between devices, butterfly_sum(): values = values + lax.ppermute(values, axis, pairs)  22 us
    pallas_call x3, Pallas kernels, stencil_stage(): pl.pallas_call(finish_kernel(stage, planes, ny), grid=(blocks,), in_specs...  11.6 us
    ppermute x3, starting transfers between devices, exchange(): lax.ppermute(sends[1], axis, backward)  9.77 us
    ppermute x1, waiting for transfers between devices, shards(): partner = lax.ppermute(own_block, 'band', [(0, 1), (1, 0)])  5.01 us
    dot_general x4, matrix products, shards(): jnp.einsum('cb,ck->bk', rows, cols, preferred_element_type=jnp.float32)  3.22 us
    concatenate x3, other arithmetic, stencil_stage(): halos = jnp.concatenate([low, high], axis=0)  3.21 us
    ppermute x8, starting transfers between devices, butterfly_sum(): values = values + lax.ppermute(values, axis, pairs)  2.81 us
  transfers between devices with their start and end apart: 15, of which 10 were waited for; matrix products, arithmetic and copies ran while one was open for 6% of the time, Pallas kernels for 35%

profile of v15, /device:TPU:0, one launch (start us, length us, event | category | flops | bytes accessed | tf_op | source)
XLA Modules:
  0.0 96.7 jit_solution(6237132327517700616)
XLA Ops:
  0.6 1.3 %fusion = (bf16[4,16,32,128]{3,2,1,0:T(8,128)(2,1)S(1)}, bf16[4,16,32,128]{3,2,1,0:T(8,128)(2,1)S(1)}) fusion(bf16[8,16,32,128]{3,2,1,0:T(8,128)(2,1)} %refs_2_.1), kind=kLoop, calls=%fused_computation.9 | loop fusion | bytes 2097152 | tf_op jit(solution)/shard_map/slice | solution.py:293
  2.0 0.5 collective-permute-start
  2.5 5.0 %collective-permute-start.1 = (bf16[4,16,32,128]{3,2,1,0:T(8,128)(2,1)S(1)}, bf16[4,16,32,128]{3,2,1,0:T(8,128)(2,1)S(1)}, u32[]{:S(2)}, u32[]{:S(2)}) collective-permute-start(bf16[4,16,32,128]{3,2,1,0:T(8,128)(2,1)S(1)} %get-tuple-element.16), channel_id=1, source_target_pairs={{1,0},{2,1},{3,2},{4,3},{5,4},{6,5},{7,6},{8,7},{9,8},{10,9},{11,1... | collective-permute-start | bytes 1572872 | tf_op jit(solution)/shard_map/ppermute | solution.py:264
  7.5 0.8 copy.5
  8.3 10.1 %interior_first.1.refs_1_ = f32[8,16,32,128]{3,2,1,0:T(8,128)} custom-call(bf16[8,16,32,128]{3,2,1,0:T(8,128)(2,1)} %refs_2_.1, f32[8,32,16]{2,1,0:T(8,128)} %bitcast.22), custom_call_target="tpu_custom_call" | custom-call | tf_op jit(solution)/shard_map/interior_first/pallas_call | solution.py:136
  18.4 1.1 %pad_maximum_fusion.refs_0_ = bf16[8,16,32,128]{3,2,1,0:T(8,128)(2,1)} fusion(bf16[4,16,32,128]{3,2,1,0:T(8,128)(2,1)S(1)} %collective-permute-done.1, bf16[4,16,32,128]{3,2,1,0:T(8,128)(2,1)S(1)} %collective-permute-done), kind=kLoop, calls=%fused_computation.2 | loop fusion | flops 524288 | bytes 2097152 | tf_op jit(solution)/shard_map/concatenate | solution.py:148
  19.5 3.9 %finish_first.1 = (bf16[8,16,32,128]{3,2,1,0:T(8,128)(2,1)}, bf16[4,16,32,128]{3,2,1,0:T(8,128)(2,1)}, bf16[4,16,32,128]{3,2,1,0:T(8,128)(2,1)}) custom-call(bf16[8,16,32,128]{3,2,1,0:T(8,128)(2,1)} %pad_maximum_fusion.refs_0_, f32[8,16,32,128]{3,2,1,0:T(8,128)} %interior_first.1.refs_1_), custom_call_target="tpu_custom_call" | custom-call | tf_op jit(solution)/shard_map/finish_first/pallas_call | solution.py:161
  23.4 0.9 collective-permute-start.2
  24.3 3.5 %collective-permute-start.3 = (bf16[4,16,32,128]{3,2,1,0:T(8,128)(2,1)}, bf16[4,16,32,128]{3,2,1,0:T(8,128)(2,1)S(1)}, u32[]{:S(2)}, u32[]{:S(2)}) collective-permute-start(bf16[4,16,32,128]{3,2,1,0:T(8,128)(2,1)} %get-tuple-element.10), channel_id=1, source_target_pairs={{1,0},{2,1},{3,2},{4,3},{5,4},{6,5},{7,6},{8,7},{9,8},{10,9},{11,1... | collective-permute-start | bytes 1572872 | tf_op jit(solution)/shard_map/ppermute | solution.py:264
  27.8 10.1 %interior_filtered.1.refs_1_ = f32[8,16,32,128]{3,2,1,0:T(8,128)} custom-call(bf16[8,16,32,128]{3,2,1,0:T(8,128)(2,1)} %get-tuple-element.11.own_narrow, f32[8,32,16]{2,1,0:T(8,128)} %bitcast.23), custom_call_target="tpu_custom_call" | custom-call | tf_op jit(solution)/shard_map/interior_filtered/pallas_call | solution.py:136
  37.9 1.1 %pad_maximum_fusion.1.refs_0_ = bf16[8,16,32,128]{3,2,1,0:T(8,128)(2,1)} fusion(bf16[4,16,32,128]{3,2,1,0:T(8,128)(2,1)S(1)} %collective-permute-done.3, bf16[4,16,32,128]{3,2,1,0:T(8,128)(2,1)S(1)} %collective-permute-done.2), kind=kLoop, calls=%fused_computation.3 | loop fusion | flops 524288 | bytes 2097152 | tf_op jit(solution)/shard_map/concatenate | solution.py:148
  39.0 4.2 %finish_filtered.1 = (bf16[8,16,32,128]{3,2,1,0:T(8,128)(2,1)}, bf16[4,16,32,128]{3,2,1,0:T(8,128)(2,1)}, bf16[4,16,32,128]{3,2,1,0:T(8,128)(2,1)}) custom-call(bf16[8,16,32,128]{3,2,1,0:T(8,128)(2,1)} %pad_maximum_fusion.1.refs_0_, f32[8,16,32,128]{3,2,1,0:T(8,128)} %interior_filtered.1.refs_1_, bf16[8,16,32,128]{3,2,1,0:T(8,128)(2,1)} %refs_2_.1), custom_call_target="tpu_custom_call" | custom-call | tf_op jit(solution)/shard_map/finish_filtered/pallas_call | solution.py:161
  43.3 2.0 %collective-permute-start.4 = (bf16[4096,128]{1,0:T(8,128)(2,1)}, bf16[4096,128]{1,0:T(8,128)(2,1)S(1)}, u32[]{:S(2)}, u32[]{:S(2)}) collective-permute-start(bf16[4096,128]{1,0:T(8,128)(2,1)} %bitcast.19), channel_id=1, source_target_pairs={{0,16},{16,0},{1,17},{17,1},{2,18},{18,2},{3,19},{19,3},{4,20},{20... | collective-permute-start | bytes 3145736 | tf_op jit(solution)/shard_map/ppermute | solution.py:301
  45.3 1.2 %collective-permute-start.10 = (bf16[4,16,32,128]{3,2,1,0:T(8,128)(2,1)}, bf16[4,16,32,128]{3,2,1,0:T(8,128)(2,1)S(1)}, u32[]{:S(2)}, u32[]{:S(2)}) collective-permute-start(bf16[4,16,32,128]{3,2,1,0:T(8,128)(2,1)} %get-tuple-element.14), channel_id=1, source_target_pairs={{1,0},{2,1},{3,2},{4,3},{5,4},{6,5},{7,6},{8,7},{9,8},{10,9},{11,1... | collective-permute-start | bytes 1572872 | tf_op jit(solution)/shard_map/ppermute | solution.py:264
  46.5 10.0 %interior_applied.1.refs_1_ = f32[8,16,32,128]{3,2,1,0:T(8,128)} custom-call(bf16[8,16,32,128]{3,2,1,0:T(8,128)(2,1)} %get-tuple-element.6.own_narrow, f32[8,32,16]{2,1,0:T(8,128)} %bitcast.24), custom_call_target="tpu_custom_call" | custom-call | tf_op jit(solution)/shard_map/interior_applied/pallas_call | solution.py:136
  57.0 1.1 %collective-permute-done.9 = bf16[4,16,32,128]{3,2,1,0:T(8,128)(2,1)S(1)} collective-permute-done((bf16[4,16,32,128]{3,2,1,0:T(8,128)(2,1)}, bf16[4,16,32,128]{3,2,1,0:T(8,128)(2,1)S(1)}, u32[]{:S(2)}, u32[]{:S(2)}) %collective-permute-start.9) | collective-permute-done | bytes 524320 | tf_op jit(solution)/shard_map/ppermute | solution.py:264
  58.1 1.1 %pad_maximum_fusion.2.refs_0_ = bf16[8,16,32,128]{3,2,1,0:T(8,128)(2,1)} fusion(bf16[4,16,32,128]{3,2,1,0:T(8,128)(2,1)S(1)} %collective-permute-done.10, bf16[4,16,32,128]{3,2,1,0:T(8,128)(2,1)S(1)} %collective-permute-done.9), kind=kLoop, calls=%fused_computation.4 | loop fusion | flops 524288 | bytes 2097152 | tf_op jit(solution)/shard_map/concatenate | solution.py:148
  59.2 3.5 %finish_applied.1 = bf16[8,16,32,128]{3,2,1,0:T(8,128)(2,1)} custom-call(bf16[8,16,32,128]{3,2,1,0:T(8,128)(2,1)} %pad_maximum_fusion.2.refs_0_, f32[8,16,32,128]{3,2,1,0:T(8,128)} %interior_applied.1.refs_1_), custom_call_target="tpu_custom_call" | custom-call | tf_op jit(solution)/shard_map/finish_applied/pallas_call | solution.py:161
  62.6 1.8 %convolution_bitcast_fusion = f32[128,128]{1,0:T(8,128)S(1)} fusion(bf16[8,16,32,128]{3,2,1,0:T(8,128)(2,1)} %finish_applied.1, bf16[8,16,32,128]{3,2,1,0:T(8,128)(2,1)S(1)} %copy-done), kind=kOutput, calls=%fused_computation | convolution fusion | flops 134217728 | bytes 2162688 | tf_op jit(solution)/shard_map/cb,ck->bk/dot_general | solution.py:284
  64.4 5.0 %collective-permute-done.4 = bf16[4096,128]{1,0:T(8,128)(2,1)S(1)} collective-permute-done((bf16[4096,128]{1,0:T(8,128)(2,1)}, bf16[4096,128]{1,0:T(8,128)(2,1)S(1)}, u32[]{:S(2)}, u32[]{:S(2)}) %collective-permute-start.4) | collective-permute-done | bytes 1048608 | tf_op jit(solution)/shard_map/ppermute | solution.py:301
  69.5 0.5 fusion.2
  70.5 0.6 collective-permute-start.5
  71.5 0.6 collective-permute-done.5
  72.1 1.5 %collective-permute-start.6 = (f32[128,256]{1,0:T(8,128)S(1)}, f32[128,256]{1,0:T(8,128)S(1)}, u32[]{:S(2)}, u32[]{:S(2)}) collective-permute-start(f32[128,256]{1,0:T(8,128)S(1)} %add.24), channel_id=1, source_target_pairs={{0,2},{1,3},{2,0},{3,1},{4,6},{5,7},{6,4},{7,5},{8,10},{9,11},{10,... | collective-permute-start | bytes 393224 | tf_op jit(solution)/shard_map/ppermute | solution.py:272
  73.6 4.2 %collective-permute-done.12 = f32[128,256]{1,0:T(8,128)S(1)} collective-permute-done((f32[128,256]{1,0:T(8,128)S(1)}, f32[128,256]{1,0:T(8,128)S(1)}, u32[]{:S(2)}, u32[]{:S(2)}) %collective-permute-start.12) | collective-permute-done | bytes 131104 | tf_op jit(solution)/shard_map/ppermute | solution.py:272
  77.9 1.9 %collective-permute-done.6 = f32[128,256]{1,0:T(8,128)S(1)} collective-permute-done((f32[128,256]{1,0:T(8,128)S(1)}, f32[128,256]{1,0:T(8,128)S(1)}, u32[]{:S(2)}, u32[]{:S(2)}) %collective-permute-start.6) | collective-permute-done | bytes 131104 | tf_op jit(solution)/shard_map/ppermute | solution.py:272
  80.0 4.3 %collective-permute-done.13 = f32[128,256]{1,0:T(8,128)S(1)} collective-permute-done((f32[128,256]{1,0:T(8,128)S(1)}, f32[128,256]{1,0:T(8,128)S(1)}, u32[]{:S(2)}, u32[]{:S(2)}) %collective-permute-start.13) | collective-permute-done | bytes 131104 | tf_op jit(solution)/shard_map/ppermute | solution.py:272
  84.4 2.6 %collective-permute-done.7 = f32[128,256]{1,0:T(8,128)S(1)} collective-permute-done((f32[128,256]{1,0:T(8,128)S(1)}, f32[128,256]{1,0:T(8,128)S(1)}, u32[]{:S(2)}, u32[]{:S(2)}) %collective-permute-start.7) | collective-permute-done | bytes 131104 | tf_op jit(solution)/shard_map/ppermute | solution.py:272
  87.4 7.2 %collective-permute-done.14 = f32[128,256]{1,0:T(8,128)S(1)} collective-permute-done((f32[128,256]{1,0:T(8,128)S(1)}, f32[128,256]{1,0:T(8,128)S(1)}, u32[]{:S(2)}, u32[]{:S(2)}) %collective-permute-start.14) | collective-permute-done | bytes 131104 | tf_op jit(solution)/shard_map/ppermute | solution.py:272
  94.7 0.7 add_multiply_fusion
  95.3 0.7 collective-permute-done.8
  96.1 0.7 add_multiply_fusion.1
  (29 shorter events, 2.2 us)
Async XLA Ops:
  0.6 6.9 %copy-start.2 = (f32[8,16,32]{2,1,0:T(8,128)S(1)}, f32[8,16,32]{2,1,0:T(8,128)}, u32[]{:S(2)}) copy-start(f32[8,16,32]{2,1,0:T(8,128)} %param.3) | copy-start | bytes 49156
  2.0 16.4 %collective-permute-start = (bf16[4,16,32,128]{3,2,1,0:T(8,128)(2,1)S(1)}, bf16[4,16,32,128]{3,2,1,0:T(8,128)(2,1)S(1)}, u32[]{:S(2)}, u32[]{:S(2)}) collective-permute-start(bf16[4,16,32,128]{3,2,1,0:T(8,128)(2,1)S(1)} %get-tuple-element.15), channel_id=1, source_target_pairs={{0,1},{1,2},{2,3},{3,4},{4,5},{5,6},{6,7},{7,8},{8,9},{9,10},{10,1... | collective-permute-start | bytes 1572872 | tf_op jit(solution)/shard_map/ppermute | solution.py:264
  2.5 15.9 %collective-permute-start.1 = (bf16[4,16,32,128]{3,2,1,0:T(8,128)(2,1)S(1)}, bf16[4,16,32,128]{3,2,1,0:T(8,128)(2,1)S(1)}, u32[]{:S(2)}, u32[]{:S(2)}) collective-permute-start(bf16[4,16,32,128]{3,2,1,0:T(8,128)(2,1)S(1)} %get-tuple-element.16), channel_id=1, source_target_pairs={{1,0},{2,1},{3,2},{4,3},{5,4},{6,5},{7,6},{8,7},{9,8},{10,9},{11,1... | collective-permute-start | bytes 1572872 | tf_op jit(solution)/shard_map/ppermute | solution.py:264
  23.4 14.6 %collective-permute-start.2 = (bf16[4,16,32,128]{3,2,1,0:T(8,128)(2,1)}, bf16[4,16,32,128]{3,2,1,0:T(8,128)(2,1)S(1)}, u32[]{:S(2)}, u32[]{:S(2)}) collective-permute-start(bf16[4,16,32,128]{3,2,1,0:T(8,128)(2,1)} %get-tuple-element.9), channel_id=1, source_target_pairs={{0,1},{1,2},{2,3},{3,4},{4,5},{5,6},{6,7},{7,8},{8,9},{9,10},{10,1... | collective-permute-start | bytes 1572872 | tf_op jit(solution)/shard_map/ppermute | solution.py:264
  24.3 13.6 %collective-permute-start.3 = (bf16[4,16,32,128]{3,2,1,0:T(8,128)(2,1)}, bf16[4,16,32,128]{3,2,1,0:T(8,128)(2,1)S(1)}, u32[]{:S(2)}, u32[]{:S(2)}) collective-permute-start(bf16[4,16,32,128]{3,2,1,0:T(8,128)(2,1)} %get-tuple-element.10), channel_id=1, source_target_pairs={{1,0},{2,1},{3,2},{4,3},{5,4},{6,5},{7,6},{8,7},{9,8},{10,9},{11,1... | collective-permute-start | bytes 1572872 | tf_op jit(solution)/shard_map/ppermute | solution.py:264
  43.3 13.2 %copy-start = (bf16[8,16,32,128]{3,2,1,0:T(8,128)(2,1)S(1)}, bf16[8,16,32,128]{3,2,1,0:T(8,128)(2,1)}, u32[]{:S(2)}) copy-start(bf16[8,16,32,128]{3,2,1,0:T(8,128)(2,1)} %get-tuple-element.6.own_narrow) | copy-start | bytes 3145732
  43.3 26.2 %collective-permute-start.4 = (bf16[4096,128]{1,0:T(8,128)(2,1)}, bf16[4096,128]{1,0:T(8,128)(2,1)S(1)}, u32[]{:S(2)}, u32[]{:S(2)}) collective-permute-start(bf16[4096,128]{1,0:T(8,128)(2,1)} %bitcast.19), channel_id=1, source_target_pairs={{0,16},{16,0},{1,17},{17,1},{2,18},{18,2},{3,19},{19,3},{4,20},{20... | collective-permute-start | bytes 3145736 | tf_op jit(solution)/shard_map/ppermute | solution.py:301
  45.3 11.7 %collective-permute-start.10 = (bf16[4,16,32,128]{3,2,1,0:T(8,128)(2,1)}, bf16[4,16,32,128]{3,2,1,0:T(8,128)(2,1)S(1)}, u32[]{:S(2)}, u32[]{:S(2)}) collective-permute-start(bf16[4,16,32,128]{3,2,1,0:T(8,128)(2,1)} %get-tuple-element.14), channel_id=1, source_target_pairs={{1,0},{2,1},{3,2},{4,3},{5,4},{6,5},{7,6},{8,7},{9,8},{10,9},{11,1... | collective-permute-start | bytes 1572872 | tf_op jit(solution)/shard_map/ppermute | solution.py:264
  46.5 11.6 %collective-permute-start.9 = (bf16[4,16,32,128]{3,2,1,0:T(8,128)(2,1)}, bf16[4,16,32,128]{3,2,1,0:T(8,128)(2,1)S(1)}, u32[]{:S(2)}, u32[]{:S(2)}) collective-permute-start(bf16[4,16,32,128]{3,2,1,0:T(8,128)(2,1)} %get-tuple-element.13), channel_id=1, source_target_pairs={{0,1},{1,2},{2,3},{3,4},{4,5},{5,6},{6,7},{7,8},{8,9},{9,10},{10,1... | collective-permute-start | bytes 1572872 | tf_op jit(solution)/shard_map/ppermute | solution.py:264
  62.6 6.8 %copy-start.1 = (bf16[8,16,32,128]{3,2,1,0:T(8,128)(2,1)S(1)}, bf16[8,16,32,128]{3,2,1,0:T(8,128)(2,1)}, u32[]{:S(2)}) copy-start(bf16[8,16,32,128]{3,2,1,0:T(8,128)(2,1)} %finish_applied.1) | copy-start | bytes 3145732
  70.0 1.4 %collective-permute-start.11 = (f32[128,256]{1,0:T(8,128)S(1)}, f32[128,256]{1,0:T(8,128)S(1)}, u32[]{:S(2)}, u32[]{:S(2)}) collective-permute-start(f32[128,256]{1,0:T(8,128)S(1)} %maximum_select_fusion.1), channel_id=1, source_target_pairs={{0,1},{1,0},{2,3},{3,2},{4,5},{5,4},{6,7},{7,6},{8,9},{9,8},{10,11... | collective-permute-start | bytes 393224 | tf_op jit(solution)/shard_map/ppermute | solution.py:272
  70.5 1.5 %collective-permute-start.5 = (f32[128,256]{1,0:T(8,128)S(1)}, f32[128,256]{1,0:T(8,128)S(1)}, u32[]{:S(2)}, u32[]{:S(2)}) collective-permute-start(f32[128,256]{1,0:T(8,128)S(1)} %maximum_select_fusion), channel_id=1, source_target_pairs={{0,1},{1,0},{2,3},{3,2},{4,5},{5,4},{6,7},{7,6},{8,9},{9,8},{10,11... | collective-permute-start | bytes 393224 | tf_op jit(solution)/shard_map/ppermute | solution.py:272
  71.4 6.4 %collective-permute-start.12 = (f32[128,256]{1,0:T(8,128)S(1)}, f32[128,256]{1,0:T(8,128)S(1)}, u32[]{:S(2)}, u32[]{:S(2)}) collective-permute-start(f32[128,256]{1,0:T(8,128)S(1)} %add.28), channel_id=1, source_target_pairs={{0,2},{1,3},{2,0},{3,1},{4,6},{5,7},{6,4},{7,5},{8,10},{9,11},{10,... | collective-permute-start | bytes 393224 | tf_op jit(solution)/shard_map/ppermute | solution.py:272
  72.1 7.7 %collective-permute-start.6 = (f32[128,256]{1,0:T(8,128)S(1)}, f32[128,256]{1,0:T(8,128)S(1)}, u32[]{:S(2)}, u32[]{:S(2)}) collective-permute-start(f32[128,256]{1,0:T(8,128)S(1)} %add.24), channel_id=1, source_target_pairs={{0,2},{1,3},{2,0},{3,1},{4,6},{5,7},{6,4},{7,5},{8,10},{9,11},{10,... | collective-permute-start | bytes 393224 | tf_op jit(solution)/shard_map/ppermute | solution.py:272
  77.8 6.5 %collective-permute-start.13 = (f32[128,256]{1,0:T(8,128)S(1)}, f32[128,256]{1,0:T(8,128)S(1)}, u32[]{:S(2)}, u32[]{:S(2)}) collective-permute-start(f32[128,256]{1,0:T(8,128)S(1)} %add.29), channel_id=1, source_target_pairs={{0,4},{1,5},{2,6},{3,7},{4,0},{5,1},{6,2},{7,3},{8,12},{9,13},{10,... | collective-permute-start | bytes 393224 | tf_op jit(solution)/shard_map/ppermute | solution.py:272
  79.8 7.2 %collective-permute-start.7 = (f32[128,256]{1,0:T(8,128)S(1)}, f32[128,256]{1,0:T(8,128)S(1)}, u32[]{:S(2)}, u32[]{:S(2)}) collective-permute-start(f32[128,256]{1,0:T(8,128)S(1)} %add.25), channel_id=1, source_target_pairs={{0,4},{1,5},{2,6},{3,7},{4,0},{5,1},{6,2},{7,3},{8,12},{9,13},{10,... | collective-permute-start | bytes 393224 | tf_op jit(solution)/shard_map/ppermute | solution.py:272
  84.3 10.3 %collective-permute-start.14 = (f32[128,256]{1,0:T(8,128)S(1)}, f32[128,256]{1,0:T(8,128)S(1)}, u32[]{:S(2)}, u32[]{:S(2)}) collective-permute-start(f32[128,256]{1,0:T(8,128)S(1)} %add.30), channel_id=1, source_target_pairs={{0,8},{1,9},{2,10},{3,11},{4,12},{5,13},{6,14},{7,15},{8,0},{9,1},... | collective-permute-start | bytes 393224 | tf_op jit(solution)/shard_map/ppermute | solution.py:272
  87.1 9.0 %collective-permute-start.8 = (f32[128,256]{1,0:T(8,128)S(1)}, f32[128,256]{1,0:T(8,128)S(1)}, u32[]{:S(2)}, u32[]{:S(2)}) collective-permute-start(f32[128,256]{1,0:T(8,128)S(1)} %add.26), channel_id=1, source_target_pairs={{0,8},{1,9},{2,10},{3,11},{4,12},{5,13},{6,14},{7,15},{8,0},{9,1},... | collective-permute-start | bytes 393224 | tf_op jit(solution)/shard_map/ppermute | solution.py:272

commit v16 on v14

--- a/solution.py
+++ b/solution.py
@@ -246,6 +246,31 @@
     return lax.ppermute(sends[0], axis, forward), lax.ppermute(sends[1], axis, backward)
 
 
+def edge_copies(block):
+    planes = block.shape[0]
+    edge = jax.ShapeDtypeStruct((RADIUS,) + block.shape[1:], block.dtype)
+
+    def kernel(source, upper, lower, done):
+        copies = [
+            pltpu.make_async_copy(source.at[pl.ds(planes - RADIUS, RADIUS)], upper, done.at[0]),
+            pltpu.make_async_copy(source.at[pl.ds(0, RADIUS)], lower, done.at[1]),
+        ]
+        for copy in copies:
+            copy.start()
+        for copy in copies:
+            copy.wait()
+
+    anywhere = pl.BlockSpec(memory_space=pl.ANY)
+    return pl.pallas_call(
+        kernel,
+        in_specs=[anywhere],
+        out_specs=(anywhere, anywhere),
+        out_shape=(edge, edge),
+        scratch_shapes=[pltpu.SemaphoreType.DMA((2,))],
+        name="edge_copies",
+    )(block)
+
+
 def butterfly_sum(values, axis):
     count = lax.axis_size(axis)
     bit = 1
@@ -271,10 +296,7 @@
         jnp.concatenate([mine, theirs], axis=1),
         jnp.concatenate([theirs, mine], axis=1),
     )
-    planes_sent = (
-        lax.slice_in_dim(orbitals, planes - RADIUS, None, axis=0),
-        lax.slice_in_dim(orbitals, 0, RADIUS, axis=0),
-    )
+    planes_sent = edge_copies(orbitals)
     first, *first_sent = stencil_stage("first", orbitals, planes_sent, potential_wide)
     filtered, *filtered_sent = stencil_stage(
         "filtered", first, first_sent, potential_wide, orbitals

time: 93.1 us -> 125 us (1.34)
  Pallas kernels: 34.3 us -> 67.1 us
    pallas_call x0 -> x1, Pallas kernels: none -> 32.9 us  [edge_copies(): pl.pallas_call(kernel, in_specs=[anywhere], out_specs=(anywhere, anywhere...]
    slice x1 -> x0, local copies, waits for them, and re-layouts: 1.34 us -> none  [shards(): lax.slice_in_dim(orbitals, planes - RADIUS, None, axis=0)]
  transfers between devices with their start and end apart: 15 -> 15, of which waited for: 9 -> 9; matrix products, arithmetic and copies ran while one was open for 7% -> 6% of each run, Pallas kernels for 28% -> 21%
where the time goes in v16:
time: 125 us
  Pallas kernels  67.1 us (54%)
  waiting for transfers between devices  25.4 us (20%)
  starting transfers between devices  20.9 us (17%)
  other arithmetic  4.67 us (4%)
  matrix products  3.22 us (3%)
  local copies, waits for them, and re-layouts  2.79 us (2%)
    pallas_call x1, Pallas kernels, edge_copies(): pl.pallas_call(kernel, in_specs=[anywhere], out_specs=(anywhere, anywhere...  32.9 us
    pallas_call x3, Pallas kernels, stencil_stage(): pl.pallas_call(interior_kernel(stage, planes, ny, nz), grid=(blocks,), in...  22.5 us
    ppermute x8, waiting for transfers between devices, butterfly_sum(): values = values + lax.ppermute(values, axis, pairs)  21.7 us
    pallas_call x3, Pallas kernels, stencil_stage(): pl.pallas_call(finish_kernel(stage, planes, ny), grid=(blocks,), in_specs...  11.7 us
    ppermute x3, starting transfers between devices, exchange(): lax.ppermute(sends[1], axis, backward)  11.6 us
    ppermute x8, starting transfers between devices, butterfly_sum(): values = values + lax.ppermute(values, axis, pairs)  5.2 us
    ppermute x3, waiting for transfers between devices, exchange(): lax.ppermute(sends[0], axis, forward)  3.66 us
    dot_general x4, matrix products, shards(): jnp.einsum('cb,ck->bk', rows, cols, preferred_element_type=jnp.float32)  3.22 us
  transfers between devices with their start and end apart: 15, of which 9 were waited for; matrix products, arithmetic and copies ran while one was open for 6% of the time, Pallas kernels for 21%

profile of v16, /device:TPU:0, one launch (start us, length us, event | category | flops | bytes accessed | tf_op | source)
XLA Modules:
  0.0 124.9 jit_solution(4641960734321105734)
XLA Ops:
  0.6 32.9 %edge_copies.1 = (bf16[4,16,32,128]{3,2,1,0:T(8,128)(2,1)}, bf16[4,16,32,128]{3,2,1,0:T(8,128)(2,1)}) custom-call(bf16[8,16,32,128]{3,2,1,0:T(8,128)(2,1)} %refs_2_.1), custom_call_target="tpu_custom_call" | custom-call | tf_op jit(solution)/shard_map/edge_copies/pallas_call | solution.py:264
  33.5 0.5 collective-permute-start
  34.0 5.0 %collective-permute-start.1 = (bf16[4,16,32,128]{3,2,1,0:T(8,128)(2,1)}, bf16[4,16,32,128]{3,2,1,0:T(8,128)(2,1)S(1)}, u32[]{:S(2)}, u32[]{:S(2)}) collective-permute-start(bf16[4,16,32,128]{3,2,1,0:T(8,128)(2,1)} %get-tuple-element.12), channel_id=1, source_target_pairs={{1,0},{2,1},{3,2},{4,3},{5,4},{6,5},{7,6},{8,7},{9,8},{10,9},{11,1... | collective-permute-start | bytes 1572872 | tf_op jit(solution)/shard_map/ppermute | solution.py:246
  39.1 2.8 %broadcast_in_dim.2.pot = f32[8,16,32,128]{3,2,1,0:T(8,128)} broadcast(f32[8,16,32]{2,1,0:T(8,128)} %param.3), dimensions={0,1,2} | broadcast | bytes 2113536 | tf_op jit(solution)/shard_map/broadcast_in_dim | solution.py:286
  41.8 7.5 %interior_first.1.refs_1_ = f32[8,16,32,128]{3,2,1,0:T(8,128)} custom-call(bf16[8,16,32,128]{3,2,1,0:T(8,128)(2,1)} %refs_2_.1, f32[8,16,32,128]{3,2,1,0:T(8,128)} %broadcast_in_dim.2.pot), custom_call_target="tpu_custom_call" | custom-call | tf_op jit(solution)/shard_map/interior_first/pallas_call | solution.py:124
  49.4 1.1 pad_maximum_fusion.refs_0_
  50.4 4.0 %finish_first.1 = (bf16[8,16,32,128]{3,2,1,0:T(8,128)(2,1)}, bf16[4,16,32,128]{3,2,1,0:T(8,128)(2,1)}, bf16[4,16,32,128]{3,2,1,0:T(8,128)(2,1)}) custom-call(bf16[8,16,32,128]{3,2,1,0:T(8,128)(2,1)} %pad_maximum_fusion.refs_0_, f32[8,16,32,128]{3,2,1,0:T(8,128)} %interior_first.1.refs_1_), custom_call_target="tpu_custom_call" | custom-call | tf_op jit(solution)/shard_map/finish_first/pallas_call | solution.py:146
  54.4 1.7 %collective-permute-start.2 = (bf16[4,16,32,128]{3,2,1,0:T(8,128)(2,1)}, bf16[4,16,32,128]{3,2,1,0:T(8,128)(2,1)S(1)}, u32[]{:S(2)}, u32[]{:S(2)}) collective-permute-start(bf16[4,16,32,128]{3,2,1,0:T(8,128)(2,1)} %get-tuple-element.13), channel_id=1, source_target_pairs={{0,1},{1,2},{2,3},{3,4},{4,5},{5,6},{6,7},{7,8},{8,9},{9,10},{10,1... | collective-permute-start | bytes 1572872 | tf_op jit(solution)/shard_map/ppermute | solution.py:246
  56.1 2.8 %collective-permute-start.3 = (bf16[4,16,32,128]{3,2,1,0:T(8,128)(2,1)}, bf16[4,16,32,128]{3,2,1,0:T(8,128)(2,1)S(1)}, u32[]{:S(2)}, u32[]{:S(2)}) collective-permute-start(bf16[4,16,32,128]{3,2,1,0:T(8,128)(2,1)} %get-tuple-element.14), channel_id=1, source_target_pairs={{1,0},{2,1},{3,2},{4,3},{5,4},{6,5},{7,6},{8,7},{9,8},{10,9},{11,1... | collective-permute-start | bytes 1572872 | tf_op jit(solution)/shard_map/ppermute | solution.py:246
  58.9 7.5 %interior_filtered.1.refs_1_ = f32[8,16,32,128]{3,2,1,0:T(8,128)} custom-call(bf16[8,16,32,128]{3,2,1,0:T(8,128)(2,1)} %get-tuple-element.15.own_narrow, f32[8,16,32,128]{3,2,1,0:T(8,128)} %broadcast_in_dim.2.pot), custom_call_target="tpu_custom_call" | custom-call | tf_op jit(solution)/shard_map/interior_filtered/pallas_call | solution.py:124
  66.4 1.1 pad_maximum_fusion.1.refs_0_
  67.5 4.3 %finish_filtered.1 = (bf16[8,16,32,128]{3,2,1,0:T(8,128)(2,1)}, bf16[4,16,32,128]{3,2,1,0:T(8,128)(2,1)}, bf16[4,16,32,128]{3,2,1,0:T(8,128)(2,1)}) custom-call(bf16[8,16,32,128]{3,2,1,0:T(8,128)(2,1)} %pad_maximum_fusion.1.refs_0_, f32[8,16,32,128]{3,2,1,0:T(8,128)} %interior_filtered.1.refs_1_, bf16[8,16,32,128]{3,2,1,0:T(8,128)(2,1)} %refs_2_.1), custom_call_target="tpu_custom_call" | custom-call | tf_op jit(solution)/shard_map/finish_filtered/pallas_call | solution.py:146
  71.7 1.9 %collective-permute-start.4 = (bf16[4096,128]{1,0:T(8,128)(2,1)}, bf16[4096,128]{1,0:T(8,128)(2,1)S(1)}, u32[]{:S(2)}, u32[]{:S(2)}) collective-permute-start(bf16[4096,128]{1,0:T(8,128)(2,1)} %bitcast.18), channel_id=1, source_target_pairs={{0,16},{16,0},{1,17},{17,1},{2,18},{18,2},{3,19},{19,3},{4,20},{20... | collective-permute-start | bytes 3145736 | tf_op jit(solution)/shard_map/ppermute | solution.py:305
  73.6 3.8 %collective-permute-start.10 = (bf16[4,16,32,128]{3,2,1,0:T(8,128)(2,1)}, bf16[4,16,32,128]{3,2,1,0:T(8,128)(2,1)S(1)}, u32[]{:S(2)}, u32[]{:S(2)}) collective-permute-start(bf16[4,16,32,128]{3,2,1,0:T(8,128)(2,1)} %get-tuple-element.18), channel_id=1, source_target_pairs={{1,0},{2,1},{3,2},{4,3},{5,4},{6,5},{7,6},{8,7},{9,8},{10,9},{11,1... | collective-permute-start | bytes 1572872 | tf_op jit(solution)/shard_map/ppermute | solution.py:246
  77.5 7.5 %interior_applied.1.refs_1_ = f32[8,16,32,128]{3,2,1,0:T(8,128)} custom-call(bf16[8,16,32,128]{3,2,1,0:T(8,128)(2,1)} %get-tuple-element.8.own_narrow, f32[8,16,32,128]{3,2,1,0:T(8,128)} %broadcast_in_dim.2.pot), custom_call_target="tpu_custom_call" | custom-call | tf_op jit(solution)/shard_map/interior_applied/pallas_call | solution.py:124
  84.9 0.5 convolution_bitcast_fusion.1
  85.4 3.7 %collective-permute-done.9 = bf16[4,16,32,128]{3,2,1,0:T(8,128)(2,1)S(1)} collective-permute-done((bf16[4,16,32,128]{3,2,1,0:T(8,128)(2,1)}, bf16[4,16,32,128]{3,2,1,0:T(8,128)(2,1)S(1)}, u32[]{:S(2)}, u32[]{:S(2)}) %collective-permute-start.9) | collective-permute-done | bytes 524320 | tf_op jit(solution)/shard_map/ppermute | solution.py:246
  89.1 1.1 pad_maximum_fusion.2.refs_0_
  90.1 3.5 %finish_applied.1 = bf16[8,16,32,128]{3,2,1,0:T(8,128)(2,1)} custom-call(bf16[8,16,32,128]{3,2,1,0:T(8,128)(2,1)} %pad_maximum_fusion.2.refs_0_, f32[8,16,32,128]{3,2,1,0:T(8,128)} %interior_applied.1.refs_1_), custom_call_target="tpu_custom_call" | custom-call | tf_op jit(solution)/shard_map/finish_applied/pallas_call | solution.py:146
  93.6 1.8 %convolution_bitcast_fusion = f32[128,128]{1,0:T(8,128)S(1)} fusion(bf16[8,16,32,128]{3,2,1,0:T(8,128)(2,1)} %finish_applied.1, bf16[8,16,32,128]{3,2,1,0:T(8,128)(2,1)S(1)} %copy-done), kind=kOutput, calls=%fused_computation | convolution fusion | flops 134217728 | bytes 2162688 | tf_op jit(solution)/shard_map/cb,ck->bk/dot_general | solution.py:291
  95.5 0.5 fusion.1
  96.0 2.9 %collective-permute-start.11 = (f32[128,256]{1,0:T(8,128)S(1)}, f32[128,256]{1,0:T(8,128)S(1)}, u32[]{:S(2)}, u32[]{:S(2)}) collective-permute-start(f32[128,256]{1,0:T(8,128)S(1)} %maximum_select_fusion.1), channel_id=1, source_target_pairs={{0,1},{1,0},{2,3},{3,2},{4,5},{5,4},{6,7},{7,6},{8,9},{9,8},{10,11... | collective-permute-start | bytes 393224 | tf_op jit(solution)/shard_map/ppermute | solution.py:279
  99.9 0.8 collective-permute-done.5
  100.8 1.3 %collective-permute-start.6 = (f32[128,256]{1,0:T(8,128)S(1)}, f32[128,256]{1,0:T(8,128)S(1)}, u32[]{:S(2)}, u32[]{:S(2)}) collective-permute-start(f32[128,256]{1,0:T(8,128)S(1)} %add.24), channel_id=1, source_target_pairs={{0,2},{1,3},{2,0},{3,1},{4,6},{5,7},{6,4},{7,5},{8,10},{9,11},{10,... | collective-permute-start | bytes 393224 | tf_op jit(solution)/shard_map/ppermute | solution.py:279
  102.1 4.2 %collective-permute-done.12 = f32[128,256]{1,0:T(8,128)S(1)} collective-permute-done((f32[128,256]{1,0:T(8,128)S(1)}, f32[128,256]{1,0:T(8,128)S(1)}, u32[]{:S(2)}, u32[]{:S(2)}) %collective-permute-start.12) | collective-permute-done | bytes 131104 | tf_op jit(solution)/shard_map/ppermute | solution.py:279
  106.3 2.1 %collective-permute-done.6 = f32[128,256]{1,0:T(8,128)S(1)} collective-permute-done((f32[128,256]{1,0:T(8,128)S(1)}, f32[128,256]{1,0:T(8,128)S(1)}, u32[]{:S(2)}, u32[]{:S(2)}) %collective-permute-start.6) | collective-permute-done | bytes 131104 | tf_op jit(solution)/shard_map/ppermute | solution.py:279
  108.6 3.3 %collective-permute-done.13 = f32[128,256]{1,0:T(8,128)S(1)} collective-permute-done((f32[128,256]{1,0:T(8,128)S(1)}, f32[128,256]{1,0:T(8,128)S(1)}, u32[]{:S(2)}, u32[]{:S(2)}) %collective-permute-start.13) | collective-permute-done | bytes 131104 | tf_op jit(solution)/shard_map/ppermute | solution.py:279
  112.3 3.2 %collective-permute-done.7 = f32[128,256]{1,0:T(8,128)S(1)} collective-permute-done((f32[128,256]{1,0:T(8,128)S(1)}, f32[128,256]{1,0:T(8,128)S(1)}, u32[]{:S(2)}, u32[]{:S(2)}) %collective-permute-start.7) | collective-permute-done | bytes 131104 | tf_op jit(solution)/shard_map/ppermute | solution.py:279
  115.9 6.7 %collective-permute-done.14 = f32[128,256]{1,0:T(8,128)S(1)} collective-permute-done((f32[128,256]{1,0:T(8,128)S(1)}, f32[128,256]{1,0:T(8,128)S(1)}, u32[]{:S(2)}, u32[]{:S(2)}) %collective-permute-start.14) | collective-permute-done | bytes 131104 | tf_op jit(solution)/shard_map/ppermute | solution.py:279
  122.7 0.7 add_multiply_fusion
  123.4 0.8 collective-permute-done.8
  124.2 0.7 add_multiply_fusion.1
  (27 shorter events, 2.1 us)
Async XLA Ops:
  33.5 15.8 %collective-permute-start = (bf16[4,16,32,128]{3,2,1,0:T(8,128)(2,1)}, bf16[4,16,32,128]{3,2,1,0:T(8,128)(2,1)S(1)}, u32[]{:S(2)}, u32[]{:S(2)}) collective-permute-start(bf16[4,16,32,128]{3,2,1,0:T(8,128)(2,1)} %get-tuple-element.11), channel_id=1, source_target_pairs={{0,1},{1,2},{2,3},{3,4},{4,5},{5,6},{6,7},{7,8},{8,9},{9,10},{10,1... | collective-permute-start | bytes 1572872 | tf_op jit(solution)/shard_map/ppermute | solution.py:246
  34.0 15.3 %collective-permute-start.1 = (bf16[4,16,32,128]{3,2,1,0:T(8,128)(2,1)}, bf16[4,16,32,128]{3,2,1,0:T(8,128)(2,1)S(1)}, u32[]{:S(2)}, u32[]{:S(2)}) collective-permute-start(bf16[4,16,32,128]{3,2,1,0:T(8,128)(2,1)} %get-tuple-element.12), channel_id=1, source_target_pairs={{1,0},{2,1},{3,2},{4,3},{5,4},{6,5},{7,6},{8,7},{9,8},{10,9},{11,1... | collective-permute-start | bytes 1572872 | tf_op jit(solution)/shard_map/ppermute | solution.py:246
  54.4 12.0 %collective-permute-start.2 = (bf16[4,16,32,128]{3,2,1,0:T(8,128)(2,1)}, bf16[4,16,32,128]{3,2,1,0:T(8,128)(2,1)S(1)}, u32[]{:S(2)}, u32[]{:S(2)}) collective-permute-start(bf16[4,16,32,128]{3,2,1,0:T(8,128)(2,1)} %get-tuple-element.13), channel_id=1, source_target_pairs={{0,1},{1,2},{2,3},{3,4},{4,5},{5,6},{6,7},{7,8},{8,9},{9,10},{10,1... | collective-permute-start | bytes 1572872 | tf_op jit(solution)/shard_map/ppermute | solution.py:246
  56.1 10.3 %collective-permute-start.3 = (bf16[4,16,32,128]{3,2,1,0:T(8,128)(2,1)}, bf16[4,16,32,128]{3,2,1,0:T(8,128)(2,1)S(1)}, u32[]{:S(2)}, u32[]{:S(2)}) collective-permute-start(bf16[4,16,32,128]{3,2,1,0:T(8,128)(2,1)} %get-tuple-element.14), channel_id=1, source_target_pairs={{1,0},{2,1},{3,2},{4,3},{5,4},{6,5},{7,6},{8,7},{9,8},{10,9},{11,1... | collective-permute-start | bytes 1572872 | tf_op jit(solution)/shard_map/ppermute | solution.py:246
  71.7 23.7 %collective-permute-start.4 = (bf16[4096,128]{1,0:T(8,128)(2,1)}, bf16[4096,128]{1,0:T(8,128)(2,1)S(1)}, u32[]{:S(2)}, u32[]{:S(2)}) collective-permute-start(bf16[4096,128]{1,0:T(8,128)(2,1)} %bitcast.18), channel_id=1, source_target_pairs={{0,16},{16,0},{1,17},{17,1},{2,18},{18,2},{3,19},{19,3},{4,20},{20... | collective-permute-start | bytes 3145736 | tf_op jit(solution)/shard_map/ppermute | solution.py:305
  73.6 11.8 %collective-permute-start.10 = (bf16[4,16,32,128]{3,2,1,0:T(8,128)(2,1)}, bf16[4,16,32,128]{3,2,1,0:T(8,128)(2,1)S(1)}, u32[]{:S(2)}, u32[]{:S(2)}) collective-permute-start(bf16[4,16,32,128]{3,2,1,0:T(8,128)(2,1)} %get-tuple-element.18), channel_id=1, source_target_pairs={{1,0},{2,1},{3,2},{4,3},{5,4},{6,5},{7,6},{8,7},{9,8},{10,9},{11,1... | collective-permute-start | bytes 1572872 | tf_op jit(solution)/shard_map/ppermute | solution.py:246
  77.5 11.6 %collective-permute-start.9 = (bf16[4,16,32,128]{3,2,1,0:T(8,128)(2,1)}, bf16[4,16,32,128]{3,2,1,0:T(8,128)(2,1)S(1)}, u32[]{:S(2)}, u32[]{:S(2)}) collective-permute-start(bf16[4,16,32,128]{3,2,1,0:T(8,128)(2,1)} %get-tuple-element.17), channel_id=1, source_target_pairs={{0,1},{1,2},{2,3},{3,4},{4,5},{5,6},{6,7},{7,8},{8,9},{9,10},{10,1... | collective-permute-start | bytes 1572872 | tf_op jit(solution)/shard_map/ppermute | solution.py:246
  77.5 7.5 %copy-start = (bf16[8,16,32,128]{3,2,1,0:T(8,128)(2,1)S(1)}, bf16[8,16,32,128]{3,2,1,0:T(8,128)(2,1)}, u32[]{:S(2)}) copy-start(bf16[8,16,32,128]{3,2,1,0:T(8,128)(2,1)} %get-tuple-element.8.own_narrow) | copy-start | bytes 3145732
  93.6 1.8 %copy-start.1 = (bf16[8,16,32,128]{3,2,1,0:T(8,128)(2,1)S(1)}, bf16[8,16,32,128]{3,2,1,0:T(8,128)(2,1)}, u32[]{:S(2)}) copy-start(bf16[8,16,32,128]{3,2,1,0:T(8,128)(2,1)} %finish_applied.1) | copy-start | bytes 3145732
  96.0 3.9 %collective-permute-start.11 = (f32[128,256]{1,0:T(8,128)S(1)}, f32[128,256]{1,0:T(8,128)S(1)}, u32[]{:S(2)}, u32[]{:S(2)}) collective-permute-start(f32[128,256]{1,0:T(8,128)S(1)} %maximum_select_fusion.1), channel_id=1, source_target_pairs={{0,1},{1,0},{2,3},{3,2},{4,5},{5,4},{6,7},{7,6},{8,9},{9,8},{10,11... | collective-permute-start | bytes 393224 | tf_op jit(solution)/shard_map/ppermute | solution.py:279
  99.3 1.4 %collective-permute-start.5 = (f32[128,256]{1,0:T(8,128)S(1)}, f32[128,256]{1,0:T(8,128)S(1)}, u32[]{:S(2)}, u32[]{:S(2)}) collective-permute-start(f32[128,256]{1,0:T(8,128)S(1)} %maximum_select_fusion), channel_id=1, source_target_pairs={{0,1},{1,0},{2,3},{3,2},{4,5},{5,4},{6,7},{7,6},{8,9},{9,8},{10,11... | collective-permute-start | bytes 393224 | tf_op jit(solution)/shard_map/ppermute | solution.py:279
  99.9 6.4 %collective-permute-start.12 = (f32[128,256]{1,0:T(8,128)S(1)}, f32[128,256]{1,0:T(8,128)S(1)}, u32[]{:S(2)}, u32[]{:S(2)}) collective-permute-start(f32[128,256]{1,0:T(8,128)S(1)} %add.28), channel_id=1, source_target_pairs={{0,2},{1,3},{2,0},{3,1},{4,6},{5,7},{6,4},{7,5},{8,10},{9,11},{10,... | collective-permute-start | bytes 393224 | tf_op jit(solution)/shard_map/ppermute | solution.py:279
  100.8 7.7 %collective-permute-start.6 = (f32[128,256]{1,0:T(8,128)S(1)}, f32[128,256]{1,0:T(8,128)S(1)}, u32[]{:S(2)}, u32[]{:S(2)}) collective-permute-start(f32[128,256]{1,0:T(8,128)S(1)} %add.24), channel_id=1, source_target_pairs={{0,2},{1,3},{2,0},{3,1},{4,6},{5,7},{6,4},{7,5},{8,10},{9,11},{10,... | collective-permute-start | bytes 393224 | tf_op jit(solution)/shard_map/ppermute | solution.py:279
  106.3 5.6 %collective-permute-start.13 = (f32[128,256]{1,0:T(8,128)S(1)}, f32[128,256]{1,0:T(8,128)S(1)}, u32[]{:S(2)}, u32[]{:S(2)}) collective-permute-start(f32[128,256]{1,0:T(8,128)S(1)} %add.29), channel_id=1, source_target_pairs={{0,4},{1,5},{2,6},{3,7},{4,0},{5,1},{6,2},{7,3},{8,12},{9,13},{10,... | collective-permute-start | bytes 393224 | tf_op jit(solution)/shard_map/ppermute | solution.py:279
  108.5 7.0 %collective-permute-start.7 = (f32[128,256]{1,0:T(8,128)S(1)}, f32[128,256]{1,0:T(8,128)S(1)}, u32[]{:S(2)}, u32[]{:S(2)}) collective-permute-start(f32[128,256]{1,0:T(8,128)S(1)} %add.25), channel_id=1, source_target_pairs={{0,4},{1,5},{2,6},{3,7},{4,0},{5,1},{6,2},{7,3},{8,12},{9,13},{10,... | collective-permute-start | bytes 393224 | tf_op jit(solution)/shard_map/ppermute | solution.py:279
  111.9 10.8 %collective-permute-start.14 = (f32[128,256]{1,0:T(8,128)S(1)}, f32[128,256]{1,0:T(8,128)S(1)}, u32[]{:S(2)}, u32[]{:S(2)}) collective-permute-start(f32[128,256]{1,0:T(8,128)S(1)} %add.30), channel_id=1, source_target_pairs={{0,8},{1,9},{2,10},{3,11},{4,12},{5,13},{6,14},{7,15},{8,0},{9,1},... | collective-permute-start | bytes 393224 | tf_op jit(solution)/shard_map/ppermute | solution.py:279
  115.5 8.7 %collective-permute-start.8 = (f32[128,256]{1,0:T(8,128)S(1)}, f32[128,256]{1,0:T(8,128)S(1)}, u32[]{:S(2)}, u32[]{:S(2)}) collective-permute-start(f32[128,256]{1,0:T(8,128)S(1)} %add.26), channel_id=1, source_target_pairs={{0,8},{1,9},{2,10},{3,11},{4,12},{5,13},{6,14},{7,15},{8,0},{9,1},... | collective-permute-start | bytes 393224 | tf_op jit(solution)/shard_map/ppermute | solution.py:279

commit v17 on v14

--- a/solution.py
+++ b/solution.py
@@ -282,13 +282,14 @@
     own_block = filtered.reshape(cell_count, nb)
     partner = lax.ppermute(own_block, "band", [(0, 1), (1, 0)])
     correlation_piece = placed(gram(own_block, own_block), gram(own_block, partner))
-    correlation = butterfly_sum(correlation_piece, "domain") * cell_weight
     (applied_grid,) = stencil_stage(
         "applied", filtered, filtered_sent, potential_wide, keep_sends=False
     )
     applied = applied_grid.reshape(cell_count, nb)
     energy_piece = placed(gram(applied, own_block), gram(applied, partner))
-    projected = butterfly_sum(energy_piece, "domain") * cell_weight
+    summed = butterfly_sum(jnp.stack((correlation_piece, energy_piece)), "domain") * cell_weight
+    correlation = summed[0]
+    projected = summed[1]
     return (filtered, correlation, projected)
 
 

time: 93.1 us -> 98.7 us (1.060)
  waiting for transfers between devices: 24.7 us -> 30.3 us
  other arithmetic: 4.7 us -> 3.41 us
    ppermute x8 -> x4, waiting for transfers between devices: 21.4 us -> 28.7 us  [butterfly_sum(): values = values + lax.ppermute(values, axis, pairs)]
    ppermute x3, starting transfers between devices: 3.16 us -> 6.94 us  [exchange(): lax.ppermute(sends[0], axis, forward)]
    ppermute x3, starting transfers between devices: 11 us -> 7.48 us  [exchange(): lax.ppermute(sends[1], axis, backward)]
    ppermute x3, waiting for transfers between devices: 3.26 us -> 0.01 us  [exchange(): lax.ppermute(sends[0], axis, forward)]
    ppermute x1, waiting for transfers between devices: 0.01 us -> 1.54 us  [shards(): partner = lax.ppermute(own_block, 'band', [(0, 1), (1, 0)])]
    mul x2 -> x1, other arithmetic: 1.34 us -> 0.04 us  [shards(): butterfly_sum(jnp.stack((correlation_piece, energy_piece)), 'domain')]
    ppermute x8 -> x4, starting transfers between devices: 5.92 us -> 6.13 us  [butterfly_sum(): values = values + lax.ppermute(values, axis, pairs)]
  transfers between devices with their start and end apart: 15 -> 11, of which waited for: 9 -> 5; matrix products, arithmetic and copies ran while one was open for 7% -> 5% of each run, Pallas kernels for 28% -> 26%
where the time goes in v17:
time: 98.7 us; the launch traced here: 98.5 us
  Pallas kernels  34.3 us (35%)
  waiting for transfers between devices  30.3 us (31%)
  starting transfers between devices  22.5 us (23%)
  local copies, waits for them, and re-layouts  4.01 us (4%)
  other arithmetic  3.41 us (3%)
  matrix products  3.22 us (3%)
    ppermute x4, waiting for transfers between devices, butterfly_sum(): values = values + lax.ppermute(values, axis, pairs)  28.7 us
    pallas_call x3, Pallas kernels, stencil_stage(): pl.pallas_call(interior_kernel(stage, planes, ny, nz), grid=(blocks,), in...  22.6 us
    pallas_call x3, Pallas kernels, stencil_stage(): pl.pallas_call(finish_kernel(stage, planes, ny), grid=(blocks,), in_specs...  11.7 us
    ppermute x3, starting transfers between devices, exchange(): lax.ppermute(sends[1], axis, backward)  7.48 us
    ppermute x3, starting transfers between devices, exchange(): lax.ppermute(sends[0], axis, forward)  6.94 us
    ppermute x4, starting transfers between devices, butterfly_sum(): values = values + lax.ppermute(values, axis, pairs)  6.13 us
    dot_general x4, matrix products, shards(): jnp.einsum('cb,ck->bk', rows, cols, preferred_element_type=jnp.float32)  3.22 us
    concatenate x3, other arithmetic, stencil_stage(): halos = jnp.concatenate([low, high], axis=0)  3.2 us
  transfers between devices with their start and end apart: 11, of which 5 were waited for; matrix products, arithmetic and copies ran while one was open for 5% of the time, Pallas kernels for 26%

profile of v17, /device:TPU:0, one launch (start us, length us, event | category | flops | bytes accessed | tf_op | source)
XLA Modules:
  0.0 98.5 jit_solution(14337563231951946381)
XLA Ops:
  0.6 1.3 %fusion.1 = (bf16[4,16,32,128]{3,2,1,0:T(8,128)(2,1)S(1)}, bf16[4,16,32,128]{3,2,1,0:T(8,128)(2,1)S(1)}) fusion(bf16[8,16,32,128]{3,2,1,0:T(8,128)(2,1)} %refs_2_.1), kind=kLoop, calls=%fused_computation.14 | loop fusion | bytes 2097152 | tf_op jit(solution)/shard_map/slice | solution.py:275
  2.0 0.5 collective-permute-start
  2.5 5.0 %collective-permute-start.1 = (bf16[4,16,32,128]{3,2,1,0:T(8,128)(2,1)S(1)}, bf16[4,16,32,128]{3,2,1,0:T(8,128)(2,1)S(1)}, u32[]{:S(2)}, u32[]{:S(2)}) collective-permute-start(bf16[4,16,32,128]{3,2,1,0:T(8,128)(2,1)S(1)} %get-tuple-element.16), channel_id=1, source_target_pairs={{1,0},{2,1},{3,2},{4,3},{5,4},{6,5},{7,6},{8,7},{9,8},{10,9},{11,1... | collective-permute-start | bytes 1572872 | tf_op jit(solution)/shard_map/ppermute | solution.py:246
  7.5 1.9 %broadcast_in_dim.2.pot = f32[8,16,32,128]{3,2,1,0:T(8,128)} broadcast(f32[8,16,32]{2,1,0:T(8,128)S(1)} %copy-done.2), dimensions={0,1,2} | broadcast | bytes 2113536 | tf_op jit(solution)/shard_map/broadcast_in_dim | solution.py:261
  9.5 7.5 %interior_first.1.refs_1_ = f32[8,16,32,128]{3,2,1,0:T(8,128)} custom-call(bf16[8,16,32,128]{3,2,1,0:T(8,128)(2,1)} %refs_2_.1, f32[8,16,32,128]{3,2,1,0:T(8,128)} %broadcast_in_dim.2.pot), custom_call_target="tpu_custom_call" | custom-call | tf_op jit(solution)/shard_map/interior_first/pallas_call | solution.py:124
  17.0 1.1 %pad_maximum_fusion.refs_0_ = bf16[8,16,32,128]{3,2,1,0:T(8,128)(2,1)} fusion(bf16[4,16,32,128]{3,2,1,0:T(8,128)(2,1)S(1)} %collective-permute-done.1, bf16[4,16,32,128]{3,2,1,0:T(8,128)(2,1)S(1)} %collective-permute-done), kind=kLoop, calls=%fused_computation.4 | loop fusion | flops 524288 | bytes 2097152 | tf_op jit(solution)/shard_map/concatenate | solution.py:133
  18.1 4.0 %finish_first.1 = (bf16[8,16,32,128]{3,2,1,0:T(8,128)(2,1)}, bf16[4,16,32,128]{3,2,1,0:T(8,128)(2,1)}, bf16[4,16,32,128]{3,2,1,0:T(8,128)(2,1)}) custom-call(bf16[8,16,32,128]{3,2,1,0:T(8,128)(2,1)} %pad_maximum_fusion.refs_0_, f32[8,16,32,128]{3,2,1,0:T(8,128)} %interior_first.1.refs_1_), custom_call_target="tpu_custom_call" | custom-call | tf_op jit(solution)/shard_map/finish_first/pallas_call | solution.py:146
  22.0 2.3 %collective-permute-start.2 = (bf16[4,16,32,128]{3,2,1,0:T(8,128)(2,1)}, bf16[4,16,32,128]{3,2,1,0:T(8,128)(2,1)S(1)}, u32[]{:S(2)}, u32[]{:S(2)}) collective-permute-start(bf16[4,16,32,128]{3,2,1,0:T(8,128)(2,1)} %get-tuple-element.9), channel_id=1, source_target_pairs={{0,1},{1,2},{2,3},{3,4},{4,5},{5,6},{6,7},{7,8},{8,9},{9,10},{10,1... | collective-permute-start | bytes 1572872 | tf_op jit(solution)/shard_map/ppermute | solution.py:246
  24.4 2.1 %collective-permute-start.3 = (bf16[4,16,32,128]{3,2,1,0:T(8,128)(2,1)}, bf16[4,16,32,128]{3,2,1,0:T(8,128)(2,1)S(1)}, u32[]{:S(2)}, u32[]{:S(2)}) collective-permute-start(bf16[4,16,32,128]{3,2,1,0:T(8,128)(2,1)} %get-tuple-element.10), channel_id=1, source_target_pairs={{1,0},{2,1},{3,2},{4,3},{5,4},{6,5},{7,6},{8,7},{9,8},{10,9},{11,1... | collective-permute-start | bytes 1572872 | tf_op jit(solution)/shard_map/ppermute | solution.py:246
  26.5 7.5 %interior_filtered.1.refs_1_ = f32[8,16,32,128]{3,2,1,0:T(8,128)} custom-call(bf16[8,16,32,128]{3,2,1,0:T(8,128)(2,1)} %get-tuple-element.11.own_narrow, f32[8,16,32,128]{3,2,1,0:T(8,128)} %broadcast_in_dim.2.pot), custom_call_target="tpu_custom_call" | custom-call | tf_op jit(solution)/shard_map/interior_filtered/pallas_call | solution.py:124
  34.0 1.1 %pad_maximum_fusion.1.refs_0_ = bf16[8,16,32,128]{3,2,1,0:T(8,128)(2,1)} fusion(bf16[4,16,32,128]{3,2,1,0:T(8,128)(2,1)S(1)} %collective-permute-done.3, bf16[4,16,32,128]{3,2,1,0:T(8,128)(2,1)S(1)} %collective-permute-done.2), kind=kLoop, calls=%fused_computation.5 | loop fusion | flops 524288 | bytes 2097152 | tf_op jit(solution)/shard_map/concatenate | solution.py:133
  35.1 4.3 %finish_filtered.1 = (bf16[8,16,32,128]{3,2,1,0:T(8,128)(2,1)}, bf16[4,16,32,128]{3,2,1,0:T(8,128)(2,1)}, bf16[4,16,32,128]{3,2,1,0:T(8,128)(2,1)}) custom-call(bf16[8,16,32,128]{3,2,1,0:T(8,128)(2,1)} %pad_maximum_fusion.1.refs_0_, f32[8,16,32,128]{3,2,1,0:T(8,128)} %interior_filtered.1.refs_1_, bf16[8,16,32,128]{3,2,1,0:T(8,128)(2,1)} %refs_2_.1), custom_call_target="tpu_custom_call" | custom-call | tf_op jit(solution)/shard_map/finish_filtered/pallas_call | solution.py:146
  39.4 1.9 %collective-permute-start.4 = (bf16[4096,128]{1,0:T(8,128)(2,1)}, bf16[4096,128]{1,0:T(8,128)(2,1)S(1)}, u32[]{:S(2)}, u32[]{:S(2)}) collective-permute-start(bf16[4096,128]{1,0:T(8,128)(2,1)} %bitcast.30), channel_id=1, source_target_pairs={{0,16},{16,0},{1,17},{17,1},{2,18},{18,2},{3,19},{19,3},{4,20},{20... | collective-permute-start | bytes 3145736 | tf_op jit(solution)/shard_map/ppermute | solution.py:283
  41.3 4.1 %collective-permute-start.5 = (bf16[4,16,32,128]{3,2,1,0:T(8,128)(2,1)}, bf16[4,16,32,128]{3,2,1,0:T(8,128)(2,1)S(1)}, u32[]{:S(2)}, u32[]{:S(2)}) collective-permute-start(bf16[4,16,32,128]{3,2,1,0:T(8,128)(2,1)} %get-tuple-element.13), channel_id=1, source_target_pairs={{0,1},{1,2},{2,3},{3,4},{4,5},{5,6},{6,7},{7,8},{8,9},{9,10},{10,1... | collective-permute-start | bytes 1572872 | tf_op jit(solution)/shard_map/ppermute | solution.py:246
  45.4 0.3 collective-permute-start.6
  45.7 7.6 %interior_applied.1.refs_1_ = f32[8,16,32,128]{3,2,1,0:T(8,128)} custom-call(bf16[8,16,32,128]{3,2,1,0:T(8,128)(2,1)} %get-tuple-element.6.own_narrow, f32[8,16,32,128]{3,2,1,0:T(8,128)} %broadcast_in_dim.2.pot), custom_call_target="tpu_custom_call" | custom-call | tf_op jit(solution)/shard_map/interior_applied/pallas_call | solution.py:124
  53.3 0.5 convolution_bitcast_fusion.3
  53.8 1.1 %pad_maximum_fusion.2.refs_0_ = bf16[8,16,32,128]{3,2,1,0:T(8,128)(2,1)} fusion(bf16[4,16,32,128]{3,2,1,0:T(8,128)(2,1)S(1)} %collective-permute-done.6, bf16[4,16,32,128]{3,2,1,0:T(8,128)(2,1)S(1)} %collective-permute-done.5), kind=kLoop, calls=%fused_computation.6 | loop fusion | flops 524288 | bytes 2097152 | tf_op jit(solution)/shard_map/concatenate | solution.py:133
  54.9 3.5 %finish_applied.1 = bf16[8,16,32,128]{3,2,1,0:T(8,128)(2,1)} custom-call(bf16[8,16,32,128]{3,2,1,0:T(8,128)(2,1)} %pad_maximum_fusion.2.refs_0_, f32[8,16,32,128]{3,2,1,0:T(8,128)} %interior_applied.1.refs_1_), custom_call_target="tpu_custom_call" | custom-call | tf_op jit(solution)/shard_map/finish_applied/pallas_call | solution.py:146
  58.4 1.8 %convolution_bitcast_fusion.1 = f32[1,128,128]{2,1,0:T(8,128)S(1)} fusion(bf16[8,16,32,128]{3,2,1,0:T(8,128)(2,1)} %finish_applied.1, bf16[8,16,32,128]{3,2,1,0:T(8,128)(2,1)S(1)} %copy-done), kind=kOutput, calls=%fused_computation.1 | convolution fusion | flops 134217728 | bytes 2162688 | tf_op jit(solution)/shard_map/cb,ck->bk/dot_general | solution.py:266
  60.2 1.5 %collective-permute-done.4 = bf16[4096,128]{1,0:T(8,128)(2,1)S(1)} collective-permute-done((bf16[4096,128]{1,0:T(8,128)(2,1)}, bf16[4096,128]{1,0:T(8,128)(2,1)S(1)}, u32[]{:S(2)}, u32[]{:S(2)}) %collective-permute-start.4) | collective-permute-done | bytes 1048608 | tf_op jit(solution)/shard_map/ppermute | solution.py:283
  61.7 0.5 convolution_bitcast_fusion.2
  62.2 0.5 convolution_bitcast_fusion
  62.7 3.8 %collective-permute-start.7 = (f32[2,128,256]{2,1,0:T(8,128)S(1)}, f32[2,128,256]{2,1,0:T(8,128)S(1)}, u32[]{:S(2)}, u32[]{:S(2)}) collective-permute-start(f32[2,128,256]{2,1,0:T(8,128)S(1)} %pad_maximum_fusion.3), channel_id=1, source_target_pairs={{0,1},{1,0},{2,3},{3,2},{4,5},{5,4},{6,7},{7,6},{8,9},{9,8},{10,11... | collective-permute-start | bytes 786440 | tf_op jit(solution)/shard_map/ppermute | solution.py:254
  66.5 1.2 %collective-permute-done.7 = f32[2,128,256]{2,1,0:T(8,128)S(1)} collective-permute-done((f32[2,128,256]{2,1,0:T(8,128)S(1)}, f32[2,128,256]{2,1,0:T(8,128)S(1)}, u32[]{:S(2)}, u32[]{:S(2)}) %collective-permute-start.7) | collective-permute-done | bytes 262176 | tf_op jit(solution)/shard_map/ppermute | solution.py:254
  67.7 0.4 collective-permute-start.8
  68.1 8.3 %collective-permute-done.8 = f32[2,128,256]{2,1,0:T(8,128)S(1)} collective-permute-done((f32[2,128,256]{2,1,0:T(8,128)S(1)}, f32[2,128,256]{2,1,0:T(8,128)S(1)}, u32[]{:S(2)}, u32[]{:S(2)}) %collective-permute-start.8) | collective-permute-done | bytes 262176 | tf_op jit(solution)/shard_map/ppermute | solution.py:254
  76.4 0.1 collective-permute-start.9
  76.5 7.8 %collective-permute-done.9 = f32[2,128,256]{2,1,0:T(8,128)S(1)} collective-permute-done((f32[2,128,256]{2,1,0:T(8,128)S(1)}, f32[2,128,256]{2,1,0:T(8,128)S(1)}, u32[]{:S(2)}, u32[]{:S(2)}) %collective-permute-start.9) | collective-permute-done | bytes 262176 | tf_op jit(solution)/shard_map/ppermute | solution.py:254
  84.3 1.9 %collective-permute-start.10 = (f32[2,128,256]{2,1,0:T(8,128)S(1)}, f32[2,128,256]{2,1,0:T(8,128)S(1)}, u32[]{:S(2)}, u32[]{:S(2)}) collective-permute-start(f32[2,128,256]{2,1,0:T(8,128)S(1)} %add.14), channel_id=1, source_target_pairs={{0,8},{1,9},{2,10},{3,11},{4,12},{5,13},{6,14},{7,15},{8,0},{9,1},... | collective-permute-start | bytes 786440 | tf_op jit(solution)/shard_map/ppermute | solution.py:254
  86.2 11.6 %collective-permute-done.10 = f32[2,128,256]{2,1,0:T(8,128)S(1)} collective-permute-done((f32[2,128,256]{2,1,0:T(8,128)S(1)}, f32[2,128,256]{2,1,0:T(8,128)S(1)}, u32[]{:S(2)}, u32[]{:S(2)}) %collective-permute-start.10) | collective-permute-done | bytes 262176 | tf_op jit(solution)/shard_map/ppermute | solution.py:254
  97.8 0.7 slice_bitcast_fusion
  (18 shorter events, 0.2 us)
Async XLA Ops:
  0.6 6.9 %copy-start.2 = (f32[8,16,32]{2,1,0:T(8,128)S(1)}, f32[8,16,32]{2,1,0:T(8,128)}, u32[]{:S(2)}) copy-start(f32[8,16,32]{2,1,0:T(8,128)} %param.3) | copy-start | bytes 49156
  2.0 15.0 %collective-permute-start = (bf16[4,16,32,128]{3,2,1,0:T(8,128)(2,1)S(1)}, bf16[4,16,32,128]{3,2,1,0:T(8,128)(2,1)S(1)}, u32[]{:S(2)}, u32[]{:S(2)}) collective-permute-start(bf16[4,16,32,128]{3,2,1,0:T(8,128)(2,1)S(1)} %get-tuple-element.15), channel_id=1, source_target_pairs={{0,1},{1,2},{2,3},{3,4},{4,5},{5,6},{6,7},{7,8},{8,9},{9,10},{10,1... | collective-permute-start | bytes 1572872 | tf_op jit(solution)/shard_map/ppermute | solution.py:246
  2.5 14.5 %collective-permute-start.1 = (bf16[4,16,32,128]{3,2,1,0:T(8,128)(2,1)S(1)}, bf16[4,16,32,128]{3,2,1,0:T(8,128)(2,1)S(1)}, u32[]{:S(2)}, u32[]{:S(2)}) collective-permute-start(bf16[4,16,32,128]{3,2,1,0:T(8,128)(2,1)S(1)} %get-tuple-element.16), channel_id=1, source_target_pairs={{1,0},{2,1},{3,2},{4,3},{5,4},{6,5},{7,6},{8,7},{9,8},{10,9},{11,1... | collective-permute-start | bytes 1572872 | tf_op jit(solution)/shard_map/ppermute | solution.py:246
  22.0 12.0 %collective-permute-start.2 = (bf16[4,16,32,128]{3,2,1,0:T(8,128)(2,1)}, bf16[4,16,32,128]{3,2,1,0:T(8,128)(2,1)S(1)}, u32[]{:S(2)}, u32[]{:S(2)}) collective-permute-start(bf16[4,16,32,128]{3,2,1,0:T(8,128)(2,1)} %get-tuple-element.9), channel_id=1, source_target_pairs={{0,1},{1,2},{2,3},{3,4},{4,5},{5,6},{6,7},{7,8},{8,9},{9,10},{10,1... | collective-permute-start | bytes 1572872 | tf_op jit(solution)/shard_map/ppermute | solution.py:246
  24.4 9.7 %collective-permute-start.3 = (bf16[4,16,32,128]{3,2,1,0:T(8,128)(2,1)}, bf16[4,16,32,128]{3,2,1,0:T(8,128)(2,1)S(1)}, u32[]{:S(2)}, u32[]{:S(2)}) collective-permute-start(bf16[4,16,32,128]{3,2,1,0:T(8,128)(2,1)} %get-tuple-element.10), channel_id=1, source_target_pairs={{1,0},{2,1},{3,2},{4,3},{5,4},{6,5},{7,6},{8,7},{9,8},{10,9},{11,1... | collective-permute-start | bytes 1572872 | tf_op jit(solution)/shard_map/ppermute | solution.py:246
  39.4 22.3 %collective-permute-start.4 = (bf16[4096,128]{1,0:T(8,128)(2,1)}, bf16[4096,128]{1,0:T(8,128)(2,1)S(1)}, u32[]{:S(2)}, u32[]{:S(2)}) collective-permute-start(bf16[4096,128]{1,0:T(8,128)(2,1)} %bitcast.30), channel_id=1, source_target_pairs={{0,16},{16,0},{1,17},{17,1},{2,18},{18,2},{3,19},{19,3},{4,20},{20... | collective-permute-start | bytes 3145736 | tf_op jit(solution)/shard_map/ppermute | solution.py:283
  41.3 12.5 %collective-permute-start.5 = (bf16[4,16,32,128]{3,2,1,0:T(8,128)(2,1)}, bf16[4,16,32,128]{3,2,1,0:T(8,128)(2,1)S(1)}, u32[]{:S(2)}, u32[]{:S(2)}) collective-permute-start(bf16[4,16,32,128]{3,2,1,0:T(8,128)(2,1)} %get-tuple-element.13), channel_id=1, source_target_pairs={{0,1},{1,2},{2,3},{3,4},{4,5},{5,6},{6,7},{7,8},{8,9},{9,10},{10,1... | collective-permute-start | bytes 1572872 | tf_op jit(solution)/shard_map/ppermute | solution.py:246
  45.4 8.4 %collective-permute-start.6 = (bf16[4,16,32,128]{3,2,1,0:T(8,128)(2,1)}, bf16[4,16,32,128]{3,2,1,0:T(8,128)(2,1)S(1)}, u32[]{:S(2)}, u32[]{:S(2)}) collective-permute-start(bf16[4,16,32,128]{3,2,1,0:T(8,128)(2,1)} %get-tuple-element.14), channel_id=1, source_target_pairs={{1,0},{2,1},{3,2},{4,3},{5,4},{6,5},{7,6},{8,7},{9,8},{10,9},{11,1... | collective-permute-start | bytes 1572872 | tf_op jit(solution)/shard_map/ppermute | solution.py:246
  45.7 7.6 %copy-start = (bf16[8,16,32,128]{3,2,1,0:T(8,128)(2,1)S(1)}, bf16[8,16,32,128]{3,2,1,0:T(8,128)(2,1)}, u32[]{:S(2)}) copy-start(bf16[8,16,32,128]{3,2,1,0:T(8,128)(2,1)} %get-tuple-element.6.own_narrow) | copy-start | bytes 3145732
  58.4 3.8 %copy-start.1 = (bf16[8,16,32,128]{3,2,1,0:T(8,128)(2,1)S(1)}, bf16[8,16,32,128]{3,2,1,0:T(8,128)(2,1)}, u32[]{:S(2)}) copy-start(bf16[8,16,32,128]{3,2,1,0:T(8,128)(2,1)} %finish_applied.1) | copy-start | bytes 3145732
  62.7 5.0 %collective-permute-start.7 = (f32[2,128,256]{2,1,0:T(8,128)S(1)}, f32[2,128,256]{2,1,0:T(8,128)S(1)}, u32[]{:S(2)}, u32[]{:S(2)}) collective-permute-start(f32[2,128,256]{2,1,0:T(8,128)S(1)} %pad_maximum_fusion.3), channel_id=1, source_target_pairs={{0,1},{1,0},{2,3},{3,2},{4,5},{5,4},{6,7},{7,6},{8,9},{9,8},{10,11... | collective-permute-start | bytes 786440 | tf_op jit(solution)/shard_map/ppermute | solution.py:254
  67.7 8.7 %collective-permute-start.8 = (f32[2,128,256]{2,1,0:T(8,128)S(1)}, f32[2,128,256]{2,1,0:T(8,128)S(1)}, u32[]{:S(2)}, u32[]{:S(2)}) collective-permute-start(f32[2,128,256]{2,1,0:T(8,128)S(1)} %fusion), channel_id=1, source_target_pairs={{0,2},{1,3},{2,0},{3,1},{4,6},{5,7},{6,4},{7,5},{8,10},{9,11},{10,... | collective-permute-start | bytes 786440 | tf_op jit(solution)/shard_map/ppermute | solution.py:254
  76.4 7.8 %collective-permute-start.9 = (f32[2,128,256]{2,1,0:T(8,128)S(1)}, f32[2,128,256]{2,1,0:T(8,128)S(1)}, u32[]{:S(2)}, u32[]{:S(2)}) collective-permute-start(f32[2,128,256]{2,1,0:T(8,128)S(1)} %fusion.10), channel_id=1, source_target_pairs={{0,4},{1,5},{2,6},{3,7},{4,0},{5,1},{6,2},{7,3},{8,12},{9,13},{10,... | collective-permute-start | bytes 786440 | tf_op jit(solution)/shard_map/ppermute | solution.py:254
  84.3 13.4 %collective-permute-start.10 = (f32[2,128,256]{2,1,0:T(8,128)S(1)}, f32[2,128,256]{2,1,0:T(8,128)S(1)}, u32[]{:S(2)}, u32[]{:S(2)}) collective-permute-start(f32[2,128,256]{2,1,0:T(8,128)S(1)} %add.14), channel_id=1, source_target_pairs={{0,8},{1,9},{2,10},{3,11},{4,12},{5,13},{6,14},{7,15},{8,0},{9,1},... | collective-permute-start | bytes 786440 | tf_op jit(solution)/shard_map/ppermute | solution.py:254

commit v18 on v14

--- a/solution.py
+++ b/solution.py
@@ -256,6 +256,13 @@
     return values
 
 
+def split_sum(values, axis):
+    half = values.shape[0] // 2
+    return jnp.concatenate(
+        [butterfly_sum(values[:half], axis), butterfly_sum(values[half:], axis)], axis=0
+    )
+
+
 def shards(orbitals, potential):
     planes, ny, nz, nb = orbitals.shape
     potential_wide = jnp.broadcast_to(potential[:, :, :, None], (planes, ny, nz, nb))
@@ -282,13 +289,13 @@
     own_block = filtered.reshape(cell_count, nb)
     partner = lax.ppermute(own_block, "band", [(0, 1), (1, 0)])
     correlation_piece = placed(gram(own_block, own_block), gram(own_block, partner))
-    correlation = butterfly_sum(correlation_piece, "domain") * cell_weight
+    correlation = split_sum(correlation_piece, "domain") * cell_weight
     (applied_grid,) = stencil_stage(
         "applied", filtered, filtered_sent, potential_wide, keep_sends=False
     )
     applied = applied_grid.reshape(cell_count, nb)
     energy_piece = placed(gram(applied, own_block), gram(applied, partner))
-    projected = butterfly_sum(energy_piece, "domain") * cell_weight
+    projected = split_sum(energy_piece, "domain") * cell_weight
     return (filtered, correlation, projected)
 
 

time: 93.1 us -> 93 us (level)
  waiting for transfers between devices: 24.7 us -> 11.7 us
  starting transfers between devices: 22 us -> 34.7 us
    ppermute x8 -> x16, starting transfers between devices: 5.92 us -> 18.4 us  [butterfly_sum(): values = values + lax.ppermute(values, axis, pairs)]
    ppermute x8 -> x16, waiting for transfers between devices: 21.4 us -> 10.1 us  [butterfly_sum(): values = values + lax.ppermute(values, axis, pairs)]
    ppermute x3, starting transfers between devices: 3.16 us -> 7 us  [exchange(): lax.ppermute(sends[0], axis, forward)]
    ppermute x3, starting transfers between devices: 11 us -> 7.42 us  [exchange(): lax.ppermute(sends[1], axis, backward)]
    ppermute x3, waiting for transfers between devices: 3.26 us -> 0.01 us  [exchange(): lax.ppermute(sends[0], axis, forward)]
    ppermute x1, waiting for transfers between devices: 0.01 us -> 1.58 us  [shards(): partner = lax.ppermute(own_block, 'band', [(0, 1), (1, 0)])]
  transfers between devices with their start and end apart: 15 -> 23, of which waited for: 9 -> 9; matrix products, arithmetic and copies ran while one was open for 7% -> 7% of each run, Pallas kernels for 28% -> 28%
where the time goes in v18:
time: 93 us; the launch traced here: 92.8 us
  starting transfers between devices  34.7 us (37%)
  Pallas kernels  34.2 us (37%)
  waiting for transfers between devices  11.7 us (13%)
  other arithmetic  4.76 us (5%)
  local copies, waits for them, and re-layouts  3.33 us (4%)
  matrix products  3.22 us (3%)
    pallas_call x3, Pallas kernels, stencil_stage(): pl.pallas_call(interior_kernel(stage, planes, ny, nz), grid=(blocks,), in...  22.5 us
    ppermute x16, starting transfers between devices, butterfly_sum(): values = values + lax.ppermute(values, axis, pairs)  18.4 us
    pallas_call x3, Pallas kernels, stencil_stage(): pl.pallas_call(finish_kernel(stage, planes, ny), grid=(blocks,), in_specs...  11.7 us
    ppermute x16, waiting for transfers between devices, butterfly_sum(): values = values + lax.ppermute(values, axis, pairs)  10.1 us
    ppermute x3, starting transfers between devices, exchange(): lax.ppermute(sends[1], axis, backward)  7.42 us
    ppermute x3, starting transfers between devices, exchange(): lax.ppermute(sends[0], axis, forward)  7 us
    concatenate x3, other arithmetic, stencil_stage(): halos = jnp.concatenate([low, high], axis=0)  3.25 us
    dot_general x4, matrix products, shards(): jnp.einsum('cb,ck->bk', rows, cols, preferred_element_type=jnp.float32)  3.22 us
  transfers between devices with their start and end apart: 23, of which 9 were waited for; matrix products, arithmetic and copies ran while one was open for 7% of the time, Pallas kernels for 28%

profile of v18, /device:TPU:0, one launch (start us, length us, event | category | flops | bytes accessed | tf_op | source)
XLA Modules:
  0.0 92.8 jit_solution(14391440732947052407)
XLA Ops:
  0.6 1.3 %fusion = (bf16[4,16,32,128]{3,2,1,0:T(8,128)(2,1)S(1)}, bf16[4,16,32,128]{3,2,1,0:T(8,128)(2,1)S(1)}) fusion(bf16[8,16,32,128]{3,2,1,0:T(8,128)(2,1)} %refs_2_.1), kind=kLoop, calls=%fused_computation.13 | loop fusion | bytes 2097152 | tf_op jit(solution)/shard_map/slice | solution.py:282
  2.5 5.0 %collective-permute-start.1 = (bf16[4,16,32,128]{3,2,1,0:T(8,128)(2,1)S(1)}, bf16[4,16,32,128]{3,2,1,0:T(8,128)(2,1)S(1)}, u32[]{:S(2)}, u32[]{:S(2)}) collective-permute-start(bf16[4,16,32,128]{3,2,1,0:T(8,128)(2,1)S(1)} %get-tuple-element.16), channel_id=1, source_target_pairs={{1,0},{2,1},{3,2},{4,3},{5,4},{6,5},{7,6},{8,7},{9,8},{10,9},{11,1... | collective-permute-start | bytes 1572872 | tf_op jit(solution)/shard_map/ppermute | solution.py:246
  7.5 2.0 %broadcast_in_dim.2.pot = f32[8,16,32,128]{3,2,1,0:T(8,128)} broadcast(f32[8,16,32]{2,1,0:T(8,128)S(1)} %copy-done.2), dimensions={0,1,2} | broadcast | bytes 2113536 | tf_op jit(solution)/shard_map/broadcast_in_dim | solution.py:268
  9.5 7.5 %interior_first.1.refs_1_ = f32[8,16,32,128]{3,2,1,0:T(8,128)} custom-call(bf16[8,16,32,128]{3,2,1,0:T(8,128)(2,1)} %refs_2_.1, f32[8,16,32,128]{3,2,1,0:T(8,128)} %broadcast_in_dim.2.pot), custom_call_target="tpu_custom_call" | custom-call | tf_op jit(solution)/shard_map/interior_first/pallas_call | solution.py:124
  17.0 1.1 %pad_maximum_fusion.refs_0_ = bf16[8,16,32,128]{3,2,1,0:T(8,128)(2,1)} fusion(bf16[4,16,32,128]{3,2,1,0:T(8,128)(2,1)S(1)} %collective-permute-done.1, bf16[4,16,32,128]{3,2,1,0:T(8,128)(2,1)S(1)} %collective-permute-done), kind=kLoop, calls=%fused_computation.2 | loop fusion | flops 524288 | bytes 2097152 | tf_op jit(solution)/shard_map/concatenate | solution.py:133
  18.1 4.0 %finish_first.1 = (bf16[8,16,32,128]{3,2,1,0:T(8,128)(2,1)}, bf16[4,16,32,128]{3,2,1,0:T(8,128)(2,1)}, bf16[4,16,32,128]{3,2,1,0:T(8,128)(2,1)}) custom-call(bf16[8,16,32,128]{3,2,1,0:T(8,128)(2,1)} %pad_maximum_fusion.refs_0_, f32[8,16,32,128]{3,2,1,0:T(8,128)} %interior_first.1.refs_1_), custom_call_target="tpu_custom_call" | custom-call | tf_op jit(solution)/shard_map/finish_first/pallas_call | solution.py:146
  22.0 2.3 %collective-permute-start.2 = (bf16[4,16,32,128]{3,2,1,0:T(8,128)(2,1)}, bf16[4,16,32,128]{3,2,1,0:T(8,128)(2,1)S(1)}, u32[]{:S(2)}, u32[]{:S(2)}) collective-permute-start(bf16[4,16,32,128]{3,2,1,0:T(8,128)(2,1)} %get-tuple-element.9), channel_id=1, source_target_pairs={{0,1},{1,2},{2,3},{3,4},{4,5},{5,6},{6,7},{7,8},{8,9},{9,10},{10,1... | collective-permute-start | bytes 1572872 | tf_op jit(solution)/shard_map/ppermute | solution.py:246
  24.4 2.1 %collective-permute-start.3 = (bf16[4,16,32,128]{3,2,1,0:T(8,128)(2,1)}, bf16[4,16,32,128]{3,2,1,0:T(8,128)(2,1)S(1)}, u32[]{:S(2)}, u32[]{:S(2)}) collective-permute-start(bf16[4,16,32,128]{3,2,1,0:T(8,128)(2,1)} %get-tuple-element.10), channel_id=1, source_target_pairs={{1,0},{2,1},{3,2},{4,3},{5,4},{6,5},{7,6},{8,7},{9,8},{10,9},{11,1... | collective-permute-start | bytes 1572872 | tf_op jit(solution)/shard_map/ppermute | solution.py:246
  26.5 7.5 %interior_filtered.1.refs_1_ = f32[8,16,32,128]{3,2,1,0:T(8,128)} custom-call(bf16[8,16,32,128]{3,2,1,0:T(8,128)(2,1)} %get-tuple-element.11.own_narrow, f32[8,16,32,128]{3,2,1,0:T(8,128)} %broadcast_in_dim.2.pot), custom_call_target="tpu_custom_call" | custom-call | tf_op jit(solution)/shard_map/interior_filtered/pallas_call | solution.py:124
  34.0 1.1 %pad_maximum_fusion.1.refs_0_ = bf16[8,16,32,128]{3,2,1,0:T(8,128)(2,1)} fusion(bf16[4,16,32,128]{3,2,1,0:T(8,128)(2,1)S(1)} %collective-permute-done.3, bf16[4,16,32,128]{3,2,1,0:T(8,128)(2,1)S(1)} %collective-permute-done.2), kind=kLoop, calls=%fused_computation.3 | loop fusion | flops 524288 | bytes 2097152 | tf_op jit(solution)/shard_map/concatenate | solution.py:133
  35.1 4.3 %finish_filtered.1 = (bf16[8,16,32,128]{3,2,1,0:T(8,128)(2,1)}, bf16[4,16,32,128]{3,2,1,0:T(8,128)(2,1)}, bf16[4,16,32,128]{3,2,1,0:T(8,128)(2,1)}) custom-call(bf16[8,16,32,128]{3,2,1,0:T(8,128)(2,1)} %pad_maximum_fusion.1.refs_0_, f32[8,16,32,128]{3,2,1,0:T(8,128)} %interior_filtered.1.refs_1_, bf16[8,16,32,128]{3,2,1,0:T(8,128)(2,1)} %refs_2_.1), custom_call_target="tpu_custom_call" | custom-call | tf_op jit(solution)/shard_map/finish_filtered/pallas_call | solution.py:146
  39.4 1.9 %collective-permute-start.4 = (bf16[4096,128]{1,0:T(8,128)(2,1)}, bf16[4096,128]{1,0:T(8,128)(2,1)S(1)}, u32[]{:S(2)}, u32[]{:S(2)}) collective-permute-start(bf16[4096,128]{1,0:T(8,128)(2,1)} %bitcast.18), channel_id=1, source_target_pairs={{0,16},{16,0},{1,17},{17,1},{2,18},{18,2},{3,19},{19,3},{4,20},{20... | collective-permute-start | bytes 3145736 | tf_op jit(solution)/shard_map/ppermute | solution.py:290
  41.3 4.2 %collective-permute-start.13 = (bf16[4,16,32,128]{3,2,1,0:T(8,128)(2,1)}, bf16[4,16,32,128]{3,2,1,0:T(8,128)(2,1)S(1)}, u32[]{:S(2)}, u32[]{:S(2)}) collective-permute-start(bf16[4,16,32,128]{3,2,1,0:T(8,128)(2,1)} %get-tuple-element.13), channel_id=1, source_target_pairs={{0,1},{1,2},{2,3},{3,4},{4,5},{5,6},{6,7},{7,8},{8,9},{9,10},{10,1... | collective-permute-start | bytes 1572872 | tf_op jit(solution)/shard_map/ppermute | solution.py:246
  45.7 7.5 %interior_applied.1.refs_1_ = f32[8,16,32,128]{3,2,1,0:T(8,128)} custom-call(bf16[8,16,32,128]{3,2,1,0:T(8,128)(2,1)} %get-tuple-element.6.own_narrow, f32[8,16,32,128]{3,2,1,0:T(8,128)} %broadcast_in_dim.2.pot), custom_call_target="tpu_custom_call" | custom-call | tf_op jit(solution)/shard_map/interior_applied/pallas_call | solution.py:124
  53.8 1.1 %pad_maximum_fusion.2.refs_0_ = bf16[8,16,32,128]{3,2,1,0:T(8,128)(2,1)} fusion(bf16[4,16,32,128]{3,2,1,0:T(8,128)(2,1)S(1)} %collective-permute-done.14, bf16[4,16,32,128]{3,2,1,0:T(8,128)(2,1)S(1)} %collective-permute-done.13), kind=kLoop, calls=%fused_computation.4 | loop fusion | flops 524288 | bytes 2097152 | tf_op jit(solution)/shard_map/concatenate | solution.py:133
  54.8 3.5 %finish_applied.1 = bf16[8,16,32,128]{3,2,1,0:T(8,128)(2,1)} custom-call(bf16[8,16,32,128]{3,2,1,0:T(8,128)(2,1)} %pad_maximum_fusion.2.refs_0_, f32[8,16,32,128]{3,2,1,0:T(8,128)} %interior_applied.1.refs_1_), custom_call_target="tpu_custom_call" | custom-call | tf_op jit(solution)/shard_map/finish_applied/pallas_call | solution.py:146
  58.3 1.8 %convolution_bitcast_fusion = f32[128,128]{1,0:T(8,128)S(1)} fusion(bf16[8,16,32,128]{3,2,1,0:T(8,128)(2,1)} %finish_applied.1, bf16[8,16,32,128]{3,2,1,0:T(8,128)(2,1)S(1)} %copy-done), kind=kOutput, calls=%fused_computation | convolution fusion | flops 134217728 | bytes 2162688 | tf_op jit(solution)/shard_map/cb,ck->bk/dot_general | solution.py:273
  60.1 1.6 %collective-permute-done.4 = bf16[4096,128]{1,0:T(8,128)(2,1)S(1)} collective-permute-done((bf16[4096,128]{1,0:T(8,128)(2,1)}, bf16[4096,128]{1,0:T(8,128)(2,1)S(1)}, u32[]{:S(2)}, u32[]{:S(2)}) %collective-permute-start.4) | collective-permute-done | bytes 1048608 | tf_op jit(solution)/shard_map/ppermute | solution.py:290
  62.7 3.8 %collective-permute-start.15 = (f32[64,256]{1,0:T(8,128)S(1)}, f32[64,256]{1,0:T(8,128)S(1)}, u32[]{:S(2)}, u32[]{:S(2)}) collective-permute-start(f32[64,256]{1,0:T(8,128)S(1)} %get-tuple-element.19), channel_id=1, source_target_pairs={{0,1},{1,0},{2,3},{3,2},{4,5},{5,4},{6,7},{7,6},{8,9},{9,8},{10,11... | collective-permute-start | bytes 196616 | tf_op jit(solution)/shard_map/ppermute | solution.py:254
  68.0 1.9 %collective-permute-start.20 = (f32[64,256]{1,0:T(8,128)S(1)}, f32[64,256]{1,0:T(8,128)S(1)}, u32[]{:S(2)}, u32[]{:S(2)}) collective-permute-start(f32[64,256]{1,0:T(8,128)S(1)} %get-tuple-element.18), channel_id=1, source_target_pairs={{0,2},{1,3},{2,0},{3,1},{4,6},{5,7},{6,4},{7,5},{8,10},{9,11},{10,... | collective-permute-start | bytes 196616 | tf_op jit(solution)/shard_map/ppermute | solution.py:254
  70.1 1.9 %collective-permute-start.10 = (f32[64,256]{1,0:T(8,128)S(1)}, f32[64,256]{1,0:T(8,128)S(1)}, u32[]{:S(2)}, u32[]{:S(2)}) collective-permute-start(f32[64,256]{1,0:T(8,128)S(1)} %get-tuple-element.22), channel_id=1, source_target_pairs={{0,2},{1,3},{2,0},{3,1},{4,6},{5,7},{6,4},{7,5},{8,10},{9,11},{10,... | collective-permute-start | bytes 196616 | tf_op jit(solution)/shard_map/ppermute | solution.py:254
  72.0 0.8 collective-permute-done.16
  72.9 1.3 %collective-permute-done.20 = f32[64,256]{1,0:T(8,128)S(1)} collective-permute-done((f32[64,256]{1,0:T(8,128)S(1)}, f32[64,256]{1,0:T(8,128)S(1)}, u32[]{:S(2)}, u32[]{:S(2)}) %collective-permute-start.20) | collective-permute-done | bytes 65568 | tf_op jit(solution)/shard_map/ppermute | solution.py:254
  74.2 0.8 collective-permute-start.21
  75.5 0.9 collective-permute-start.7
  76.4 1.3 %collective-permute-start.11 = (f32[64,256]{1,0:T(8,128)S(1)}, f32[64,256]{1,0:T(8,128)S(1)}, u32[]{:S(2)}, u32[]{:S(2)}) collective-permute-start(f32[64,256]{1,0:T(8,128)S(1)} %add.53), channel_id=1, source_target_pairs={{0,4},{1,5},{2,6},{3,7},{4,0},{5,1},{6,2},{7,3},{8,12},{9,13},{10,... | collective-permute-start | bytes 196616 | tf_op jit(solution)/shard_map/ppermute | solution.py:254
  77.7 2.7 %collective-permute-start.18 = (f32[64,256]{1,0:T(8,128)S(1)}, f32[64,256]{1,0:T(8,128)S(1)}, u32[]{:S(2)}, u32[]{:S(2)}) collective-permute-start(f32[64,256]{1,0:T(8,128)S(1)} %add.58), channel_id=1, source_target_pairs={{0,8},{1,9},{2,10},{3,11},{4,12},{5,13},{6,14},{7,15},{8,0},{9,1},... | collective-permute-start | bytes 196616 | tf_op jit(solution)/shard_map/ppermute | solution.py:254
  80.8 2.7 %collective-permute-start.8 = (f32[64,256]{1,0:T(8,128)S(1)}, f32[64,256]{1,0:T(8,128)S(1)}, u32[]{:S(2)}, u32[]{:S(2)}) collective-permute-start(f32[64,256]{1,0:T(8,128)S(1)} %add.50), channel_id=1, source_target_pairs={{0,8},{1,9},{2,10},{3,11},{4,12},{5,13},{6,14},{7,15},{8,0},{9,1},... | collective-permute-start | bytes 196616 | tf_op jit(solution)/shard_map/ppermute | solution.py:254
  83.5 1.0 %collective-permute-start.12 = (f32[64,256]{1,0:T(8,128)S(1)}, f32[64,256]{1,0:T(8,128)S(1)}, u32[]{:S(2)}, u32[]{:S(2)}) collective-permute-start(f32[64,256]{1,0:T(8,128)S(1)} %add.54), channel_id=1, source_target_pairs={{0,8},{1,9},{2,10},{3,11},{4,12},{5,13},{6,14},{7,15},{8,0},{9,1},... | collective-permute-start | bytes 196616 | tf_op jit(solution)/shard_map/ppermute | solution.py:254
  84.5 3.4 %collective-permute-done.18 = f32[64,256]{1,0:T(8,128)S(1)} collective-permute-done((f32[64,256]{1,0:T(8,128)S(1)}, f32[64,256]{1,0:T(8,128)S(1)}, u32[]{:S(2)}, u32[]{:S(2)}) %collective-permute-start.18) | collective-permute-done | bytes 65568 | tf_op jit(solution)/shard_map/ppermute | solution.py:254
  87.9 2.1 %collective-permute-done.22 = f32[64,256]{1,0:T(8,128)S(1)} collective-permute-done((f32[64,256]{1,0:T(8,128)S(1)}, f32[64,256]{1,0:T(8,128)S(1)}, u32[]{:S(2)}, u32[]{:S(2)}) %collective-permute-start.22) | collective-permute-done | bytes 65568 | tf_op jit(solution)/shard_map/ppermute | solution.py:254
  90.0 1.4 %collective-permute-done.8 = f32[64,256]{1,0:T(8,128)S(1)} collective-permute-done((f32[64,256]{1,0:T(8,128)S(1)}, f32[64,256]{1,0:T(8,128)S(1)}, u32[]{:S(2)}, u32[]{:S(2)}) %collective-permute-start.8) | collective-permute-done | bytes 65568 | tf_op jit(solution)/shard_map/ppermute | solution.py:254
  (54 shorter events, 6.4 us)
Async XLA Ops:
  0.6 6.9 %copy-start.2 = (f32[8,16,32]{2,1,0:T(8,128)S(1)}, f32[8,16,32]{2,1,0:T(8,128)}, u32[]{:S(2)}) copy-start(f32[8,16,32]{2,1,0:T(8,128)} %param.3) | copy-start | bytes 49156
  2.0 15.0 %collective-permute-start = (bf16[4,16,32,128]{3,2,1,0:T(8,128)(2,1)S(1)}, bf16[4,16,32,128]{3,2,1,0:T(8,128)(2,1)S(1)}, u32[]{:S(2)}, u32[]{:S(2)}) collective-permute-start(bf16[4,16,32,128]{3,2,1,0:T(8,128)(2,1)S(1)} %get-tuple-element.15), channel_id=1, source_target_pairs={{0,1},{1,2},{2,3},{3,4},{4,5},{5,6},{6,7},{7,8},{8,9},{9,10},{10,1... | collective-permute-start | bytes 1572872 | tf_op jit(solution)/shard_map/ppermute | solution.py:246
  2.5 14.5 %collective-permute-start.1 = (bf16[4,16,32,128]{3,2,1,0:T(8,128)(2,1)S(1)}, bf16[4,16,32,128]{3,2,1,0:T(8,128)(2,1)S(1)}, u32[]{:S(2)}, u32[]{:S(2)}) collective-permute-start(bf16[4,16,32,128]{3,2,1,0:T(8,128)(2,1)S(1)} %get-tuple-element.16), channel_id=1, source_target_pairs={{1,0},{2,1},{3,2},{4,3},{5,4},{6,5},{7,6},{8,7},{9,8},{10,9},{11,1... | collective-permute-start | bytes 1572872 | tf_op jit(solution)/shard_map/ppermute | solution.py:246
  22.0 11.9 %collective-permute-start.2 = (bf16[4,16,32,128]{3,2,1,0:T(8,128)(2,1)}, bf16[4,16,32,128]{3,2,1,0:T(8,128)(2,1)S(1)}, u32[]{:S(2)}, u32[]{:S(2)}) collective-permute-start(bf16[4,16,32,128]{3,2,1,0:T(8,128)(2,1)} %get-tuple-element.9), channel_id=1, source_target_pairs={{0,1},{1,2},{2,3},{3,4},{4,5},{5,6},{6,7},{7,8},{8,9},{9,10},{10,1... | collective-permute-start | bytes 1572872 | tf_op jit(solution)/shard_map/ppermute | solution.py:246
  24.4 9.6 %collective-permute-start.3 = (bf16[4,16,32,128]{3,2,1,0:T(8,128)(2,1)}, bf16[4,16,32,128]{3,2,1,0:T(8,128)(2,1)S(1)}, u32[]{:S(2)}, u32[]{:S(2)}) collective-permute-start(bf16[4,16,32,128]{3,2,1,0:T(8,128)(2,1)} %get-tuple-element.10), channel_id=1, source_target_pairs={{1,0},{2,1},{3,2},{4,3},{5,4},{6,5},{7,6},{8,7},{9,8},{10,9},{11,1... | collective-permute-start | bytes 1572872 | tf_op jit(solution)/shard_map/ppermute | solution.py:246
  39.4 22.3 %collective-permute-start.4 = (bf16[4096,128]{1,0:T(8,128)(2,1)}, bf16[4096,128]{1,0:T(8,128)(2,1)S(1)}, u32[]{:S(2)}, u32[]{:S(2)}) collective-permute-start(bf16[4096,128]{1,0:T(8,128)(2,1)} %bitcast.18), channel_id=1, source_target_pairs={{0,16},{16,0},{1,17},{17,1},{2,18},{18,2},{3,19},{19,3},{4,20},{20... | collective-permute-start | bytes 3145736 | tf_op jit(solution)/shard_map/ppermute | solution.py:290
  41.3 12.4 %collective-permute-start.13 = (bf16[4,16,32,128]{3,2,1,0:T(8,128)(2,1)}, bf16[4,16,32,128]{3,2,1,0:T(8,128)(2,1)S(1)}, u32[]{:S(2)}, u32[]{:S(2)}) collective-permute-start(bf16[4,16,32,128]{3,2,1,0:T(8,128)(2,1)} %get-tuple-element.13), channel_id=1, source_target_pairs={{0,1},{1,2},{2,3},{3,4},{4,5},{5,6},{6,7},{7,8},{8,9},{9,10},{10,1... | collective-permute-start | bytes 1572872 | tf_op jit(solution)/shard_map/ppermute | solution.py:246
  45.5 8.3 %collective-permute-start.14 = (bf16[4,16,32,128]{3,2,1,0:T(8,128)(2,1)}, bf16[4,16,32,128]{3,2,1,0:T(8,128)(2,1)S(1)}, u32[]{:S(2)}, u32[]{:S(2)}) collective-permute-start(bf16[4,16,32,128]{3,2,1,0:T(8,128)(2,1)} %get-tuple-element.14), channel_id=1, source_target_pairs={{1,0},{2,1},{3,2},{4,3},{5,4},{6,5},{7,6},{8,7},{9,8},{10,9},{11,1... | collective-permute-start | bytes 1572872 | tf_op jit(solution)/shard_map/ppermute | solution.py:246
  45.7 7.5 %copy-start = (bf16[8,16,32,128]{3,2,1,0:T(8,128)(2,1)S(1)}, bf16[8,16,32,128]{3,2,1,0:T(8,128)(2,1)}, u32[]{:S(2)}) copy-start(bf16[8,16,32,128]{3,2,1,0:T(8,128)(2,1)} %get-tuple-element.6.own_narrow) | copy-start | bytes 3145732
  58.3 3.9 %copy-start.1 = (bf16[8,16,32,128]{3,2,1,0:T(8,128)(2,1)S(1)}, bf16[8,16,32,128]{3,2,1,0:T(8,128)(2,1)}, u32[]{:S(2)}) copy-start(bf16[8,16,32,128]{3,2,1,0:T(8,128)(2,1)} %finish_applied.1) | copy-start | bytes 3145732
  62.7 4.8 %collective-permute-start.15 = (f32[64,256]{1,0:T(8,128)S(1)}, f32[64,256]{1,0:T(8,128)S(1)}, u32[]{:S(2)}, u32[]{:S(2)}) collective-permute-start(f32[64,256]{1,0:T(8,128)S(1)} %get-tuple-element.19), channel_id=1, source_target_pairs={{0,1},{1,0},{2,3},{3,2},{4,5},{5,4},{6,7},{7,6},{8,9},{9,8},{10,11... | collective-permute-start | bytes 196616 | tf_op jit(solution)/shard_map/ppermute | solution.py:254
  66.5 1.3 %collective-permute-start.19 = (f32[64,256]{1,0:T(8,128)S(1)}, f32[64,256]{1,0:T(8,128)S(1)}, u32[]{:S(2)}, u32[]{:S(2)}) collective-permute-start(f32[64,256]{1,0:T(8,128)S(1)} %get-tuple-element.20), channel_id=1, source_target_pairs={{0,1},{1,0},{2,3},{3,2},{4,5},{5,4},{6,7},{7,6},{8,9},{9,8},{10,11... | collective-permute-start | bytes 196616 | tf_op jit(solution)/shard_map/ppermute | solution.py:254
  66.6 3.3 %collective-permute-start.5 = (f32[64,256]{1,0:T(8,128)S(1)}, f32[64,256]{1,0:T(8,128)S(1)}, u32[]{:S(2)}, u32[]{:S(2)}) collective-permute-start(f32[64,256]{1,0:T(8,128)S(1)} %get-tuple-element.23), channel_id=1, source_target_pairs={{0,1},{1,0},{2,3},{3,2},{4,5},{5,4},{6,7},{7,6},{8,9},{9,8},{10,11... | collective-permute-start | bytes 196616 | tf_op jit(solution)/shard_map/ppermute | solution.py:254
  67.1 2.8 %collective-permute-start.9 = (f32[64,256]{1,0:T(8,128)S(1)}, f32[64,256]{1,0:T(8,128)S(1)}, u32[]{:S(2)}, u32[]{:S(2)}) collective-permute-start(f32[64,256]{1,0:T(8,128)S(1)} %get-tuple-element.24), channel_id=1, source_target_pairs={{0,1},{1,0},{2,3},{3,2},{4,5},{5,4},{6,7},{7,6},{8,9},{9,8},{10,11... | collective-permute-start | bytes 196616 | tf_op jit(solution)/shard_map/ppermute | solution.py:254
  67.8 5.0 %collective-permute-start.16 = (f32[64,256]{1,0:T(8,128)S(1)}, f32[64,256]{1,0:T(8,128)S(1)}, u32[]{:S(2)}, u32[]{:S(2)}) collective-permute-start(f32[64,256]{1,0:T(8,128)S(1)} %get-tuple-element.17), channel_id=1, source_target_pairs={{0,2},{1,3},{2,0},{3,1},{4,6},{5,7},{6,4},{7,5},{8,10},{9,11},{10,... | collective-permute-start | bytes 196616 | tf_op jit(solution)/shard_map/ppermute | solution.py:254
  68.0 6.2 %collective-permute-start.20 = (f32[64,256]{1,0:T(8,128)S(1)}, f32[64,256]{1,0:T(8,128)S(1)}, u32[]{:S(2)}, u32[]{:S(2)}) collective-permute-start(f32[64,256]{1,0:T(8,128)S(1)} %get-tuple-element.18), channel_id=1, source_target_pairs={{0,2},{1,3},{2,0},{3,1},{4,6},{5,7},{6,4},{7,5},{8,10},{9,11},{10,... | collective-permute-start | bytes 196616 | tf_op jit(solution)/shard_map/ppermute | solution.py:254
  69.9 5.6 %collective-permute-start.6 = (f32[64,256]{1,0:T(8,128)S(1)}, f32[64,256]{1,0:T(8,128)S(1)}, u32[]{:S(2)}, u32[]{:S(2)}) collective-permute-start(f32[64,256]{1,0:T(8,128)S(1)} %get-tuple-element.21), channel_id=1, source_target_pairs={{0,2},{1,3},{2,0},{3,1},{4,6},{5,7},{6,4},{7,5},{8,10},{9,11},{10,... | collective-permute-start | bytes 196616 | tf_op jit(solution)/shard_map/ppermute | solution.py:254
  70.1 6.3 %collective-permute-start.10 = (f32[64,256]{1,0:T(8,128)S(1)}, f32[64,256]{1,0:T(8,128)S(1)}, u32[]{:S(2)}, u32[]{:S(2)}) collective-permute-start(f32[64,256]{1,0:T(8,128)S(1)} %get-tuple-element.22), channel_id=1, source_target_pairs={{0,2},{1,3},{2,0},{3,1},{4,6},{5,7},{6,4},{7,5},{8,10},{9,11},{10,... | collective-permute-start | bytes 196616 | tf_op jit(solution)/shard_map/ppermute | solution.py:254
  72.8 4.9 %collective-permute-start.17 = (f32[64,256]{1,0:T(8,128)S(1)}, f32[64,256]{1,0:T(8,128)S(1)}, u32[]{:S(2)}, u32[]{:S(2)}) collective-permute-start(f32[64,256]{1,0:T(8,128)S(1)} %add.57), channel_id=1, source_target_pairs={{0,4},{1,5},{2,6},{3,7},{4,0},{5,1},{6,2},{7,3},{8,12},{9,13},{10,... | collective-permute-start | bytes 196616 | tf_op jit(solution)/shard_map/ppermute | solution.py:254
  74.2 6.2 %collective-permute-start.21 = (f32[64,256]{1,0:T(8,128)S(1)}, f32[64,256]{1,0:T(8,128)S(1)}, u32[]{:S(2)}, u32[]{:S(2)}) collective-permute-start(f32[64,256]{1,0:T(8,128)S(1)} %add.61), channel_id=1, source_target_pairs={{0,4},{1,5},{2,6},{3,7},{4,0},{5,1},{6,2},{7,3},{8,12},{9,13},{10,... | collective-permute-start | bytes 196616 | tf_op jit(solution)/shard_map/ppermute | solution.py:254
  75.5 5.3 %collective-permute-start.7 = (f32[64,256]{1,0:T(8,128)S(1)}, f32[64,256]{1,0:T(8,128)S(1)}, u32[]{:S(2)}, u32[]{:S(2)}) collective-permute-start(f32[64,256]{1,0:T(8,128)S(1)} %add.49), channel_id=1, source_target_pairs={{0,4},{1,5},{2,6},{3,7},{4,0},{5,1},{6,2},{7,3},{8,12},{9,13},{10,... | collective-permute-start | bytes 196616 | tf_op jit(solution)/shard_map/ppermute | solution.py:254
  76.4 7.1 %collective-permute-start.11 = (f32[64,256]{1,0:T(8,128)S(1)}, f32[64,256]{1,0:T(8,128)S(1)}, u32[]{:S(2)}, u32[]{:S(2)}) collective-permute-start(f32[64,256]{1,0:T(8,128)S(1)} %add.53), channel_id=1, source_target_pairs={{0,4},{1,5},{2,6},{3,7},{4,0},{5,1},{6,2},{7,3},{8,12},{9,13},{10,... | collective-permute-start | bytes 196616 | tf_op jit(solution)/shard_map/ppermute | solution.py:254
  77.7 10.1 %collective-permute-start.18 = (f32[64,256]{1,0:T(8,128)S(1)}, f32[64,256]{1,0:T(8,128)S(1)}, u32[]{:S(2)}, u32[]{:S(2)}) collective-permute-start(f32[64,256]{1,0:T(8,128)S(1)} %add.58), channel_id=1, source_target_pairs={{0,8},{1,9},{2,10},{3,11},{4,12},{5,13},{6,14},{7,15},{8,0},{9,1},... | collective-permute-start | bytes 196616 | tf_op jit(solution)/shard_map/ppermute | solution.py:254
  80.4 9.5 %collective-permute-start.22 = (f32[64,256]{1,0:T(8,128)S(1)}, f32[64,256]{1,0:T(8,128)S(1)}, u32[]{:S(2)}, u32[]{:S(2)}) collective-permute-start(f32[64,256]{1,0:T(8,128)S(1)} %add.62), channel_id=1, source_target_pairs={{0,8},{1,9},{2,10},{3,11},{4,12},{5,13},{6,14},{7,15},{8,0},{9,1},... | collective-permute-start | bytes 196616 | tf_op jit(solution)/shard_map/ppermute | solution.py:254
  80.8 10.6 %collective-permute-start.8 = (f32[64,256]{1,0:T(8,128)S(1)}, f32[64,256]{1,0:T(8,128)S(1)}, u32[]{:S(2)}, u32[]{:S(2)}) collective-permute-start(f32[64,256]{1,0:T(8,128)S(1)} %add.50), channel_id=1, source_target_pairs={{0,8},{1,9},{2,10},{3,11},{4,12},{5,13},{6,14},{7,15},{8,0},{9,1},... | collective-permute-start | bytes 196616 | tf_op jit(solution)/shard_map/ppermute | solution.py:254
  83.5 8.6 %collective-permute-start.12 = (f32[64,256]{1,0:T(8,128)S(1)}, f32[64,256]{1,0:T(8,128)S(1)}, u32[]{:S(2)}, u32[]{:S(2)}) collective-permute-start(f32[64,256]{1,0:T(8,128)S(1)} %add.54), channel_id=1, source_target_pairs={{0,8},{1,9},{2,10},{3,11},{4,12},{5,13},{6,14},{7,15},{8,0},{9,1},... | collective-permute-start | bytes 196616 | tf_op jit(solution)/shard_map/ppermute | solution.py:254

commit v19 on v14

--- a/solution.py
+++ b/solution.py
@@ -280,14 +280,20 @@
         "filtered", first, first_sent, potential_wide, orbitals
     )
     own_block = filtered.reshape(cell_count, nb)
-    partner = lax.ppermute(own_block, "band", [(0, 1), (1, 0)])
-    correlation_piece = placed(gram(own_block, own_block), gram(own_block, partner))
+    swap = [(0, 1), (1, 0)]
+    halves = [half.reshape(-1, nb) for half in (filtered_sent[1], filtered_sent[0])]
+    partner_halves = [lax.ppermute(half, "band", swap) for half in halves]
+    split_rows = lambda block: (block[: cell_count // 2], block[cell_count // 2 :])
+    cross = lambda block: sum(
+        gram(rows, cols) for rows, cols in zip(split_rows(block), partner_halves)
+    )
+    correlation_piece = placed(gram(own_block, own_block), cross(own_block))
     correlation = butterfly_sum(correlation_piece, "domain") * cell_weight
     (applied_grid,) = stencil_stage(
         "applied", filtered, filtered_sent, potential_wide, keep_sends=False
     )
     applied = applied_grid.reshape(cell_count, nb)
-    energy_piece = placed(gram(applied, own_block), gram(applied, partner))
+    energy_piece = placed(gram(applied, own_block), cross(applied))
     projected = butterfly_sum(energy_piece, "domain") * cell_weight
     return (filtered, correlation, projected)
 

time: 93.1 us -> 97.4 us (1.046)
  waiting for transfers between devices: 24.7 us -> 28.8 us
  starting transfers between devices: 22 us -> 20.1 us
  local copies, waits for them, and re-layouts: 3.29 us -> 4.84 us
    ppermute x1 -> x2, waiting for transfers between devices: 0.01 us -> 7.36 us  [shards(): partner_halves = [lax.ppermute(half, 'band', swap) for half in halves]]
    ppermute x3, starting transfers between devices: 3.16 us -> 7.76 us  [exchange(): lax.ppermute(sends[0], axis, forward)]
    ppermute x3, starting transfers between devices: 11 us -> 7.14 us  [exchange(): lax.ppermute(sends[1], axis, backward)]
    ppermute x3, waiting for transfers between devices: 3.26 us -> 0.01 us  [exchange(): lax.ppermute(sends[0], axis, forward)]
    ppermute x8, starting transfers between devices: 5.92 us -> 3.17 us  [butterfly_sum(): values = values + lax.ppermute(values, axis, pairs)]
    slice x0 -> x2, local copies, waits for them, and re-layouts: none -> 1.52 us  [shards(): block[:cell_count // 2]]
    dot_general x4 -> x6, matrix products: 3.22 us -> 3.87 us  [shards(): jnp.einsum('cb,ck->bk', rows, cols, preferred_element_type=jnp.float32)]
    ppermute x1 -> x2, starting transfers between devices: 1.93 us -> 2.03 us  [shards(): partner_halves = [lax.ppermute(half, 'band', swap) for half in halves]]
  transfers between devices with their start and end apart: 15 -> 16, of which waited for: 9 -> 9; matrix products, arithmetic and copies ran while one was open for 7% -> 9% of each run, Pallas kernels for 28% -> 27%
where the time goes in v19:
time: 97.4 us; the launch traced here: 97.2 us
  Pallas kernels  34.1 us (35%)
  waiting for transfers between devices  28.8 us (30%)
  starting transfers between devices  20.1 us (21%)
  local copies, waits for them, and re-layouts  4.84 us (5%)
  other arithmetic  4.71 us (5%)
  matrix products  3.87 us (4%)
    pallas_call x3, Pallas kernels, stencil_stage(): pl.pallas_call(interior_kernel(stage, planes, ny, nz), grid=(blocks,), in...  22.4 us
    ppermute x8, waiting for transfers between devices, butterfly_sum(): values = values + lax.ppermute(values, axis, pairs)  21.4 us
    pallas_call x3, Pallas kernels, stencil_stage(): pl.pallas_call(finish_kernel(stage, planes, ny), grid=(blocks,), in_specs...  11.7 us
    ppermute x3, starting transfers between devices, exchange(): lax.ppermute(sends[0], axis, forward)  7.76 us
    ppermute x2, waiting for transfers between devices, shards(): partner_halves = [lax.ppermute(half, 'band', swap) for half in halves]  7.36 us
    ppermute x3, starting transfers between devices, exchange(): lax.ppermute(sends[1], axis, backward)  7.14 us
    dot_general x6, matrix products, shards(): jnp.einsum('cb,ck->bk', rows, cols, preferred_element_type=jnp.float32)  3.87 us
    concatenate x3, other arithmetic, stencil_stage(): halos = jnp.concatenate([low, high], axis=0)  3.23 us
  transfers between devices with their start and end apart: 16, of which 9 were waited for; matrix products, arithmetic and copies ran while one was open for 9% of the time, Pallas kernels for 27%

profile of v19, /device:TPU:0, one launch (start us, length us, event | category | flops | bytes accessed | tf_op | source)
XLA Modules:
  0.0 97.2 jit_solution(13665669133565919360)
XLA Ops:
  0.6 1.3 %fusion.2 = (bf16[4,16,32,128]{3,2,1,0:T(8,128)(2,1)S(1)}, bf16[4,16,32,128]{3,2,1,0:T(8,128)(2,1)S(1)}) fusion(bf16[8,16,32,128]{3,2,1,0:T(8,128)(2,1)} %refs_2_.1), kind=kLoop, calls=%fused_computation.13 | loop fusion | bytes 2097152 | tf_op jit(solution)/shard_map/slice | solution.py:275
  2.5 5.0 %collective-permute-start.1 = (bf16[4,16,32,128]{3,2,1,0:T(8,128)(2,1)S(1)}, bf16[4,16,32,128]{3,2,1,0:T(8,128)(2,1)S(1)}, u32[]{:S(2)}, u32[]{:S(2)}) collective-permute-start(bf16[4,16,32,128]{3,2,1,0:T(8,128)(2,1)S(1)} %get-tuple-element.20), channel_id=1, source_target_pairs={{1,0},{2,1},{3,2},{4,3},{5,4},{6,5},{7,6},{8,7},{9,8},{10,9},{11,1... | collective-permute-start | bytes 1572872 | tf_op jit(solution)/shard_map/ppermute | solution.py:246
  7.5 1.9 %broadcast_in_dim.2.pot = f32[8,16,32,128]{3,2,1,0:T(8,128)} broadcast(f32[8,16,32]{2,1,0:T(8,128)S(1)} %copy-done.3), dimensions={0,1,2} | broadcast | bytes 2113536 | tf_op jit(solution)/shard_map/broadcast_in_dim | solution.py:261
  9.5 7.5 %interior_first.1.refs_1_ = f32[8,16,32,128]{3,2,1,0:T(8,128)} custom-call(bf16[8,16,32,128]{3,2,1,0:T(8,128)(2,1)} %refs_2_.1, f32[8,16,32,128]{3,2,1,0:T(8,128)} %broadcast_in_dim.2.pot), custom_call_target="tpu_custom_call" | custom-call | tf_op jit(solution)/shard_map/interior_first/pallas_call | solution.py:124
  17.0 1.1 %pad_maximum_fusion.refs_0_ = bf16[8,16,32,128]{3,2,1,0:T(8,128)(2,1)} fusion(bf16[4,16,32,128]{3,2,1,0:T(8,128)(2,1)S(1)} %collective-permute-done.1, bf16[4,16,32,128]{3,2,1,0:T(8,128)(2,1)S(1)} %collective-permute-done), kind=kLoop, calls=%fused_computation.4 | loop fusion | flops 524288 | bytes 2097152 | tf_op jit(solution)/shard_map/concatenate | solution.py:133
  18.0 3.9 %finish_first.1 = (bf16[8,16,32,128]{3,2,1,0:T(8,128)(2,1)}, bf16[4,16,32,128]{3,2,1,0:T(8,128)(2,1)}, bf16[4,16,32,128]{3,2,1,0:T(8,128)(2,1)}) custom-call(bf16[8,16,32,128]{3,2,1,0:T(8,128)(2,1)} %pad_maximum_fusion.refs_0_, f32[8,16,32,128]{3,2,1,0:T(8,128)} %interior_first.1.refs_1_), custom_call_target="tpu_custom_call" | custom-call | tf_op jit(solution)/shard_map/finish_first/pallas_call | solution.py:146
  22.0 2.3 %collective-permute-start.2 = (bf16[4,16,32,128]{3,2,1,0:T(8,128)(2,1)}, bf16[4,16,32,128]{3,2,1,0:T(8,128)(2,1)S(1)}, u32[]{:S(2)}, u32[]{:S(2)}) collective-permute-start(bf16[4,16,32,128]{3,2,1,0:T(8,128)(2,1)} %get-tuple-element.9), channel_id=1, source_target_pairs={{0,1},{1,2},{2,3},{3,4},{4,5},{5,6},{6,7},{7,8},{8,9},{9,10},{10,1... | collective-permute-start | bytes 1572872 | tf_op jit(solution)/shard_map/ppermute | solution.py:246
  24.3 2.1 %collective-permute-start.3 = (bf16[4,16,32,128]{3,2,1,0:T(8,128)(2,1)}, bf16[4,16,32,128]{3,2,1,0:T(8,128)(2,1)S(1)}, u32[]{:S(2)}, u32[]{:S(2)}) collective-permute-start(bf16[4,16,32,128]{3,2,1,0:T(8,128)(2,1)} %get-tuple-element.10), channel_id=1, source_target_pairs={{1,0},{2,1},{3,2},{4,3},{5,4},{6,5},{7,6},{8,7},{9,8},{10,9},{11,1... | collective-permute-start | bytes 1572872 | tf_op jit(solution)/shard_map/ppermute | solution.py:246
  26.4 7.5 %interior_filtered.1.refs_1_ = f32[8,16,32,128]{3,2,1,0:T(8,128)} custom-call(bf16[8,16,32,128]{3,2,1,0:T(8,128)(2,1)} %get-tuple-element.11.own_narrow, f32[8,16,32,128]{3,2,1,0:T(8,128)} %broadcast_in_dim.2.pot), custom_call_target="tpu_custom_call" | custom-call | tf_op jit(solution)/shard_map/interior_filtered/pallas_call | solution.py:124
  33.9 1.1 %pad_maximum_fusion.1.refs_0_ = bf16[8,16,32,128]{3,2,1,0:T(8,128)(2,1)} fusion(bf16[4,16,32,128]{3,2,1,0:T(8,128)(2,1)S(1)} %collective-permute-done.3, bf16[4,16,32,128]{3,2,1,0:T(8,128)(2,1)S(1)} %collective-permute-done.2), kind=kLoop, calls=%fused_computation.5 | loop fusion | flops 524288 | bytes 2097152 | tf_op jit(solution)/shard_map/concatenate | solution.py:133
  35.1 4.3 %finish_filtered.1 = (bf16[8,16,32,128]{3,2,1,0:T(8,128)(2,1)}, bf16[4,16,32,128]{3,2,1,0:T(8,128)(2,1)}, bf16[4,16,32,128]{3,2,1,0:T(8,128)(2,1)}) custom-call(bf16[8,16,32,128]{3,2,1,0:T(8,128)(2,1)} %pad_maximum_fusion.1.refs_0_, f32[8,16,32,128]{3,2,1,0:T(8,128)} %interior_filtered.1.refs_1_, bf16[8,16,32,128]{3,2,1,0:T(8,128)(2,1)} %refs_2_.1), custom_call_target="tpu_custom_call" | custom-call | tf_op jit(solution)/shard_map/finish_filtered/pallas_call | solution.py:146
  39.3 4.9 %collective-permute-start.10 = (bf16[4,16,32,128]{3,2,1,0:T(8,128)(2,1)}, bf16[4,16,32,128]{3,2,1,0:T(8,128)(2,1)S(1)}, u32[]{:S(2)}, u32[]{:S(2)}) collective-permute-start(bf16[4,16,32,128]{3,2,1,0:T(8,128)(2,1)} %get-tuple-element.14), channel_id=1, source_target_pairs={{0,1},{1,2},{2,3},{3,4},{4,5},{5,6},{6,7},{7,8},{8,9},{9,10},{10,1... | collective-permute-start | bytes 1572872 | tf_op jit(solution)/shard_map/ppermute | solution.py:246
  44.2 1.5 %collective-permute-start.5 = (bf16[2048,128]{1,0:T(8,128)(2,1)}, bf16[2048,128]{1,0:T(8,128)(2,1)S(1)}, u32[]{:S(2)}, u32[]{:S(2)}) collective-permute-start(bf16[2048,128]{1,0:T(8,128)(2,1)} %bitcast.31), channel_id=1, source_target_pairs={{0,16},{16,0},{1,17},{17,1},{2,18},{18,2},{3,19},{19,3},{4,20},{20... | collective-permute-start | bytes 1572872 | tf_op jit(solution)/shard_map/ppermute | solution.py:285
  45.8 2.0 %convolution_bitcast_fusion.1 = f32[128,128]{1,0:T(8,128)S(1)} fusion(bf16[8,16,32,128]{3,2,1,0:T(8,128)(2,1)} %get-tuple-element.6.own_narrow), kind=kOutput, calls=%fused_computation.3 | convolution fusion | flops 134217728 | bytes 1114112 | tf_op jit(solution)/shard_map/cb,ck->bk/dot_general | solution.py:266
  47.9 7.4 %interior_applied.1.refs_1_ = f32[8,16,32,128]{3,2,1,0:T(8,128)} custom-call(bf16[8,16,32,128]{3,2,1,0:T(8,128)(2,1)} %get-tuple-element.6.own_narrow, f32[8,16,32,128]{3,2,1,0:T(8,128)} %broadcast_in_dim.2.pot), custom_call_target="tpu_custom_call" | custom-call | tf_op jit(solution)/shard_map/interior_applied/pallas_call | solution.py:124
  55.3 0.5 collective-permute-start.4
  55.8 1.1 %pad_maximum_fusion.2.refs_0_ = bf16[8,16,32,128]{3,2,1,0:T(8,128)(2,1)} fusion(bf16[4,16,32,128]{3,2,1,0:T(8,128)(2,1)S(1)} %collective-permute-done.11, bf16[4,16,32,128]{3,2,1,0:T(8,128)(2,1)S(1)} %collective-permute-done.10), kind=kLoop, calls=%fused_computation.6 | loop fusion | flops 524288 | bytes 2097152 | tf_op jit(solution)/shard_map/concatenate | solution.py:133
  56.8 3.5 %finish_applied.1 = bf16[8,16,32,128]{3,2,1,0:T(8,128)(2,1)} custom-call(bf16[8,16,32,128]{3,2,1,0:T(8,128)(2,1)} %pad_maximum_fusion.2.refs_0_, f32[8,16,32,128]{3,2,1,0:T(8,128)} %interior_applied.1.refs_1_), custom_call_target="tpu_custom_call" | custom-call | tf_op jit(solution)/shard_map/finish_applied/pallas_call | solution.py:146
  60.3 1.4 %fusion = (bf16[4,16,32,128]{3,2,1,0:T(8,128)(2,1)S(1)}, bf16[4,16,32,128]{3,2,1,0:T(8,128)(2,1)S(1)}) fusion(bf16[8,16,32,128]{3,2,1,0:T(8,128)(2,1)} %finish_applied.1), kind=kLoop, calls=%fused_computation.11 | loop fusion | bytes 2097152 | tf_op jit(solution)/shard_map/slice | solution.py:286
  62.7 7.4 %collective-permute-done.4 = bf16[2048,128]{1,0:T(8,128)(2,1)S(1)} collective-permute-done((bf16[2048,128]{1,0:T(8,128)(2,1)}, bf16[2048,128]{1,0:T(8,128)(2,1)S(1)}, u32[]{:S(2)}, u32[]{:S(2)}) %collective-permute-start.4) | collective-permute-done | bytes 524320 | tf_op jit(solution)/shard_map/ppermute | solution.py:285
  71.2 0.6 collective-permute-start.6
  71.9 0.8 collective-permute-done.6
  72.7 1.3 %collective-permute-start.7 = (f32[128,256]{1,0:T(8,128)S(1)}, f32[128,256]{1,0:T(8,128)S(1)}, u32[]{:S(2)}, u32[]{:S(2)}) collective-permute-start(f32[128,256]{1,0:T(8,128)S(1)} %add.31), channel_id=1, source_target_pairs={{0,2},{1,3},{2,0},{3,1},{4,6},{5,7},{6,4},{7,5},{8,10},{9,11},{10,... | collective-permute-start | bytes 393224 | tf_op jit(solution)/shard_map/ppermute | solution.py:254
  74.0 4.2 %collective-permute-done.13 = f32[128,256]{1,0:T(8,128)S(1)} collective-permute-done((f32[128,256]{1,0:T(8,128)S(1)}, f32[128,256]{1,0:T(8,128)S(1)}, u32[]{:S(2)}, u32[]{:S(2)}) %collective-permute-start.13) | collective-permute-done | bytes 131104 | tf_op jit(solution)/shard_map/ppermute | solution.py:254
  78.3 1.9 %collective-permute-done.7 = f32[128,256]{1,0:T(8,128)S(1)} collective-permute-done((f32[128,256]{1,0:T(8,128)S(1)}, f32[128,256]{1,0:T(8,128)S(1)}, u32[]{:S(2)}, u32[]{:S(2)}) %collective-permute-start.7) | collective-permute-done | bytes 131104 | tf_op jit(solution)/shard_map/ppermute | solution.py:254
  80.4 4.9 %collective-permute-done.14 = f32[128,256]{1,0:T(8,128)S(1)} collective-permute-done((f32[128,256]{1,0:T(8,128)S(1)}, f32[128,256]{1,0:T(8,128)S(1)}, u32[]{:S(2)}, u32[]{:S(2)}) %collective-permute-start.14) | collective-permute-done | bytes 131104 | tf_op jit(solution)/shard_map/ppermute | solution.py:254
  85.4 2.1 %collective-permute-done.8 = f32[128,256]{1,0:T(8,128)S(1)} collective-permute-done((f32[128,256]{1,0:T(8,128)S(1)}, f32[128,256]{1,0:T(8,128)S(1)}, u32[]{:S(2)}, u32[]{:S(2)}) %collective-permute-start.8) | collective-permute-done | bytes 131104 | tf_op jit(solution)/shard_map/ppermute | solution.py:254
  87.5 0.9 collective-permute-start.9
  88.4 6.7 %collective-permute-done.15 = f32[128,256]{1,0:T(8,128)S(1)} collective-permute-done((f32[128,256]{1,0:T(8,128)S(1)}, f32[128,256]{1,0:T(8,128)S(1)}, u32[]{:S(2)}, u32[]{:S(2)}) %collective-permute-start.15) | collective-permute-done | bytes 131104 | tf_op jit(solution)/shard_map/ppermute | solution.py:254
  95.1 0.7 add_multiply_fusion
  95.7 0.7 collective-permute-done.9
  96.5 0.7 add_multiply_fusion.1
  (37 shorter events, 3.1 us)
Async XLA Ops:
  0.6 6.9 %copy-start.3 = (f32[8,16,32]{2,1,0:T(8,128)S(1)}, f32[8,16,32]{2,1,0:T(8,128)}, u32[]{:S(2)}) copy-start(f32[8,16,32]{2,1,0:T(8,128)} %param.3) | copy-start | bytes 49156
  2.0 15.0 %collective-permute-start = (bf16[4,16,32,128]{3,2,1,0:T(8,128)(2,1)S(1)}, bf16[4,16,32,128]{3,2,1,0:T(8,128)(2,1)S(1)}, u32[]{:S(2)}, u32[]{:S(2)}) collective-permute-start(bf16[4,16,32,128]{3,2,1,0:T(8,128)(2,1)S(1)} %get-tuple-element.19), channel_id=1, source_target_pairs={{0,1},{1,2},{2,3},{3,4},{4,5},{5,6},{6,7},{7,8},{8,9},{9,10},{10,1... | collective-permute-start | bytes 1572872 | tf_op jit(solution)/shard_map/ppermute | solution.py:246
  2.5 14.5 %collective-permute-start.1 = (bf16[4,16,32,128]{3,2,1,0:T(8,128)(2,1)S(1)}, bf16[4,16,32,128]{3,2,1,0:T(8,128)(2,1)S(1)}, u32[]{:S(2)}, u32[]{:S(2)}) collective-permute-start(bf16[4,16,32,128]{3,2,1,0:T(8,128)(2,1)S(1)} %get-tuple-element.20), channel_id=1, source_target_pairs={{1,0},{2,1},{3,2},{4,3},{5,4},{6,5},{7,6},{8,7},{9,8},{10,9},{11,1... | collective-permute-start | bytes 1572872 | tf_op jit(solution)/shard_map/ppermute | solution.py:246
  22.0 11.9 %collective-permute-start.2 = (bf16[4,16,32,128]{3,2,1,0:T(8,128)(2,1)}, bf16[4,16,32,128]{3,2,1,0:T(8,128)(2,1)S(1)}, u32[]{:S(2)}, u32[]{:S(2)}) collective-permute-start(bf16[4,16,32,128]{3,2,1,0:T(8,128)(2,1)} %get-tuple-element.9), channel_id=1, source_target_pairs={{0,1},{1,2},{2,3},{3,4},{4,5},{5,6},{6,7},{7,8},{8,9},{9,10},{10,1... | collective-permute-start | bytes 1572872 | tf_op jit(solution)/shard_map/ppermute | solution.py:246
  24.3 9.6 %collective-permute-start.3 = (bf16[4,16,32,128]{3,2,1,0:T(8,128)(2,1)}, bf16[4,16,32,128]{3,2,1,0:T(8,128)(2,1)S(1)}, u32[]{:S(2)}, u32[]{:S(2)}) collective-permute-start(bf16[4,16,32,128]{3,2,1,0:T(8,128)(2,1)} %get-tuple-element.10), channel_id=1, source_target_pairs={{1,0},{2,1},{3,2},{4,3},{5,4},{6,5},{7,6},{8,7},{9,8},{10,9},{11,1... | collective-permute-start | bytes 1572872 | tf_op jit(solution)/shard_map/ppermute | solution.py:246
  39.3 8.5 %copy-start = (bf16[8,16,32,128]{3,2,1,0:T(8,128)(2,1)S(1)}, bf16[8,16,32,128]{3,2,1,0:T(8,128)(2,1)}, u32[]{:S(2)}) copy-start(bf16[8,16,32,128]{3,2,1,0:T(8,128)(2,1)} %get-tuple-element.6.own_narrow) | copy-start | bytes 3145732
  39.3 16.5 %collective-permute-start.10 = (bf16[4,16,32,128]{3,2,1,0:T(8,128)(2,1)}, bf16[4,16,32,128]{3,2,1,0:T(8,128)(2,1)S(1)}, u32[]{:S(2)}, u32[]{:S(2)}) collective-permute-start(bf16[4,16,32,128]{3,2,1,0:T(8,128)(2,1)} %get-tuple-element.14), channel_id=1, source_target_pairs={{0,1},{1,2},{2,3},{3,4},{4,5},{5,6},{6,7},{7,8},{8,9},{9,10},{10,1... | collective-permute-start | bytes 1572872 | tf_op jit(solution)/shard_map/ppermute | solution.py:246
  44.2 11.5 %collective-permute-start.11 = (bf16[4,16,32,128]{3,2,1,0:T(8,128)(2,1)}, bf16[4,16,32,128]{3,2,1,0:T(8,128)(2,1)S(1)}, u32[]{:S(2)}, u32[]{:S(2)}) collective-permute-start(bf16[4,16,32,128]{3,2,1,0:T(8,128)(2,1)} %get-tuple-element.13), channel_id=1, source_target_pairs={{1,0},{2,1},{3,2},{4,3},{5,4},{6,5},{7,6},{8,7},{9,8},{10,9},{11,1... | collective-permute-start | bytes 1572872 | tf_op jit(solution)/shard_map/ppermute | solution.py:246
  44.2 17.5 %collective-permute-start.5 = (bf16[2048,128]{1,0:T(8,128)(2,1)}, bf16[2048,128]{1,0:T(8,128)(2,1)S(1)}, u32[]{:S(2)}, u32[]{:S(2)}) collective-permute-start(bf16[2048,128]{1,0:T(8,128)(2,1)} %bitcast.31), channel_id=1, source_target_pairs={{0,16},{16,0},{1,17},{17,1},{2,18},{18,2},{3,19},{19,3},{4,20},{20... | collective-permute-start | bytes 1572872 | tf_op jit(solution)/shard_map/ppermute | solution.py:285
  55.3 14.8 %collective-permute-start.4 = (bf16[2048,128]{1,0:T(8,128)(2,1)}, bf16[2048,128]{1,0:T(8,128)(2,1)S(1)}, u32[]{:S(2)}, u32[]{:S(2)}) collective-permute-start(bf16[2048,128]{1,0:T(8,128)(2,1)} %bitcast.30), channel_id=1, source_target_pairs={{0,16},{16,0},{1,17},{17,1},{2,18},{18,2},{3,19},{19,3},{4,20},{20... | collective-permute-start | bytes 1572872 | tf_op jit(solution)/shard_map/ppermute | solution.py:285
  60.3 1.8 %copy-start.1 = (bf16[8,16,32,128]{3,2,1,0:T(8,128)(2,1)S(1)}, bf16[8,16,32,128]{3,2,1,0:T(8,128)(2,1)}, u32[]{:S(2)}) copy-start(bf16[8,16,32,128]{3,2,1,0:T(8,128)(2,1)} %get-tuple-element.6.own_narrow) | copy-start | bytes 3145732
  60.3 1.9 %copy-start.2 = (bf16[8,16,32,128]{3,2,1,0:T(8,128)(2,1)S(1)}, bf16[8,16,32,128]{3,2,1,0:T(8,128)(2,1)}, u32[]{:S(2)}) copy-start(bf16[8,16,32,128]{3,2,1,0:T(8,128)(2,1)} %finish_applied.1) | copy-start | bytes 3145732
  70.4 1.4 %collective-permute-start.12 = (f32[128,256]{1,0:T(8,128)S(1)}, f32[128,256]{1,0:T(8,128)S(1)}, u32[]{:S(2)}, u32[]{:S(2)}) collective-permute-start(f32[128,256]{1,0:T(8,128)S(1)} %maximum_select_fusion.1), channel_id=1, source_target_pairs={{0,1},{1,0},{2,3},{3,2},{4,5},{5,4},{6,7},{7,6},{8,9},{9,8},{10,11... | collective-permute-start | bytes 393224 | tf_op jit(solution)/shard_map/ppermute | solution.py:254
  71.2 1.5 %collective-permute-start.6 = (f32[128,256]{1,0:T(8,128)S(1)}, f32[128,256]{1,0:T(8,128)S(1)}, u32[]{:S(2)}, u32[]{:S(2)}) collective-permute-start(f32[128,256]{1,0:T(8,128)S(1)} %maximum_select_fusion), channel_id=1, source_target_pairs={{0,1},{1,0},{2,3},{3,2},{4,5},{5,4},{6,7},{7,6},{8,9},{9,8},{10,11... | collective-permute-start | bytes 393224 | tf_op jit(solution)/shard_map/ppermute | solution.py:254
  71.8 6.4 %collective-permute-start.13 = (f32[128,256]{1,0:T(8,128)S(1)}, f32[128,256]{1,0:T(8,128)S(1)}, u32[]{:S(2)}, u32[]{:S(2)}) collective-permute-start(f32[128,256]{1,0:T(8,128)S(1)} %add.36), channel_id=1, source_target_pairs={{0,2},{1,3},{2,0},{3,1},{4,6},{5,7},{6,4},{7,5},{8,10},{9,11},{10,... | collective-permute-start | bytes 393224 | tf_op jit(solution)/shard_map/ppermute | solution.py:254
  72.7 7.5 %collective-permute-start.7 = (f32[128,256]{1,0:T(8,128)S(1)}, f32[128,256]{1,0:T(8,128)S(1)}, u32[]{:S(2)}, u32[]{:S(2)}) collective-permute-start(f32[128,256]{1,0:T(8,128)S(1)} %add.31), channel_id=1, source_target_pairs={{0,2},{1,3},{2,0},{3,1},{4,6},{5,7},{6,4},{7,5},{8,10},{9,11},{10,... | collective-permute-start | bytes 393224 | tf_op jit(solution)/shard_map/ppermute | solution.py:254
  78.2 7.1 %collective-permute-start.14 = (f32[128,256]{1,0:T(8,128)S(1)}, f32[128,256]{1,0:T(8,128)S(1)}, u32[]{:S(2)}, u32[]{:S(2)}) collective-permute-start(f32[128,256]{1,0:T(8,128)S(1)} %add.37), channel_id=1, source_target_pairs={{0,4},{1,5},{2,6},{3,7},{4,0},{5,1},{6,2},{7,3},{8,12},{9,13},{10,... | collective-permute-start | bytes 393224 | tf_op jit(solution)/shard_map/ppermute | solution.py:254
  80.3 7.2 %collective-permute-start.8 = (f32[128,256]{1,0:T(8,128)S(1)}, f32[128,256]{1,0:T(8,128)S(1)}, u32[]{:S(2)}, u32[]{:S(2)}) collective-permute-start(f32[128,256]{1,0:T(8,128)S(1)} %add.32), channel_id=1, source_target_pairs={{0,4},{1,5},{2,6},{3,7},{4,0},{5,1},{6,2},{7,3},{8,12},{9,13},{10,... | collective-permute-start | bytes 393224 | tf_op jit(solution)/shard_map/ppermute | solution.py:254
  85.3 9.7 %collective-permute-start.15 = (f32[128,256]{1,0:T(8,128)S(1)}, f32[128,256]{1,0:T(8,128)S(1)}, u32[]{:S(2)}, u32[]{:S(2)}) collective-permute-start(f32[128,256]{1,0:T(8,128)S(1)} %add.38), channel_id=1, source_target_pairs={{0,8},{1,9},{2,10},{3,11},{4,12},{5,13},{6,14},{7,15},{8,0},{9,1},... | collective-permute-start | bytes 393224 | tf_op jit(solution)/shard_map/ppermute | solution.py:254
  87.5 9.0 %collective-permute-start.9 = (f32[128,256]{1,0:T(8,128)S(1)}, f32[128,256]{1,0:T(8,128)S(1)}, u32[]{:S(2)}, u32[]{:S(2)}) collective-permute-start(f32[128,256]{1,0:T(8,128)S(1)} %add.33), channel_id=1, source_target_pairs={{0,8},{1,9},{2,10},{3,11},{4,12},{5,13},{6,14},{7,15},{8,0},{9,1},... | collective-permute-start | bytes 393224 | tf_op jit(solution)/shard_map/ppermute | solution.py:254

commit v20 on v14

--- a/solution.py
+++ b/solution.py
@@ -62,8 +62,7 @@
     return kernel
 
 
-def finish_kernel(stage, planes, ny):
-    blocks, depth = plane_blocks(planes)
+def finish_kernel(stage, planes, ny, blocks, depth):
 
     def kernel(*refs):
         refs = list(refs)
@@ -130,22 +129,27 @@
         scratch_shapes=[pltpu.VMEM(block.shape, jnp.float32)],
         name=f"interior_{stage}",
     )(block, potential_wide)
+    fine = RADIUS // 2 if RADIUS % 2 == 0 else RADIUS
+    fine_blocks = planes // fine
+    fine_part = pl.BlockSpec((fine, ny, nz, nb), lambda i: (i, 0, 0, 0))
     halos = jnp.concatenate([low, high], axis=0)
-    halo_block = pl.BlockSpec((RADIUS, ny, nz, nb), lambda i: (jnp.minimum(i, 1), 0, 0, 0))
+    halo_block = pl.BlockSpec(
+        (RADIUS, ny, nz, nb), lambda i: (jnp.where(i * fine < RADIUS, 0, 1), 0, 0, 0)
+    )
     operands = [halos, partial]
-    in_specs = [halo_block, part]
+    in_specs = [halo_block, fine_part]
     if initial is not None:
         operands.append(initial)
-        in_specs.append(part)
+        in_specs.append(fine_part)
     shapes = [jax.ShapeDtypeStruct(block.shape, jnp.bfloat16)]
-    out_specs = [part]
+    out_specs = [fine_part]
     if keep_sends:
         edge_shape = jax.ShapeDtypeStruct((RADIUS, ny, nz, nb), jnp.bfloat16)
         shapes += [edge_shape, edge_shape]
         out_specs += [edge, edge]
     return pl.pallas_call(
-        finish_kernel(stage, planes, ny),
-        grid=(blocks,),
+        finish_kernel(stage, planes, ny, fine_blocks, fine),
+        grid=(fine_blocks,),
         in_specs=in_specs,
         out_specs=tuple(out_specs),
         out_shape=tuple(shapes),

time: 93.1 us -> 96.2 us (1.033)
  Pallas kernels: 34.3 us -> 37.1 us
    pallas_call x3, Pallas kernels: 11.7 us -> 14.5 us  [stencil_stage(): pl.pallas_call(finish_kernel(stage, planes, ny, fine_blocks, fine), grid=...]
where the time goes in v20:
time: 96.2 us; the launch traced here: 95.8 us
  Pallas kernels  37.1 us (39%)
  waiting for transfers between devices  24.7 us (26%)
  starting transfers between devices  22 us (23%)
  other arithmetic  4.7 us (5%)
  local copies, waits for them, and re-layouts  3.29 us (3%)
  matrix products  3.22 us (3%)
    pallas_call x3, Pallas kernels, stencil_stage(): pl.pallas_call(interior_kernel(stage, planes, ny, nz), grid=(blocks,), in...  22.6 us
    ppermute x8, waiting for transfers between devices, butterfly_sum(): values = values + lax.ppermute(values, axis, pairs)  21.4 us
    pallas_call x3, Pallas kernels, stencil_stage(): pl.pallas_call(finish_kernel(stage, planes, ny, fine_blocks, fine), grid=...  14.5 us
    ppermute x3, starting transfers between devices, exchange(): lax.ppermute(sends[1], axis, backward)  11 us
    ppermute x8, starting transfers between devices, butterfly_sum(): values = values + lax.ppermute(values, axis, pairs)  5.94 us
    ppermute x3, waiting for transfers between devices, exchange(): lax.ppermute(sends[0], axis, forward)  3.26 us
    dot_general x4, matrix products, shards(): jnp.einsum('cb,ck->bk', rows, cols, preferred_element_type=jnp.float32)  3.22 us
    concatenate x3, other arithmetic, stencil_stage(): halos = jnp.concatenate([low, high], axis=0)  3.22 us
  transfers between devices with their start and end apart: 15, of which 9 were waited for; matrix products, arithmetic and copies ran while one was open for 7% of the time, Pallas kernels for 28%

profile of v20, /device:TPU:0, one launch (start us, length us, event | category | flops | bytes accessed | tf_op | source)
XLA Modules:
  0.0 95.8 jit_solution(7860267944897523772)
XLA Ops:
  0.6 1.3 %fusion = (bf16[4,16,32,128]{3,2,1,0:T(8,128)(2,1)S(1)}, bf16[4,16,32,128]{3,2,1,0:T(8,128)(2,1)S(1)}) fusion(bf16[8,16,32,128]{3,2,1,0:T(8,128)(2,1)} %refs_2_.1), kind=kLoop, calls=%fused_computation.9 | loop fusion | bytes 2097152 | tf_op jit(solution)/shard_map/slice | solution.py:279
  2.0 0.5 collective-permute-start
  2.5 5.0 %collective-permute-start.1 = (bf16[4,16,32,128]{3,2,1,0:T(8,128)(2,1)S(1)}, bf16[4,16,32,128]{3,2,1,0:T(8,128)(2,1)S(1)}, u32[]{:S(2)}, u32[]{:S(2)}) collective-permute-start(bf16[4,16,32,128]{3,2,1,0:T(8,128)(2,1)S(1)} %get-tuple-element.16), channel_id=1, source_target_pairs={{1,0},{2,1},{3,2},{4,3},{5,4},{6,5},{7,6},{8,7},{9,8},{10,9},{11,1... | collective-permute-start | bytes 1572872 | tf_op jit(solution)/shard_map/ppermute | solution.py:250
  7.5 1.9 %broadcast_in_dim.2.pot = f32[8,16,32,128]{3,2,1,0:T(8,128)} broadcast(f32[8,16,32]{2,1,0:T(8,128)S(1)} %copy-done.2), dimensions={0,1,2} | broadcast | bytes 2113536 | tf_op jit(solution)/shard_map/broadcast_in_dim | solution.py:265
  9.5 7.5 %interior_first.1.refs_1_ = f32[8,16,32,128]{3,2,1,0:T(8,128)} custom-call(bf16[8,16,32,128]{3,2,1,0:T(8,128)(2,1)} %refs_2_.1, f32[8,16,32,128]{3,2,1,0:T(8,128)} %broadcast_in_dim.2.pot), custom_call_target="tpu_custom_call" | custom-call | tf_op jit(solution)/shard_map/interior_first/pallas_call | solution.py:123
  17.0 1.1 %pad_maximum_fusion.refs_0_ = bf16[8,16,32,128]{3,2,1,0:T(8,128)(2,1)} fusion(bf16[4,16,32,128]{3,2,1,0:T(8,128)(2,1)S(1)} %collective-permute-done.1, bf16[4,16,32,128]{3,2,1,0:T(8,128)(2,1)S(1)} %collective-permute-done), kind=kLoop, calls=%fused_computation.2 | loop fusion | flops 524288 | bytes 2097152 | tf_op jit(solution)/shard_map/concatenate | solution.py:135
  18.1 4.9 %finish_first.1 = (bf16[8,16,32,128]{3,2,1,0:T(8,128)(2,1)}, bf16[4,16,32,128]{3,2,1,0:T(8,128)(2,1)}, bf16[4,16,32,128]{3,2,1,0:T(8,128)(2,1)}) custom-call(bf16[8,16,32,128]{3,2,1,0:T(8,128)(2,1)} %pad_maximum_fusion.refs_0_, f32[8,16,32,128]{3,2,1,0:T(8,128)} %interior_first.1.refs_1_), custom_call_target="tpu_custom_call" | custom-call | tf_op jit(solution)/shard_map/finish_first/pallas_call | solution.py:150
  23.0 2.3 %collective-permute-start.2 = (bf16[4,16,32,128]{3,2,1,0:T(8,128)(2,1)}, bf16[4,16,32,128]{3,2,1,0:T(8,128)(2,1)S(1)}, u32[]{:S(2)}, u32[]{:S(2)}) collective-permute-start(bf16[4,16,32,128]{3,2,1,0:T(8,128)(2,1)} %get-tuple-element.9), channel_id=1, source_target_pairs={{0,1},{1,2},{2,3},{3,4},{4,5},{5,6},{6,7},{7,8},{8,9},{9,10},{10,1... | collective-permute-start | bytes 1572872 | tf_op jit(solution)/shard_map/ppermute | solution.py:250
  25.3 2.1 %collective-permute-start.3 = (bf16[4,16,32,128]{3,2,1,0:T(8,128)(2,1)}, bf16[4,16,32,128]{3,2,1,0:T(8,128)(2,1)S(1)}, u32[]{:S(2)}, u32[]{:S(2)}) collective-permute-start(bf16[4,16,32,128]{3,2,1,0:T(8,128)(2,1)} %get-tuple-element.10), channel_id=1, source_target_pairs={{1,0},{2,1},{3,2},{4,3},{5,4},{6,5},{7,6},{8,7},{9,8},{10,9},{11,1... | collective-permute-start | bytes 1572872 | tf_op jit(solution)/shard_map/ppermute | solution.py:250
  27.4 7.5 %interior_filtered.1.refs_1_ = f32[8,16,32,128]{3,2,1,0:T(8,128)} custom-call(bf16[8,16,32,128]{3,2,1,0:T(8,128)(2,1)} %get-tuple-element.11.own_narrow, f32[8,16,32,128]{3,2,1,0:T(8,128)} %broadcast_in_dim.2.pot), custom_call_target="tpu_custom_call" | custom-call | tf_op jit(solution)/shard_map/interior_filtered/pallas_call | solution.py:123
  35.0 1.1 %pad_maximum_fusion.1.refs_0_ = bf16[8,16,32,128]{3,2,1,0:T(8,128)(2,1)} fusion(bf16[4,16,32,128]{3,2,1,0:T(8,128)(2,1)S(1)} %collective-permute-done.3, bf16[4,16,32,128]{3,2,1,0:T(8,128)(2,1)S(1)} %collective-permute-done.2), kind=kLoop, calls=%fused_computation.3 | loop fusion | flops 524288 | bytes 2097152 | tf_op jit(solution)/shard_map/concatenate | solution.py:135
  36.0 5.1 %finish_filtered.1 = (bf16[8,16,32,128]{3,2,1,0:T(8,128)(2,1)}, bf16[4,16,32,128]{3,2,1,0:T(8,128)(2,1)}, bf16[4,16,32,128]{3,2,1,0:T(8,128)(2,1)}) custom-call(bf16[8,16,32,128]{3,2,1,0:T(8,128)(2,1)} %pad_maximum_fusion.1.refs_0_, f32[8,16,32,128]{3,2,1,0:T(8,128)} %interior_filtered.1.refs_1_, bf16[8,16,32,128]{3,2,1,0:T(8,128)(2,1)} %refs_2_.1), custom_call_target="tpu_custom_call" | custom-call | tf_op jit(solution)/shard_map/finish_filtered/pallas_call | solution.py:150
  41.2 1.9 %collective-permute-start.4 = (bf16[4096,128]{1,0:T(8,128)(2,1)}, bf16[4096,128]{1,0:T(8,128)(2,1)S(1)}, u32[]{:S(2)}, u32[]{:S(2)}) collective-permute-start(bf16[4096,128]{1,0:T(8,128)(2,1)} %bitcast.18), channel_id=1, source_target_pairs={{0,16},{16,0},{1,17},{17,1},{2,18},{18,2},{3,19},{19,3},{4,20},{20... | collective-permute-start | bytes 3145736 | tf_op jit(solution)/shard_map/ppermute | solution.py:287
  43.1 3.8 %collective-permute-start.10 = (bf16[4,16,32,128]{3,2,1,0:T(8,128)(2,1)}, bf16[4,16,32,128]{3,2,1,0:T(8,128)(2,1)S(1)}, u32[]{:S(2)}, u32[]{:S(2)}) collective-permute-start(bf16[4,16,32,128]{3,2,1,0:T(8,128)(2,1)} %get-tuple-element.14), channel_id=1, source_target_pairs={{1,0},{2,1},{3,2},{4,3},{5,4},{6,5},{7,6},{8,7},{9,8},{10,9},{11,1... | collective-permute-start | bytes 1572872 | tf_op jit(solution)/shard_map/ppermute | solution.py:250
  47.2 7.5 %interior_applied.1.refs_1_ = f32[8,16,32,128]{3,2,1,0:T(8,128)} custom-call(bf16[8,16,32,128]{3,2,1,0:T(8,128)(2,1)} %get-tuple-element.6.own_narrow, f32[8,16,32,128]{3,2,1,0:T(8,128)} %broadcast_in_dim.2.pot), custom_call_target="tpu_custom_call" | custom-call | tf_op jit(solution)/shard_map/interior_applied/pallas_call | solution.py:123
  55.3 3.3 %collective-permute-done.9 = bf16[4,16,32,128]{3,2,1,0:T(8,128)(2,1)S(1)} collective-permute-done((bf16[4,16,32,128]{3,2,1,0:T(8,128)(2,1)}, bf16[4,16,32,128]{3,2,1,0:T(8,128)(2,1)S(1)}, u32[]{:S(2)}, u32[]{:S(2)}) %collective-permute-start.9) | collective-permute-done | bytes 524320 | tf_op jit(solution)/shard_map/ppermute | solution.py:250
  58.5 1.1 %pad_maximum_fusion.2.refs_0_ = bf16[8,16,32,128]{3,2,1,0:T(8,128)(2,1)} fusion(bf16[4,16,32,128]{3,2,1,0:T(8,128)(2,1)S(1)} %collective-permute-done.10, bf16[4,16,32,128]{3,2,1,0:T(8,128)(2,1)S(1)} %collective-permute-done.9), kind=kLoop, calls=%fused_computation.4 | loop fusion | flops 524288 | bytes 2097152 | tf_op jit(solution)/shard_map/concatenate | solution.py:135
  59.6 4.5 %finish_applied.1 = bf16[8,16,32,128]{3,2,1,0:T(8,128)(2,1)} custom-call(bf16[8,16,32,128]{3,2,1,0:T(8,128)(2,1)} %pad_maximum_fusion.2.refs_0_, f32[8,16,32,128]{3,2,1,0:T(8,128)} %interior_applied.1.refs_1_), custom_call_target="tpu_custom_call" | custom-call | tf_op jit(solution)/shard_map/finish_applied/pallas_call | solution.py:150
  64.1 1.8 %convolution_bitcast_fusion = f32[128,128]{1,0:T(8,128)S(1)} fusion(bf16[8,16,32,128]{3,2,1,0:T(8,128)(2,1)} %finish_applied.1, bf16[8,16,32,128]{3,2,1,0:T(8,128)(2,1)S(1)} %copy-done), kind=kOutput, calls=%fused_computation | convolution fusion | flops 134217728 | bytes 2162688 | tf_op jit(solution)/shard_map/cb,ck->bk/dot_general | solution.py:270
  65.9 0.5 fusion.2
  66.4 3.5 %collective-permute-start.11 = (f32[128,256]{1,0:T(8,128)S(1)}, f32[128,256]{1,0:T(8,128)S(1)}, u32[]{:S(2)}, u32[]{:S(2)}) collective-permute-start(f32[128,256]{1,0:T(8,128)S(1)} %maximum_select_fusion.1), channel_id=1, source_target_pairs={{0,1},{1,0},{2,3},{3,2},{4,5},{5,4},{6,7},{7,6},{8,9},{9,8},{10,11... | collective-permute-start | bytes 393224 | tf_op jit(solution)/shard_map/ppermute | solution.py:258
  71.0 0.8 collective-permute-done.5
  71.9 1.3 %collective-permute-start.6 = (f32[128,256]{1,0:T(8,128)S(1)}, f32[128,256]{1,0:T(8,128)S(1)}, u32[]{:S(2)}, u32[]{:S(2)}) collective-permute-start(f32[128,256]{1,0:T(8,128)S(1)} %add.24), channel_id=1, source_target_pairs={{0,2},{1,3},{2,0},{3,1},{4,6},{5,7},{6,4},{7,5},{8,10},{9,11},{10,... | collective-permute-start | bytes 393224 | tf_op jit(solution)/shard_map/ppermute | solution.py:258
  73.1 4.2 %collective-permute-done.12 = f32[128,256]{1,0:T(8,128)S(1)} collective-permute-done((f32[128,256]{1,0:T(8,128)S(1)}, f32[128,256]{1,0:T(8,128)S(1)}, u32[]{:S(2)}, u32[]{:S(2)}) %collective-permute-start.12) | collective-permute-done | bytes 131104 | tf_op jit(solution)/shard_map/ppermute | solution.py:258
  77.4 2.1 %collective-permute-done.6 = f32[128,256]{1,0:T(8,128)S(1)} collective-permute-done((f32[128,256]{1,0:T(8,128)S(1)}, f32[128,256]{1,0:T(8,128)S(1)}, u32[]{:S(2)}, u32[]{:S(2)}) %collective-permute-start.6) | collective-permute-done | bytes 131104 | tf_op jit(solution)/shard_map/ppermute | solution.py:258
  79.7 3.3 %collective-permute-done.13 = f32[128,256]{1,0:T(8,128)S(1)} collective-permute-done((f32[128,256]{1,0:T(8,128)S(1)}, f32[128,256]{1,0:T(8,128)S(1)}, u32[]{:S(2)}, u32[]{:S(2)}) %collective-permute-start.13) | collective-permute-done | bytes 131104 | tf_op jit(solution)/shard_map/ppermute | solution.py:258
  83.0 0.7 collective-permute-start.14
  83.7 2.9 %collective-permute-done.7 = f32[128,256]{1,0:T(8,128)S(1)} collective-permute-done((f32[128,256]{1,0:T(8,128)S(1)}, f32[128,256]{1,0:T(8,128)S(1)}, u32[]{:S(2)}, u32[]{:S(2)}) %collective-permute-start.7) | collective-permute-done | bytes 131104 | tf_op jit(solution)/shard_map/ppermute | solution.py:258
  86.8 6.8 %collective-permute-done.14 = f32[128,256]{1,0:T(8,128)S(1)} collective-permute-done((f32[128,256]{1,0:T(8,128)S(1)}, f32[128,256]{1,0:T(8,128)S(1)}, u32[]{:S(2)}, u32[]{:S(2)}) %collective-permute-start.14) | collective-permute-done | bytes 131104 | tf_op jit(solution)/shard_map/ppermute | solution.py:258
  93.6 0.7 add_multiply_fusion
  94.2 0.9 collective-permute-done.8
  95.1 0.7 add_multiply_fusion.1
  (29 shorter events, 2.3 us)
Async XLA Ops:
  0.6 6.9 %copy-start.2 = (f32[8,16,32]{2,1,0:T(8,128)S(1)}, f32[8,16,32]{2,1,0:T(8,128)}, u32[]{:S(2)}) copy-start(f32[8,16,32]{2,1,0:T(8,128)} %param.3) | copy-start | bytes 49156
  2.0 15.0 %collective-permute-start = (bf16[4,16,32,128]{3,2,1,0:T(8,128)(2,1)S(1)}, bf16[4,16,32,128]{3,2,1,0:T(8,128)(2,1)S(1)}, u32[]{:S(2)}, u32[]{:S(2)}) collective-permute-start(bf16[4,16,32,128]{3,2,1,0:T(8,128)(2,1)S(1)} %get-tuple-element.15), channel_id=1, source_target_pairs={{0,1},{1,2},{2,3},{3,4},{4,5},{5,6},{6,7},{7,8},{8,9},{9,10},{10,1... | collective-permute-start | bytes 1572872 | tf_op jit(solution)/shard_map/ppermute | solution.py:250
  2.5 14.5 %collective-permute-start.1 = (bf16[4,16,32,128]{3,2,1,0:T(8,128)(2,1)S(1)}, bf16[4,16,32,128]{3,2,1,0:T(8,128)(2,1)S(1)}, u32[]{:S(2)}, u32[]{:S(2)}) collective-permute-start(bf16[4,16,32,128]{3,2,1,0:T(8,128)(2,1)S(1)} %get-tuple-element.16), channel_id=1, source_target_pairs={{1,0},{2,1},{3,2},{4,3},{5,4},{6,5},{7,6},{8,7},{9,8},{10,9},{11,1... | collective-permute-start | bytes 1572872 | tf_op jit(solution)/shard_map/ppermute | solution.py:250
  23.0 12.0 %collective-permute-start.2 = (bf16[4,16,32,128]{3,2,1,0:T(8,128)(2,1)}, bf16[4,16,32,128]{3,2,1,0:T(8,128)(2,1)S(1)}, u32[]{:S(2)}, u32[]{:S(2)}) collective-permute-start(bf16[4,16,32,128]{3,2,1,0:T(8,128)(2,1)} %get-tuple-element.9), channel_id=1, source_target_pairs={{0,1},{1,2},{2,3},{3,4},{4,5},{5,6},{6,7},{7,8},{8,9},{9,10},{10,1... | collective-permute-start | bytes 1572872 | tf_op jit(solution)/shard_map/ppermute | solution.py:250
  25.3 9.7 %collective-permute-start.3 = (bf16[4,16,32,128]{3,2,1,0:T(8,128)(2,1)}, bf16[4,16,32,128]{3,2,1,0:T(8,128)(2,1)S(1)}, u32[]{:S(2)}, u32[]{:S(2)}) collective-permute-start(bf16[4,16,32,128]{3,2,1,0:T(8,128)(2,1)} %get-tuple-element.10), channel_id=1, source_target_pairs={{1,0},{2,1},{3,2},{4,3},{5,4},{6,5},{7,6},{8,7},{9,8},{10,9},{11,1... | collective-permute-start | bytes 1572872 | tf_op jit(solution)/shard_map/ppermute | solution.py:250
  41.2 24.7 %collective-permute-start.4 = (bf16[4096,128]{1,0:T(8,128)(2,1)}, bf16[4096,128]{1,0:T(8,128)(2,1)S(1)}, u32[]{:S(2)}, u32[]{:S(2)}) collective-permute-start(bf16[4096,128]{1,0:T(8,128)(2,1)} %bitcast.18), channel_id=1, source_target_pairs={{0,16},{16,0},{1,17},{17,1},{2,18},{18,2},{3,19},{19,3},{4,20},{20... | collective-permute-start | bytes 3145736 | tf_op jit(solution)/shard_map/ppermute | solution.py:287
  43.1 12.2 %collective-permute-start.10 = (bf16[4,16,32,128]{3,2,1,0:T(8,128)(2,1)}, bf16[4,16,32,128]{3,2,1,0:T(8,128)(2,1)S(1)}, u32[]{:S(2)}, u32[]{:S(2)}) collective-permute-start(bf16[4,16,32,128]{3,2,1,0:T(8,128)(2,1)} %get-tuple-element.14), channel_id=1, source_target_pairs={{1,0},{2,1},{3,2},{4,3},{5,4},{6,5},{7,6},{8,7},{9,8},{10,9},{11,1... | collective-permute-start | bytes 1572872 | tf_op jit(solution)/shard_map/ppermute | solution.py:250
  46.9 11.6 %collective-permute-start.9 = (bf16[4,16,32,128]{3,2,1,0:T(8,128)(2,1)}, bf16[4,16,32,128]{3,2,1,0:T(8,128)(2,1)S(1)}, u32[]{:S(2)}, u32[]{:S(2)}) collective-permute-start(bf16[4,16,32,128]{3,2,1,0:T(8,128)(2,1)} %get-tuple-element.13), channel_id=1, source_target_pairs={{0,1},{1,2},{2,3},{3,4},{4,5},{5,6},{6,7},{7,8},{8,9},{9,10},{10,1... | collective-permute-start | bytes 1572872 | tf_op jit(solution)/shard_map/ppermute | solution.py:250
  47.2 7.5 %copy-start = (bf16[8,16,32,128]{3,2,1,0:T(8,128)(2,1)S(1)}, bf16[8,16,32,128]{3,2,1,0:T(8,128)(2,1)}, u32[]{:S(2)}) copy-start(bf16[8,16,32,128]{3,2,1,0:T(8,128)(2,1)} %get-tuple-element.6.own_narrow) | copy-start | bytes 3145732
  64.1 1.8 %copy-start.1 = (bf16[8,16,32,128]{3,2,1,0:T(8,128)(2,1)S(1)}, bf16[8,16,32,128]{3,2,1,0:T(8,128)(2,1)}, u32[]{:S(2)}) copy-start(bf16[8,16,32,128]{3,2,1,0:T(8,128)(2,1)} %finish_applied.1) | copy-start | bytes 3145732
  66.4 4.5 %collective-permute-start.11 = (f32[128,256]{1,0:T(8,128)S(1)}, f32[128,256]{1,0:T(8,128)S(1)}, u32[]{:S(2)}, u32[]{:S(2)}) collective-permute-start(f32[128,256]{1,0:T(8,128)S(1)} %maximum_select_fusion.1), channel_id=1, source_target_pairs={{0,1},{1,0},{2,3},{3,2},{4,5},{5,4},{6,7},{7,6},{8,9},{9,8},{10,11... | collective-permute-start | bytes 393224 | tf_op jit(solution)/shard_map/ppermute | solution.py:258
  70.4 1.4 %collective-permute-start.5 = (f32[128,256]{1,0:T(8,128)S(1)}, f32[128,256]{1,0:T(8,128)S(1)}, u32[]{:S(2)}, u32[]{:S(2)}) collective-permute-start(f32[128,256]{1,0:T(8,128)S(1)} %maximum_select_fusion), channel_id=1, source_target_pairs={{0,1},{1,0},{2,3},{3,2},{4,5},{5,4},{6,7},{7,6},{8,9},{9,8},{10,11... | collective-permute-start | bytes 393224 | tf_op jit(solution)/shard_map/ppermute | solution.py:258
  70.9 6.4 %collective-permute-start.12 = (f32[128,256]{1,0:T(8,128)S(1)}, f32[128,256]{1,0:T(8,128)S(1)}, u32[]{:S(2)}, u32[]{:S(2)}) collective-permute-start(f32[128,256]{1,0:T(8,128)S(1)} %add.28), channel_id=1, source_target_pairs={{0,2},{1,3},{2,0},{3,1},{4,6},{5,7},{6,4},{7,5},{8,10},{9,11},{10,... | collective-permute-start | bytes 393224 | tf_op jit(solution)/shard_map/ppermute | solution.py:258
  71.9 7.7 %collective-permute-start.6 = (f32[128,256]{1,0:T(8,128)S(1)}, f32[128,256]{1,0:T(8,128)S(1)}, u32[]{:S(2)}, u32[]{:S(2)}) collective-permute-start(f32[128,256]{1,0:T(8,128)S(1)} %add.24), channel_id=1, source_target_pairs={{0,2},{1,3},{2,0},{3,1},{4,6},{5,7},{6,4},{7,5},{8,10},{9,11},{10,... | collective-permute-start | bytes 393224 | tf_op jit(solution)/shard_map/ppermute | solution.py:258
  77.4 5.6 %collective-permute-start.13 = (f32[128,256]{1,0:T(8,128)S(1)}, f32[128,256]{1,0:T(8,128)S(1)}, u32[]{:S(2)}, u32[]{:S(2)}) collective-permute-start(f32[128,256]{1,0:T(8,128)S(1)} %add.29), channel_id=1, source_target_pairs={{0,4},{1,5},{2,6},{3,7},{4,0},{5,1},{6,2},{7,3},{8,12},{9,13},{10,... | collective-permute-start | bytes 393224 | tf_op jit(solution)/shard_map/ppermute | solution.py:258
  79.6 7.0 %collective-permute-start.7 = (f32[128,256]{1,0:T(8,128)S(1)}, f32[128,256]{1,0:T(8,128)S(1)}, u32[]{:S(2)}, u32[]{:S(2)}) collective-permute-start(f32[128,256]{1,0:T(8,128)S(1)} %add.25), channel_id=1, source_target_pairs={{0,4},{1,5},{2,6},{3,7},{4,0},{5,1},{6,2},{7,3},{8,12},{9,13},{10,... | collective-permute-start | bytes 393224 | tf_op jit(solution)/shard_map/ppermute | solution.py:258
  83.0 10.5 %collective-permute-start.14 = (f32[128,256]{1,0:T(8,128)S(1)}, f32[128,256]{1,0:T(8,128)S(1)}, u32[]{:S(2)}, u32[]{:S(2)}) collective-permute-start(f32[128,256]{1,0:T(8,128)S(1)} %add.30), channel_id=1, source_target_pairs={{0,8},{1,9},{2,10},{3,11},{4,12},{5,13},{6,14},{7,15},{8,0},{9,1},... | collective-permute-start | bytes 393224 | tf_op jit(solution)/shard_map/ppermute | solution.py:258
  86.6 8.5 %collective-permute-start.8 = (f32[128,256]{1,0:T(8,128)S(1)}, f32[128,256]{1,0:T(8,128)S(1)}, u32[]{:S(2)}, u32[]{:S(2)}) collective-permute-start(f32[128,256]{1,0:T(8,128)S(1)} %add.26), channel_id=1, source_target_pairs={{0,8},{1,9},{2,10},{3,11},{4,12},{5,13},{6,14},{7,15},{8,0},{9,1},... | collective-permute-start | bytes 393224 | tf_op jit(solution)/shard_map/ppermute | solution.py:258

commit v21 on v14

--- a/solution.py
+++ b/solution.py
@@ -248,11 +248,11 @@
 
 def butterfly_sum(values, axis):
     count = lax.axis_size(axis)
-    bit = 1
-    while bit < count:
+    bit = count // 2
+    while bit >= 1:
         pairs = [(i, i ^ bit) for i in range(count)]
         values = values + lax.ppermute(values, axis, pairs)
-        bit *= 2
+        bit //= 2
     return values
 
 

time: 93.1 us -> 91.5 us (0.983)
  starting transfers between devices: 22 us -> 19.5 us
    ppermute x8, starting transfers between devices: 5.92 us -> 3.47 us  [butterfly_sum(): values = values + lax.ppermute(values, axis, pairs)]
  transfers between devices with their start and end apart: 15 -> 15, of which waited for: 9 -> 8; matrix products, arithmetic and copies ran while one was open for 7% -> 7% of each run, Pallas kernels for 28% -> 29%
where the time goes in v21:
time: 91.5 us; the launch traced here: 91.3 us
  Pallas kernels  34.3 us (37%)
  waiting for transfers between devices  25.4 us (28%)
  starting transfers between devices  19.5 us (21%)
  other arithmetic  4.7 us (5%)
  local copies, waits for them, and re-layouts  3.29 us (4%)
  matrix products  3.22 us (4%)
    pallas_call x3, Pallas kernels, stencil_stage(): pl.pallas_call(interior_kernel(stage, planes, ny, nz), grid=(blocks,), in...  22.6 us
    ppermute x8, waiting for transfers between devices, butterfly_sum(): values = values + lax.ppermute(values, axis, pairs)  22.2 us
    pallas_call x3, Pallas kernels, stencil_stage(): pl.pallas_call(finish_kernel(stage, planes, ny), grid=(blocks,), in_specs...  11.7 us
    ppermute x3, starting transfers between devices, exchange(): lax.ppermute(sends[1], axis, backward)  11 us
    ppermute x8, starting transfers between devices, butterfly_sum(): values = values + lax.ppermute(values, axis, pairs)  3.47 us
    ppermute x3, waiting for transfers between devices, exchange(): lax.ppermute(sends[0], axis, forward)  3.26 us
    concatenate x3, other arithmetic, stencil_stage(): halos = jnp.concatenate([low, high], axis=0)  3.22 us
    dot_general x4, matrix products, shards(): jnp.einsum('cb,ck->bk', rows, cols, preferred_element_type=jnp.float32)  3.22 us
  transfers between devices with their start and end apart: 15, of which 8 were waited for; matrix products, arithmetic and copies ran while one was open for 7% of the time, Pallas kernels for 29%

profile of v21, /device:TPU:0, one launch (start us, length us, event | category | flops | bytes accessed | tf_op | source)
XLA Modules:
  0.0 91.3 jit_solution(2239839630976936817)
XLA Ops:
  0.6 1.3 %fusion = (bf16[4,16,32,128]{3,2,1,0:T(8,128)(2,1)S(1)}, bf16[4,16,32,128]{3,2,1,0:T(8,128)(2,1)S(1)}) fusion(bf16[8,16,32,128]{3,2,1,0:T(8,128)(2,1)} %refs_2_.1), kind=kLoop, calls=%fused_computation.9 | loop fusion | bytes 2097152 | tf_op jit(solution)/shard_map/slice | solution.py:275
  2.0 0.5 collective-permute-start
  2.5 5.0 %collective-permute-start.1 = (bf16[4,16,32,128]{3,2,1,0:T(8,128)(2,1)S(1)}, bf16[4,16,32,128]{3,2,1,0:T(8,128)(2,1)S(1)}, u32[]{:S(2)}, u32[]{:S(2)}) collective-permute-start(bf16[4,16,32,128]{3,2,1,0:T(8,128)(2,1)S(1)} %get-tuple-element.16), channel_id=1, source_target_pairs={{1,0},{2,1},{3,2},{4,3},{5,4},{6,5},{7,6},{8,7},{9,8},{10,9},{11,1... | collective-permute-start | bytes 1572872 | tf_op jit(solution)/shard_map/ppermute | solution.py:246
  7.5 1.9 %broadcast_in_dim.2.pot = f32[8,16,32,128]{3,2,1,0:T(8,128)} broadcast(f32[8,16,32]{2,1,0:T(8,128)S(1)} %copy-done.2), dimensions={0,1,2} | broadcast | bytes 2113536 | tf_op jit(solution)/shard_map/broadcast_in_dim | solution.py:261
  9.5 7.5 %interior_first.1.refs_1_ = f32[8,16,32,128]{3,2,1,0:T(8,128)} custom-call(bf16[8,16,32,128]{3,2,1,0:T(8,128)(2,1)} %refs_2_.1, f32[8,16,32,128]{3,2,1,0:T(8,128)} %broadcast_in_dim.2.pot), custom_call_target="tpu_custom_call" | custom-call | tf_op jit(solution)/shard_map/interior_first/pallas_call | solution.py:124
  17.0 1.1 %pad_maximum_fusion.refs_0_ = bf16[8,16,32,128]{3,2,1,0:T(8,128)(2,1)} fusion(bf16[4,16,32,128]{3,2,1,0:T(8,128)(2,1)S(1)} %collective-permute-done.1, bf16[4,16,32,128]{3,2,1,0:T(8,128)(2,1)S(1)} %collective-permute-done), kind=kLoop, calls=%fused_computation.2 | loop fusion | flops 524288 | bytes 2097152 | tf_op jit(solution)/shard_map/concatenate | solution.py:133
  18.1 4.0 %finish_first.1 = (bf16[8,16,32,128]{3,2,1,0:T(8,128)(2,1)}, bf16[4,16,32,128]{3,2,1,0:T(8,128)(2,1)}, bf16[4,16,32,128]{3,2,1,0:T(8,128)(2,1)}) custom-call(bf16[8,16,32,128]{3,2,1,0:T(8,128)(2,1)} %pad_maximum_fusion.refs_0_, f32[8,16,32,128]{3,2,1,0:T(8,128)} %interior_first.1.refs_1_), custom_call_target="tpu_custom_call" | custom-call | tf_op jit(solution)/shard_map/finish_first/pallas_call | solution.py:146
  22.0 2.3 %collective-permute-start.2 = (bf16[4,16,32,128]{3,2,1,0:T(8,128)(2,1)}, bf16[4,16,32,128]{3,2,1,0:T(8,128)(2,1)S(1)}, u32[]{:S(2)}, u32[]{:S(2)}) collective-permute-start(bf16[4,16,32,128]{3,2,1,0:T(8,128)(2,1)} %get-tuple-element.9), channel_id=1, source_target_pairs={{0,1},{1,2},{2,3},{3,4},{4,5},{5,6},{6,7},{7,8},{8,9},{9,10},{10,1... | collective-permute-start | bytes 1572872 | tf_op jit(solution)/shard_map/ppermute | solution.py:246
  24.3 2.1 %collective-permute-start.3 = (bf16[4,16,32,128]{3,2,1,0:T(8,128)(2,1)}, bf16[4,16,32,128]{3,2,1,0:T(8,128)(2,1)S(1)}, u32[]{:S(2)}, u32[]{:S(2)}) collective-permute-start(bf16[4,16,32,128]{3,2,1,0:T(8,128)(2,1)} %get-tuple-element.10), channel_id=1, source_target_pairs={{1,0},{2,1},{3,2},{4,3},{5,4},{6,5},{7,6},{8,7},{9,8},{10,9},{11,1... | collective-permute-start | bytes 1572872 | tf_op jit(solution)/shard_map/ppermute | solution.py:246
  26.5 7.5 %interior_filtered.1.refs_1_ = f32[8,16,32,128]{3,2,1,0:T(8,128)} custom-call(bf16[8,16,32,128]{3,2,1,0:T(8,128)(2,1)} %get-tuple-element.11.own_narrow, f32[8,16,32,128]{3,2,1,0:T(8,128)} %broadcast_in_dim.2.pot), custom_call_target="tpu_custom_call" | custom-call | tf_op jit(solution)/shard_map/interior_filtered/pallas_call | solution.py:124
  34.0 1.1 %pad_maximum_fusion.1.refs_0_ = bf16[8,16,32,128]{3,2,1,0:T(8,128)(2,1)} fusion(bf16[4,16,32,128]{3,2,1,0:T(8,128)(2,1)S(1)} %collective-permute-done.3, bf16[4,16,32,128]{3,2,1,0:T(8,128)(2,1)S(1)} %collective-permute-done.2), kind=kLoop, calls=%fused_computation.3 | loop fusion | flops 524288 | bytes 2097152 | tf_op jit(solution)/shard_map/concatenate | solution.py:133
  35.1 4.3 %finish_filtered.1 = (bf16[8,16,32,128]{3,2,1,0:T(8,128)(2,1)}, bf16[4,16,32,128]{3,2,1,0:T(8,128)(2,1)}, bf16[4,16,32,128]{3,2,1,0:T(8,128)(2,1)}) custom-call(bf16[8,16,32,128]{3,2,1,0:T(8,128)(2,1)} %pad_maximum_fusion.1.refs_0_, f32[8,16,32,128]{3,2,1,0:T(8,128)} %interior_filtered.1.refs_1_, bf16[8,16,32,128]{3,2,1,0:T(8,128)(2,1)} %refs_2_.1), custom_call_target="tpu_custom_call" | custom-call | tf_op jit(solution)/shard_map/finish_filtered/pallas_call | solution.py:146
  39.3 1.9 %collective-permute-start.4 = (bf16[4096,128]{1,0:T(8,128)(2,1)}, bf16[4096,128]{1,0:T(8,128)(2,1)S(1)}, u32[]{:S(2)}, u32[]{:S(2)}) collective-permute-start(bf16[4096,128]{1,0:T(8,128)(2,1)} %bitcast.18), channel_id=1, source_target_pairs={{0,16},{16,0},{1,17},{17,1},{2,18},{18,2},{3,19},{19,3},{4,20},{20... | collective-permute-start | bytes 3145736 | tf_op jit(solution)/shard_map/ppermute | solution.py:283
  41.3 3.8 %collective-permute-start.10 = (bf16[4,16,32,128]{3,2,1,0:T(8,128)(2,1)}, bf16[4,16,32,128]{3,2,1,0:T(8,128)(2,1)S(1)}, u32[]{:S(2)}, u32[]{:S(2)}) collective-permute-start(bf16[4,16,32,128]{3,2,1,0:T(8,128)(2,1)} %get-tuple-element.14), channel_id=1, source_target_pairs={{1,0},{2,1},{3,2},{4,3},{5,4},{6,5},{7,6},{8,7},{9,8},{10,9},{11,1... | collective-permute-start | bytes 1572872 | tf_op jit(solution)/shard_map/ppermute | solution.py:246
  45.4 7.5 %interior_applied.1.refs_1_ = f32[8,16,32,128]{3,2,1,0:T(8,128)} custom-call(bf16[8,16,32,128]{3,2,1,0:T(8,128)(2,1)} %get-tuple-element.6.own_narrow, f32[8,16,32,128]{3,2,1,0:T(8,128)} %broadcast_in_dim.2.pot), custom_call_target="tpu_custom_call" | custom-call | tf_op jit(solution)/shard_map/interior_applied/pallas_call | solution.py:124
  53.0 0.5 convolution_bitcast_fusion.1
  53.4 3.3 %collective-permute-done.9 = bf16[4,16,32,128]{3,2,1,0:T(8,128)(2,1)S(1)} collective-permute-done((bf16[4,16,32,128]{3,2,1,0:T(8,128)(2,1)}, bf16[4,16,32,128]{3,2,1,0:T(8,128)(2,1)S(1)}, u32[]{:S(2)}, u32[]{:S(2)}) %collective-permute-start.9) | collective-permute-done | bytes 524320 | tf_op jit(solution)/shard_map/ppermute | solution.py:246
  56.7 1.1 %pad_maximum_fusion.2.refs_0_ = bf16[8,16,32,128]{3,2,1,0:T(8,128)(2,1)} fusion(bf16[4,16,32,128]{3,2,1,0:T(8,128)(2,1)S(1)} %collective-permute-done.10, bf16[4,16,32,128]{3,2,1,0:T(8,128)(2,1)S(1)} %collective-permute-done.9), kind=kLoop, calls=%fused_computation.4 | loop fusion | flops 524288 | bytes 2097152 | tf_op jit(solution)/shard_map/concatenate | solution.py:133
  57.8 3.5 %finish_applied.1 = bf16[8,16,32,128]{3,2,1,0:T(8,128)(2,1)} custom-call(bf16[8,16,32,128]{3,2,1,0:T(8,128)(2,1)} %pad_maximum_fusion.2.refs_0_, f32[8,16,32,128]{3,2,1,0:T(8,128)} %interior_applied.1.refs_1_), custom_call_target="tpu_custom_call" | custom-call | tf_op jit(solution)/shard_map/finish_applied/pallas_call | solution.py:146
  61.3 1.8 %convolution_bitcast_fusion = f32[128,128]{1,0:T(8,128)S(1)} fusion(bf16[8,16,32,128]{3,2,1,0:T(8,128)(2,1)} %finish_applied.1, bf16[8,16,32,128]{3,2,1,0:T(8,128)(2,1)S(1)} %copy-done), kind=kOutput, calls=%fused_computation | convolution fusion | flops 134217728 | bytes 2162688 | tf_op jit(solution)/shard_map/cb,ck->bk/dot_general | solution.py:266
  63.1 0.5 fusion.2
  63.7 0.5 fusion.1
  64.2 3.0 %collective-permute-start.5 = (f32[128,256]{1,0:T(8,128)S(1)}, f32[128,256]{1,0:T(8,128)S(1)}, u32[]{:S(2)}, u32[]{:S(2)}) collective-permute-start(f32[128,256]{1,0:T(8,128)S(1)} %maximum_select_fusion), channel_id=1, source_target_pairs={{0,8},{1,9},{2,10},{3,11},{4,12},{5,13},{6,14},{7,15},{8,0},{9,1},... | collective-permute-start | bytes 393224 | tf_op jit(solution)/shard_map/ppermute | solution.py:254
  67.2 7.7 %collective-permute-done.11 = f32[128,256]{1,0:T(8,128)S(1)} collective-permute-done((f32[128,256]{1,0:T(8,128)S(1)}, f32[128,256]{1,0:T(8,128)S(1)}, u32[]{:S(2)}, u32[]{:S(2)}) %collective-permute-start.11) | collective-permute-done | bytes 131104 | tf_op jit(solution)/shard_map/ppermute | solution.py:254
  75.0 2.7 %collective-permute-done.5 = f32[128,256]{1,0:T(8,128)S(1)} collective-permute-done((f32[128,256]{1,0:T(8,128)S(1)}, f32[128,256]{1,0:T(8,128)S(1)}, u32[]{:S(2)}, u32[]{:S(2)}) %collective-permute-start.5) | collective-permute-done | bytes 131104 | tf_op jit(solution)/shard_map/ppermute | solution.py:254
  77.8 3.5 %collective-permute-done.12 = f32[128,256]{1,0:T(8,128)S(1)} collective-permute-done((f32[128,256]{1,0:T(8,128)S(1)}, f32[128,256]{1,0:T(8,128)S(1)}, u32[]{:S(2)}, u32[]{:S(2)}) %collective-permute-start.12) | collective-permute-done | bytes 131104 | tf_op jit(solution)/shard_map/ppermute | solution.py:254
  81.4 2.4 %collective-permute-done.6 = f32[128,256]{1,0:T(8,128)S(1)} collective-permute-done((f32[128,256]{1,0:T(8,128)S(1)}, f32[128,256]{1,0:T(8,128)S(1)}, u32[]{:S(2)}, u32[]{:S(2)}) %collective-permute-start.6) | collective-permute-done | bytes 131104 | tf_op jit(solution)/shard_map/ppermute | solution.py:254
  83.9 2.5 %collective-permute-done.13 = f32[128,256]{1,0:T(8,128)S(1)} collective-permute-done((f32[128,256]{1,0:T(8,128)S(1)}, f32[128,256]{1,0:T(8,128)S(1)}, u32[]{:S(2)}, u32[]{:S(2)}) %collective-permute-start.13) | collective-permute-done | bytes 131104 | tf_op jit(solution)/shard_map/ppermute | solution.py:254
  86.5 2.7 %collective-permute-done.7 = f32[128,256]{1,0:T(8,128)S(1)} collective-permute-done((f32[128,256]{1,0:T(8,128)S(1)}, f32[128,256]{1,0:T(8,128)S(1)}, u32[]{:S(2)}, u32[]{:S(2)}) %collective-permute-start.7) | collective-permute-done | bytes 131104 | tf_op jit(solution)/shard_map/ppermute | solution.py:254
  89.3 0.7 add_multiply_fusion
  90.0 0.7 collective-permute-done.8
  90.6 0.7 add_multiply_fusion.1
  (29 shorter events, 1.0 us)
Async XLA Ops:
  0.6 6.9 %copy-start.2 = (f32[8,16,32]{2,1,0:T(8,128)S(1)}, f32[8,16,32]{2,1,0:T(8,128)}, u32[]{:S(2)}) copy-start(f32[8,16,32]{2,1,0:T(8,128)} %param.3) | copy-start | bytes 49156
  2.0 15.0 %collective-permute-start = (bf16[4,16,32,128]{3,2,1,0:T(8,128)(2,1)S(1)}, bf16[4,16,32,128]{3,2,1,0:T(8,128)(2,1)S(1)}, u32[]{:S(2)}, u32[]{:S(2)}) collective-permute-start(bf16[4,16,32,128]{3,2,1,0:T(8,128)(2,1)S(1)} %get-tuple-element.15), channel_id=1, source_target_pairs={{0,1},{1,2},{2,3},{3,4},{4,5},{5,6},{6,7},{7,8},{8,9},{9,10},{10,1... | collective-permute-start | bytes 1572872 | tf_op jit(solution)/shard_map/ppermute | solution.py:246
  2.5 14.5 %collective-permute-start.1 = (bf16[4,16,32,128]{3,2,1,0:T(8,128)(2,1)S(1)}, bf16[4,16,32,128]{3,2,1,0:T(8,128)(2,1)S(1)}, u32[]{:S(2)}, u32[]{:S(2)}) collective-permute-start(bf16[4,16,32,128]{3,2,1,0:T(8,128)(2,1)S(1)} %get-tuple-element.16), channel_id=1, source_target_pairs={{1,0},{2,1},{3,2},{4,3},{5,4},{6,5},{7,6},{8,7},{9,8},{10,9},{11,1... | collective-permute-start | bytes 1572872 | tf_op jit(solution)/shard_map/ppermute | solution.py:246
  22.0 12.0 %collective-permute-start.2 = (bf16[4,16,32,128]{3,2,1,0:T(8,128)(2,1)}, bf16[4,16,32,128]{3,2,1,0:T(8,128)(2,1)S(1)}, u32[]{:S(2)}, u32[]{:S(2)}) collective-permute-start(bf16[4,16,32,128]{3,2,1,0:T(8,128)(2,1)} %get-tuple-element.9), channel_id=1, source_target_pairs={{0,1},{1,2},{2,3},{3,4},{4,5},{5,6},{6,7},{7,8},{8,9},{9,10},{10,1... | collective-permute-start | bytes 1572872 | tf_op jit(solution)/shard_map/ppermute | solution.py:246
  24.3 9.7 %collective-permute-start.3 = (bf16[4,16,32,128]{3,2,1,0:T(8,128)(2,1)}, bf16[4,16,32,128]{3,2,1,0:T(8,128)(2,1)S(1)}, u32[]{:S(2)}, u32[]{:S(2)}) collective-permute-start(bf16[4,16,32,128]{3,2,1,0:T(8,128)(2,1)} %get-tuple-element.10), channel_id=1, source_target_pairs={{1,0},{2,1},{3,2},{4,3},{5,4},{6,5},{7,6},{8,7},{9,8},{10,9},{11,1... | collective-permute-start | bytes 1572872 | tf_op jit(solution)/shard_map/ppermute | solution.py:246
  39.3 23.7 %collective-permute-start.4 = (bf16[4096,128]{1,0:T(8,128)(2,1)}, bf16[4096,128]{1,0:T(8,128)(2,1)S(1)}, u32[]{:S(2)}, u32[]{:S(2)}) collective-permute-start(bf16[4096,128]{1,0:T(8,128)(2,1)} %bitcast.18), channel_id=1, source_target_pairs={{0,16},{16,0},{1,17},{17,1},{2,18},{18,2},{3,19},{19,3},{4,20},{20... | collective-permute-start | bytes 3145736 | tf_op jit(solution)/shard_map/ppermute | solution.py:283
  41.3 12.2 %collective-permute-start.10 = (bf16[4,16,32,128]{3,2,1,0:T(8,128)(2,1)}, bf16[4,16,32,128]{3,2,1,0:T(8,128)(2,1)S(1)}, u32[]{:S(2)}, u32[]{:S(2)}) collective-permute-start(bf16[4,16,32,128]{3,2,1,0:T(8,128)(2,1)} %get-tuple-element.14), channel_id=1, source_target_pairs={{1,0},{2,1},{3,2},{4,3},{5,4},{6,5},{7,6},{8,7},{9,8},{10,9},{11,1... | collective-permute-start | bytes 1572872 | tf_op jit(solution)/shard_map/ppermute | solution.py:246
  45.1 11.6 %collective-permute-start.9 = (bf16[4,16,32,128]{3,2,1,0:T(8,128)(2,1)}, bf16[4,16,32,128]{3,2,1,0:T(8,128)(2,1)S(1)}, u32[]{:S(2)}, u32[]{:S(2)}) collective-permute-start(bf16[4,16,32,128]{3,2,1,0:T(8,128)(2,1)} %get-tuple-element.13), channel_id=1, source_target_pairs={{0,1},{1,2},{2,3},{3,4},{4,5},{5,6},{6,7},{7,8},{8,9},{9,10},{10,1... | collective-permute-start | bytes 1572872 | tf_op jit(solution)/shard_map/ppermute | solution.py:246
  45.4 7.5 %copy-start = (bf16[8,16,32,128]{3,2,1,0:T(8,128)(2,1)S(1)}, bf16[8,16,32,128]{3,2,1,0:T(8,128)(2,1)}, u32[]{:S(2)}) copy-start(bf16[8,16,32,128]{3,2,1,0:T(8,128)(2,1)} %get-tuple-element.6.own_narrow) | copy-start | bytes 3145732
  61.3 1.8 %copy-start.1 = (bf16[8,16,32,128]{3,2,1,0:T(8,128)(2,1)S(1)}, bf16[8,16,32,128]{3,2,1,0:T(8,128)(2,1)}, u32[]{:S(2)}) copy-start(bf16[8,16,32,128]{3,2,1,0:T(8,128)(2,1)} %finish_applied.1) | copy-start | bytes 3145732
  63.6 11.3 %collective-permute-start.11 = (f32[128,256]{1,0:T(8,128)S(1)}, f32[128,256]{1,0:T(8,128)S(1)}, u32[]{:S(2)}, u32[]{:S(2)}) collective-permute-start(f32[128,256]{1,0:T(8,128)S(1)} %maximum_select_fusion.1), channel_id=1, source_target_pairs={{0,8},{1,9},{2,10},{3,11},{4,12},{5,13},{6,14},{7,15},{8,0},{9,1},... | collective-permute-start | bytes 393224 | tf_op jit(solution)/shard_map/ppermute | solution.py:254
  64.2 13.5 %collective-permute-start.5 = (f32[128,256]{1,0:T(8,128)S(1)}, f32[128,256]{1,0:T(8,128)S(1)}, u32[]{:S(2)}, u32[]{:S(2)}) collective-permute-start(f32[128,256]{1,0:T(8,128)S(1)} %maximum_select_fusion), channel_id=1, source_target_pairs={{0,8},{1,9},{2,10},{3,11},{4,12},{5,13},{6,14},{7,15},{8,0},{9,1},... | collective-permute-start | bytes 393224 | tf_op jit(solution)/shard_map/ppermute | solution.py:254
  74.9 6.4 %collective-permute-start.12 = (f32[128,256]{1,0:T(8,128)S(1)}, f32[128,256]{1,0:T(8,128)S(1)}, u32[]{:S(2)}, u32[]{:S(2)}) collective-permute-start(f32[128,256]{1,0:T(8,128)S(1)} %add.28), channel_id=1, source_target_pairs={{0,4},{1,5},{2,6},{3,7},{4,0},{5,1},{6,2},{7,3},{8,12},{9,13},{10,... | collective-permute-start | bytes 393224 | tf_op jit(solution)/shard_map/ppermute | solution.py:254
  77.7 6.1 %collective-permute-start.6 = (f32[128,256]{1,0:T(8,128)S(1)}, f32[128,256]{1,0:T(8,128)S(1)}, u32[]{:S(2)}, u32[]{:S(2)}) collective-permute-start(f32[128,256]{1,0:T(8,128)S(1)} %add.24), channel_id=1, source_target_pairs={{0,4},{1,5},{2,6},{3,7},{4,0},{5,1},{6,2},{7,3},{8,12},{9,13},{10,... | collective-permute-start | bytes 393224 | tf_op jit(solution)/shard_map/ppermute | solution.py:254
  81.3 5.1 %collective-permute-start.13 = (f32[128,256]{1,0:T(8,128)S(1)}, f32[128,256]{1,0:T(8,128)S(1)}, u32[]{:S(2)}, u32[]{:S(2)}) collective-permute-start(f32[128,256]{1,0:T(8,128)S(1)} %add.29), channel_id=1, source_target_pairs={{0,2},{1,3},{2,0},{3,1},{4,6},{5,7},{6,4},{7,5},{8,10},{9,11},{10,... | collective-permute-start | bytes 393224 | tf_op jit(solution)/shard_map/ppermute | solution.py:254
  83.9 5.3 %collective-permute-start.7 = (f32[128,256]{1,0:T(8,128)S(1)}, f32[128,256]{1,0:T(8,128)S(1)}, u32[]{:S(2)}, u32[]{:S(2)}) collective-permute-start(f32[128,256]{1,0:T(8,128)S(1)} %add.25), channel_id=1, source_target_pairs={{0,2},{1,3},{2,0},{3,1},{4,6},{5,7},{6,4},{7,5},{8,10},{9,11},{10,... | collective-permute-start | bytes 393224 | tf_op jit(solution)/shard_map/ppermute | solution.py:254
  86.4 2.8 %collective-permute-start.14 = (f32[128,256]{1,0:T(8,128)S(1)}, f32[128,256]{1,0:T(8,128)S(1)}, u32[]{:S(2)}, u32[]{:S(2)}) collective-permute-start(f32[128,256]{1,0:T(8,128)S(1)} %add.30), channel_id=1, source_target_pairs={{0,1},{1,0},{2,3},{3,2},{4,5},{5,4},{6,7},{7,6},{8,9},{9,8},{10,11... | collective-permute-start | bytes 393224 | tf_op jit(solution)/shard_map/ppermute | solution.py:254
  89.2 1.4 %collective-permute-start.8 = (f32[128,256]{1,0:T(8,128)S(1)}, f32[128,256]{1,0:T(8,128)S(1)}, u32[]{:S(2)}, u32[]{:S(2)}) collective-permute-start(f32[128,256]{1,0:T(8,128)S(1)} %add.26), channel_id=1, source_target_pairs={{0,1},{1,0},{2,3},{3,2},{4,5},{5,4},{6,7},{7,6},{8,9},{9,8},{10,11... | collective-permute-start | bytes 393224 | tf_op jit(solution)/shard_map/ppermute | solution.py:254

commit v22 on v21

--- a/solution.py
+++ b/solution.py
@@ -248,12 +248,23 @@
 
 def butterfly_sum(values, axis):
     count = lax.axis_size(axis)
+    index = lax.axis_index(axis)
+    pairs_of = lambda bit: [(i, i ^ bit) for i in range(count)]
+    half = values.shape[0] // 2
+    upper = index % 2
+    keep = lax.dynamic_slice_in_dim(values, upper * half, half, axis=0)
+    send = lax.dynamic_slice_in_dim(values, (1 - upper) * half, half, axis=0)
+    values = keep + lax.ppermute(send, axis, pairs_of(1))
     bit = count // 2
-    while bit >= 1:
-        pairs = [(i, i ^ bit) for i in range(count)]
-        values = values + lax.ppermute(values, axis, pairs)
+    while bit >= 2:
+        values = values + lax.ppermute(values, axis, pairs_of(bit))
         bit //= 2
-    return values
+    other = lax.ppermute(values, axis, pairs_of(1))
+    return jnp.where(
+        upper == 0,
+        jnp.concatenate([values, other], axis=0),
+        jnp.concatenate([other, values], axis=0),
+    )
 
 
 def shards(orbitals, potential):

time: 91.5 us -> 87 us (0.951)
  waiting for transfers between devices: 25.4 us -> 15.5 us
  starting transfers between devices: 19.5 us -> 25.1 us
    ppermute x8 -> x10, waiting for transfers between devices: 22.2 us -> 14 us  [the longest x6 12.7 us: butterfly_sum(): values = values + lax.ppermute(values, axis, pairs_of(bit))]
    ppermute x8 -> x10, starting transfers between devices: 3.47 us -> 8.74 us  [the longest x6 4.66 us: butterfly_sum(): values = values + lax.ppermute(values, axis, pairs_of(bit))]
    ppermute x3, starting transfers between devices: 3.16 us -> 7.04 us  [exchange(): lax.ppermute(sends[0], axis, forward)]
    ppermute x3, starting transfers between devices: 11 us -> 7.38 us  [exchange(): lax.ppermute(sends[1], axis, backward)]
    ppermute x3, waiting for transfers between devices: 3.26 us -> 0.01 us  [exchange(): lax.ppermute(sends[0], axis, forward)]
    ppermute x1, waiting for transfers between devices: 0.01 us -> 1.52 us  [shards(): partner = lax.ppermute(own_block, 'band', [(0, 1), (1, 0)])]
  transfers between devices with their start and end apart: 15 -> 17, of which waited for: 8 -> 11; matrix products, arithmetic and copies ran while one was open for 7% -> 8% of each run, Pallas kernels for 29% -> 30%
where the time goes in v22:
time: 87 us; the launch traced here: 86.9 us
  Pallas kernels  34.2 us (39%)
  starting transfers between devices  25.1 us (29%)
  waiting for transfers between devices  15.5 us (18%)
  other arithmetic  4.68 us (5%)
  local copies, waits for them, and re-layouts  3.31 us (4%)
  matrix products  3.22 us (4%)
    pallas_call x3, Pallas kernels, stencil_stage(): pl.pallas_call(interior_kernel(stage, planes, ny, nz), grid=(blocks,), in...  22.5 us
    ppermute x6, waiting for transfers between devices, butterfly_sum(): values = values + lax.ppermute(values, axis, pairs_of(bit))  12.7 us
    pallas_call x3, Pallas kernels, stencil_stage(): pl.pallas_call(finish_kernel(stage, planes, ny), grid=(blocks,), in_specs...  11.7 us
    ppermute x3, starting transfers between devices, exchange(): lax.ppermute(sends[1], axis, backward)  7.38 us
    ppermute x3, starting transfers between devices, exchange(): lax.ppermute(sends[0], axis, forward)  7.04 us
    ppermute x6, starting transfers between devices, butterfly_sum(): values = values + lax.ppermute(values, axis, pairs_of(bit))  4.66 us
    ppermute x2, starting transfers between devices, butterfly_sum(): values = keep + lax.ppermute(send, axis, pairs_of(1))  3.94 us
    concatenate x3, other arithmetic, stencil_stage(): halos = jnp.concatenate([low, high], axis=0)  3.24 us
  transfers between devices with their start and end apart: 17, of which 11 were waited for; matrix products, arithmetic and copies ran while one was open for 8% of the time, Pallas kernels for 30%

profile of v22, /device:TPU:0, one launch (start us, length us, event | category | flops | bytes accessed | tf_op | source)
XLA Modules:
  0.0 86.9 jit_solution(12757770111992432318)
XLA Ops:
  0.6 1.3 %fusion.2 = (bf16[4,16,32,128]{3,2,1,0:T(8,128)(2,1)S(1)}, bf16[4,16,32,128]{3,2,1,0:T(8,128)(2,1)S(1)}) fusion(bf16[8,16,32,128]{3,2,1,0:T(8,128)(2,1)} %refs_2_.1), kind=kLoop, calls=%fused_computation.15 | loop fusion | bytes 2097152 | tf_op jit(solution)/shard_map/slice | solution.py:286
  2.0 0.5 collective-permute-start
  2.5 5.0 %collective-permute-start.1 = (bf16[4,16,32,128]{3,2,1,0:T(8,128)(2,1)S(1)}, bf16[4,16,32,128]{3,2,1,0:T(8,128)(2,1)S(1)}, u32[]{:S(2)}, u32[]{:S(2)}) collective-permute-start(bf16[4,16,32,128]{3,2,1,0:T(8,128)(2,1)S(1)} %get-tuple-element.16), channel_id=1, source_target_pairs={{1,0},{2,1},{3,2},{4,3},{5,4},{6,5},{7,6},{8,7},{9,8},{10,9},{11,1... | collective-permute-start | bytes 1572872 | tf_op jit(solution)/shard_map/ppermute | solution.py:246
  7.5 1.9 %broadcast_in_dim.2.pot = f32[8,16,32,128]{3,2,1,0:T(8,128)} broadcast(f32[8,16,32]{2,1,0:T(8,128)S(1)} %copy-done.2), dimensions={0,1,2} | broadcast | bytes 2113536 | tf_op jit(solution)/shard_map/broadcast_in_dim | solution.py:272
  9.5 7.5 %interior_first.1.refs_1_ = f32[8,16,32,128]{3,2,1,0:T(8,128)} custom-call(bf16[8,16,32,128]{3,2,1,0:T(8,128)(2,1)} %refs_2_.1, f32[8,16,32,128]{3,2,1,0:T(8,128)} %broadcast_in_dim.2.pot), custom_call_target="tpu_custom_call" | custom-call | tf_op jit(solution)/shard_map/interior_first/pallas_call | solution.py:124
  17.0 1.1 %pad_maximum_fusion.refs_0_ = bf16[8,16,32,128]{3,2,1,0:T(8,128)(2,1)} fusion(bf16[4,16,32,128]{3,2,1,0:T(8,128)(2,1)S(1)} %collective-permute-done.1, bf16[4,16,32,128]{3,2,1,0:T(8,128)(2,1)S(1)} %collective-permute-done), kind=kLoop, calls=%fused_computation.2 | loop fusion | flops 524288 | bytes 2097152 | tf_op jit(solution)/shard_map/concatenate | solution.py:133
  18.0 4.0 %finish_first.1 = (bf16[8,16,32,128]{3,2,1,0:T(8,128)(2,1)}, bf16[4,16,32,128]{3,2,1,0:T(8,128)(2,1)}, bf16[4,16,32,128]{3,2,1,0:T(8,128)(2,1)}) custom-call(bf16[8,16,32,128]{3,2,1,0:T(8,128)(2,1)} %pad_maximum_fusion.refs_0_, f32[8,16,32,128]{3,2,1,0:T(8,128)} %interior_first.1.refs_1_), custom_call_target="tpu_custom_call" | custom-call | tf_op jit(solution)/shard_map/finish_first/pallas_call | solution.py:146
  22.0 2.3 %collective-permute-start.2 = (bf16[4,16,32,128]{3,2,1,0:T(8,128)(2,1)}, bf16[4,16,32,128]{3,2,1,0:T(8,128)(2,1)S(1)}, u32[]{:S(2)}, u32[]{:S(2)}) collective-permute-start(bf16[4,16,32,128]{3,2,1,0:T(8,128)(2,1)} %get-tuple-element.9), channel_id=1, source_target_pairs={{0,1},{1,2},{2,3},{3,4},{4,5},{5,6},{6,7},{7,8},{8,9},{9,10},{10,1... | collective-permute-start | bytes 1572872 | tf_op jit(solution)/shard_map/ppermute | solution.py:246
  24.3 2.1 %collective-permute-start.3 = (bf16[4,16,32,128]{3,2,1,0:T(8,128)(2,1)}, bf16[4,16,32,128]{3,2,1,0:T(8,128)(2,1)S(1)}, u32[]{:S(2)}, u32[]{:S(2)}) collective-permute-start(bf16[4,16,32,128]{3,2,1,0:T(8,128)(2,1)} %get-tuple-element.10), channel_id=1, source_target_pairs={{1,0},{2,1},{3,2},{4,3},{5,4},{6,5},{7,6},{8,7},{9,8},{10,9},{11,1... | collective-permute-start | bytes 1572872 | tf_op jit(solution)/shard_map/ppermute | solution.py:246
  26.4 7.5 %interior_filtered.1.refs_1_ = f32[8,16,32,128]{3,2,1,0:T(8,128)} custom-call(bf16[8,16,32,128]{3,2,1,0:T(8,128)(2,1)} %get-tuple-element.11.own_narrow, f32[8,16,32,128]{3,2,1,0:T(8,128)} %broadcast_in_dim.2.pot), custom_call_target="tpu_custom_call" | custom-call | tf_op jit(solution)/shard_map/interior_filtered/pallas_call | solution.py:124
  34.0 1.1 %pad_maximum_fusion.1.refs_0_ = bf16[8,16,32,128]{3,2,1,0:T(8,128)(2,1)} fusion(bf16[4,16,32,128]{3,2,1,0:T(8,128)(2,1)S(1)} %collective-permute-done.3, bf16[4,16,32,128]{3,2,1,0:T(8,128)(2,1)S(1)} %collective-permute-done.2), kind=kLoop, calls=%fused_computation.3 | loop fusion | flops 524288 | bytes 2097152 | tf_op jit(solution)/shard_map/concatenate | solution.py:133
  35.0 4.3 %finish_filtered.1 = (bf16[8,16,32,128]{3,2,1,0:T(8,128)(2,1)}, bf16[4,16,32,128]{3,2,1,0:T(8,128)(2,1)}, bf16[4,16,32,128]{3,2,1,0:T(8,128)(2,1)}) custom-call(bf16[8,16,32,128]{3,2,1,0:T(8,128)(2,1)} %pad_maximum_fusion.1.refs_0_, f32[8,16,32,128]{3,2,1,0:T(8,128)} %interior_filtered.1.refs_1_, bf16[8,16,32,128]{3,2,1,0:T(8,128)(2,1)} %refs_2_.1), custom_call_target="tpu_custom_call" | custom-call | tf_op jit(solution)/shard_map/finish_filtered/pallas_call | solution.py:146
  39.3 1.9 %collective-permute-start.4 = (bf16[4096,128]{1,0:T(8,128)(2,1)}, bf16[4096,128]{1,0:T(8,128)(2,1)S(1)}, u32[]{:S(2)}, u32[]{:S(2)}) collective-permute-start(bf16[4096,128]{1,0:T(8,128)(2,1)} %bitcast.18), channel_id=1, source_target_pairs={{0,16},{16,0},{1,17},{17,1},{2,18},{18,2},{3,19},{19,3},{4,20},{20... | collective-permute-start | bytes 3145736 | tf_op jit(solution)/shard_map/ppermute | solution.py:294
  41.2 4.2 %collective-permute-start.10 = (bf16[4,16,32,128]{3,2,1,0:T(8,128)(2,1)}, bf16[4,16,32,128]{3,2,1,0:T(8,128)(2,1)S(1)}, u32[]{:S(2)}, u32[]{:S(2)}) collective-permute-start(bf16[4,16,32,128]{3,2,1,0:T(8,128)(2,1)} %get-tuple-element.13), channel_id=1, source_target_pairs={{0,1},{1,2},{2,3},{3,4},{4,5},{5,6},{6,7},{7,8},{8,9},{9,10},{10,1... | collective-permute-start | bytes 1572872 | tf_op jit(solution)/shard_map/ppermute | solution.py:246
  45.7 7.5 %interior_applied.1.refs_1_ = f32[8,16,32,128]{3,2,1,0:T(8,128)} custom-call(bf16[8,16,32,128]{3,2,1,0:T(8,128)(2,1)} %get-tuple-element.6.own_narrow, f32[8,16,32,128]{3,2,1,0:T(8,128)} %broadcast_in_dim.2.pot), custom_call_target="tpu_custom_call" | custom-call | tf_op jit(solution)/shard_map/interior_applied/pallas_call | solution.py:124
  53.7 1.1 %pad_maximum_fusion.2.refs_0_ = bf16[8,16,32,128]{3,2,1,0:T(8,128)(2,1)} fusion(bf16[4,16,32,128]{3,2,1,0:T(8,128)(2,1)S(1)} %collective-permute-done.11, bf16[4,16,32,128]{3,2,1,0:T(8,128)(2,1)S(1)} %collective-permute-done.10), kind=kLoop, calls=%fused_computation.4 | loop fusion | flops 524288 | bytes 2097152 | tf_op jit(solution)/shard_map/concatenate | solution.py:133
  54.8 3.5 %finish_applied.1 = bf16[8,16,32,128]{3,2,1,0:T(8,128)(2,1)} custom-call(bf16[8,16,32,128]{3,2,1,0:T(8,128)(2,1)} %pad_maximum_fusion.2.refs_0_, f32[8,16,32,128]{3,2,1,0:T(8,128)} %interior_applied.1.refs_1_), custom_call_target="tpu_custom_call" | custom-call | tf_op jit(solution)/shard_map/finish_applied/pallas_call | solution.py:146
  58.2 1.8 %convolution_bitcast_fusion = f32[128,128]{1,0:T(8,128)S(1)} fusion(bf16[8,16,32,128]{3,2,1,0:T(8,128)(2,1)} %finish_applied.1, bf16[8,16,32,128]{3,2,1,0:T(8,128)(2,1)S(1)} %copy-done), kind=kOutput, calls=%fused_computation | convolution fusion | flops 134217728 | bytes 2162688 | tf_op jit(solution)/shard_map/cb,ck->bk/dot_general | solution.py:277
  60.0 1.5 %collective-permute-done.4 = bf16[4096,128]{1,0:T(8,128)(2,1)S(1)} collective-permute-done((bf16[4096,128]{1,0:T(8,128)(2,1)}, bf16[4096,128]{1,0:T(8,128)(2,1)S(1)}, u32[]{:S(2)}, u32[]{:S(2)}) %collective-permute-start.4) | collective-permute-done | bytes 1048608 | tf_op jit(solution)/shard_map/ppermute | solution.py:294
  61.6 0.5 fusion.4
  62.1 3.9 %collective-permute-start.12 = (f32[64,256]{1,0:T(8,128)S(1)}, f32[64,256]{1,0:T(8,128)S(1)}, u32[]{:S(2)}, u32[]{:S(2)}) collective-permute-start(f32[64,256]{1,0:T(8,128)S(1)} %constant_dynamic-slice_fusion), channel_id=1, source_target_pairs={{0,1},{1,0},{2,3},{3,2},{4,5},{5,4},{6,7},{7,6},{8,9},{9,8},{10,11... | collective-permute-start | bytes 196616 | tf_op jit(solution)/shard_map/ppermute | solution.py:257
  67.8 2.1 %collective-permute-start.6 = (f32[64,256]{1,0:T(8,128)S(1)}, f32[64,256]{1,0:T(8,128)S(1)}, u32[]{:S(2)}, u32[]{:S(2)}) collective-permute-start(f32[64,256]{1,0:T(8,128)S(1)} %dynamic-slice_add_fusion.1), channel_id=1, source_target_pairs={{0,8},{1,9},{2,10},{3,11},{4,12},{5,13},{6,14},{7,15},{8,0},{9,1},... | collective-permute-start | bytes 196616 | tf_op jit(solution)/shard_map/ppermute | solution.py:260
  69.9 4.8 %collective-permute-done.13 = f32[64,256]{1,0:T(8,128)S(1)} collective-permute-done((f32[64,256]{1,0:T(8,128)S(1)}, f32[64,256]{1,0:T(8,128)S(1)}, u32[]{:S(2)}, u32[]{:S(2)}) %collective-permute-start.13) | collective-permute-done | bytes 65568 | tf_op jit(solution)/shard_map/ppermute | solution.py:260
  74.8 1.3 %collective-permute-done.6 = f32[64,256]{1,0:T(8,128)S(1)} collective-permute-done((f32[64,256]{1,0:T(8,128)S(1)}, f32[64,256]{1,0:T(8,128)S(1)}, u32[]{:S(2)}, u32[]{:S(2)}) %collective-permute-start.6) | collective-permute-done | bytes 65568 | tf_op jit(solution)/shard_map/ppermute | solution.py:260
  76.1 0.8 collective-permute-start.7
  76.9 2.5 %collective-permute-done.14 = f32[64,256]{1,0:T(8,128)S(1)} collective-permute-done((f32[64,256]{1,0:T(8,128)S(1)}, f32[64,256]{1,0:T(8,128)S(1)}, u32[]{:S(2)}, u32[]{:S(2)}) %collective-permute-start.14) | collective-permute-done | bytes 65568 | tf_op jit(solution)/shard_map/ppermute | solution.py:260
  79.5 1.0 %collective-permute-done.7 = f32[64,256]{1,0:T(8,128)S(1)} collective-permute-done((f32[64,256]{1,0:T(8,128)S(1)}, f32[64,256]{1,0:T(8,128)S(1)}, u32[]{:S(2)}, u32[]{:S(2)}) %collective-permute-start.7) | collective-permute-done | bytes 65568 | tf_op jit(solution)/shard_map/ppermute | solution.py:260
  80.5 1.1 %collective-permute-start.8 = (f32[64,256]{1,0:T(8,128)S(1)}, f32[64,256]{1,0:T(8,128)S(1)}, u32[]{:S(2)}, u32[]{:S(2)}) collective-permute-start(f32[64,256]{1,0:T(8,128)S(1)} %add.42), channel_id=1, source_target_pairs={{0,2},{1,3},{2,0},{3,1},{4,6},{5,7},{6,4},{7,5},{8,10},{9,11},{10,... | collective-permute-start | bytes 196616 | tf_op jit(solution)/shard_map/ppermute | solution.py:260
  81.6 2.4 %collective-permute-done.15 = f32[64,256]{1,0:T(8,128)S(1)} collective-permute-done((f32[64,256]{1,0:T(8,128)S(1)}, f32[64,256]{1,0:T(8,128)S(1)}, u32[]{:S(2)}, u32[]{:S(2)}) %collective-permute-start.15) | collective-permute-done | bytes 65568 | tf_op jit(solution)/shard_map/ppermute | solution.py:260
  84.2 0.7 collective-permute-done.8
  85.4 0.7 fusion.1
  86.2 0.7 fusion
  (37 shorter events, 3.5 us)
Async XLA Ops:
  0.6 6.9 %copy-start.2 = (f32[8,16,32]{2,1,0:T(8,128)S(1)}, f32[8,16,32]{2,1,0:T(8,128)}, u32[]{:S(2)}) copy-start(f32[8,16,32]{2,1,0:T(8,128)} %param.3) | copy-start | bytes 49156
  2.0 15.0 %collective-permute-start = (bf16[4,16,32,128]{3,2,1,0:T(8,128)(2,1)S(1)}, bf16[4,16,32,128]{3,2,1,0:T(8,128)(2,1)S(1)}, u32[]{:S(2)}, u32[]{:S(2)}) collective-permute-start(bf16[4,16,32,128]{3,2,1,0:T(8,128)(2,1)S(1)} %get-tuple-element.15), channel_id=1, source_target_pairs={{0,1},{1,2},{2,3},{3,4},{4,5},{5,6},{6,7},{7,8},{8,9},{9,10},{10,1... | collective-permute-start | bytes 1572872 | tf_op jit(solution)/shard_map/ppermute | solution.py:246
  2.5 14.5 %collective-permute-start.1 = (bf16[4,16,32,128]{3,2,1,0:T(8,128)(2,1)S(1)}, bf16[4,16,32,128]{3,2,1,0:T(8,128)(2,1)S(1)}, u32[]{:S(2)}, u32[]{:S(2)}) collective-permute-start(bf16[4,16,32,128]{3,2,1,0:T(8,128)(2,1)S(1)} %get-tuple-element.16), channel_id=1, source_target_pairs={{1,0},{2,1},{3,2},{4,3},{5,4},{6,5},{7,6},{8,7},{9,8},{10,9},{11,1... | collective-permute-start | bytes 1572872 | tf_op jit(solution)/shard_map/ppermute | solution.py:246
  22.0 12.0 %collective-permute-start.2 = (bf16[4,16,32,128]{3,2,1,0:T(8,128)(2,1)}, bf16[4,16,32,128]{3,2,1,0:T(8,128)(2,1)S(1)}, u32[]{:S(2)}, u32[]{:S(2)}) collective-permute-start(bf16[4,16,32,128]{3,2,1,0:T(8,128)(2,1)} %get-tuple-element.9), channel_id=1, source_target_pairs={{0,1},{1,2},{2,3},{3,4},{4,5},{5,6},{6,7},{7,8},{8,9},{9,10},{10,1... | collective-permute-start | bytes 1572872 | tf_op jit(solution)/shard_map/ppermute | solution.py:246
  24.3 9.6 %collective-permute-start.3 = (bf16[4,16,32,128]{3,2,1,0:T(8,128)(2,1)}, bf16[4,16,32,128]{3,2,1,0:T(8,128)(2,1)S(1)}, u32[]{:S(2)}, u32[]{:S(2)}) collective-permute-start(bf16[4,16,32,128]{3,2,1,0:T(8,128)(2,1)} %get-tuple-element.10), channel_id=1, source_target_pairs={{1,0},{2,1},{3,2},{4,3},{5,4},{6,5},{7,6},{8,7},{9,8},{10,9},{11,1... | collective-permute-start | bytes 1572872 | tf_op jit(solution)/shard_map/ppermute | solution.py:246
  39.3 22.3 %collective-permute-start.4 = (bf16[4096,128]{1,0:T(8,128)(2,1)}, bf16[4096,128]{1,0:T(8,128)(2,1)S(1)}, u32[]{:S(2)}, u32[]{:S(2)}) collective-permute-start(bf16[4096,128]{1,0:T(8,128)(2,1)} %bitcast.18), channel_id=1, source_target_pairs={{0,16},{16,0},{1,17},{17,1},{2,18},{18,2},{3,19},{19,3},{4,20},{20... | collective-permute-start | bytes 3145736 | tf_op jit(solution)/shard_map/ppermute | solution.py:294
  41.2 12.4 %collective-permute-start.10 = (bf16[4,16,32,128]{3,2,1,0:T(8,128)(2,1)}, bf16[4,16,32,128]{3,2,1,0:T(8,128)(2,1)S(1)}, u32[]{:S(2)}, u32[]{:S(2)}) collective-permute-start(bf16[4,16,32,128]{3,2,1,0:T(8,128)(2,1)} %get-tuple-element.13), channel_id=1, source_target_pairs={{0,1},{1,2},{2,3},{3,4},{4,5},{5,6},{6,7},{7,8},{8,9},{9,10},{10,1... | collective-permute-start | bytes 1572872 | tf_op jit(solution)/shard_map/ppermute | solution.py:246
  45.4 8.2 %collective-permute-start.11 = (bf16[4,16,32,128]{3,2,1,0:T(8,128)(2,1)}, bf16[4,16,32,128]{3,2,1,0:T(8,128)(2,1)S(1)}, u32[]{:S(2)}, u32[]{:S(2)}) collective-permute-start(bf16[4,16,32,128]{3,2,1,0:T(8,128)(2,1)} %get-tuple-element.14), channel_id=1, source_target_pairs={{1,0},{2,1},{3,2},{4,3},{5,4},{6,5},{7,6},{8,7},{9,8},{10,9},{11,1... | collective-permute-start | bytes 1572872 | tf_op jit(solution)/shard_map/ppermute | solution.py:246
  45.7 7.5 %copy-start = (bf16[8,16,32,128]{3,2,1,0:T(8,128)(2,1)S(1)}, bf16[8,16,32,128]{3,2,1,0:T(8,128)(2,1)}, u32[]{:S(2)}) copy-start(bf16[8,16,32,128]{3,2,1,0:T(8,128)(2,1)} %get-tuple-element.6.own_narrow) | copy-start | bytes 3145732
  58.2 3.3 %copy-start.1 = (bf16[8,16,32,128]{3,2,1,0:T(8,128)(2,1)S(1)}, bf16[8,16,32,128]{3,2,1,0:T(8,128)(2,1)}, u32[]{:S(2)}) copy-start(bf16[8,16,32,128]{3,2,1,0:T(8,128)(2,1)} %finish_applied.1) | copy-start | bytes 3145732
  62.1 4.8 %collective-permute-start.12 = (f32[64,256]{1,0:T(8,128)S(1)}, f32[64,256]{1,0:T(8,128)S(1)}, u32[]{:S(2)}, u32[]{:S(2)}) collective-permute-start(f32[64,256]{1,0:T(8,128)S(1)} %constant_dynamic-slice_fusion), channel_id=1, source_target_pairs={{0,1},{1,0},{2,3},{3,2},{4,5},{5,4},{6,7},{7,6},{8,9},{9,8},{10,11... | collective-permute-start | bytes 196616 | tf_op jit(solution)/shard_map/ppermute | solution.py:257
  66.5 1.3 %collective-permute-start.5 = (f32[64,256]{1,0:T(8,128)S(1)}, f32[64,256]{1,0:T(8,128)S(1)}, u32[]{:S(2)}, u32[]{:S(2)}) collective-permute-start(f32[64,256]{1,0:T(8,128)S(1)} %constant_dynamic-slice_fusion.1), channel_id=1, source_target_pairs={{0,1},{1,0},{2,3},{3,2},{4,5},{5,4},{6,7},{7,6},{8,9},{9,8},{10,11... | collective-permute-start | bytes 196616 | tf_op jit(solution)/shard_map/ppermute | solution.py:257
  66.9 7.9 %collective-permute-start.13 = (f32[64,256]{1,0:T(8,128)S(1)}, f32[64,256]{1,0:T(8,128)S(1)}, u32[]{:S(2)}, u32[]{:S(2)}) collective-permute-start(f32[64,256]{1,0:T(8,128)S(1)} %dynamic-slice_add_fusion), channel_id=1, source_target_pairs={{0,8},{1,9},{2,10},{3,11},{4,12},{5,13},{6,14},{7,15},{8,0},{9,1},... | collective-permute-start | bytes 196616 | tf_op jit(solution)/shard_map/ppermute | solution.py:260
  67.8 8.3 %collective-permute-start.6 = (f32[64,256]{1,0:T(8,128)S(1)}, f32[64,256]{1,0:T(8,128)S(1)}, u32[]{:S(2)}, u32[]{:S(2)}) collective-permute-start(f32[64,256]{1,0:T(8,128)S(1)} %dynamic-slice_add_fusion.1), channel_id=1, source_target_pairs={{0,8},{1,9},{2,10},{3,11},{4,12},{5,13},{6,14},{7,15},{8,0},{9,1},... | collective-permute-start | bytes 196616 | tf_op jit(solution)/shard_map/ppermute | solution.py:260
  74.8 4.7 %collective-permute-start.14 = (f32[64,256]{1,0:T(8,128)S(1)}, f32[64,256]{1,0:T(8,128)S(1)}, u32[]{:S(2)}, u32[]{:S(2)}) collective-permute-start(f32[64,256]{1,0:T(8,128)S(1)} %add.45), channel_id=1, source_target_pairs={{0,4},{1,5},{2,6},{3,7},{4,0},{5,1},{6,2},{7,3},{8,12},{9,13},{10,... | collective-permute-start | bytes 196616 | tf_op jit(solution)/shard_map/ppermute | solution.py:260
  76.1 4.4 %collective-permute-start.7 = (f32[64,256]{1,0:T(8,128)S(1)}, f32[64,256]{1,0:T(8,128)S(1)}, u32[]{:S(2)}, u32[]{:S(2)}) collective-permute-start(f32[64,256]{1,0:T(8,128)S(1)} %add.41), channel_id=1, source_target_pairs={{0,4},{1,5},{2,6},{3,7},{4,0},{5,1},{6,2},{7,3},{8,12},{9,13},{10,... | collective-permute-start | bytes 196616 | tf_op jit(solution)/shard_map/ppermute | solution.py:260
  79.5 4.6 %collective-permute-start.15 = (f32[64,256]{1,0:T(8,128)S(1)}, f32[64,256]{1,0:T(8,128)S(1)}, u32[]{:S(2)}, u32[]{:S(2)}) collective-permute-start(f32[64,256]{1,0:T(8,128)S(1)} %add.46), channel_id=1, source_target_pairs={{0,2},{1,3},{2,0},{3,1},{4,6},{5,7},{6,4},{7,5},{8,10},{9,11},{10,... | collective-permute-start | bytes 196616 | tf_op jit(solution)/shard_map/ppermute | solution.py:260
  80.5 4.3 %collective-permute-start.8 = (f32[64,256]{1,0:T(8,128)S(1)}, f32[64,256]{1,0:T(8,128)S(1)}, u32[]{:S(2)}, u32[]{:S(2)}) collective-permute-start(f32[64,256]{1,0:T(8,128)S(1)} %add.42), channel_id=1, source_target_pairs={{0,2},{1,3},{2,0},{3,1},{4,6},{5,7},{6,4},{7,5},{8,10},{9,11},{10,... | collective-permute-start | bytes 196616 | tf_op jit(solution)/shard_map/ppermute | solution.py:260
  84.1 1.3 %collective-permute-start.16 = (f32[64,256]{1,0:T(8,128)S(1)}, f32[64,256]{1,0:T(8,128)S(1)}, u32[]{:S(2)}, u32[]{:S(2)}) collective-permute-start(f32[64,256]{1,0:T(8,128)S(1)} %add.47), channel_id=1, source_target_pairs={{0,1},{1,0},{2,3},{3,2},{4,5},{5,4},{6,7},{7,6},{8,9},{9,8},{10,11... | collective-permute-start | bytes 196616 | tf_op jit(solution)/shard_map/ppermute | solution.py:262
  84.9 1.3 %collective-permute-start.9 = (f32[64,256]{1,0:T(8,128)S(1)}, f32[64,256]{1,0:T(8,128)S(1)}, u32[]{:S(2)}, u32[]{:S(2)}) collective-permute-start(f32[64,256]{1,0:T(8,128)S(1)} %add.43), channel_id=1, source_target_pairs={{0,1},{1,0},{2,3},{3,2},{4,5},{5,4},{6,7},{7,6},{8,9},{9,8},{10,11... | collective-permute-start | bytes 196616 | tf_op jit(solution)/shard_map/ppermute | solution.py:262

commit v23 on v21

--- a/solution.py
+++ b/solution.py
@@ -248,11 +248,27 @@
 
 def butterfly_sum(values, axis):
     count = lax.axis_size(axis)
-    bit = count // 2
-    while bit >= 1:
-        pairs = [(i, i ^ bit) for i in range(count)]
-        values = values + lax.ppermute(values, axis, pairs)
+    index = lax.axis_index(axis)
+    pairs_of = lambda bit: [(i, i ^ bit) for i in range(count)]
+    scattered = [1, count // 2] if count >= 4 else [1]
+    for bit in scattered:
+        half = values.shape[0] // 2
+        upper = (index // bit) % 2
+        keep = lax.dynamic_slice_in_dim(values, upper * half, half, axis=0)
+        send = lax.dynamic_slice_in_dim(values, (1 - upper) * half, half, axis=0)
+        values = keep + lax.ppermute(send, axis, pairs_of(bit))
+    bit = count // 4
+    while bit >= 2:
+        values = values + lax.ppermute(values, axis, pairs_of(bit))
         bit //= 2
+    for bit in reversed(scattered):
+        upper = (index // bit) % 2
+        other = lax.ppermute(values, axis, pairs_of(bit))
+        values = jnp.where(
+            upper == 0,
+            jnp.concatenate([values, other], axis=0),
+            jnp.concatenate([other, values], axis=0),
+        )
     return values
 
 

time: 91.5 us -> 88.9 us (0.972)
  waiting for transfers between devices: 25.4 us -> 10.6 us
  starting transfers between devices: 19.5 us -> 31.9 us
    ppermute x8 -> x12, waiting for transfers between devices: 22.2 us -> 9 us  [the longest x4 3.56 us: butterfly_sum(): other = lax.ppermute(values, axis, pairs_of(bit))]
    ppermute x8 -> x12, starting transfers between devices: 3.47 us -> 15.5 us  [the longest x4 6.5 us: butterfly_sum(): values = keep + lax.ppermute(send, axis, pairs_of(bit))]
    ppermute x3, starting transfers between devices: 3.16 us -> 7.02 us  [exchange(): lax.ppermute(sends[0], axis, forward)]
    ppermute x3, starting transfers between devices: 11 us -> 7.4 us  [exchange(): lax.ppermute(sends[1], axis, backward)]
    ppermute x3, waiting for transfers between devices: 3.26 us -> 0.01 us  [exchange(): lax.ppermute(sends[0], axis, forward)]
    ppermute x1, waiting for transfers between devices: 0.01 us -> 1.56 us  [shards(): partner = lax.ppermute(own_block, 'band', [(0, 1), (1, 0)])]
  transfers between devices with their start and end apart: 15 -> 19, of which waited for: 8 -> 10; matrix products, arithmetic and copies ran while one was open for 7% -> 7% of each run, Pallas kernels for 29% -> 29%
where the time goes in v23:
time: 88.9 us; the launch traced here: 88.7 us
  Pallas kernels  34.2 us (38%)
  starting transfers between devices  31.9 us (36%)
  waiting for transfers between devices  10.6 us (12%)
  other arithmetic  4.69 us (5%)
  local copies, waits for them, and re-layouts  3.34 us (4%)
  matrix products  3.22 us (4%)
    pallas_call x3, Pallas kernels, stencil_stage(): pl.pallas_call(interior_kernel(stage, planes, ny, nz), grid=(blocks,), in...  22.5 us
    pallas_call x3, Pallas kernels, stencil_stage(): pl.pallas_call(finish_kernel(stage, planes, ny), grid=(blocks,), in_specs...  11.7 us
    ppermute x3, starting transfers between devices, exchange(): lax.ppermute(sends[1], axis, backward)  7.4 us
    ppermute x3, starting transfers between devices, exchange(): lax.ppermute(sends[0], axis, forward)  7.02 us
    ppermute x4, starting transfers between devices, butterfly_sum(): values = keep + lax.ppermute(send, axis, pairs_of(bit))  6.5 us
    ppermute x4, starting transfers between devices, butterfly_sum(): values = values + lax.ppermute(values, axis, pairs_of(bit))  5.29 us
    ppermute x4, starting transfers between devices, butterfly_sum(): other = lax.ppermute(values, axis, pairs_of(bit))  3.73 us
    ppermute x4, waiting for transfers between devices, butterfly_sum(): other = lax.ppermute(values, axis, pairs_of(bit))  3.56 us
  transfers between devices with their start and end apart: 19, of which 10 were waited for; matrix products, arithmetic and copies ran while one was open for 7% of the time, Pallas kernels for 29%

profile of v23, /device:TPU:0, one launch (start us, length us, event | category | flops | bytes accessed | tf_op | source)
XLA Modules:
  0.0 88.7 jit_solution(11935151514508897163)
XLA Ops:
  0.6 1.3 %fusion.2 = (bf16[4,16,32,128]{3,2,1,0:T(8,128)(2,1)S(1)}, bf16[4,16,32,128]{3,2,1,0:T(8,128)(2,1)S(1)}) fusion(bf16[8,16,32,128]{3,2,1,0:T(8,128)(2,1)} %refs_2_.1), kind=kLoop, calls=%fused_computation.21 | loop fusion | bytes 2097152 | tf_op jit(solution)/shard_map/slice | solution.py:291
  2.5 5.0 %collective-permute-start.1 = (bf16[4,16,32,128]{3,2,1,0:T(8,128)(2,1)S(1)}, bf16[4,16,32,128]{3,2,1,0:T(8,128)(2,1)S(1)}, u32[]{:S(2)}, u32[]{:S(2)}) collective-permute-start(bf16[4,16,32,128]{3,2,1,0:T(8,128)(2,1)S(1)} %get-tuple-element.16), channel_id=1, source_target_pairs={{1,0},{2,1},{3,2},{4,3},{5,4},{6,5},{7,6},{8,7},{9,8},{10,9},{11,1... | collective-permute-start | bytes 1572872 | tf_op jit(solution)/shard_map/ppermute | solution.py:246
  7.5 1.9 %broadcast_in_dim.2.pot = f32[8,16,32,128]{3,2,1,0:T(8,128)} broadcast(f32[8,16,32]{2,1,0:T(8,128)S(1)} %copy-done.2), dimensions={0,1,2} | broadcast | bytes 2113536 | tf_op jit(solution)/shard_map/broadcast_in_dim | solution.py:277
  9.5 7.5 %interior_first.1.refs_1_ = f32[8,16,32,128]{3,2,1,0:T(8,128)} custom-call(bf16[8,16,32,128]{3,2,1,0:T(8,128)(2,1)} %refs_2_.1, f32[8,16,32,128]{3,2,1,0:T(8,128)} %broadcast_in_dim.2.pot), custom_call_target="tpu_custom_call" | custom-call | tf_op jit(solution)/shard_map/interior_first/pallas_call | solution.py:124
  17.0 1.1 %pad_maximum_fusion.refs_0_ = bf16[8,16,32,128]{3,2,1,0:T(8,128)(2,1)} fusion(bf16[4,16,32,128]{3,2,1,0:T(8,128)(2,1)S(1)} %collective-permute-done.1, bf16[4,16,32,128]{3,2,1,0:T(8,128)(2,1)S(1)} %collective-permute-done), kind=kLoop, calls=%fused_computation.2 | loop fusion | flops 524288 | bytes 2097152 | tf_op jit(solution)/shard_map/concatenate | solution.py:133
  18.0 3.9 %finish_first.1 = (bf16[8,16,32,128]{3,2,1,0:T(8,128)(2,1)}, bf16[4,16,32,128]{3,2,1,0:T(8,128)(2,1)}, bf16[4,16,32,128]{3,2,1,0:T(8,128)(2,1)}) custom-call(bf16[8,16,32,128]{3,2,1,0:T(8,128)(2,1)} %pad_maximum_fusion.refs_0_, f32[8,16,32,128]{3,2,1,0:T(8,128)} %interior_first.1.refs_1_), custom_call_target="tpu_custom_call" | custom-call | tf_op jit(solution)/shard_map/finish_first/pallas_call | solution.py:146
  22.0 2.3 %collective-permute-start.2 = (bf16[4,16,32,128]{3,2,1,0:T(8,128)(2,1)}, bf16[4,16,32,128]{3,2,1,0:T(8,128)(2,1)S(1)}, u32[]{:S(2)}, u32[]{:S(2)}) collective-permute-start(bf16[4,16,32,128]{3,2,1,0:T(8,128)(2,1)} %get-tuple-element.9), channel_id=1, source_target_pairs={{0,1},{1,2},{2,3},{3,4},{4,5},{5,6},{6,7},{7,8},{8,9},{9,10},{10,1... | collective-permute-start | bytes 1572872 | tf_op jit(solution)/shard_map/ppermute | solution.py:246
  24.3 2.1 %collective-permute-start.3 = (bf16[4,16,32,128]{3,2,1,0:T(8,128)(2,1)}, bf16[4,16,32,128]{3,2,1,0:T(8,128)(2,1)S(1)}, u32[]{:S(2)}, u32[]{:S(2)}) collective-permute-start(bf16[4,16,32,128]{3,2,1,0:T(8,128)(2,1)} %get-tuple-element.10), channel_id=1, source_target_pairs={{1,0},{2,1},{3,2},{4,3},{5,4},{6,5},{7,6},{8,7},{9,8},{10,9},{11,1... | collective-permute-start | bytes 1572872 | tf_op jit(solution)/shard_map/ppermute | solution.py:246
  26.4 7.5 %interior_filtered.1.refs_1_ = f32[8,16,32,128]{3,2,1,0:T(8,128)} custom-call(bf16[8,16,32,128]{3,2,1,0:T(8,128)(2,1)} %get-tuple-element.11.own_narrow, f32[8,16,32,128]{3,2,1,0:T(8,128)} %broadcast_in_dim.2.pot), custom_call_target="tpu_custom_call" | custom-call | tf_op jit(solution)/shard_map/interior_filtered/pallas_call | solution.py:124
  33.9 1.1 %pad_maximum_fusion.1.refs_0_ = bf16[8,16,32,128]{3,2,1,0:T(8,128)(2,1)} fusion(bf16[4,16,32,128]{3,2,1,0:T(8,128)(2,1)S(1)} %collective-permute-done.3, bf16[4,16,32,128]{3,2,1,0:T(8,128)(2,1)S(1)} %collective-permute-done.2), kind=kLoop, calls=%fused_computation.3 | loop fusion | flops 524288 | bytes 2097152 | tf_op jit(solution)/shard_map/concatenate | solution.py:133
  35.1 4.3 %finish_filtered.1 = (bf16[8,16,32,128]{3,2,1,0:T(8,128)(2,1)}, bf16[4,16,32,128]{3,2,1,0:T(8,128)(2,1)}, bf16[4,16,32,128]{3,2,1,0:T(8,128)(2,1)}) custom-call(bf16[8,16,32,128]{3,2,1,0:T(8,128)(2,1)} %pad_maximum_fusion.1.refs_0_, f32[8,16,32,128]{3,2,1,0:T(8,128)} %interior_filtered.1.refs_1_, bf16[8,16,32,128]{3,2,1,0:T(8,128)(2,1)} %refs_2_.1), custom_call_target="tpu_custom_call" | custom-call | tf_op jit(solution)/shard_map/finish_filtered/pallas_call | solution.py:146
  39.3 1.9 %collective-permute-start.4 = (bf16[4096,128]{1,0:T(8,128)(2,1)}, bf16[4096,128]{1,0:T(8,128)(2,1)S(1)}, u32[]{:S(2)}, u32[]{:S(2)}) collective-permute-start(bf16[4096,128]{1,0:T(8,128)(2,1)} %bitcast.18), channel_id=1, source_target_pairs={{0,16},{16,0},{1,17},{17,1},{2,18},{18,2},{3,19},{19,3},{4,20},{20... | collective-permute-start | bytes 3145736 | tf_op jit(solution)/shard_map/ppermute | solution.py:299
  41.3 4.2 %collective-permute-start.11 = (bf16[4,16,32,128]{3,2,1,0:T(8,128)(2,1)}, bf16[4,16,32,128]{3,2,1,0:T(8,128)(2,1)S(1)}, u32[]{:S(2)}, u32[]{:S(2)}) collective-permute-start(bf16[4,16,32,128]{3,2,1,0:T(8,128)(2,1)} %get-tuple-element.13), channel_id=1, source_target_pairs={{0,1},{1,2},{2,3},{3,4},{4,5},{5,6},{6,7},{7,8},{8,9},{9,10},{10,1... | collective-permute-start | bytes 1572872 | tf_op jit(solution)/shard_map/ppermute | solution.py:246
  45.7 7.5 %interior_applied.1.refs_1_ = f32[8,16,32,128]{3,2,1,0:T(8,128)} custom-call(bf16[8,16,32,128]{3,2,1,0:T(8,128)(2,1)} %get-tuple-element.6.own_narrow, f32[8,16,32,128]{3,2,1,0:T(8,128)} %broadcast_in_dim.2.pot), custom_call_target="tpu_custom_call" | custom-call | tf_op jit(solution)/shard_map/interior_applied/pallas_call | solution.py:124
  53.7 1.1 %pad_maximum_fusion.2.refs_0_ = bf16[8,16,32,128]{3,2,1,0:T(8,128)(2,1)} fusion(bf16[4,16,32,128]{3,2,1,0:T(8,128)(2,1)S(1)} %collective-permute-done.12, bf16[4,16,32,128]{3,2,1,0:T(8,128)(2,1)S(1)} %collective-permute-done.11), kind=kLoop, calls=%fused_computation.4 | loop fusion | flops 524288 | bytes 2097152 | tf_op jit(solution)/shard_map/concatenate | solution.py:133
  54.8 3.5 %finish_applied.1 = bf16[8,16,32,128]{3,2,1,0:T(8,128)(2,1)} custom-call(bf16[8,16,32,128]{3,2,1,0:T(8,128)(2,1)} %pad_maximum_fusion.2.refs_0_, f32[8,16,32,128]{3,2,1,0:T(8,128)} %interior_applied.1.refs_1_), custom_call_target="tpu_custom_call" | custom-call | tf_op jit(solution)/shard_map/finish_applied/pallas_call | solution.py:146
  58.3 1.8 %convolution_bitcast_fusion = f32[128,128]{1,0:T(8,128)S(1)} fusion(bf16[8,16,32,128]{3,2,1,0:T(8,128)(2,1)} %finish_applied.1, bf16[8,16,32,128]{3,2,1,0:T(8,128)(2,1)S(1)} %copy-done), kind=kOutput, calls=%fused_computation | convolution fusion | flops 134217728 | bytes 2162688 | tf_op jit(solution)/shard_map/cb,ck->bk/dot_general | solution.py:282
  60.0 1.6 %collective-permute-done.4 = bf16[4096,128]{1,0:T(8,128)(2,1)S(1)} collective-permute-done((bf16[4096,128]{1,0:T(8,128)(2,1)}, bf16[4096,128]{1,0:T(8,128)(2,1)S(1)}, u32[]{:S(2)}, u32[]{:S(2)}) %collective-permute-start.4) | collective-permute-done | bytes 1048608 | tf_op jit(solution)/shard_map/ppermute | solution.py:299
  62.1 3.9 %collective-permute-start.13 = (f32[64,256]{1,0:T(8,128)S(1)}, f32[64,256]{1,0:T(8,128)S(1)}, u32[]{:S(2)}, u32[]{:S(2)}) collective-permute-start(f32[64,256]{1,0:T(8,128)S(1)} %constant_dynamic-slice_fusion.1), channel_id=1, source_target_pairs={{0,1},{1,0},{2,3},{3,2},{4,5},{5,4},{6,7},{7,6},{8,9},{9,8},{10,11... | collective-permute-start | bytes 196616 | tf_op jit(solution)/shard_map/ppermute | solution.py:259
  67.9 2.2 %collective-permute-start.6 = (f32[32,256]{1,0:T(8,128)S(1)}, f32[32,256]{1,0:T(8,128)S(1)}, u32[]{:S(2)}, u32[]{:S(2)}) collective-permute-start(f32[32,256]{1,0:T(8,128)S(1)} %constant_dynamic-slice_fusion.2), channel_id=1, source_target_pairs={{0,8},{1,9},{2,10},{3,11},{4,12},{5,13},{6,14},{7,15},{8,0},{9,1},... | collective-permute-start | bytes 98312 | tf_op jit(solution)/shard_map/ppermute | solution.py:259
  70.0 2.1 %collective-permute-done.14 = f32[32,256]{1,0:T(8,128)S(1)} collective-permute-done((f32[32,256]{1,0:T(8,128)S(1)}, f32[32,256]{1,0:T(8,128)S(1)}, u32[]{:S(2)}, u32[]{:S(2)}) %collective-permute-start.14) | collective-permute-done | bytes 32800 | tf_op jit(solution)/shard_map/ppermute | solution.py:259
  72.8 2.1 %collective-permute-start.7 = (f32[32,256]{1,0:T(8,128)S(1)}, f32[32,256]{1,0:T(8,128)S(1)}, u32[]{:S(2)}, u32[]{:S(2)}) collective-permute-start(f32[32,256]{1,0:T(8,128)S(1)} %dynamic-slice_add_fusion.3), channel_id=1, source_target_pairs={{0,4},{1,5},{2,6},{3,7},{4,0},{5,1},{6,2},{7,3},{8,12},{9,13},{10,... | collective-permute-start | bytes 98312 | tf_op jit(solution)/shard_map/ppermute | solution.py:262
  74.8 1.2 %collective-permute-done.15 = f32[32,256]{1,0:T(8,128)S(1)} collective-permute-done((f32[32,256]{1,0:T(8,128)S(1)}, f32[32,256]{1,0:T(8,128)S(1)}, u32[]{:S(2)}, u32[]{:S(2)}) %collective-permute-start.15) | collective-permute-done | bytes 32800 | tf_op jit(solution)/shard_map/ppermute | solution.py:262
  76.1 1.4 %collective-permute-start.16 = (f32[32,256]{1,0:T(8,128)S(1)}, f32[32,256]{1,0:T(8,128)S(1)}, u32[]{:S(2)}, u32[]{:S(2)}) collective-permute-start(f32[32,256]{1,0:T(8,128)S(1)} %add.67), channel_id=1, source_target_pairs={{0,2},{1,3},{2,0},{3,1},{4,6},{5,7},{6,4},{7,5},{8,10},{9,11},{10,... | collective-permute-start | bytes 98312 | tf_op jit(solution)/shard_map/ppermute | solution.py:262
  77.5 1.8 %collective-permute-start.8 = (f32[32,256]{1,0:T(8,128)S(1)}, f32[32,256]{1,0:T(8,128)S(1)}, u32[]{:S(2)}, u32[]{:S(2)}) collective-permute-start(f32[32,256]{1,0:T(8,128)S(1)} %add.63), channel_id=1, source_target_pairs={{0,2},{1,3},{2,0},{3,1},{4,6},{5,7},{6,4},{7,5},{8,10},{9,11},{10,... | collective-permute-start | bytes 98312 | tf_op jit(solution)/shard_map/ppermute | solution.py:262
  79.3 0.7 collective-permute-done.16
  80.0 1.8 %collective-permute-start.17 = (f32[32,256]{1,0:T(8,128)S(1)}, f32[32,256]{1,0:T(8,128)S(1)}, u32[]{:S(2)}, u32[]{:S(2)}) collective-permute-start(f32[32,256]{1,0:T(8,128)S(1)} %add.68), channel_id=1, source_target_pairs={{0,8},{1,9},{2,10},{3,11},{4,12},{5,13},{6,14},{7,15},{8,0},{9,1},... | collective-permute-start | bytes 98312 | tf_op jit(solution)/shard_map/ppermute | solution.py:266
  81.8 1.8 %collective-permute-start.9 = (f32[32,256]{1,0:T(8,128)S(1)}, f32[32,256]{1,0:T(8,128)S(1)}, u32[]{:S(2)}, u32[]{:S(2)}) collective-permute-start(f32[32,256]{1,0:T(8,128)S(1)} %add.64), channel_id=1, source_target_pairs={{0,8},{1,9},{2,10},{3,11},{4,12},{5,13},{6,14},{7,15},{8,0},{9,1},... | collective-permute-start | bytes 98312 | tf_op jit(solution)/shard_map/ppermute | solution.py:266
  83.6 1.3 %collective-permute-done.17 = f32[32,256]{1,0:T(8,128)S(1)} collective-permute-done((f32[32,256]{1,0:T(8,128)S(1)}, f32[32,256]{1,0:T(8,128)S(1)}, u32[]{:S(2)}, u32[]{:S(2)}) %collective-permute-start.17) | collective-permute-done | bytes 32800 | tf_op jit(solution)/shard_map/ppermute | solution.py:266
  85.0 1.7 %collective-permute-done.9 = f32[32,256]{1,0:T(8,128)S(1)} collective-permute-done((f32[32,256]{1,0:T(8,128)S(1)}, f32[32,256]{1,0:T(8,128)S(1)}, u32[]{:S(2)}, u32[]{:S(2)}) %collective-permute-start.9) | collective-permute-done | bytes 32800 | tf_op jit(solution)/shard_map/ppermute | solution.py:266
  86.8 0.7 fusion.1
  88.0 0.7 fusion
  (45 shorter events, 5.0 us)
Async XLA Ops:
  0.6 6.9 %copy-start.2 = (f32[8,16,32]{2,1,0:T(8,128)S(1)}, f32[8,16,32]{2,1,0:T(8,128)}, u32[]{:S(2)}) copy-start(f32[8,16,32]{2,1,0:T(8,128)} %param.3) | copy-start | bytes 49156
  2.0 15.0 %collective-permute-start = (bf16[4,16,32,128]{3,2,1,0:T(8,128)(2,1)S(1)}, bf16[4,16,32,128]{3,2,1,0:T(8,128)(2,1)S(1)}, u32[]{:S(2)}, u32[]{:S(2)}) collective-permute-start(bf16[4,16,32,128]{3,2,1,0:T(8,128)(2,1)S(1)} %get-tuple-element.15), channel_id=1, source_target_pairs={{0,1},{1,2},{2,3},{3,4},{4,5},{5,6},{6,7},{7,8},{8,9},{9,10},{10,1... | collective-permute-start | bytes 1572872 | tf_op jit(solution)/shard_map/ppermute | solution.py:246
  2.5 14.5 %collective-permute-start.1 = (bf16[4,16,32,128]{3,2,1,0:T(8,128)(2,1)S(1)}, bf16[4,16,32,128]{3,2,1,0:T(8,128)(2,1)S(1)}, u32[]{:S(2)}, u32[]{:S(2)}) collective-permute-start(bf16[4,16,32,128]{3,2,1,0:T(8,128)(2,1)S(1)} %get-tuple-element.16), channel_id=1, source_target_pairs={{1,0},{2,1},{3,2},{4,3},{5,4},{6,5},{7,6},{8,7},{9,8},{10,9},{11,1... | collective-permute-start | bytes 1572872 | tf_op jit(solution)/shard_map/ppermute | solution.py:246
  22.0 11.9 %collective-permute-start.2 = (bf16[4,16,32,128]{3,2,1,0:T(8,128)(2,1)}, bf16[4,16,32,128]{3,2,1,0:T(8,128)(2,1)S(1)}, u32[]{:S(2)}, u32[]{:S(2)}) collective-permute-start(bf16[4,16,32,128]{3,2,1,0:T(8,128)(2,1)} %get-tuple-element.9), channel_id=1, source_target_pairs={{0,1},{1,2},{2,3},{3,4},{4,5},{5,6},{6,7},{7,8},{8,9},{9,10},{10,1... | collective-permute-start | bytes 1572872 | tf_op jit(solution)/shard_map/ppermute | solution.py:246
  24.3 9.6 %collective-permute-start.3 = (bf16[4,16,32,128]{3,2,1,0:T(8,128)(2,1)}, bf16[4,16,32,128]{3,2,1,0:T(8,128)(2,1)S(1)}, u32[]{:S(2)}, u32[]{:S(2)}) collective-permute-start(bf16[4,16,32,128]{3,2,1,0:T(8,128)(2,1)} %get-tuple-element.10), channel_id=1, source_target_pairs={{1,0},{2,1},{3,2},{4,3},{5,4},{6,5},{7,6},{8,7},{9,8},{10,9},{11,1... | collective-permute-start | bytes 1572872 | tf_op jit(solution)/shard_map/ppermute | solution.py:246
  39.3 22.3 %collective-permute-start.4 = (bf16[4096,128]{1,0:T(8,128)(2,1)}, bf16[4096,128]{1,0:T(8,128)(2,1)S(1)}, u32[]{:S(2)}, u32[]{:S(2)}) collective-permute-start(bf16[4096,128]{1,0:T(8,128)(2,1)} %bitcast.18), channel_id=1, source_target_pairs={{0,16},{16,0},{1,17},{17,1},{2,18},{18,2},{3,19},{19,3},{4,20},{20... | collective-permute-start | bytes 3145736 | tf_op jit(solution)/shard_map/ppermute | solution.py:299
  41.3 12.4 %collective-permute-start.11 = (bf16[4,16,32,128]{3,2,1,0:T(8,128)(2,1)}, bf16[4,16,32,128]{3,2,1,0:T(8,128)(2,1)S(1)}, u32[]{:S(2)}, u32[]{:S(2)}) collective-permute-start(bf16[4,16,32,128]{3,2,1,0:T(8,128)(2,1)} %get-tuple-element.13), channel_id=1, source_target_pairs={{0,1},{1,2},{2,3},{3,4},{4,5},{5,6},{6,7},{7,8},{8,9},{9,10},{10,1... | collective-permute-start | bytes 1572872 | tf_op jit(solution)/shard_map/ppermute | solution.py:246
  45.4 8.3 %collective-permute-start.12 = (bf16[4,16,32,128]{3,2,1,0:T(8,128)(2,1)}, bf16[4,16,32,128]{3,2,1,0:T(8,128)(2,1)S(1)}, u32[]{:S(2)}, u32[]{:S(2)}) collective-permute-start(bf16[4,16,32,128]{3,2,1,0:T(8,128)(2,1)} %get-tuple-element.14), channel_id=1, source_target_pairs={{1,0},{2,1},{3,2},{4,3},{5,4},{6,5},{7,6},{8,7},{9,8},{10,9},{11,1... | collective-permute-start | bytes 1572872 | tf_op jit(solution)/shard_map/ppermute | solution.py:246
  45.7 7.5 %copy-start = (bf16[8,16,32,128]{3,2,1,0:T(8,128)(2,1)S(1)}, bf16[8,16,32,128]{3,2,1,0:T(8,128)(2,1)}, u32[]{:S(2)}) copy-start(bf16[8,16,32,128]{3,2,1,0:T(8,128)(2,1)} %get-tuple-element.6.own_narrow) | copy-start | bytes 3145732
  58.3 3.4 %copy-start.1 = (bf16[8,16,32,128]{3,2,1,0:T(8,128)(2,1)S(1)}, bf16[8,16,32,128]{3,2,1,0:T(8,128)(2,1)}, u32[]{:S(2)}) copy-start(bf16[8,16,32,128]{3,2,1,0:T(8,128)(2,1)} %finish_applied.1) | copy-start | bytes 3145732
  62.1 4.8 %collective-permute-start.13 = (f32[64,256]{1,0:T(8,128)S(1)}, f32[64,256]{1,0:T(8,128)S(1)}, u32[]{:S(2)}, u32[]{:S(2)}) collective-permute-start(f32[64,256]{1,0:T(8,128)S(1)} %constant_dynamic-slice_fusion.1), channel_id=1, source_target_pairs={{0,1},{1,0},{2,3},{3,2},{4,5},{5,4},{6,7},{7,6},{8,9},{9,8},{10,11... | collective-permute-start | bytes 196616 | tf_op jit(solution)/shard_map/ppermute | solution.py:259
  66.5 1.3 %collective-permute-start.5 = (f32[64,256]{1,0:T(8,128)S(1)}, f32[64,256]{1,0:T(8,128)S(1)}, u32[]{:S(2)}, u32[]{:S(2)}) collective-permute-start(f32[64,256]{1,0:T(8,128)S(1)} %constant_dynamic-slice_fusion.3), channel_id=1, source_target_pairs={{0,1},{1,0},{2,3},{3,2},{4,5},{5,4},{6,7},{7,6},{8,9},{9,8},{10,11... | collective-permute-start | bytes 196616 | tf_op jit(solution)/shard_map/ppermute | solution.py:259
  66.9 5.2 %collective-permute-start.14 = (f32[32,256]{1,0:T(8,128)S(1)}, f32[32,256]{1,0:T(8,128)S(1)}, u32[]{:S(2)}, u32[]{:S(2)}) collective-permute-start(f32[32,256]{1,0:T(8,128)S(1)} %constant_dynamic-slice_fusion), channel_id=1, source_target_pairs={{0,8},{1,9},{2,10},{3,11},{4,12},{5,13},{6,14},{7,15},{8,0},{9,1},... | collective-permute-start | bytes 98312 | tf_op jit(solution)/shard_map/ppermute | solution.py:259
  67.9 4.9 %collective-permute-start.6 = (f32[32,256]{1,0:T(8,128)S(1)}, f32[32,256]{1,0:T(8,128)S(1)}, u32[]{:S(2)}, u32[]{:S(2)}) collective-permute-start(f32[32,256]{1,0:T(8,128)S(1)} %constant_dynamic-slice_fusion.2), channel_id=1, source_target_pairs={{0,8},{1,9},{2,10},{3,11},{4,12},{5,13},{6,14},{7,15},{8,0},{9,1},... | collective-permute-start | bytes 98312 | tf_op jit(solution)/shard_map/ppermute | solution.py:259
  72.2 3.9 %collective-permute-start.15 = (f32[32,256]{1,0:T(8,128)S(1)}, f32[32,256]{1,0:T(8,128)S(1)}, u32[]{:S(2)}, u32[]{:S(2)}) collective-permute-start(f32[32,256]{1,0:T(8,128)S(1)} %dynamic-slice_add_fusion.2), channel_id=1, source_target_pairs={{0,4},{1,5},{2,6},{3,7},{4,0},{5,1},{6,2},{7,3},{8,12},{9,13},{10,... | collective-permute-start | bytes 98312 | tf_op jit(solution)/shard_map/ppermute | solution.py:262
  72.8 4.7 %collective-permute-start.7 = (f32[32,256]{1,0:T(8,128)S(1)}, f32[32,256]{1,0:T(8,128)S(1)}, u32[]{:S(2)}, u32[]{:S(2)}) collective-permute-start(f32[32,256]{1,0:T(8,128)S(1)} %dynamic-slice_add_fusion.3), channel_id=1, source_target_pairs={{0,4},{1,5},{2,6},{3,7},{4,0},{5,1},{6,2},{7,3},{8,12},{9,13},{10,... | collective-permute-start | bytes 98312 | tf_op jit(solution)/shard_map/ppermute | solution.py:262
  76.1 3.9 %collective-permute-start.16 = (f32[32,256]{1,0:T(8,128)S(1)}, f32[32,256]{1,0:T(8,128)S(1)}, u32[]{:S(2)}, u32[]{:S(2)}) collective-permute-start(f32[32,256]{1,0:T(8,128)S(1)} %add.67), channel_id=1, source_target_pairs={{0,2},{1,3},{2,0},{3,1},{4,6},{5,7},{6,4},{7,5},{8,10},{9,11},{10,... | collective-permute-start | bytes 98312 | tf_op jit(solution)/shard_map/ppermute | solution.py:262
  77.5 4.3 %collective-permute-start.8 = (f32[32,256]{1,0:T(8,128)S(1)}, f32[32,256]{1,0:T(8,128)S(1)}, u32[]{:S(2)}, u32[]{:S(2)}) collective-permute-start(f32[32,256]{1,0:T(8,128)S(1)} %add.63), channel_id=1, source_target_pairs={{0,2},{1,3},{2,0},{3,1},{4,6},{5,7},{6,4},{7,5},{8,10},{9,11},{10,... | collective-permute-start | bytes 98312 | tf_op jit(solution)/shard_map/ppermute | solution.py:262
  80.0 4.9 %collective-permute-start.17 = (f32[32,256]{1,0:T(8,128)S(1)}, f32[32,256]{1,0:T(8,128)S(1)}, u32[]{:S(2)}, u32[]{:S(2)}) collective-permute-start(f32[32,256]{1,0:T(8,128)S(1)} %add.68), channel_id=1, source_target_pairs={{0,8},{1,9},{2,10},{3,11},{4,12},{5,13},{6,14},{7,15},{8,0},{9,1},... | collective-permute-start | bytes 98312 | tf_op jit(solution)/shard_map/ppermute | solution.py:266
  81.8 4.9 %collective-permute-start.9 = (f32[32,256]{1,0:T(8,128)S(1)}, f32[32,256]{1,0:T(8,128)S(1)}, u32[]{:S(2)}, u32[]{:S(2)}) collective-permute-start(f32[32,256]{1,0:T(8,128)S(1)} %add.64), channel_id=1, source_target_pairs={{0,8},{1,9},{2,10},{3,11},{4,12},{5,13},{6,14},{7,15},{8,0},{9,1},... | collective-permute-start | bytes 98312 | tf_op jit(solution)/shard_map/ppermute | solution.py:266
  84.9 1.9 %collective-permute-start.18 = (f32[64,256]{1,0:T(8,128)S(1)}, f32[64,256]{1,0:T(8,128)S(1)}, u32[]{:S(2)}, u32[]{:S(2)}) collective-permute-start(f32[64,256]{1,0:T(8,128)S(1)} %maximum_select_fusion.5), channel_id=1, source_target_pairs={{0,1},{1,0},{2,3},{3,2},{4,5},{5,4},{6,7},{7,6},{8,9},{9,8},{10,11... | collective-permute-start | bytes 196616 | tf_op jit(solution)/shard_map/ppermute | solution.py:266
  86.7 1.3 %collective-permute-start.10 = (f32[64,256]{1,0:T(8,128)S(1)}, f32[64,256]{1,0:T(8,128)S(1)}, u32[]{:S(2)}, u32[]{:S(2)}) collective-permute-start(f32[64,256]{1,0:T(8,128)S(1)} %maximum_select_fusion.4), channel_id=1, source_target_pairs={{0,1},{1,0},{2,3},{3,2},{4,5},{5,4},{6,7},{7,6},{8,9},{9,8},{10,11... | collective-permute-start | bytes 196616 | tf_op jit(solution)/shard_map/ppermute | solution.py:266

commit v24 on v22

--- a/solution.py
+++ b/solution.py
@@ -246,7 +246,7 @@
     return lax.ppermute(sends[0], axis, forward), lax.ppermute(sends[1], axis, backward)
 
 
-def butterfly_sum(values, axis):
+def butterfly_sum(values, axis, far_first=True):
     count = lax.axis_size(axis)
     index = lax.axis_index(axis)
     pairs_of = lambda bit: [(i, i ^ bit) for i in range(count)]
@@ -255,10 +255,13 @@
     keep = lax.dynamic_slice_in_dim(values, upper * half, half, axis=0)
     send = lax.dynamic_slice_in_dim(values, (1 - upper) * half, half, axis=0)
     values = keep + lax.ppermute(send, axis, pairs_of(1))
+    bits = []
     bit = count // 2
     while bit >= 2:
+        bits.append(bit)
+        bit //= 2
+    for bit in bits if far_first else reversed(bits):
         values = values + lax.ppermute(values, axis, pairs_of(bit))
-        bit //= 2
     other = lax.ppermute(values, axis, pairs_of(1))
     return jnp.where(
         upper == 0,
@@ -293,7 +296,7 @@
     own_block = filtered.reshape(cell_count, nb)
     partner = lax.ppermute(own_block, "band", [(0, 1), (1, 0)])
     correlation_piece = placed(gram(own_block, own_block), gram(own_block, partner))
-    correlation = butterfly_sum(correlation_piece, "domain") * cell_weight
+    correlation = butterfly_sum(correlation_piece, "domain", far_first=False) * cell_weight
     (applied_grid,) = stencil_stage(
         "applied", filtered, filtered_sent, potential_wide, keep_sends=False
     )

time: 87 us -> 87 us (level)
  waiting for transfers between devices: 15.5 us -> 13.5 us
  starting transfers between devices: 25.1 us -> 27 us
    ppermute x6, waiting for transfers between devices: 12.7 us -> 10.7 us  [butterfly_sum(): values = values + lax.ppermute(values, axis, pairs_of(bit))]
    ppermute x6, starting transfers between devices: 4.66 us -> 6.58 us  [butterfly_sum(): values = values + lax.ppermute(values, axis, pairs_of(bit))]
  transfers between devices with their start and end apart: 17 -> 17, of which waited for: 11 -> 9; matrix products, arithmetic and copies ran while one was open for 8% -> 8% of each run, Pallas kernels for 30% -> 30%
where the time goes in v24:
time: 87 us; the launch traced here: 86.8 us
  Pallas kernels  34.2 us (39%)
  starting transfers between devices  27 us (31%)
  waiting for transfers between devices  13.5 us (16%)
  other arithmetic  4.68 us (5%)
  local copies, waits for them, and re-layouts  3.31 us (4%)
  matrix products  3.22 us (4%)
    pallas_call x3, Pallas kernels, stencil_stage(): pl.pallas_call(interior_kernel(stage, planes, ny, nz), grid=(blocks,), in...  22.5 us
    pallas_call x3, Pallas kernels, stencil_stage(): pl.pallas_call(finish_kernel(stage, planes, ny), grid=(blocks,), in_specs...  11.7 us
    ppermute x6, waiting for transfers between devices, butterfly_sum(): values = values + lax.ppermute(values, axis, pairs_of(bit))  10.7 us
    ppermute x3, starting transfers between devices, exchange(): lax.ppermute(sends[1], axis, backward)  7.38 us
    ppermute x3, starting transfers between devices, exchange(): lax.ppermute(sends[0], axis, forward)  7.04 us
    ppermute x6, starting transfers between devices, butterfly_sum(): values = values + lax.ppermute(values, axis, pairs_of(bit))  6.58 us
    ppermute x2, starting transfers between devices, butterfly_sum(): values = keep + lax.ppermute(send, axis, pairs_of(1))  3.94 us
    concatenate x3, other arithmetic, stencil_stage(): halos = jnp.concatenate([low, high], axis=0)  3.24 us
  transfers between devices with their start and end apart: 17, of which 9 were waited for; matrix products, arithmetic and copies ran while one was open for 8% of the time, Pallas kernels for 30%

profile of v24, /device:TPU:0, one launch (start us, length us, event | category | flops | bytes accessed | tf_op | source)
XLA Modules:
  0.0 86.8 jit_solution(14532515786962938054)
XLA Ops:
  0.6 1.3 %fusion.2 = (bf16[4,16,32,128]{3,2,1,0:T(8,128)(2,1)S(1)}, bf16[4,16,32,128]{3,2,1,0:T(8,128)(2,1)S(1)}) fusion(bf16[8,16,32,128]{3,2,1,0:T(8,128)(2,1)} %refs_2_.1), kind=kLoop, calls=%fused_computation.15 | loop fusion | bytes 2097152 | tf_op jit(solution)/shard_map/slice | solution.py:289
  2.0 0.5 collective-permute-start
  2.5 5.0 %collective-permute-start.1 = (bf16[4,16,32,128]{3,2,1,0:T(8,128)(2,1)S(1)}, bf16[4,16,32,128]{3,2,1,0:T(8,128)(2,1)S(1)}, u32[]{:S(2)}, u32[]{:S(2)}) collective-permute-start(bf16[4,16,32,128]{3,2,1,0:T(8,128)(2,1)S(1)} %get-tuple-element.16), channel_id=1, source_target_pairs={{1,0},{2,1},{3,2},{4,3},{5,4},{6,5},{7,6},{8,7},{9,8},{10,9},{11,1... | collective-permute-start | bytes 1572872 | tf_op jit(solution)/shard_map/ppermute | solution.py:246
  7.5 1.9 %broadcast_in_dim.2.pot = f32[8,16,32,128]{3,2,1,0:T(8,128)} broadcast(f32[8,16,32]{2,1,0:T(8,128)S(1)} %copy-done.2), dimensions={0,1,2} | broadcast | bytes 2113536 | tf_op jit(solution)/shard_map/broadcast_in_dim | solution.py:275
  9.5 7.5 %interior_first.1.refs_1_ = f32[8,16,32,128]{3,2,1,0:T(8,128)} custom-call(bf16[8,16,32,128]{3,2,1,0:T(8,128)(2,1)} %refs_2_.1, f32[8,16,32,128]{3,2,1,0:T(8,128)} %broadcast_in_dim.2.pot), custom_call_target="tpu_custom_call" | custom-call | tf_op jit(solution)/shard_map/interior_first/pallas_call | solution.py:124
  17.0 1.1 %pad_maximum_fusion.refs_0_ = bf16[8,16,32,128]{3,2,1,0:T(8,128)(2,1)} fusion(bf16[4,16,32,128]{3,2,1,0:T(8,128)(2,1)S(1)} %collective-permute-done.1, bf16[4,16,32,128]{3,2,1,0:T(8,128)(2,1)S(1)} %collective-permute-done), kind=kLoop, calls=%fused_computation.2 | loop fusion | flops 524288 | bytes 2097152 | tf_op jit(solution)/shard_map/concatenate | solution.py:133
  18.0 4.0 %finish_first.1 = (bf16[8,16,32,128]{3,2,1,0:T(8,128)(2,1)}, bf16[4,16,32,128]{3,2,1,0:T(8,128)(2,1)}, bf16[4,16,32,128]{3,2,1,0:T(8,128)(2,1)}) custom-call(bf16[8,16,32,128]{3,2,1,0:T(8,128)(2,1)} %pad_maximum_fusion.refs_0_, f32[8,16,32,128]{3,2,1,0:T(8,128)} %interior_first.1.refs_1_), custom_call_target="tpu_custom_call" | custom-call | tf_op jit(solution)/shard_map/finish_first/pallas_call | solution.py:146
  22.0 2.3 %collective-permute-start.2 = (bf16[4,16,32,128]{3,2,1,0:T(8,128)(2,1)}, bf16[4,16,32,128]{3,2,1,0:T(8,128)(2,1)S(1)}, u32[]{:S(2)}, u32[]{:S(2)}) collective-permute-start(bf16[4,16,32,128]{3,2,1,0:T(8,128)(2,1)} %get-tuple-element.9), channel_id=1, source_target_pairs={{0,1},{1,2},{2,3},{3,4},{4,5},{5,6},{6,7},{7,8},{8,9},{9,10},{10,1... | collective-permute-start | bytes 1572872 | tf_op jit(solution)/shard_map/ppermute | solution.py:246
  24.3 2.1 %collective-permute-start.3 = (bf16[4,16,32,128]{3,2,1,0:T(8,128)(2,1)}, bf16[4,16,32,128]{3,2,1,0:T(8,128)(2,1)S(1)}, u32[]{:S(2)}, u32[]{:S(2)}) collective-permute-start(bf16[4,16,32,128]{3,2,1,0:T(8,128)(2,1)} %get-tuple-element.10), channel_id=1, source_target_pairs={{1,0},{2,1},{3,2},{4,3},{5,4},{6,5},{7,6},{8,7},{9,8},{10,9},{11,1... | collective-permute-start | bytes 1572872 | tf_op jit(solution)/shard_map/ppermute | solution.py:246
  26.4 7.5 %interior_filtered.1.refs_1_ = f32[8,16,32,128]{3,2,1,0:T(8,128)} custom-call(bf16[8,16,32,128]{3,2,1,0:T(8,128)(2,1)} %get-tuple-element.11.own_narrow, f32[8,16,32,128]{3,2,1,0:T(8,128)} %broadcast_in_dim.2.pot), custom_call_target="tpu_custom_call" | custom-call | tf_op jit(solution)/shard_map/interior_filtered/pallas_call | solution.py:124
  34.0 1.1 %pad_maximum_fusion.1.refs_0_ = bf16[8,16,32,128]{3,2,1,0:T(8,128)(2,1)} fusion(bf16[4,16,32,128]{3,2,1,0:T(8,128)(2,1)S(1)} %collective-permute-done.3, bf16[4,16,32,128]{3,2,1,0:T(8,128)(2,1)S(1)} %collective-permute-done.2), kind=kLoop, calls=%fused_computation.3 | loop fusion | flops 524288 | bytes 2097152 | tf_op jit(solution)/shard_map/concatenate | solution.py:133
  35.0 4.3 %finish_filtered.1 = (bf16[8,16,32,128]{3,2,1,0:T(8,128)(2,1)}, bf16[4,16,32,128]{3,2,1,0:T(8,128)(2,1)}, bf16[4,16,32,128]{3,2,1,0:T(8,128)(2,1)}) custom-call(bf16[8,16,32,128]{3,2,1,0:T(8,128)(2,1)} %pad_maximum_fusion.1.refs_0_, f32[8,16,32,128]{3,2,1,0:T(8,128)} %interior_filtered.1.refs_1_, bf16[8,16,32,128]{3,2,1,0:T(8,128)(2,1)} %refs_2_.1), custom_call_target="tpu_custom_call" | custom-call | tf_op jit(solution)/shard_map/finish_filtered/pallas_call | solution.py:146
  39.3 1.9 %collective-permute-start.4 = (bf16[4096,128]{1,0:T(8,128)(2,1)}, bf16[4096,128]{1,0:T(8,128)(2,1)S(1)}, u32[]{:S(2)}, u32[]{:S(2)}) collective-permute-start(bf16[4096,128]{1,0:T(8,128)(2,1)} %bitcast.18), channel_id=1, source_target_pairs={{0,16},{16,0},{1,17},{17,1},{2,18},{18,2},{3,19},{19,3},{4,20},{20... | collective-permute-start | bytes 3145736 | tf_op jit(solution)/shard_map/ppermute | solution.py:297
  41.2 4.2 %collective-permute-start.10 = (bf16[4,16,32,128]{3,2,1,0:T(8,128)(2,1)}, bf16[4,16,32,128]{3,2,1,0:T(8,128)(2,1)S(1)}, u32[]{:S(2)}, u32[]{:S(2)}) collective-permute-start(bf16[4,16,32,128]{3,2,1,0:T(8,128)(2,1)} %get-tuple-element.13), channel_id=1, source_target_pairs={{0,1},{1,2},{2,3},{3,4},{4,5},{5,6},{6,7},{7,8},{8,9},{9,10},{10,1... | collective-permute-start | bytes 1572872 | tf_op jit(solution)/shard_map/ppermute | solution.py:246
  45.7 7.5 %interior_applied.1.refs_1_ = f32[8,16,32,128]{3,2,1,0:T(8,128)} custom-call(bf16[8,16,32,128]{3,2,1,0:T(8,128)(2,1)} %get-tuple-element.6.own_narrow, f32[8,16,32,128]{3,2,1,0:T(8,128)} %broadcast_in_dim.2.pot), custom_call_target="tpu_custom_call" | custom-call | tf_op jit(solution)/shard_map/interior_applied/pallas_call | solution.py:124
  53.7 1.1 %pad_maximum_fusion.2.refs_0_ = bf16[8,16,32,128]{3,2,1,0:T(8,128)(2,1)} fusion(bf16[4,16,32,128]{3,2,1,0:T(8,128)(2,1)S(1)} %collective-permute-done.11, bf16[4,16,32,128]{3,2,1,0:T(8,128)(2,1)S(1)} %collective-permute-done.10), kind=kLoop, calls=%fused_computation.4 | loop fusion | flops 524288 | bytes 2097152 | tf_op jit(solution)/shard_map/concatenate | solution.py:133
  54.8 3.5 %finish_applied.1 = bf16[8,16,32,128]{3,2,1,0:T(8,128)(2,1)} custom-call(bf16[8,16,32,128]{3,2,1,0:T(8,128)(2,1)} %pad_maximum_fusion.2.refs_0_, f32[8,16,32,128]{3,2,1,0:T(8,128)} %interior_applied.1.refs_1_), custom_call_target="tpu_custom_call" | custom-call | tf_op jit(solution)/shard_map/finish_applied/pallas_call | solution.py:146
  58.2 1.8 %convolution_bitcast_fusion = f32[128,128]{1,0:T(8,128)S(1)} fusion(bf16[8,16,32,128]{3,2,1,0:T(8,128)(2,1)} %finish_applied.1, bf16[8,16,32,128]{3,2,1,0:T(8,128)(2,1)S(1)} %copy-done), kind=kOutput, calls=%fused_computation | convolution fusion | flops 134217728 | bytes 2162688 | tf_op jit(solution)/shard_map/cb,ck->bk/dot_general | solution.py:280
  60.0 1.5 %collective-permute-done.4 = bf16[4096,128]{1,0:T(8,128)(2,1)S(1)} collective-permute-done((bf16[4096,128]{1,0:T(8,128)(2,1)}, bf16[4096,128]{1,0:T(8,128)(2,1)S(1)}, u32[]{:S(2)}, u32[]{:S(2)}) %collective-permute-start.4) | collective-permute-done | bytes 1048608 | tf_op jit(solution)/shard_map/ppermute | solution.py:297
  61.6 0.5 fusion.4
  62.1 3.9 %collective-permute-start.12 = (f32[64,256]{1,0:T(8,128)S(1)}, f32[64,256]{1,0:T(8,128)S(1)}, u32[]{:S(2)}, u32[]{:S(2)}) collective-permute-start(f32[64,256]{1,0:T(8,128)S(1)} %constant_dynamic-slice_fusion), channel_id=1, source_target_pairs={{0,1},{1,0},{2,3},{3,2},{4,5},{5,4},{6,7},{7,6},{8,9},{9,8},{10,11... | collective-permute-start | bytes 196616 | tf_op jit(solution)/shard_map/ppermute | solution.py:257
  67.8 2.2 %collective-permute-start.6 = (f32[64,256]{1,0:T(8,128)S(1)}, f32[64,256]{1,0:T(8,128)S(1)}, u32[]{:S(2)}, u32[]{:S(2)}) collective-permute-start(f32[64,256]{1,0:T(8,128)S(1)} %dynamic-slice_add_fusion.1), channel_id=1, source_target_pairs={{0,2},{1,3},{2,0},{3,1},{4,6},{5,7},{6,4},{7,5},{8,10},{9,11},{10,... | collective-permute-start | bytes 196616 | tf_op jit(solution)/shard_map/ppermute | solution.py:264
  70.0 3.3 %collective-permute-done.13 = f32[64,256]{1,0:T(8,128)S(1)} collective-permute-done((f32[64,256]{1,0:T(8,128)S(1)}, f32[64,256]{1,0:T(8,128)S(1)}, u32[]{:S(2)}, u32[]{:S(2)}) %collective-permute-start.13) | collective-permute-done | bytes 65568 | tf_op jit(solution)/shard_map/ppermute | solution.py:264
  73.4 2.1 %collective-permute-start.7 = (f32[64,256]{1,0:T(8,128)S(1)}, f32[64,256]{1,0:T(8,128)S(1)}, u32[]{:S(2)}, u32[]{:S(2)}) collective-permute-start(f32[64,256]{1,0:T(8,128)S(1)} %add.41), channel_id=1, source_target_pairs={{0,4},{1,5},{2,6},{3,7},{4,0},{5,1},{6,2},{7,3},{8,12},{9,13},{10,... | collective-permute-start | bytes 196616 | tf_op jit(solution)/shard_map/ppermute | solution.py:264
  75.5 2.6 %collective-permute-done.14 = f32[64,256]{1,0:T(8,128)S(1)} collective-permute-done((f32[64,256]{1,0:T(8,128)S(1)}, f32[64,256]{1,0:T(8,128)S(1)}, u32[]{:S(2)}, u32[]{:S(2)}) %collective-permute-start.14) | collective-permute-done | bytes 65568 | tf_op jit(solution)/shard_map/ppermute | solution.py:264
  78.2 0.6 collective-permute-done.7
  78.8 1.7 %collective-permute-start.8 = (f32[64,256]{1,0:T(8,128)S(1)}, f32[64,256]{1,0:T(8,128)S(1)}, u32[]{:S(2)}, u32[]{:S(2)}) collective-permute-start(f32[64,256]{1,0:T(8,128)S(1)} %add.42), channel_id=1, source_target_pairs={{0,8},{1,9},{2,10},{3,11},{4,12},{5,13},{6,14},{7,15},{8,0},{9,1},... | collective-permute-start | bytes 196616 | tf_op jit(solution)/shard_map/ppermute | solution.py:264
  80.6 1.9 %collective-permute-done.15 = f32[64,256]{1,0:T(8,128)S(1)} collective-permute-done((f32[64,256]{1,0:T(8,128)S(1)}, f32[64,256]{1,0:T(8,128)S(1)}, u32[]{:S(2)}, u32[]{:S(2)}) %collective-permute-start.15) | collective-permute-done | bytes 65568 | tf_op jit(solution)/shard_map/ppermute | solution.py:264
  82.6 2.2 %collective-permute-done.8 = f32[64,256]{1,0:T(8,128)S(1)} collective-permute-done((f32[64,256]{1,0:T(8,128)S(1)}, f32[64,256]{1,0:T(8,128)S(1)}, u32[]{:S(2)}, u32[]{:S(2)}) %collective-permute-start.8) | collective-permute-done | bytes 65568 | tf_op jit(solution)/shard_map/ppermute | solution.py:264
  84.9 0.7 fusion.1
  85.6 0.6 collective-permute-done.9
  86.1 0.7 fusion
  (37 shorter events, 3.0 us)
Async XLA Ops:
  0.6 6.9 %copy-start.2 = (f32[8,16,32]{2,1,0:T(8,128)S(1)}, f32[8,16,32]{2,1,0:T(8,128)}, u32[]{:S(2)}) copy-start(f32[8,16,32]{2,1,0:T(8,128)} %param.3) | copy-start | bytes 49156
  2.0 15.0 %collective-permute-start = (bf16[4,16,32,128]{3,2,1,0:T(8,128)(2,1)S(1)}, bf16[4,16,32,128]{3,2,1,0:T(8,128)(2,1)S(1)}, u32[]{:S(2)}, u32[]{:S(2)}) collective-permute-start(bf16[4,16,32,128]{3,2,1,0:T(8,128)(2,1)S(1)} %get-tuple-element.15), channel_id=1, source_target_pairs={{0,1},{1,2},{2,3},{3,4},{4,5},{5,6},{6,7},{7,8},{8,9},{9,10},{10,1... | collective-permute-start | bytes 1572872 | tf_op jit(solution)/shard_map/ppermute | solution.py:246
  2.5 14.5 %collective-permute-start.1 = (bf16[4,16,32,128]{3,2,1,0:T(8,128)(2,1)S(1)}, bf16[4,16,32,128]{3,2,1,0:T(8,128)(2,1)S(1)}, u32[]{:S(2)}, u32[]{:S(2)}) collective-permute-start(bf16[4,16,32,128]{3,2,1,0:T(8,128)(2,1)S(1)} %get-tuple-element.16), channel_id=1, source_target_pairs={{1,0},{2,1},{3,2},{4,3},{5,4},{6,5},{7,6},{8,7},{9,8},{10,9},{11,1... | collective-permute-start | bytes 1572872 | tf_op jit(solution)/shard_map/ppermute | solution.py:246
  22.0 12.0 %collective-permute-start.2 = (bf16[4,16,32,128]{3,2,1,0:T(8,128)(2,1)}, bf16[4,16,32,128]{3,2,1,0:T(8,128)(2,1)S(1)}, u32[]{:S(2)}, u32[]{:S(2)}) collective-permute-start(bf16[4,16,32,128]{3,2,1,0:T(8,128)(2,1)} %get-tuple-element.9), channel_id=1, source_target_pairs={{0,1},{1,2},{2,3},{3,4},{4,5},{5,6},{6,7},{7,8},{8,9},{9,10},{10,1... | collective-permute-start | bytes 1572872 | tf_op jit(solution)/shard_map/ppermute | solution.py:246
  24.3 9.6 %collective-permute-start.3 = (bf16[4,16,32,128]{3,2,1,0:T(8,128)(2,1)}, bf16[4,16,32,128]{3,2,1,0:T(8,128)(2,1)S(1)}, u32[]{:S(2)}, u32[]{:S(2)}) collective-permute-start(bf16[4,16,32,128]{3,2,1,0:T(8,128)(2,1)} %get-tuple-element.10), channel_id=1, source_target_pairs={{1,0},{2,1},{3,2},{4,3},{5,4},{6,5},{7,6},{8,7},{9,8},{10,9},{11,1... | collective-permute-start | bytes 1572872 | tf_op jit(solution)/shard_map/ppermute | solution.py:246
  39.3 22.3 %collective-permute-start.4 = (bf16[4096,128]{1,0:T(8,128)(2,1)}, bf16[4096,128]{1,0:T(8,128)(2,1)S(1)}, u32[]{:S(2)}, u32[]{:S(2)}) collective-permute-start(bf16[4096,128]{1,0:T(8,128)(2,1)} %bitcast.18), channel_id=1, source_target_pairs={{0,16},{16,0},{1,17},{17,1},{2,18},{18,2},{3,19},{19,3},{4,20},{20... | collective-permute-start | bytes 3145736 | tf_op jit(solution)/shard_map/ppermute | solution.py:297
  41.2 12.4 %collective-permute-start.10 = (bf16[4,16,32,128]{3,2,1,0:T(8,128)(2,1)}, bf16[4,16,32,128]{3,2,1,0:T(8,128)(2,1)S(1)}, u32[]{:S(2)}, u32[]{:S(2)}) collective-permute-start(bf16[4,16,32,128]{3,2,1,0:T(8,128)(2,1)} %get-tuple-element.13), channel_id=1, source_target_pairs={{0,1},{1,2},{2,3},{3,4},{4,5},{5,6},{6,7},{7,8},{8,9},{9,10},{10,1... | collective-permute-start | bytes 1572872 | tf_op jit(solution)/shard_map/ppermute | solution.py:246
  45.4 8.2 %collective-permute-start.11 = (bf16[4,16,32,128]{3,2,1,0:T(8,128)(2,1)}, bf16[4,16,32,128]{3,2,1,0:T(8,128)(2,1)S(1)}, u32[]{:S(2)}, u32[]{:S(2)}) collective-permute-start(bf16[4,16,32,128]{3,2,1,0:T(8,128)(2,1)} %get-tuple-element.14), channel_id=1, source_target_pairs={{1,0},{2,1},{3,2},{4,3},{5,4},{6,5},{7,6},{8,7},{9,8},{10,9},{11,1... | collective-permute-start | bytes 1572872 | tf_op jit(solution)/shard_map/ppermute | solution.py:246
  45.7 7.5 %copy-start = (bf16[8,16,32,128]{3,2,1,0:T(8,128)(2,1)S(1)}, bf16[8,16,32,128]{3,2,1,0:T(8,128)(2,1)}, u32[]{:S(2)}) copy-start(bf16[8,16,32,128]{3,2,1,0:T(8,128)(2,1)} %get-tuple-element.6.own_narrow) | copy-start | bytes 3145732
  58.2 3.3 %copy-start.1 = (bf16[8,16,32,128]{3,2,1,0:T(8,128)(2,1)S(1)}, bf16[8,16,32,128]{3,2,1,0:T(8,128)(2,1)}, u32[]{:S(2)}) copy-start(bf16[8,16,32,128]{3,2,1,0:T(8,128)(2,1)} %finish_applied.1) | copy-start | bytes 3145732
  62.1 4.8 %collective-permute-start.12 = (f32[64,256]{1,0:T(8,128)S(1)}, f32[64,256]{1,0:T(8,128)S(1)}, u32[]{:S(2)}, u32[]{:S(2)}) collective-permute-start(f32[64,256]{1,0:T(8,128)S(1)} %constant_dynamic-slice_fusion), channel_id=1, source_target_pairs={{0,1},{1,0},{2,3},{3,2},{4,5},{5,4},{6,7},{7,6},{8,9},{9,8},{10,11... | collective-permute-start | bytes 196616 | tf_op jit(solution)/shard_map/ppermute | solution.py:257
  66.5 1.3 %collective-permute-start.5 = (f32[64,256]{1,0:T(8,128)S(1)}, f32[64,256]{1,0:T(8,128)S(1)}, u32[]{:S(2)}, u32[]{:S(2)}) collective-permute-start(f32[64,256]{1,0:T(8,128)S(1)} %constant_dynamic-slice_fusion.1), channel_id=1, source_target_pairs={{0,1},{1,0},{2,3},{3,2},{4,5},{5,4},{6,7},{7,6},{8,9},{9,8},{10,11... | collective-permute-start | bytes 196616 | tf_op jit(solution)/shard_map/ppermute | solution.py:257
  66.9 6.4 %collective-permute-start.13 = (f32[64,256]{1,0:T(8,128)S(1)}, f32[64,256]{1,0:T(8,128)S(1)}, u32[]{:S(2)}, u32[]{:S(2)}) collective-permute-start(f32[64,256]{1,0:T(8,128)S(1)} %dynamic-slice_add_fusion), channel_id=1, source_target_pairs={{0,8},{1,9},{2,10},{3,11},{4,12},{5,13},{6,14},{7,15},{8,0},{9,1},... | collective-permute-start | bytes 196616 | tf_op jit(solution)/shard_map/ppermute | solution.py:264
  67.8 5.6 %collective-permute-start.6 = (f32[64,256]{1,0:T(8,128)S(1)}, f32[64,256]{1,0:T(8,128)S(1)}, u32[]{:S(2)}, u32[]{:S(2)}) collective-permute-start(f32[64,256]{1,0:T(8,128)S(1)} %dynamic-slice_add_fusion.1), channel_id=1, source_target_pairs={{0,2},{1,3},{2,0},{3,1},{4,6},{5,7},{6,4},{7,5},{8,10},{9,11},{10,... | collective-permute-start | bytes 196616 | tf_op jit(solution)/shard_map/ppermute | solution.py:264
  73.3 4.8 %collective-permute-start.14 = (f32[64,256]{1,0:T(8,128)S(1)}, f32[64,256]{1,0:T(8,128)S(1)}, u32[]{:S(2)}, u32[]{:S(2)}) collective-permute-start(f32[64,256]{1,0:T(8,128)S(1)} %add.45), channel_id=1, source_target_pairs={{0,4},{1,5},{2,6},{3,7},{4,0},{5,1},{6,2},{7,3},{8,12},{9,13},{10,... | collective-permute-start | bytes 196616 | tf_op jit(solution)/shard_map/ppermute | solution.py:264
  73.4 5.4 %collective-permute-start.7 = (f32[64,256]{1,0:T(8,128)S(1)}, f32[64,256]{1,0:T(8,128)S(1)}, u32[]{:S(2)}, u32[]{:S(2)}) collective-permute-start(f32[64,256]{1,0:T(8,128)S(1)} %add.41), channel_id=1, source_target_pairs={{0,4},{1,5},{2,6},{3,7},{4,0},{5,1},{6,2},{7,3},{8,12},{9,13},{10,... | collective-permute-start | bytes 196616 | tf_op jit(solution)/shard_map/ppermute | solution.py:264
  78.1 4.3 %collective-permute-start.15 = (f32[64,256]{1,0:T(8,128)S(1)}, f32[64,256]{1,0:T(8,128)S(1)}, u32[]{:S(2)}, u32[]{:S(2)}) collective-permute-start(f32[64,256]{1,0:T(8,128)S(1)} %add.46), channel_id=1, source_target_pairs={{0,2},{1,3},{2,0},{3,1},{4,6},{5,7},{6,4},{7,5},{8,10},{9,11},{10,... | collective-permute-start | bytes 196616 | tf_op jit(solution)/shard_map/ppermute | solution.py:264
  78.8 5.9 %collective-permute-start.8 = (f32[64,256]{1,0:T(8,128)S(1)}, f32[64,256]{1,0:T(8,128)S(1)}, u32[]{:S(2)}, u32[]{:S(2)}) collective-permute-start(f32[64,256]{1,0:T(8,128)S(1)} %add.42), channel_id=1, source_target_pairs={{0,8},{1,9},{2,10},{3,11},{4,12},{5,13},{6,14},{7,15},{8,0},{9,1},... | collective-permute-start | bytes 196616 | tf_op jit(solution)/shard_map/ppermute | solution.py:264
  82.5 2.4 %collective-permute-start.16 = (f32[64,256]{1,0:T(8,128)S(1)}, f32[64,256]{1,0:T(8,128)S(1)}, u32[]{:S(2)}, u32[]{:S(2)}) collective-permute-start(f32[64,256]{1,0:T(8,128)S(1)} %add.47), channel_id=1, source_target_pairs={{0,1},{1,0},{2,3},{3,2},{4,5},{5,4},{6,7},{7,6},{8,9},{9,8},{10,11... | collective-permute-start | bytes 196616 | tf_op jit(solution)/shard_map/ppermute | solution.py:265
  84.8 1.3 %collective-permute-start.9 = (f32[64,256]{1,0:T(8,128)S(1)}, f32[64,256]{1,0:T(8,128)S(1)}, u32[]{:S(2)}, u32[]{:S(2)}) collective-permute-start(f32[64,256]{1,0:T(8,128)S(1)} %add.43), channel_id=1, source_target_pairs={{0,1},{1,0},{2,3},{3,2},{4,5},{5,4},{6,7},{7,6},{8,9},{9,8},{10,11... | collective-permute-start | bytes 196616 | tf_op jit(solution)/shard_map/ppermute | solution.py:265

commit v25 on v22

--- a/solution.py
+++ b/solution.py
@@ -255,10 +255,13 @@
     keep = lax.dynamic_slice_in_dim(values, upper * half, half, axis=0)
     send = lax.dynamic_slice_in_dim(values, (1 - upper) * half, half, axis=0)
     values = keep + lax.ppermute(send, axis, pairs_of(1))
+    bits = []
     bit = count // 2
     while bit >= 2:
+        bits.append(bit)
+        bit //= 2
+    for bit in bits[:1] + bits[1:][::-1]:
         values = values + lax.ppermute(values, axis, pairs_of(bit))
-        bit //= 2
     other = lax.ppermute(values, axis, pairs_of(1))
     return jnp.where(
         upper == 0,

time: 87 us -> 87 us (level)
  no operation moved by 1% of the time
where the time goes in v25:
time: 87 us; the launch traced here: 86.9 us
  Pallas kernels  34.2 us (39%)
  starting transfers between devices  25.1 us (29%)
  waiting for transfers between devices  15.5 us (18%)
  other arithmetic  4.68 us (5%)
  local copies, waits for them, and re-layouts  3.31 us (4%)
  matrix products  3.22 us (4%)
    pallas_call x3, Pallas kernels, stencil_stage(): pl.pallas_call(interior_kernel(stage, planes, ny, nz), grid=(blocks,), in...  22.5 us
    ppermute x6, waiting for transfers between devices, butterfly_sum(): values = values + lax.ppermute(values, axis, pairs_of(bit))  12.7 us
    pallas_call x3, Pallas kernels, stencil_stage(): pl.pallas_call(finish_kernel(stage, planes, ny), grid=(blocks,), in_specs...  11.7 us
    ppermute x3, starting transfers between devices, exchange(): lax.ppermute(sends[1], axis, backward)  7.38 us
    ppermute x3, starting transfers between devices, exchange(): lax.ppermute(sends[0], axis, forward)  7.04 us
    ppermute x6, starting transfers between devices, butterfly_sum(): values = values + lax.ppermute(values, axis, pairs_of(bit))  4.66 us
    ppermute x2, starting transfers between devices, butterfly_sum(): values = keep + lax.ppermute(send, axis, pairs_of(1))  3.94 us
    concatenate x3, other arithmetic, stencil_stage(): halos = jnp.concatenate([low, high], axis=0)  3.24 us
  transfers between devices with their start and end apart: 17, of which 11 were waited for; matrix products, arithmetic and copies ran while one was open for 8% of the time, Pallas kernels for 30%

profile of v25, /device:TPU:0, one launch (start us, length us, event | category | flops | bytes accessed | tf_op | source)
XLA Modules:
  0.0 86.9 jit_solution(16680172794955114257)
XLA Ops:
  0.6 1.3 %fusion.2 = (bf16[4,16,32,128]{3,2,1,0:T(8,128)(2,1)S(1)}, bf16[4,16,32,128]{3,2,1,0:T(8,128)(2,1)S(1)}) fusion(bf16[8,16,32,128]{3,2,1,0:T(8,128)(2,1)} %refs_2_.1), kind=kLoop, calls=%fused_computation.15 | loop fusion | bytes 2097152 | tf_op jit(solution)/shard_map/slice | solution.py:289
  2.0 0.5 collective-permute-start
  2.5 5.0 %collective-permute-start.1 = (bf16[4,16,32,128]{3,2,1,0:T(8,128)(2,1)S(1)}, bf16[4,16,32,128]{3,2,1,0:T(8,128)(2,1)S(1)}, u32[]{:S(2)}, u32[]{:S(2)}) collective-permute-start(bf16[4,16,32,128]{3,2,1,0:T(8,128)(2,1)S(1)} %get-tuple-element.16), channel_id=1, source_target_pairs={{1,0},{2,1},{3,2},{4,3},{5,4},{6,5},{7,6},{8,7},{9,8},{10,9},{11,1... | collective-permute-start | bytes 1572872 | tf_op jit(solution)/shard_map/ppermute | solution.py:246
  7.5 1.9 %broadcast_in_dim.2.pot = f32[8,16,32,128]{3,2,1,0:T(8,128)} broadcast(f32[8,16,32]{2,1,0:T(8,128)S(1)} %copy-done.2), dimensions={0,1,2} | broadcast | bytes 2113536 | tf_op jit(solution)/shard_map/broadcast_in_dim | solution.py:275
  9.5 7.5 %interior_first.1.refs_1_ = f32[8,16,32,128]{3,2,1,0:T(8,128)} custom-call(bf16[8,16,32,128]{3,2,1,0:T(8,128)(2,1)} %refs_2_.1, f32[8,16,32,128]{3,2,1,0:T(8,128)} %broadcast_in_dim.2.pot), custom_call_target="tpu_custom_call" | custom-call | tf_op jit(solution)/shard_map/interior_first/pallas_call | solution.py:124
  17.0 1.1 %pad_maximum_fusion.refs_0_ = bf16[8,16,32,128]{3,2,1,0:T(8,128)(2,1)} fusion(bf16[4,16,32,128]{3,2,1,0:T(8,128)(2,1)S(1)} %collective-permute-done.1, bf16[4,16,32,128]{3,2,1,0:T(8,128)(2,1)S(1)} %collective-permute-done), kind=kLoop, calls=%fused_computation.2 | loop fusion | flops 524288 | bytes 2097152 | tf_op jit(solution)/shard_map/concatenate | solution.py:133
  18.0 4.0 %finish_first.1 = (bf16[8,16,32,128]{3,2,1,0:T(8,128)(2,1)}, bf16[4,16,32,128]{3,2,1,0:T(8,128)(2,1)}, bf16[4,16,32,128]{3,2,1,0:T(8,128)(2,1)}) custom-call(bf16[8,16,32,128]{3,2,1,0:T(8,128)(2,1)} %pad_maximum_fusion.refs_0_, f32[8,16,32,128]{3,2,1,0:T(8,128)} %interior_first.1.refs_1_), custom_call_target="tpu_custom_call" | custom-call | tf_op jit(solution)/shard_map/finish_first/pallas_call | solution.py:146
  22.0 2.3 %collective-permute-start.2 = (bf16[4,16,32,128]{3,2,1,0:T(8,128)(2,1)}, bf16[4,16,32,128]{3,2,1,0:T(8,128)(2,1)S(1)}, u32[]{:S(2)}, u32[]{:S(2)}) collective-permute-start(bf16[4,16,32,128]{3,2,1,0:T(8,128)(2,1)} %get-tuple-element.9), channel_id=1, source_target_pairs={{0,1},{1,2},{2,3},{3,4},{4,5},{5,6},{6,7},{7,8},{8,9},{9,10},{10,1... | collective-permute-start | bytes 1572872 | tf_op jit(solution)/shard_map/ppermute | solution.py:246
  24.3 2.1 %collective-permute-start.3 = (bf16[4,16,32,128]{3,2,1,0:T(8,128)(2,1)}, bf16[4,16,32,128]{3,2,1,0:T(8,128)(2,1)S(1)}, u32[]{:S(2)}, u32[]{:S(2)}) collective-permute-start(bf16[4,16,32,128]{3,2,1,0:T(8,128)(2,1)} %get-tuple-element.10), channel_id=1, source_target_pairs={{1,0},{2,1},{3,2},{4,3},{5,4},{6,5},{7,6},{8,7},{9,8},{10,9},{11,1... | collective-permute-start | bytes 1572872 | tf_op jit(solution)/shard_map/ppermute | solution.py:246
  26.4 7.5 %interior_filtered.1.refs_1_ = f32[8,16,32,128]{3,2,1,0:T(8,128)} custom-call(bf16[8,16,32,128]{3,2,1,0:T(8,128)(2,1)} %get-tuple-element.11.own_narrow, f32[8,16,32,128]{3,2,1,0:T(8,128)} %broadcast_in_dim.2.pot), custom_call_target="tpu_custom_call" | custom-call | tf_op jit(solution)/shard_map/interior_filtered/pallas_call | solution.py:124
  34.0 1.1 %pad_maximum_fusion.1.refs_0_ = bf16[8,16,32,128]{3,2,1,0:T(8,128)(2,1)} fusion(bf16[4,16,32,128]{3,2,1,0:T(8,128)(2,1)S(1)} %collective-permute-done.3, bf16[4,16,32,128]{3,2,1,0:T(8,128)(2,1)S(1)} %collective-permute-done.2), kind=kLoop, calls=%fused_computation.3 | loop fusion | flops 524288 | bytes 2097152 | tf_op jit(solution)/shard_map/concatenate | solution.py:133
  35.0 4.3 %finish_filtered.1 = (bf16[8,16,32,128]{3,2,1,0:T(8,128)(2,1)}, bf16[4,16,32,128]{3,2,1,0:T(8,128)(2,1)}, bf16[4,16,32,128]{3,2,1,0:T(8,128)(2,1)}) custom-call(bf16[8,16,32,128]{3,2,1,0:T(8,128)(2,1)} %pad_maximum_fusion.1.refs_0_, f32[8,16,32,128]{3,2,1,0:T(8,128)} %interior_filtered.1.refs_1_, bf16[8,16,32,128]{3,2,1,0:T(8,128)(2,1)} %refs_2_.1), custom_call_target="tpu_custom_call" | custom-call | tf_op jit(solution)/shard_map/finish_filtered/pallas_call | solution.py:146
  39.3 1.9 %collective-permute-start.4 = (bf16[4096,128]{1,0:T(8,128)(2,1)}, bf16[4096,128]{1,0:T(8,128)(2,1)S(1)}, u32[]{:S(2)}, u32[]{:S(2)}) collective-permute-start(bf16[4096,128]{1,0:T(8,128)(2,1)} %bitcast.18), channel_id=1, source_target_pairs={{0,16},{16,0},{1,17},{17,1},{2,18},{18,2},{3,19},{19,3},{4,20},{20... | collective-permute-start | bytes 3145736 | tf_op jit(solution)/shard_map/ppermute | solution.py:297
  41.2 4.2 %collective-permute-start.10 = (bf16[4,16,32,128]{3,2,1,0:T(8,128)(2,1)}, bf16[4,16,32,128]{3,2,1,0:T(8,128)(2,1)S(1)}, u32[]{:S(2)}, u32[]{:S(2)}) collective-permute-start(bf16[4,16,32,128]{3,2,1,0:T(8,128)(2,1)} %get-tuple-element.13), channel_id=1, source_target_pairs={{0,1},{1,2},{2,3},{3,4},{4,5},{5,6},{6,7},{7,8},{8,9},{9,10},{10,1... | collective-permute-start | bytes 1572872 | tf_op jit(solution)/shard_map/ppermute | solution.py:246
  45.7 7.5 %interior_applied.1.refs_1_ = f32[8,16,32,128]{3,2,1,0:T(8,128)} custom-call(bf16[8,16,32,128]{3,2,1,0:T(8,128)(2,1)} %get-tuple-element.6.own_narrow, f32[8,16,32,128]{3,2,1,0:T(8,128)} %broadcast_in_dim.2.pot), custom_call_target="tpu_custom_call" | custom-call | tf_op jit(solution)/shard_map/interior_applied/pallas_call | solution.py:124
  53.7 1.1 %pad_maximum_fusion.2.refs_0_ = bf16[8,16,32,128]{3,2,1,0:T(8,128)(2,1)} fusion(bf16[4,16,32,128]{3,2,1,0:T(8,128)(2,1)S(1)} %collective-permute-done.11, bf16[4,16,32,128]{3,2,1,0:T(8,128)(2,1)S(1)} %collective-permute-done.10), kind=kLoop, calls=%fused_computation.4 | loop fusion | flops 524288 | bytes 2097152 | tf_op jit(solution)/shard_map/concatenate | solution.py:133
  54.8 3.5 %finish_applied.1 = bf16[8,16,32,128]{3,2,1,0:T(8,128)(2,1)} custom-call(bf16[8,16,32,128]{3,2,1,0:T(8,128)(2,1)} %pad_maximum_fusion.2.refs_0_, f32[8,16,32,128]{3,2,1,0:T(8,128)} %interior_applied.1.refs_1_), custom_call_target="tpu_custom_call" | custom-call | tf_op jit(solution)/shard_map/finish_applied/pallas_call | solution.py:146
  58.2 1.8 %convolution_bitcast_fusion = f32[128,128]{1,0:T(8,128)S(1)} fusion(bf16[8,16,32,128]{3,2,1,0:T(8,128)(2,1)} %finish_applied.1, bf16[8,16,32,128]{3,2,1,0:T(8,128)(2,1)S(1)} %copy-done), kind=kOutput, calls=%fused_computation | convolution fusion | flops 134217728 | bytes 2162688 | tf_op jit(solution)/shard_map/cb,ck->bk/dot_general | solution.py:280
  60.0 1.5 %collective-permute-done.4 = bf16[4096,128]{1,0:T(8,128)(2,1)S(1)} collective-permute-done((bf16[4096,128]{1,0:T(8,128)(2,1)}, bf16[4096,128]{1,0:T(8,128)(2,1)S(1)}, u32[]{:S(2)}, u32[]{:S(2)}) %collective-permute-start.4) | collective-permute-done | bytes 1048608 | tf_op jit(solution)/shard_map/ppermute | solution.py:297
  61.6 0.5 fusion.4
  62.1 3.9 %collective-permute-start.12 = (f32[64,256]{1,0:T(8,128)S(1)}, f32[64,256]{1,0:T(8,128)S(1)}, u32[]{:S(2)}, u32[]{:S(2)}) collective-permute-start(f32[64,256]{1,0:T(8,128)S(1)} %constant_dynamic-slice_fusion), channel_id=1, source_target_pairs={{0,1},{1,0},{2,3},{3,2},{4,5},{5,4},{6,7},{7,6},{8,9},{9,8},{10,11... | collective-permute-start | bytes 196616 | tf_op jit(solution)/shard_map/ppermute | solution.py:257
  67.8 2.1 %collective-permute-start.6 = (f32[64,256]{1,0:T(8,128)S(1)}, f32[64,256]{1,0:T(8,128)S(1)}, u32[]{:S(2)}, u32[]{:S(2)}) collective-permute-start(f32[64,256]{1,0:T(8,128)S(1)} %dynamic-slice_add_fusion.1), channel_id=1, source_target_pairs={{0,8},{1,9},{2,10},{3,11},{4,12},{5,13},{6,14},{7,15},{8,0},{9,1},... | collective-permute-start | bytes 196616 | tf_op jit(solution)/shard_map/ppermute | solution.py:264
  69.9 4.8 %collective-permute-done.13 = f32[64,256]{1,0:T(8,128)S(1)} collective-permute-done((f32[64,256]{1,0:T(8,128)S(1)}, f32[64,256]{1,0:T(8,128)S(1)}, u32[]{:S(2)}, u32[]{:S(2)}) %collective-permute-start.13) | collective-permute-done | bytes 65568 | tf_op jit(solution)/shard_map/ppermute | solution.py:264
  74.8 1.3 %collective-permute-done.6 = f32[64,256]{1,0:T(8,128)S(1)} collective-permute-done((f32[64,256]{1,0:T(8,128)S(1)}, f32[64,256]{1,0:T(8,128)S(1)}, u32[]{:S(2)}, u32[]{:S(2)}) %collective-permute-start.6) | collective-permute-done | bytes 65568 | tf_op jit(solution)/shard_map/ppermute | solution.py:264
  76.1 0.8 collective-permute-start.7
  76.9 2.5 %collective-permute-done.14 = f32[64,256]{1,0:T(8,128)S(1)} collective-permute-done((f32[64,256]{1,0:T(8,128)S(1)}, f32[64,256]{1,0:T(8,128)S(1)}, u32[]{:S(2)}, u32[]{:S(2)}) %collective-permute-start.14) | collective-permute-done | bytes 65568 | tf_op jit(solution)/shard_map/ppermute | solution.py:264
  79.5 1.0 %collective-permute-done.7 = f32[64,256]{1,0:T(8,128)S(1)} collective-permute-done((f32[64,256]{1,0:T(8,128)S(1)}, f32[64,256]{1,0:T(8,128)S(1)}, u32[]{:S(2)}, u32[]{:S(2)}) %collective-permute-start.7) | collective-permute-done | bytes 65568 | tf_op jit(solution)/shard_map/ppermute | solution.py:264
  80.5 1.1 %collective-permute-start.8 = (f32[64,256]{1,0:T(8,128)S(1)}, f32[64,256]{1,0:T(8,128)S(1)}, u32[]{:S(2)}, u32[]{:S(2)}) collective-permute-start(f32[64,256]{1,0:T(8,128)S(1)} %add.42), channel_id=1, source_target_pairs={{0,4},{1,5},{2,6},{3,7},{4,0},{5,1},{6,2},{7,3},{8,12},{9,13},{10,... | collective-permute-start | bytes 196616 | tf_op jit(solution)/shard_map/ppermute | solution.py:264
  81.6 2.4 %collective-permute-done.15 = f32[64,256]{1,0:T(8,128)S(1)} collective-permute-done((f32[64,256]{1,0:T(8,128)S(1)}, f32[64,256]{1,0:T(8,128)S(1)}, u32[]{:S(2)}, u32[]{:S(2)}) %collective-permute-start.15) | collective-permute-done | bytes 65568 | tf_op jit(solution)/shard_map/ppermute | solution.py:264
  84.2 0.7 collective-permute-done.8
  85.4 0.7 fusion.1
  86.2 0.7 fusion
  (37 shorter events, 3.5 us)
Async XLA Ops:
  0.6 6.9 %copy-start.2 = (f32[8,16,32]{2,1,0:T(8,128)S(1)}, f32[8,16,32]{2,1,0:T(8,128)}, u32[]{:S(2)}) copy-start(f32[8,16,32]{2,1,0:T(8,128)} %param.3) | copy-start | bytes 49156
  2.0 15.0 %collective-permute-start = (bf16[4,16,32,128]{3,2,1,0:T(8,128)(2,1)S(1)}, bf16[4,16,32,128]{3,2,1,0:T(8,128)(2,1)S(1)}, u32[]{:S(2)}, u32[]{:S(2)}) collective-permute-start(bf16[4,16,32,128]{3,2,1,0:T(8,128)(2,1)S(1)} %get-tuple-element.15), channel_id=1, source_target_pairs={{0,1},{1,2},{2,3},{3,4},{4,5},{5,6},{6,7},{7,8},{8,9},{9,10},{10,1... | collective-permute-start | bytes 1572872 | tf_op jit(solution)/shard_map/ppermute | solution.py:246
  2.5 14.5 %collective-permute-start.1 = (bf16[4,16,32,128]{3,2,1,0:T(8,128)(2,1)S(1)}, bf16[4,16,32,128]{3,2,1,0:T(8,128)(2,1)S(1)}, u32[]{:S(2)}, u32[]{:S(2)}) collective-permute-start(bf16[4,16,32,128]{3,2,1,0:T(8,128)(2,1)S(1)} %get-tuple-element.16), channel_id=1, source_target_pairs={{1,0},{2,1},{3,2},{4,3},{5,4},{6,5},{7,6},{8,7},{9,8},{10,9},{11,1... | collective-permute-start | bytes 1572872 | tf_op jit(solution)/shard_map/ppermute | solution.py:246
  22.0 12.0 %collective-permute-start.2 = (bf16[4,16,32,128]{3,2,1,0:T(8,128)(2,1)}, bf16[4,16,32,128]{3,2,1,0:T(8,128)(2,1)S(1)}, u32[]{:S(2)}, u32[]{:S(2)}) collective-permute-start(bf16[4,16,32,128]{3,2,1,0:T(8,128)(2,1)} %get-tuple-element.9), channel_id=1, source_target_pairs={{0,1},{1,2},{2,3},{3,4},{4,5},{5,6},{6,7},{7,8},{8,9},{9,10},{10,1... | collective-permute-start | bytes 1572872 | tf_op jit(solution)/shard_map/ppermute | solution.py:246
  24.3 9.6 %collective-permute-start.3 = (bf16[4,16,32,128]{3,2,1,0:T(8,128)(2,1)}, bf16[4,16,32,128]{3,2,1,0:T(8,128)(2,1)S(1)}, u32[]{:S(2)}, u32[]{:S(2)}) collective-permute-start(bf16[4,16,32,128]{3,2,1,0:T(8,128)(2,1)} %get-tuple-element.10), channel_id=1, source_target_pairs={{1,0},{2,1},{3,2},{4,3},{5,4},{6,5},{7,6},{8,7},{9,8},{10,9},{11,1... | collective-permute-start | bytes 1572872 | tf_op jit(solution)/shard_map/ppermute | solution.py:246
  39.3 22.3 %collective-permute-start.4 = (bf16[4096,128]{1,0:T(8,128)(2,1)}, bf16[4096,128]{1,0:T(8,128)(2,1)S(1)}, u32[]{:S(2)}, u32[]{:S(2)}) collective-permute-start(bf16[4096,128]{1,0:T(8,128)(2,1)} %bitcast.18), channel_id=1, source_target_pairs={{0,16},{16,0},{1,17},{17,1},{2,18},{18,2},{3,19},{19,3},{4,20},{20... | collective-permute-start | bytes 3145736 | tf_op jit(solution)/shard_map/ppermute | solution.py:297
  41.2 12.4 %collective-permute-start.10 = (bf16[4,16,32,128]{3,2,1,0:T(8,128)(2,1)}, bf16[4,16,32,128]{3,2,1,0:T(8,128)(2,1)S(1)}, u32[]{:S(2)}, u32[]{:S(2)}) collective-permute-start(bf16[4,16,32,128]{3,2,1,0:T(8,128)(2,1)} %get-tuple-element.13), channel_id=1, source_target_pairs={{0,1},{1,2},{2,3},{3,4},{4,5},{5,6},{6,7},{7,8},{8,9},{9,10},{10,1... | collective-permute-start | bytes 1572872 | tf_op jit(solution)/shard_map/ppermute | solution.py:246
  45.4 8.2 %collective-permute-start.11 = (bf16[4,16,32,128]{3,2,1,0:T(8,128)(2,1)}, bf16[4,16,32,128]{3,2,1,0:T(8,128)(2,1)S(1)}, u32[]{:S(2)}, u32[]{:S(2)}) collective-permute-start(bf16[4,16,32,128]{3,2,1,0:T(8,128)(2,1)} %get-tuple-element.14), channel_id=1, source_target_pairs={{1,0},{2,1},{3,2},{4,3},{5,4},{6,5},{7,6},{8,7},{9,8},{10,9},{11,1... | collective-permute-start | bytes 1572872 | tf_op jit(solution)/shard_map/ppermute | solution.py:246
  45.7 7.5 %copy-start = (bf16[8,16,32,128]{3,2,1,0:T(8,128)(2,1)S(1)}, bf16[8,16,32,128]{3,2,1,0:T(8,128)(2,1)}, u32[]{:S(2)}) copy-start(bf16[8,16,32,128]{3,2,1,0:T(8,128)(2,1)} %get-tuple-element.6.own_narrow) | copy-start | bytes 3145732
  58.2 3.3 %copy-start.1 = (bf16[8,16,32,128]{3,2,1,0:T(8,128)(2,1)S(1)}, bf16[8,16,32,128]{3,2,1,0:T(8,128)(2,1)}, u32[]{:S(2)}) copy-start(bf16[8,16,32,128]{3,2,1,0:T(8,128)(2,1)} %finish_applied.1) | copy-start | bytes 3145732
  62.1 4.8 %collective-permute-start.12 = (f32[64,256]{1,0:T(8,128)S(1)}, f32[64,256]{1,0:T(8,128)S(1)}, u32[]{:S(2)}, u32[]{:S(2)}) collective-permute-start(f32[64,256]{1,0:T(8,128)S(1)} %constant_dynamic-slice_fusion), channel_id=1, source_target_pairs={{0,1},{1,0},{2,3},{3,2},{4,5},{5,4},{6,7},{7,6},{8,9},{9,8},{10,11... | collective-permute-start | bytes 196616 | tf_op jit(solution)/shard_map/ppermute | solution.py:257
  66.5 1.3 %collective-permute-start.5 = (f32[64,256]{1,0:T(8,128)S(1)}, f32[64,256]{1,0:T(8,128)S(1)}, u32[]{:S(2)}, u32[]{:S(2)}) collective-permute-start(f32[64,256]{1,0:T(8,128)S(1)} %constant_dynamic-slice_fusion.1), channel_id=1, source_target_pairs={{0,1},{1,0},{2,3},{3,2},{4,5},{5,4},{6,7},{7,6},{8,9},{9,8},{10,11... | collective-permute-start | bytes 196616 | tf_op jit(solution)/shard_map/ppermute | solution.py:257
  66.9 7.9 %collective-permute-start.13 = (f32[64,256]{1,0:T(8,128)S(1)}, f32[64,256]{1,0:T(8,128)S(1)}, u32[]{:S(2)}, u32[]{:S(2)}) collective-permute-start(f32[64,256]{1,0:T(8,128)S(1)} %dynamic-slice_add_fusion), channel_id=1, source_target_pairs={{0,8},{1,9},{2,10},{3,11},{4,12},{5,13},{6,14},{7,15},{8,0},{9,1},... | collective-permute-start | bytes 196616 | tf_op jit(solution)/shard_map/ppermute | solution.py:264
  67.8 8.3 %collective-permute-start.6 = (f32[64,256]{1,0:T(8,128)S(1)}, f32[64,256]{1,0:T(8,128)S(1)}, u32[]{:S(2)}, u32[]{:S(2)}) collective-permute-start(f32[64,256]{1,0:T(8,128)S(1)} %dynamic-slice_add_fusion.1), channel_id=1, source_target_pairs={{0,8},{1,9},{2,10},{3,11},{4,12},{5,13},{6,14},{7,15},{8,0},{9,1},... | collective-permute-start | bytes 196616 | tf_op jit(solution)/shard_map/ppermute | solution.py:264
  74.8 4.7 %collective-permute-start.14 = (f32[64,256]{1,0:T(8,128)S(1)}, f32[64,256]{1,0:T(8,128)S(1)}, u32[]{:S(2)}, u32[]{:S(2)}) collective-permute-start(f32[64,256]{1,0:T(8,128)S(1)} %add.45), channel_id=1, source_target_pairs={{0,2},{1,3},{2,0},{3,1},{4,6},{5,7},{6,4},{7,5},{8,10},{9,11},{10,... | collective-permute-start | bytes 196616 | tf_op jit(solution)/shard_map/ppermute | solution.py:264
  76.1 4.4 %collective-permute-start.7 = (f32[64,256]{1,0:T(8,128)S(1)}, f32[64,256]{1,0:T(8,128)S(1)}, u32[]{:S(2)}, u32[]{:S(2)}) collective-permute-start(f32[64,256]{1,0:T(8,128)S(1)} %add.41), channel_id=1, source_target_pairs={{0,2},{1,3},{2,0},{3,1},{4,6},{5,7},{6,4},{7,5},{8,10},{9,11},{10,... | collective-permute-start | bytes 196616 | tf_op jit(solution)/shard_map/ppermute | solution.py:264
  79.5 4.6 %collective-permute-start.15 = (f32[64,256]{1,0:T(8,128)S(1)}, f32[64,256]{1,0:T(8,128)S(1)}, u32[]{:S(2)}, u32[]{:S(2)}) collective-permute-start(f32[64,256]{1,0:T(8,128)S(1)} %add.46), channel_id=1, source_target_pairs={{0,4},{1,5},{2,6},{3,7},{4,0},{5,1},{6,2},{7,3},{8,12},{9,13},{10,... | collective-permute-start | bytes 196616 | tf_op jit(solution)/shard_map/ppermute | solution.py:264
  80.5 4.3 %collective-permute-start.8 = (f32[64,256]{1,0:T(8,128)S(1)}, f32[64,256]{1,0:T(8,128)S(1)}, u32[]{:S(2)}, u32[]{:S(2)}) collective-permute-start(f32[64,256]{1,0:T(8,128)S(1)} %add.42), channel_id=1, source_target_pairs={{0,4},{1,5},{2,6},{3,7},{4,0},{5,1},{6,2},{7,3},{8,12},{9,13},{10,... | collective-permute-start | bytes 196616 | tf_op jit(solution)/shard_map/ppermute | solution.py:264
  84.1 1.3 %collective-permute-start.16 = (f32[64,256]{1,0:T(8,128)S(1)}, f32[64,256]{1,0:T(8,128)S(1)}, u32[]{:S(2)}, u32[]{:S(2)}) collective-permute-start(f32[64,256]{1,0:T(8,128)S(1)} %add.47), channel_id=1, source_target_pairs={{0,1},{1,0},{2,3},{3,2},{4,5},{5,4},{6,7},{7,6},{8,9},{9,8},{10,11... | collective-permute-start | bytes 196616 | tf_op jit(solution)/shard_map/ppermute | solution.py:265
  84.9 1.3 %collective-permute-start.9 = (f32[64,256]{1,0:T(8,128)S(1)}, f32[64,256]{1,0:T(8,128)S(1)}, u32[]{:S(2)}, u32[]{:S(2)}) collective-permute-start(f32[64,256]{1,0:T(8,128)S(1)} %add.43), channel_id=1, source_target_pairs={{0,1},{1,0},{2,3},{3,2},{4,5},{5,4},{6,7},{7,6},{8,9},{9,8},{10,11... | collective-permute-start | bytes 196616 | tf_op jit(solution)/shard_map/ppermute | solution.py:265
